TPU v7x, 32 devices: a whole 2x2x4 slice. The times are simulated.
32 devices in a mesh: ax: 4 (over z), circ: 8 (over y, x, core).
Axes of the slice: x: 2, y: 2, z: 4, core: 2. Of those that a mesh axis runs over, the one named last changes fastest.
Arguments:
- displacement: bfloat16 [64, 512, 6, 256], P('ax', 'circ'), may hold values from -6 to 6
- stiffness: bfloat16 [64, 512, 324], P('ax', 'circ'), may hold values from -0.875 to 0.875
- kernel: bfloat16 [128, 12, 2, 256, 256], P(('ax', 'circ')), may hold values from -0.109375 to 0.109375
- areas: float32 [32768], P(('ax', 'circ')), may hold values from 0.25 to 4
- near_cells: int32 [128, 12], P(('ax', 'circ')), may hold values from 0 to 15, all different within a row
- source_owner: int32 [131072, 1], P(('ax', 'circ')), may hold values from 0 to 7; in each aligned block of 4096 rows (0 to 4095, 4096 to 8191, ...) at most 1280 rows name the same one
- source_node: int32 [131072], P(('ax', 'circ')), may hold values from 0 to 1023
- target_owner: int32 [32768, 1], P(('ax', 'circ')), may hold values from 0 to 7; in each aligned block of 1024 rows (0 to 1023, 1024 to 2047, ...) at most 320 rows name the same one
- target_node: int32 [32768], P(('ax', 'circ')), may hold values from 0 to 1023
Outputs:
- shell_force: float32 [64, 512, 6, 256], P('ax', 'circ')
- pressure: float32 [2, 32768, 256], P(None, ('ax', 'circ'))
Inputs may be any that keep to these rules, and one draw needn't show every extreme that they name: `source_owner`: in the rows of one device no sector is named by more than 1280 rows. `target_owner`: in the rows of one device no sector is named by more than 320 rows. `near_cells`: the 12 entries of a row are distinct.
All inputs are finite; a program needn't handle non-finite values.
Results may differ from a plain program's by a relative error of at most 0.0019.
Values may be sent and summed in bfloat16 or wider, within the bound.
No kernel may reach another device: no remote copies, remote signals or barrier semaphores. Data moves between devices by JAX's collectives and lax.ppermute only.
A program may use at most 256 MiB of HBM per device.

v0:
```python
import jax
import jax.numpy as jnp
from jax import lax
from jax.experimental import pallas as pl
from jax.experimental.pallas import tpu as pltpu
from jax.sharding import PartitionSpec as P


def extended(cells, sides, width):
    for axis, dim in sides:
        count = lax.axis_size(axis)
        head = lax.slice_in_dim(cells, 0, width, axis=dim)
        tail = lax.slice_in_dim(cells, cells.shape[dim] - width, cells.shape[dim], axis=dim)
        cells = jnp.concatenate(
            [
                lax.ppermute(tail, axis, [(i, (i + 1) % count) for i in range(count)]),
                cells,
                lax.ppermute(head, axis, [((i + 1) % count, i) for i in range(count)]),
            ],
            axis=dim,
        )
    return cells


def slot_positions(owners, sectors, capacity):
    onehot = (owners[:, None] == jnp.arange(sectors, dtype=jnp.int32)[None, :]).astype(jnp.int32)
    before = jnp.cumsum(onehot, axis=0) - onehot
    ranking = jnp.sum(before * onehot, axis=1)
    return owners * capacity + ranking


def pressure_kernel(near_ref, kern_ref, vel_ref, area_ref, p_ref, load_ref):
    g = pl.program_id(0)
    near_count = kern_ref.shape[1]
    panel = kern_ref.shape[3]
    for n in range(near_count):
        m = near_ref[g, n]
        w = kern_ref[0, n].reshape(2 * panel, panel)
        prod = jnp.dot(w, vel_ref[m], preferred_element_type=jnp.float32)
        if n == 0:
            p_ref[...] = prod.reshape(p_ref.shape)
        else:
            p_ref[...] += prod.reshape(p_ref.shape)
    load_ref[...] = (area_ref[...] * p_ref[0]).astype(load_ref.dtype)


def near_field(kernel, source_cells, areas, near_cells):
    cells_dev, near_count, _, panel, _ = kernel.shape
    src_cells, _, vectors = source_cells.shape
    targets = cells_dev * panel
    grid_spec = pltpu.PrefetchScalarGridSpec(
        num_scalar_prefetch=1,
        grid=(cells_dev,),
        in_specs=[
            pl.BlockSpec((1, near_count, 2, panel, panel), lambda g, near: (g, 0, 0, 0, 0)),
            pl.BlockSpec((src_cells, panel, vectors), lambda g, near: (0, 0, 0)),
            pl.BlockSpec((panel, 1), lambda g, near: (g, 0)),
        ],
        out_specs=[
            pl.BlockSpec((2, panel, vectors), lambda g, near: (0, g, 0)),
            pl.BlockSpec((panel, vectors), lambda g, near: (g, 0)),
        ],
    )
    return pl.pallas_call(
        pressure_kernel,
        grid_spec=grid_spec,
        out_shape=[
            jax.ShapeDtypeStruct((2, targets, vectors), jnp.float32),
            jax.ShapeDtypeStruct((targets, vectors), jnp.bfloat16),
        ],
    )(near_cells, kernel, source_cells, areas.reshape(targets, 1))


def body(
    displacement,
    stiffness,
    kernel,
    areas,
    near_cells,
    source_owner,
    source_node,
    target_owner,
    target_node,
):
    axial_rows = displacement.shape[0]
    circum_rows = displacement.shape[1]
    degrees = displacement.shape[2]
    vectors = displacement.shape[3]
    sectors = lax.axis_size("circ")
    axial_total = axial_rows * lax.axis_size("ax")
    node_count = axial_rows * circum_rows

    radial = displacement[:, :, 0, :].reshape(node_count, vectors)
    table = lax.all_gather(radial, "circ", axis=0, tiled=True)
    slot_index = source_owner[:, 0] * node_count + source_node
    velocity = jnp.take(table, slot_index, axis=0, mode="clip")

    padded = extended(displacement, (("ax", 0), ("circ", 1)), 1)
    blocks = stiffness.reshape(axial_rows, circum_rows, 9, degrees, degrees)
    global_row = lax.axis_index("ax") * axial_rows + jnp.arange(axial_rows, dtype=jnp.int32)
    stiff = None
    for offset in range(9):
        step_axial = offset // 3 - 1
        step_around = offset % 3 - 1
        inside = ((global_row + step_axial >= 0) & (global_row + step_axial < axial_total)).astype(
            blocks.dtype
        )
        block_now = blocks[:, :, offset] * inside[:, None, None, None]
        source = padded[
            1 + step_axial : 1 + step_axial + axial_rows,
            1 + step_around : 1 + step_around + circum_rows,
        ]
        part = jnp.einsum(
            "acij,acjr->acir", block_now, source, preferred_element_type=jnp.float32
        )
        stiff = part if stiff is None else stiff + part

    panel_size = kernel.shape[3]
    source_cells = velocity.reshape(-1, panel_size, vectors)
    pressure, load_value = near_field(kernel, source_cells, areas, near_cells)

    load_owner = target_owner[:, 0]
    target_count = load_owner.shape[0]
    load_capacity = 5 * target_count // (2 * sectors)
    load_slot = slot_positions(load_owner, sectors, load_capacity)
    gather_slot = (
        load_slot[None, :] == jnp.arange(sectors * load_capacity, dtype=jnp.int32)[:, None]
    ).astype(jnp.bfloat16)
    outgoing = jnp.dot(gather_slot, load_value, preferred_element_type=jnp.float32).astype(
        jnp.bfloat16
    )
    outgoing = outgoing.reshape(sectors, load_capacity, vectors)
    node_slot = (
        jnp.full((sectors * load_capacity,), -1, jnp.int32)
        .at[load_slot]
        .set(target_node)
        .reshape(sectors, load_capacity)
    )
    arrived = lax.all_to_all(outgoing, "circ", split_axis=0, concat_axis=0, tiled=True)
    arrived_node = lax.all_to_all(node_slot, "circ", split_axis=0, concat_axis=0, tiled=True)
    selector = (
        arrived_node.reshape(-1)[None, :] == jnp.arange(node_count, dtype=jnp.int32)[:, None]
    ).astype(jnp.bfloat16)
    fluid = jnp.dot(selector, arrived.reshape(-1, vectors), preferred_element_type=jnp.float32)
    stiff = stiff.reshape(axial_rows, circum_rows, degrees, vectors)
    dof_first = (jnp.arange(degrees, dtype=jnp.int32) == 0).astype(jnp.float32)
    shell_force = stiff - dof_first[None, None, :, None] * fluid.reshape(
        axial_rows, circum_rows, 1, vectors
    )
    return (shell_force, pressure)


def solution(mesh):
    return jax.shard_map(
        body,
        mesh=mesh,
        in_specs=(
            P("ax", "circ", None, None),
            P("ax", "circ", None),
            P(("ax", "circ"), None, None, None, None),
            P(("ax", "circ")),
            P(("ax", "circ"), None),
            P(("ax", "circ"), None),
            P(("ax", "circ")),
            P(("ax", "circ"), None),
            P(("ax", "circ")),
        ),
        out_specs=(P("ax", "circ", None, None), P(None, ("ax", "circ"), None)),
        check_vma=False,
    )
```

profile of v0, /device:TPU:0, one launch (start us, length us, event | category | flops | bytes accessed | tf_op | source)
XLA Modules:
  0.0 203.9 jit_solution(1909904478405585485)
XLA Ops:
  7.2 0.0 all-gather.2.cloned.1.call-start
  7.2 1.9 slice.103
  9.1 0.0 all-gather.2.cloned.1.call-update
  9.1 0.0 copy-start.12
  9.1 4.2 %copy.28 = bf16[16,64,6,256]{3,2,1,0:T(8,128)(2,1)S(1)} copy(bf16[16,64,6,256]{3,1,2,0:T(8,128)(2,1)} %param.9) | data formatting | bytes 6291456 | tf_op args[0]
  13.3 2.0 copy-done.1
  15.3 0.8 fusion.53
  16.1 5.0 %collective-permute-start.1 = (bf16[1,64,6,256]{3,2,1,0:T(8,128)(2,1)}, bf16[1,64,6,256]{3,2,1,0:T(8,128)(2,1)S(1)}, u32[]{:S(2)}, u32[]{:S(2)}) collective-permute-start(bf16[1,64,6,256]{3,2,1,0:T(8,128)(2,1)} %get-tuple-element.13), channel_id=1, source_target_pairs={{8,0},{16,8},{24,16},{0,24},{9,1},{17,9},{25,17},{1,25},{10,2},{18... | collective-permute-start | bytes 589832 | tf_op jit(solution)/shard_map/ppermute | solution.py:18
  21.2 0.0 collective-permute-start
  21.2 2.3 %reduce-window.6 = s32[8,8,128]{2,1,0:T(8,128)S(1)} reduce-window(s32[8,8,128]{2,1,0:T(8,128)S(1)} %fusion.41, s32[]{:T(128)} %constant.12.clone.1), window={size=1x1x128 pad=0_0x0_0x127_0}, to_apply=%region_0.1 | reduce-window | flops 1040384 | bytes 65540 | tf_op jit(solution)/shard_map/reduce-window
  23.4 0.3 slice_reduce_fusion
  23.7 0.2 reduce-window.9
  23.9 0.1 add_bitcast_fusion
  24.0 0.5 copy-done.14
  24.6 4.5 %scatter_custom_fusion = s32[2560]{0:T(1024)S(1)} fusion(s32[1024]{0:T(1024)S(1)} %bitcast.92, s32[1024]{0:T(1024)} %param.17, s32[]{:T(128)} %constant.11.clone.1), kind=kCustom, calls=%fused_computation.75 | custom fusion | bytes 10752 | tf_op jit(solution)/shard_map/scatter | solution.py:136
  29.1 0.7 all_to_all.9
  29.7 4.1 %all-to-all-start = ((s32[8,1,320]{2,1,0:T(1,128)}), s32[8,1,320]{2,1,0:T(1,128)}, u32[]{:S(2)}, u32[]{:S(2)}) async-start(s32[8,1,320]{2,1,0:T(1,128)} %all_to_all.9), calls=%async_computation | async-start | bytes 24576 | tf_op jit(solution)/shard_map/all_to_all | solution.py:140
  33.8 2.8 %copy.27 = bf16[16,64,324]{1,0,2:T(8,128)(2,1)} copy(bf16[16,64,324]{2,1,0:T(8,128)(2,1)} %param.10) | data formatting | bytes 1327104 | tf_op args[1]
  36.6 2.5 %fusion.27 = (bf16[16,64,6,6]{1,0,3,2:T(8,128)(2,1)S(1)}, bf16[16,64,6,6]{1,0,3,2:T(8,128)(2,1)}, bf16[16,64,6,6]{1,0,3,2:T(8,128)(2,1)}, bf16[16,64,6,6]{1,0,3,...) fusion(bf16[16,64,9,6,6]{1,0,4,3,2:T(8,128)(2,1)} %bitcast.82, ...), kind=kLoop, calls=%fused_computation.40 | loop fusion | flops 331776 | bytes 1327200 | tf_op jit(solution)/shard_map/mul | solution.py:108
  39.1 3.0 %copy.36 = bf16[16,64,6,6]{3,2,1,0:T(8,128)(2,1)} copy(bf16[16,64,6,6]{1,0,3,2:T(8,128)(2,1)} %get-tuple-element.23) | data formatting | bytes 147456 | tf_op jit(solution)/shard_map/mul | solution.py:108
  42.1 1.3 multiply_add_fusion.1
  43.3 0.7 broadcast_multiply_fusion
  44.1 1.3 add_clamp_fusion
  45.4 7.1 %fusion.36 = f32[16,64,6,256]{3,2,1,0:T(8,128)} fusion(bf16[16,64,6,6]{3,2,1,0:T(8,128)(2,1)} %copy.36, bf16[16,64,6,256]{3,1,2,0:T(8,128)(2,1)S(1)} %copy-done.3), kind=kOutput, calls=%fused_computation.57 | convolution fusion | flops 18874368 | bytes 9510912 | tf_op jit(solution)/shard_map/acij,acjr->acir/dot_general | solution.py:113
  52.5 0.6 multiply_add_fusion
  53.1 0.6 compare_convert_fusion
  53.7 3.0 %copy.41 = bf16[16,64,6,6]{3,2,1,0:T(8,128)(2,1)} copy(bf16[16,64,6,6]{1,0,3,2:T(8,128)(2,1)} %get-tuple-element.15) | data formatting | bytes 147456 | tf_op jit(solution)/shard_map/mul | solution.py:108
  56.6 3.0 %copy.39 = bf16[16,64,6,6]{3,2,1,0:T(8,128)(2,1)} copy(bf16[16,64,6,6]{1,0,3,2:T(8,128)(2,1)} %get-tuple-element.16) | data formatting | bytes 147456 | tf_op jit(solution)/shard_map/mul | solution.py:108
  59.6 3.0 %copy.38 = bf16[16,64,6,6]{3,2,1,0:T(8,128)(2,1)} copy(bf16[16,64,6,6]{1,0,3,2:T(8,128)(2,1)} %get-tuple-element.24) | data formatting | bytes 147456 | tf_op jit(solution)/shard_map/mul | solution.py:108
  62.6 3.0 %copy.35 = bf16[16,64,6,6]{3,2,1,0:T(8,128)(2,1)} copy(bf16[16,64,6,6]{1,0,3,2:T(8,128)(2,1)} %get-tuple-element.25) | data formatting | bytes 147456 | tf_op jit(solution)/shard_map/mul | solution.py:108
  65.6 3.0 %copy.34 = bf16[16,64,6,6]{3,2,1,0:T(8,128)(2,1)} copy(bf16[16,64,6,6]{1,0,3,2:T(8,128)(2,1)} %get-tuple-element.27) | data formatting | bytes 147456 | tf_op jit(solution)/shard_map/mul | solution.py:108
  68.5 3.0 %copy.31 = bf16[16,64,6,6]{3,2,1,0:T(8,128)(2,1)} copy(bf16[16,64,6,6]{1,0,3,2:T(8,128)(2,1)} %get-tuple-element.26) | data formatting | bytes 147456 | tf_op jit(solution)/shard_map/mul | solution.py:108
  71.5 3.0 %copy.33 = bf16[16,64,6,6]{3,2,1,0:T(8,128)(2,1)} copy(bf16[16,64,6,6]{1,0,3,2:T(8,128)(2,1)} %get-tuple-element.28) | data formatting | bytes 147456 | tf_op jit(solution)/shard_map/mul | solution.py:108
  74.5 1.7 copy.43.area_ref
  76.2 2.1 %copy.42 = bf16[16,64,6,6]{3,2,1,0:T(8,128)(2,1)} copy(bf16[16,64,6,6]{1,0,3,2:T(8,128)(2,1)S(1)} %get-tuple-element.14) | data formatting | bytes 147456 | tf_op jit(solution)/shard_map/mul | solution.py:108
  78.4 0.0 all-to-all-done
  78.4 0.7 reduce.1
  79.1 0.1 eq.80
  79.2 0.0 collective-permute-done
  79.2 1.0 constant_dynamic-update-slice_fusion.1
  80.2 0.0 copy-start.10
  80.2 2.3 %copy_dynamic-update-slice_fusion = bf16[18,64,6,256]{3,2,1,0:T(8,128)(2,1)S(1)} fusion(bf16[18,64,6,256]{3,2,1,0:T(8,128)(2,1)S(1)} %constant_dynamic-update-slice_fusion.1, bf16[16,64,6,256]{3,1,2,0:T(8,128)(2,1)S(1)} %copy-done.3), kind=kLoop, calls=%fused_computation.59 | loop fusion | bytes 7340032
  82.5 0.0 collective-permute-done.1
  82.6 0.0 copy-start
  82.6 0.2 collective-permute-start.2
  82.8 2.5 %collective-permute-start.3 = (bf16[18,1,6,256]{3,2,1,0:T(8,128)(2,1)S(1)}, bf16[18,1,6,256]{3,2,1,0:T(8,128)(2,1)S(1)}, u32[]{:S(2)}, u32[]{:S(2)}) collective-permute-start(bf16[18,1,6,256]{3,2,1,0:T(8,128)(2,1)S(1)} %get-tuple-element.10), channel_id=1, source_target_pairs={{1,0},{2,1},{3,2},{4,3},{5,4},{6,5},{7,6},{0,7},{9,8},{10,9},{11,1... | collective-permute-start | bytes 165896 | tf_op jit(solution)/shard_map/ppermute | solution.py:18
  85.3 4.6 %fusion.20 = f32[16,64,6,256]{3,2,1,0:T(8,128)} fusion(bf16[16,64,6,6]{3,2,1,0:T(8,128)(2,1)S(1)} %copy-done.10, bf16[1,64,6,256]{3,2,1,0:T(8,128)(2,1)S(1)} %collective-permute-done.1, bf16[16,64,6,256]{3,2,1,0:T(8,128)(2,1)S(1)} %copy-done.2), kind=kOutput, calls=%fused_computation.30 | convolution fusion | flops 20447232 | bytes 9707520 | tf_op jit(solution)/shard_map/acij,acjr->acir/dot_general | solution.py:113
  89.9 5.7 %fusion.24 = f32[16,64,6,256]{3,2,1,0:T(8,128)} fusion(bf16[16,64,6,6]{3,2,1,0:T(8,128)(2,1)S(1)} %copy-done.11, bf16[16,64,6,256]{3,2,1,0:T(8,128)(2,1)S(1)} %copy-done.2, bf16[1,64,6,256]{3,2,1,0:T(8,128)(2,1)} %collective-permute-done), kind=kOutput, calls=%fused_computation.36 | convolution fusion | flops 20447232 | bytes 9707520 | tf_op jit(solution)/shard_map/acij,acjr->acir/dot_general | solution.py:113
  95.6 0.0 collective-permute-done.2
  95.6 4.6 %fusion.22 = f32[16,64,6,256]{3,2,1,0:T(8,128)} fusion(bf16[16,64,6,6]{3,2,1,0:T(8,128)(2,1)S(1)} %copy-done.8, bf16[18,64,6,256]{3,2,1,0:T(8,128)(2,1)S(1)} %constant_dynamic-update-slice_fusion, bf16[18,1,6,256]{3,2,1,0:T(8,128)(2,1)S(1)} %collective-permute-done.2), kind=kOutput, calls=%fused_computation.33 | convolution fusion | flops 20447232 | bytes 9959424 | tf_op jit(solution)/shard_map/acij,acjr->acir/dot_general | solution.py:113
  100.2 4.0 %fusion.13 = f32[16,64,6,256]{3,2,1,0:T(8,128)} fusion(bf16[16,64,6,6]{3,2,1,0:T(8,128)(2,1)S(1)} %copy-done.9, bf16[18,64,6,256]{3,2,1,0:T(8,128)(2,1)S(1)} %constant_dynamic-update-slice_fusion, bf16[18,1,6,256]{3,2,1,0:T(8,128)(2,1)S(1)} %collective-permute-done.2), kind=kOutput, calls=%fused_computation.23 | convolution fusion | flops 20447232 | bytes 9959424 | tf_op jit(solution)/shard_map/acij,acjr->acir/dot_general | solution.py:113
  104.2 18.6 %gather_fusion = bf16[4096,256]{1,0:T(8,128)(2,1)} fusion(bf16[8192,256]{1,0:T(8,128)(2,1)} %all-gather.2.cloned.1.call-done, s32[4096]{0:T(1024)S(1)} %copy-done.13), kind=kCustom, calls=%fused_computation | custom fusion | bytes 4210688 | tf_op jit(solution)/shard_map/jit(_take)/gather | solution.py:96
  122.8 9.7 %shard_map.104 = (f32[2,1024,256]{2,1,0:T(8,128)}, bf16[1024,256]{1,0:T(8,128)(2,1)}) custom-call(s32[4,12]{1,0:T(4,128)} %near_ref.1, bf16[4,12,2,256,256]{4,3,2,1,0:T(8,128)(2,1)} %kern_ref.1, bf16[16,256,256]{2,1,0:T(8,128)(2,1)} %bitcast.81, f32[1024,1]{1,0:T(8,128)} %copy.43.area_ref), custom_call_target="tpu_custom_call" | custom-call | tf_op jit(solution)/shard_map/pallas_call | solution.py:64
  132.5 4.3 %fusion.26 = bf16[2560,256]{1,0:T(8,128)(2,1)} fusion(bf16[1024,256]{1,0:T(8,128)(2,1)} %get-tuple-element.4, s32[1024]{0:T(1024)S(1)} %copy-done.16), kind=kOutput, calls=%fused_computation.38 | convolution fusion | flops 1345454080 | bytes 1839104 | tf_op jit(solution)/shard_map/dot_general | solution.py:129
  136.8 4.7 %all-to-all-start.1 = ((bf16[8,320,256]{2,1,0:T(8,128)(2,1)}), bf16[8,320,256]{2,1,0:T(8,128)(2,1)}, u32[]{:S(2)}, u32[]{:S(2)}) async-start(bf16[8,320,256]{2,1,0:T(8,128)(2,1)} %bitcast.84), calls=%async_computation.1 | async-start | bytes 2621440 | tf_op jit(solution)/shard_map/all_to_all | solution.py:139
  141.5 0.0 slice-start.1
  141.5 0.0 collective-permute-done.3
  141.5 6.9 %fusion.7 = f32[16,64,6,256]{3,2,1,0:T(8,128)} fusion(bf16[16,64,6,6]{3,2,1,0:T(8,128)(2,1)S(1)} %copy-done.5, bf16[18,64,6,256]{3,2,1,0:T(8,128)(2,1)} %copy-done, bf16[18,1,6,256]{3,2,1,0:T(8,128)(2,1)S(1)} %collective-permute-done.3), kind=kOutput, calls=%fused_computation.19 | convolution fusion | flops 20447232 | bytes 9959424 | tf_op jit(solution)/shard_map/acij,acjr->acir/dot_general | solution.py:113
  148.4 4.0 %fusion.10 = f32[16,64,6,256]{3,2,1,0:T(8,128)} fusion(bf16[16,64,6,6]{3,2,1,0:T(8,128)(2,1)S(1)} %copy-done.6, bf16[18,64,6,256]{3,2,1,0:T(8,128)(2,1)S(1)} %bitcast.80, bf16[18,1,6,256]{3,2,1,0:T(8,128)(2,1)S(1)} %collective-permute-done.3), kind=kOutput, calls=%fused_computation.21 | convolution fusion | flops 20447232 | bytes 9959424 | tf_op jit(solution)/shard_map/acij,acjr->acir/dot_general | solution.py:113
  152.4 4.0 %fusion.16 = f32[16,64,6,256]{3,2,1,0:T(8,128)} fusion(bf16[16,64,6,6]{3,2,1,0:T(8,128)(2,1)S(1)} %copy-done.7, bf16[18,64,6,256]{3,2,1,0:T(8,128)(2,1)S(1)} %bitcast.80, bf16[18,1,6,256]{3,2,1,0:T(8,128)(2,1)S(1)} %collective-permute-done.2), kind=kOutput, calls=%fused_computation.25 | convolution fusion | flops 20447232 | bytes 9959424 | tf_op jit(solution)/shard_map/acij,acjr->acir/dot_general | solution.py:113
  156.4 3.0 %all-to-all-done.1 = bf16[8,320,256]{2,1,0:T(8,128)(2,1)} async-done(((bf16[8,320,256]{2,1,0:T(8,128)(2,1)}), bf16[8,320,256]{2,1,0:T(8,128)(2,1)}, u32[]{:S(2)}, u32[]{:S(2)}) %all-to-all-start.1) | async-done | bytes 1310752 | tf_op jit(solution)/shard_map/all_to_all | solution.py:139
  159.4 3.1 %fusion.1 = f32[16,64,256]{2,1,0:T(8,128)S(1)} fusion(bf16[2560,256,1]{1,0,2:T(8,128)(2,1)} %bitcast.21, s32[16,64]{1,0:T(8,128)S(1)} %copy-done.15, s32[2560]{0:T(1024)S(1)} %eq.80), kind=kOutput, calls=%fused_computation.4 | convolution fusion | flops 1344798720 | bytes 2373632 | tf_op jit(solution)/shard_map/dot_general | solution.py:144
  162.5 26.5 %multiply_subtract_fusion = f32[16,64,6,256]{3,2,1,0:T(8,128)} fusion(f32[16,64,6,256]{3,2,1,0:T(8,128)} %fusion.20, f32[16,64,6,256]{3,2,1,0:T(8,128)} %fusion.22, f32[16,64,6,256]{3,2,1,0:T(8,128)} %fusion.7, f32[16,64,6,256]{3,2,1,0:T(8,128)} %fusion.36, f32[16,64,6,256]{3,2,1,0:T(8,128)} %fusion.13, f32[16,64,6,256]{3,2,1,0:T(8,128)} %fusion.10, ...), kind=kOutput, calls=%fused_computation.6 | convolution fusion | flops 36175872 | bytes 61339672 | tf_op jit(solution)/shard_map/acij,acjr->acir/dot_general | solution.py:113
  189.1 8.0 %copy.44 = f32[16,64,6,256]{3,1,2,0:T(8,128)} copy(f32[16,64,6,256]{3,2,1,0:T(8,128)} %multiply_subtract_fusion) | data formatting | bytes 12582912
  (43 shorter events, 0.2 us)
Async XLA Ops:
  7.2 97.0 %all-gather.2.cloned.1.call-start = ((), (), s32[]{:S(2)}) async-start(), calls=%async_computation.2 | async-start | bytes 4718592 | tf_op jit(solution)/shard_map/all_gather | solution.py:94
  9.1 12.0 %copy-start.12 = (s32[1024,1]{0,1:T(1,128)S(1)}, s32[1024,1]{0,1:T(1,128)}, u32[]{:S(2)}) copy-start(s32[1024,1]{0,1:T(1,128)} %param.16) | copy-start | bytes 12292
  13.3 2.0 copy-start.1
  15.3 30.1 %copy-start.3 = (bf16[16,64,6,256]{3,1,2,0:T(8,128)(2,1)S(1)}, bf16[16,64,6,256]{3,1,2,0:T(8,128)(2,1)}, u32[]{:S(2)}) copy-start(bf16[16,64,6,256]{3,1,2,0:T(8,128)(2,1)} %param.9) | copy-start | bytes 9437188
  16.1 66.4 %collective-permute-start.1 = (bf16[1,64,6,256]{3,2,1,0:T(8,128)(2,1)}, bf16[1,64,6,256]{3,2,1,0:T(8,128)(2,1)S(1)}, u32[]{:S(2)}, u32[]{:S(2)}) collective-permute-start(bf16[1,64,6,256]{3,2,1,0:T(8,128)(2,1)} %get-tuple-element.13), channel_id=1, source_target_pairs={{8,0},{16,8},{24,16},{0,24},{9,1},{17,9},{25,17},{1,25},{10,2},{18... | collective-permute-start | bytes 589832 | tf_op jit(solution)/shard_map/ppermute | solution.py:18
  21.2 58.0 %collective-permute-start = (bf16[1,64,6,256]{3,2,1,0:T(8,128)(2,1)}, bf16[1,64,6,256]{3,2,1,0:T(8,128)(2,1)}, u32[]{:S(2)}, u32[]{:S(2)}) collective-permute-start(bf16[1,64,6,256]{3,2,1,0:T(8,128)(2,1)} %get-tuple-element.12), channel_id=1, source_target_pairs={{0,8},{8,16},{16,24},{24,0},{1,9},{9,17},{17,25},{25,1},{2,10},{10... | collective-permute-start | bytes 589832 | tf_op jit(solution)/shard_map/ppermute | solution.py:16
  24.0 0.6 copy-start.14
  29.7 48.6 %all-to-all-start = ((s32[8,1,320]{2,1,0:T(1,128)}), s32[8,1,320]{2,1,0:T(1,128)}, u32[]{:S(2)}, u32[]{:S(2)}) async-start(s32[8,1,320]{2,1,0:T(1,128)} %all_to_all.9), calls=%async_computation | async-start | bytes 24576 | tf_op jit(solution)/shard_map/all_to_all | solution.py:140
  80.2 5.1 %copy-start.2 = (bf16[16,64,6,256]{3,2,1,0:T(8,128)(2,1)S(1)}, bf16[16,64,6,256]{3,2,1,0:T(8,128)(2,1)}, u32[]{:S(2)}) copy-start(bf16[16,64,6,256]{3,2,1,0:T(8,128)(2,1)} %copy-done.1) | copy-start | bytes 9437188
  80.2 5.1 %copy-start.10 = (bf16[16,64,6,6]{3,2,1,0:T(8,128)(2,1)S(1)}, bf16[16,64,6,6]{3,2,1,0:T(8,128)(2,1)}, u32[]{:S(2)}) copy-start(bf16[16,64,6,6]{3,2,1,0:T(8,128)(2,1)} %copy.41) | copy-start | bytes 221188
  82.6 17.6 %copy-start = (bf16[18,64,6,256]{3,2,1,0:T(8,128)(2,1)}, bf16[18,64,6,256]{3,2,1,0:T(8,128)(2,1)S(1)}, u32[]{:S(2)}) copy-start(bf16[18,64,6,256]{3,2,1,0:T(8,128)(2,1)S(1)} %constant_dynamic-update-slice_fusion) | copy-start | bytes 10616836
  82.6 13.0 %collective-permute-start.2 = (bf16[18,1,6,256]{3,2,1,0:T(8,128)(2,1)S(1)}, bf16[18,1,6,256]{3,2,1,0:T(8,128)(2,1)S(1)}, u32[]{:S(2)}, u32[]{:S(2)}) collective-permute-start(bf16[18,1,6,256]{3,2,1,0:T(8,128)(2,1)S(1)} %get-tuple-element.11), channel_id=1, source_target_pairs={{0,1},{1,2},{2,3},{3,4},{4,5},{5,6},{6,7},{7,0},{8,9},{9,10},{10,1... | collective-permute-start | bytes 165896 | tf_op jit(solution)/shard_map/ppermute | solution.py:16
  82.8 7.1 %copy-start.11 = (bf16[16,64,6,6]{3,2,1,0:T(8,128)(2,1)S(1)}, bf16[16,64,6,6]{3,2,1,0:T(8,128)(2,1)}, u32[]{:S(2)}) copy-start(bf16[16,64,6,6]{3,2,1,0:T(8,128)(2,1)} %copy.33) | copy-start | bytes 221188
  82.8 58.7 %collective-permute-start.3 = (bf16[18,1,6,256]{3,2,1,0:T(8,128)(2,1)S(1)}, bf16[18,1,6,256]{3,2,1,0:T(8,128)(2,1)S(1)}, u32[]{:S(2)}, u32[]{:S(2)}) collective-permute-start(bf16[18,1,6,256]{3,2,1,0:T(8,128)(2,1)S(1)} %get-tuple-element.10), channel_id=1, source_target_pairs={{1,0},{2,1},{3,2},{4,3},{5,4},{6,5},{7,6},{0,7},{9,8},{10,9},{11,1... | collective-permute-start | bytes 165896 | tf_op jit(solution)/shard_map/ppermute | solution.py:18
  89.9 5.7 %copy-start.8 = (bf16[16,64,6,6]{3,2,1,0:T(8,128)(2,1)S(1)}, bf16[16,64,6,6]{3,2,1,0:T(8,128)(2,1)}, u32[]{:S(2)}) copy-start(bf16[16,64,6,6]{3,2,1,0:T(8,128)(2,1)} %copy.39) | copy-start | bytes 221188
  95.6 4.6 %copy-start.9 = (bf16[16,64,6,6]{3,2,1,0:T(8,128)(2,1)S(1)}, bf16[16,64,6,6]{3,2,1,0:T(8,128)(2,1)}, u32[]{:S(2)}) copy-start(bf16[16,64,6,6]{3,2,1,0:T(8,128)(2,1)} %copy.35) | copy-start | bytes 221188
  100.2 4.0 %copy-start.13 = (s32[4096]{0:T(1024)S(1)}, s32[4096]{0:T(1024)}, u32[]{:S(2)}) copy-start(s32[4096]{0:T(1024)} %add_clamp_fusion) | copy-start | bytes 49156
  122.8 9.7 %copy-start.16 = (s32[1024]{0:T(1024)S(1)}, s32[1024]{0:T(1024)}, u32[]{:S(2)}) copy-start(s32[1024]{0:T(1024)} %multiply_add_fusion.1) | copy-start | bytes 12292
  132.5 9.0 %copy-start.5 = (bf16[16,64,6,6]{3,2,1,0:T(8,128)(2,1)S(1)}, bf16[16,64,6,6]{3,2,1,0:T(8,128)(2,1)}, u32[]{:S(2)}) copy-start(bf16[16,64,6,6]{3,2,1,0:T(8,128)(2,1)} %copy.38) | copy-start | bytes 221188
  136.8 11.6 %slice-start = ((s8[4718592]{0:T(1024)(128)(4,1)}), s8[524288]{0:T(1024)(128)(4,1)S(1)}, s32[]{:S(2)}) async-start(s8[4718592]{0:T(1024)(128)(4,1)} %bitcast.79), calls=%async_computation.3 | async-start | bytes 1048576
  136.8 22.6 %all-to-all-start.1 = ((bf16[8,320,256]{2,1,0:T(8,128)(2,1)}), bf16[8,320,256]{2,1,0:T(8,128)(2,1)}, u32[]{:S(2)}, u32[]{:S(2)}) async-start(bf16[8,320,256]{2,1,0:T(8,128)(2,1)} %bitcast.84), calls=%async_computation.1 | async-start | bytes 2621440 | tf_op jit(solution)/shard_map/all_to_all | solution.py:139
  141.5 6.9 %slice-start.1 = ((s8[4718592]{0:T(1024)(128)(4,1)}), s8[4194304]{0:T(1024)(128)(4,1)S(1)}, s32[]{:S(2)}) async-start(s8[4718592]{0:T(1024)(128)(4,1)} %bitcast.79), calls=%async_computation.4 | async-start | bytes 8388608
  141.5 6.9 %copy-start.6 = (bf16[16,64,6,6]{3,2,1,0:T(8,128)(2,1)S(1)}, bf16[16,64,6,6]{3,2,1,0:T(8,128)(2,1)}, u32[]{:S(2)}) copy-start(bf16[16,64,6,6]{3,2,1,0:T(8,128)(2,1)} %copy.34) | copy-start | bytes 221188
  148.4 4.0 %copy-start.7 = (bf16[16,64,6,6]{3,2,1,0:T(8,128)(2,1)S(1)}, bf16[16,64,6,6]{3,2,1,0:T(8,128)(2,1)}, u32[]{:S(2)}) copy-start(bf16[16,64,6,6]{3,2,1,0:T(8,128)(2,1)} %copy.31) | copy-start | bytes 221188
  152.4 7.0 %copy-start.15 = (s32[16,64]{1,0:T(8,128)S(1)}, s32[16,64]{1,0:T(8,128)}, u32[]{:S(2)}) copy-start(s32[16,64]{1,0:T(8,128)} %multiply_add_fusion) | copy-start | bytes 12292
  159.4 3.1 %copy-start.4 = (bf16[16,64,6,6]{3,2,1,0:T(8,128)(2,1)S(1)}, bf16[16,64,6,6]{3,2,1,0:T(8,128)(2,1)}, u32[]{:S(2)}) copy-start(bf16[16,64,6,6]{3,2,1,0:T(8,128)(2,1)} %copy.42) | copy-start | bytes 221188
  159.4 3.1 %copy-start.17 = (f32[6]{0:T(128)S(1)}, f32[6]{0:T(128)}, u32[]{:S(2)}) copy-start(f32[6]{0:T(128)} %compare_convert_fusion) | copy-start | bytes 76
Sparse Core Ops, SparseCore 0:
  9.9 39.5 all-gather.1
where the time goes:
time: 205 us; the launch traced here: 204 us
  local copies, waits for them, and re-layouts  75.4 us (37%)
  matrix products  74.7 us (36%)
  starting transfers between devices  16.5 us (8%)
  between operations  14.3 us (7%)
  other arithmetic  10.3 us (5%)
  Pallas kernels  9.71 us (5%)
  waiting for transfers between devices  3.03 us (1%)
    dot_general x9, matrix products, body(): jnp.einsum('acij,acjr->acir', block_now, source, preferred_element_type=j...  67.4 us
    mul x9, local copies, waits for them, and re-layouts, body(): block_now = blocks[:, :, offset] * inside[:, None, None, None]  25.9 us
    unnamed x45, local copies, waits for them, and re-layouts  20.9 us
    gather x1, local copies, waits for them, and re-layouts, body(): velocity = jnp.take(table, slot_index, axis=0, mode='clip')  18.6 us
    pallas_call x1, Pallas kernels, near_field(): pl.pallas_call(pressure_kernel, grid_spec=grid_spec, out_shape=[jax.Shape...  9.71 us
    ppermute x2, starting transfers between devices, extended(): lax.ppermute(head, axis, [((i + 1) % count, i) for i in range(count)])  7.57 us
    all_to_all x1, starting transfers between devices, body(): lax.all_to_all(outgoing, 'circ', split_axis=0, concat_axis=0, tiled=True)  4.66 us
    scatter x1, local copies, waits for them, and re-layouts, body(): node_slot = jnp.full((sectors * load_capacity,), -1, jnp.int32).at[load_s...  4.48 us
  transfers between devices with their start and end apart: 7, of which 1 were waited for; matrix products, arithmetic and copies ran while one was open for 58% of the time, Pallas kernels for 5%

commit v1 on v0

--- a/solution.py
+++ b/solution.py
@@ -1,3 +1,5 @@
+import functools
+
 import jax
 import jax.numpy as jnp
 from jax import lax
@@ -69,6 +71,75 @@
             jax.ShapeDtypeStruct((targets, vectors), jnp.bfloat16),
         ],
     )(near_cells, kernel, source_cells, areas.reshape(targets, 1))
+
+
+def stiff_kernel(s_ref, rows_ref, fluid_ref, out_ref, sel_ref, band_ref, *, degrees):
+    a = pl.program_id(0)
+    nodes = s_ref.shape[1]
+    offsets = band_ref.shape[0]
+    group = 128
+    span = offsets * degrees
+    wide = ((band_ref.shape[2] + group - 1) // group) * group
+
+    @pl.when(a == 0)
+    def _():
+        k = lax.broadcasted_iota(jnp.int32, sel_ref.shape, 0)
+        y = lax.broadcasted_iota(jnp.int32, sel_ref.shape, 1)
+        blk = y // group
+        lane = y % group
+        target = (
+            (blk // degrees) * (offsets * degrees * degrees)
+            + (lane // degrees) * (degrees * degrees)
+            + (blk % degrees) * degrees
+            + lane % degrees
+        )
+        sel_ref[...] = jnp.where((lane < span) & (k == target), 1.0, 0.0).astype(sel_ref.dtype)
+
+    spread = jnp.dot(s_ref[0], sel_ref[...], preferred_element_type=jnp.float32)
+    pad = jnp.zeros((nodes, wide - group), jnp.float32)
+    for d in range(offsets):
+        for i in range(degrees):
+            blk = d * degrees + i
+            piece = jnp.concatenate([spread[:, blk * group : (blk + 1) * group], pad], axis=1)
+            parts = []
+            for g in range(nodes // 8):
+                rows = piece[g * 8 : (g + 1) * 8]
+                if g:
+                    rows = pltpu.roll(rows, g * 8 * degrees, 1)
+                parts.append(pltpu.roll(rows, 0, 1, stride=degrees, stride_axis=0))
+            skewed = jnp.concatenate(parts, axis=0)
+            band_ref[d, i * nodes : (i + 1) * nodes, :] = skewed[:, : band_ref.shape[2]].astype(
+                band_ref.dtype
+            )
+    acc = None
+    for d in range(offsets):
+        part = jnp.dot(band_ref[d], rows_ref[a + d], preferred_element_type=jnp.float32)
+        acc = part if acc is None else acc + part
+    out_ref[0, :nodes, :] = acc[:nodes] - fluid_ref[0]
+    out_ref[0, nodes:, :] = acc[nodes:]
+
+
+def banded_force(blocks, rows_in, fluid, degrees):
+    axial_rows, nodes, width = blocks.shape
+    offsets = 3
+    band_cols = rows_in.shape[1]
+    vectors = rows_in.shape[-1]
+    band_rows = degrees * nodes
+    return pl.pallas_call(
+        functools.partial(stiff_kernel, degrees=degrees),
+        grid=(axial_rows,),
+        in_specs=[
+            pl.BlockSpec((1, nodes, width), lambda a: (a, 0, 0)),
+            pl.BlockSpec(rows_in.shape, lambda a: (0, 0, 0)),
+            pl.BlockSpec((1, nodes, vectors), lambda a: (a, 0, 0)),
+        ],
+        out_specs=pl.BlockSpec((1, band_rows, vectors), lambda a: (a, 0, 0)),
+        out_shape=jax.ShapeDtypeStruct((axial_rows, band_rows, vectors), jnp.float32),
+        scratch_shapes=[
+            pltpu.VMEM((width, offsets * degrees * 128), jnp.bfloat16),
+            pltpu.VMEM((offsets, band_rows, band_cols), jnp.bfloat16),
+        ],
+    )(blocks, rows_in, fluid)
 
 
 def body(
@@ -96,24 +167,13 @@
     velocity = jnp.take(table, slot_index, axis=0, mode="clip")
 
     padded = extended(displacement, (("ax", 0), ("circ", 1)), 1)
-    blocks = stiffness.reshape(axial_rows, circum_rows, 9, degrees, degrees)
+    rows_in = padded.reshape(axial_rows + 2, (circum_rows + 2) * degrees, vectors)
     global_row = lax.axis_index("ax") * axial_rows + jnp.arange(axial_rows, dtype=jnp.int32)
-    stiff = None
-    for offset in range(9):
-        step_axial = offset // 3 - 1
-        step_around = offset % 3 - 1
-        inside = ((global_row + step_axial >= 0) & (global_row + step_axial < axial_total)).astype(
-            blocks.dtype
-        )
-        block_now = blocks[:, :, offset] * inside[:, None, None, None]
-        source = padded[
-            1 + step_axial : 1 + step_axial + axial_rows,
-            1 + step_around : 1 + step_around + circum_rows,
-        ]
-        part = jnp.einsum(
-            "acij,acjr->acir", block_now, source, preferred_element_type=jnp.float32
-        )
-        stiff = part if stiff is None else stiff + part
+    lane_step = jnp.arange(stiffness.shape[2], dtype=jnp.int32) // (3 * degrees * degrees) - 1
+    inside = (global_row[:, None] + lane_step[None, :] >= 0) & (
+        global_row[:, None] + lane_step[None, :] < axial_total
+    )
+    blocks = jnp.where(inside[:, None, :], stiffness, jnp.zeros_like(stiffness))
 
     panel_size = kernel.shape[3]
     source_cells = velocity.reshape(-1, panel_size, vectors)
@@ -142,10 +202,10 @@
         arrived_node.reshape(-1)[None, :] == jnp.arange(node_count, dtype=jnp.int32)[:, None]
     ).astype(jnp.bfloat16)
     fluid = jnp.dot(selector, arrived.reshape(-1, vectors), preferred_element_type=jnp.float32)
-    stiff = stiff.reshape(axial_rows, circum_rows, degrees, vectors)
-    dof_first = (jnp.arange(degrees, dtype=jnp.int32) == 0).astype(jnp.float32)
-    shell_force = stiff - dof_first[None, None, :, None] * fluid.reshape(
-        axial_rows, circum_rows, 1, vectors
+    fluid = fluid.reshape(axial_rows, circum_rows, vectors)
+    force = banded_force(blocks, rows_in, fluid, degrees)
+    shell_force = jnp.transpose(
+        force.reshape(axial_rows, degrees, circum_rows, vectors), (0, 2, 1, 3)
     )
     return (shell_force, pressure)
 

time: 205 us -> 154 us (0.75)
  matrix products: 74.7 us -> 8 us
  local copies, waits for them, and re-layouts: 75.4 us -> 41.4 us
  waiting for transfers between devices: 3.03 us -> 28.4 us
  Pallas kernels: 9.71 us -> 32.1 us
  other arithmetic: 10.3 us -> 13.4 us
    dot_general x9 -> x0, matrix products: 67.4 us -> none  [body(): jnp.einsum('acij,acjr->acir', block_now, source, preferred_element_type=j...]
    mul x9 -> x0, local copies, waits for them, and re-layouts: 25.9 us -> none  [body(): block_now = blocks[:, :, offset] * inside[:, None, None, None]]
    pallas_call x0 -> x1, Pallas kernels: none -> 22.5 us  [banded_force(): pl.pallas_call(functools.partial(stiff_kernel, degrees=degrees), grid=(ax...]
    unnamed x45 -> x6, local copies, waits for them, and re-layouts: 20.9 us -> 2.03 us
    all_gather x1, waiting for transfers between devices: 0.01 us -> 15.8 us  [body(): table = lax.all_gather(radial, 'circ', axis=0, tiled=True)]
    ppermute x2, waiting for transfers between devices: 0.01 us -> 12.6 us  [extended(): lax.ppermute(tail, axis, [(i, (i + 1) % count) for i in range(count)])]
    reshape x0 -> x1, local copies, waits for them, and re-layouts: none -> 6.25 us  [body(): padded.reshape(axial_rows + 2, (circum_rows + 2) * degrees, vectors)]
    concatenate x0 -> x1, other arithmetic: none -> 3.81 us  [extended(): jnp.concatenate([lax.ppermute(tail, axis, [(i, (i + 1) % count) for i in...]
  transfers between devices with their start and end apart: 7 -> 7, of which waited for: 1 -> 2; matrix products, arithmetic and copies ran while one was open for 58% -> 36% of each run, Pallas kernels for 5% -> 6%
where the time goes in v1:
time: 154 us
  local copies, waits for them, and re-layouts  41.4 us (27%)
  Pallas kernels  32.1 us (21%)
  waiting for transfers between devices  28.4 us (18%)
  starting transfers between devices  16.2 us (11%)
  between operations  14.1 us (9%)
  other arithmetic  13.4 us (9%)
  matrix products  8 us (5%)
    pallas_call x1, Pallas kernels, banded_force(): pl.pallas_call(functools.partial(stiff_kernel, degrees=degrees), grid=(ax...  22.5 us
    gather x1, local copies, waits for them, and re-layouts, body(): velocity = jnp.take(table, slot_index, axis=0, mode='clip')  18.7 us
    all_gather x1, waiting for transfers between devices, body(): table = lax.all_gather(radial, 'circ', axis=0, tiled=True)  15.8 us
    ppermute x2, waiting for transfers between devices, extended(): lax.ppermute(tail, axis, [(i, (i + 1) % count) for i in range(count)])  12.6 us
    pallas_call x1, Pallas kernels, near_field(): pl.pallas_call(pressure_kernel, grid_spec=grid_spec, out_shape=[jax.Shape...  9.6 us
    reshape x1, local copies, waits for them, and re-layouts, body(): padded.reshape(axial_rows + 2, (circum_rows + 2) * degrees, vectors)  6.25 us
    ppermute x2, starting transfers between devices, extended(): lax.ppermute(head, axis, [((i + 1) % count, i) for i in range(count)])  6.05 us
    all_to_all x1, starting transfers between devices, body(): lax.all_to_all(node_slot, 'circ', split_axis=0, concat_axis=0, tiled=True)  5.17 us
  transfers between devices with their start and end apart: 7, of which 2 were waited for; matrix products, arithmetic and copies ran while one was open for 36% of the time, Pallas kernels for 6%

profile of v1, /device:TPU:0, one launch (start us, length us, event | category | flops | bytes accessed | tf_op | source)
XLA Modules:
  0.0 153.6 jit_solution(16136517155897141568)
XLA Ops:
  7.2 0.0 all-gather.2.cloned.1.call-start
  7.2 1.9 %slice.27 = bf16[16,64,1,256]{3,1,2,0:T(8,128)(2,1)} slice(bf16[16,64,6,256]{3,1,2,0:T(8,128)(2,1)} %param.9), slice={[0:16], [0:64], [0:1], [0:256]} | slice | bytes 1048576 | tf_op jit(solution)/shard_map/slice | solution.py:164
  9.1 0.0 all-gather.2.cloned.1.call-update
  9.1 0.7 fusion.10
  9.8 2.3 %reduce-window.6 = s32[8,8,128]{2,1,0:T(8,128)S(1)} reduce-window(s32[8,8,128]{2,1,0:T(8,128)S(1)} %fusion.10, s32[]{:T(128)} %constant.15.clone.1), window={size=1x1x128 pad=0_0x0_0x127_0}, to_apply=%region_0.1 | reduce-window | flops 1040384 | bytes 65540 | tf_op jit(solution)/shard_map/reduce-window
  12.1 0.3 slice_reduce_fusion
  12.4 0.2 reduce-window.9
  12.5 0.1 add_bitcast_fusion
  12.6 0.7 fusion.9
  13.3 0.7 compare_select_fusion
  14.0 4.5 %scatter_custom_fusion = s32[2560]{0:T(1024)S(1)} fusion(s32[1024]{0:T(1024)S(1)} %bitcast.48, s32[1024]{0:T(1024)} %param.17, s32[]{:T(128)} %constant.18.clone.1), kind=kCustom, calls=%fused_computation.31 | custom fusion | bytes 10752 | tf_op jit(solution)/shard_map/scatter | solution.py:196
  18.5 0.7 all_to_all.9
  19.2 5.2 %all-to-all-start = ((s32[8,1,320]{2,1,0:T(1,128)}), s32[8,1,320]{2,1,0:T(1,128)S(1)}, u32[]{:S(2)}, u32[]{:S(2)}) async-start(s32[8,1,320]{2,1,0:T(1,128)} %all_to_all.9), calls=%async_computation | async-start | bytes 24576 | tf_op jit(solution)/shard_map/all_to_all | solution.py:200
  24.4 1.8 %fusion.19 = (bf16[1,64,6,256]{3,1,2,0:T(8,128)(2,1)}, bf16[1,64,6,256]{3,1,2,0:T(8,128)(2,1)}) fusion(bf16[16,64,6,256]{3,1,2,0:T(8,128)(2,1)} %param.9), kind=kLoop, calls=%fused_computation.44 | loop fusion | bytes 786432 | tf_op jit(solution)/shard_map/slice | solution.py:14
  26.2 3.6 %collective-permute-start.1 = (bf16[1,64,6,256]{3,1,2,0:T(8,128)(2,1)}, bf16[1,64,6,256]{3,1,2,0:T(8,128)(2,1)S(1)}, u32[]{:S(2)}, u32[]{:S(2)}) collective-permute-start(bf16[1,64,6,256]{3,1,2,0:T(8,128)(2,1)} %get-tuple-element.8), channel_id=1, source_target_pairs={{8,0},{16,8},{24,16},{0,24},{9,1},{17,9},{25,17},{1,25},{10,2},{18... | collective-permute-start | bytes 589832 | tf_op jit(solution)/shard_map/ppermute | solution.py:20
  29.8 0.0 collective-permute-start
  29.8 1.7 %copy.13.area_ref = f32[1024,1]{1,0:T(8,128)} copy(f32[1024,1]{0,1:T(1,128)} %bitcast.47) | data formatting | bytes 8192 | tf_op jit(solution)/shard_map/reshape | solution.py:73
  31.5 0.7 fusion.11
  32.2 0.7 multiply_add_fusion.1
  32.9 0.7 broadcast_multiply_fusion
  33.6 0.7 add_clamp_fusion
  34.3 15.8 %all-gather.2.cloned.1.call-done = bf16[8192,256]{1,0:T(8,128)(2,1)} async-done(((bf16[1024,256]{1,0:T(8,128)(2,1)}), bf16[8192,256]{1,0:T(8,128)(2,1)}) %all-gather.2.cloned.1.call-update) | async-done | bytes 4194320 | tf_op jit(solution)/shard_map/all_gather | solution.py:165
  50.1 18.7 %gather_fusion = bf16[4096,256]{1,0:T(8,128)(2,1)} fusion(bf16[8192,256]{1,0:T(8,128)(2,1)} %all-gather.2.cloned.1.call-done, s32[4096]{0:T(1024)S(1)} %add_clamp_fusion), kind=kCustom, calls=%fused_computation | custom fusion | bytes 4210688 | tf_op jit(solution)/shard_map/jit(_take)/gather | solution.py:167
  68.7 9.6 %shard_map.104 = (f32[2,1024,256]{2,1,0:T(8,128)}, bf16[1024,256]{1,0:T(8,128)(2,1)}) custom-call(s32[4,12]{1,0:T(4,128)} %near_ref.1, bf16[4,12,2,256,256]{4,3,2,1,0:T(8,128)(2,1)} %kern_ref.1, bf16[16,256,256]{2,1,0:T(8,128)(2,1)} %bitcast.37, f32[1024,1]{1,0:T(8,128)} %copy.13.area_ref), custom_call_target="tpu_custom_call" | custom-call | tf_op jit(solution)/shard_map/pallas_call | solution.py:66
  78.3 4.1 %fusion.6 = bf16[2560,256]{1,0:T(8,128)(2,1)} fusion(bf16[1024,256]{1,0:T(8,128)(2,1)} %get-tuple-element.4, s32[1024]{0:T(1024)S(1)} %multiply_add_fusion.1), kind=kOutput, calls=%fused_computation.10 | convolution fusion | flops 1345454080 | bytes 1839104 | tf_op jit(solution)/shard_map/dot_general | solution.py:189
  82.5 0.0 copy-start
  82.5 0.0 all-to-all-done
  82.5 4.5 %all-to-all-start.1 = ((bf16[8,320,256]{2,1,0:T(8,128)(2,1)}), bf16[8,320,256]{2,1,0:T(8,128)(2,1)}, u32[]{:S(2)}, u32[]{:S(2)}) async-start(bf16[8,320,256]{2,1,0:T(8,128)(2,1)} %bitcast.40), calls=%async_computation.1 | async-start | bytes 2621440 | tf_op jit(solution)/shard_map/all_to_all | solution.py:199
  87.0 2.1 %broadcast_select_fusion.s_ref = bf16[16,64,324]{2,1,0:T(8,128)(2,1)} fusion(bf16[16,64,324]{2,1,0:T(8,128)(2,1)} %param.10, pred[16,324]{1,0:T(8,128)(4,1)} %fusion.11), kind=kLoop, calls=%fused_computation.11 | loop fusion | flops 331776 | bytes 1332288 | tf_op jit(solution)/shard_map/jit(_where)/select_n | solution.py:176
  89.1 0.0 collective-permute-done
  89.2 0.0 copy-done
  89.2 0.2 constant_dynamic-update-slice_fusion.1
  89.4 0.0 collective-permute-done.1
  89.4 0.0 copy-start.1
  89.5 1.8 %copy-done.1 = bf16[18,64,6,256]{3,1,2,0:T(8,128)(2,1)} copy-done((bf16[18,64,6,256]{3,1,2,0:T(8,128)(2,1)}, bf16[18,64,6,256]{3,1,2,0:T(8,128)(2,1)S(1)}, u32[]{:S(2)}) %copy-start.1) | copy-done | bytes 3538968
  91.2 0.2 fusion.18
  91.4 0.4 collective-permute-start.2
  91.8 2.4 %collective-permute-start.3 = (bf16[18,1,6,256]{3,1,2,0:T(2,128)(2,1)S(1)}, bf16[18,1,6,256]{3,1,2,0:T(2,128)(2,1)S(1)}, u32[]{:S(2)}, u32[]{:S(2)}) collective-permute-start(bf16[18,1,6,256]{3,1,2,0:T(2,128)(2,1)S(1)} %get-tuple-element.7), channel_id=1, source_target_pairs={{1,0},{2,1},{3,2},{4,3},{5,4},{6,5},{7,6},{0,7},{9,8},{10,9},{11,1... | collective-permute-start | bytes 165896 | tf_op jit(solution)/shard_map/ppermute | solution.py:20
  94.3 0.1 eq.72
  94.4 12.6 %collective-permute-done.2 = bf16[18,1,6,256]{3,1,2,0:T(2,128)(2,1)S(1)} collective-permute-done((bf16[18,1,6,256]{3,1,2,0:T(2,128)(2,1)S(1)}, bf16[18,1,6,256]{3,1,2,0:T(2,128)(2,1)S(1)}, u32[]{:S(2)}, u32[]{:S(2)}) %collective-permute-start.2) | collective-permute-done | bytes 55328 | tf_op jit(solution)/shard_map/ppermute | solution.py:18
  107.0 0.0 collective-permute-done.3
  107.0 3.8 %pad_maximum_fusion = bf16[18,66,6,256]{3,1,2,0:T(8,128)(2,1)S(1)} fusion(bf16[18,1,6,256]{3,1,2,0:T(2,128)(2,1)S(1)} %collective-permute-done.3, bf16[18,64,6,256]{3,1,2,0:T(8,128)(2,1)} %copy-done.1, bf16[18,1,6,256]{3,1,2,0:T(2,128)(2,1)S(1)} %collective-permute-done.2), kind=kLoop, calls=%fused_computation.9 | loop fusion | flops 10948608 | bytes 7299072 | tf_op jit(solution)/shard_map/concatenate | solution.py:16
  110.9 3.3 %copy.12 = bf16[18,66,6,256]{3,2,1,0:T(8,128)(2,1)} copy(bf16[18,66,6,256]{3,1,2,0:T(8,128)(2,1)S(1)} %pad_maximum_fusion) | data formatting | bytes 7299072 | tf_op jit(solution)/shard_map/concatenate | solution.py:16
  114.2 6.2 %reshape.118.rows_ref = bf16[18,396,256]{2,1,0:T(8,128)(2,1)} reshape(bf16[18,66,6,256]{3,2,1,0:T(8,128)(2,1)} %copy.12) | data formatting | bytes 7299072 | tf_op jit(solution)/shard_map/reshape | solution.py:170
  120.4 0.0 all-to-all-done.1
  120.4 3.9 %fusion.1.fluid_ref = f32[16,64,256]{2,1,0:T(8,128)} fusion(bf16[2560,256,1]{1,0,2:T(8,128)(2,1)} %bitcast.11, s32[16,64]{1,0:T(8,128)S(1)} %multiply_add_fusion, s32[2560]{0:T(1024)S(1)} %eq.72), kind=kOutput, calls=%fused_computation.4 | convolution fusion | flops 1344798720 | bytes 2373632 | tf_op jit(solution)/shard_map/dot_general | solution.py:204
  124.3 22.5 %shard_map.105 = f32[16,384,256]{2,1,0:T(8,128)} custom-call(bf16[16,64,324]{2,1,0:T(8,128)(2,1)} %broadcast_select_fusion.s_ref, bf16[18,396,256]{2,1,0:T(8,128)(2,1)} %reshape.118.rows_ref, f32[16,64,256]{2,1,0:T(8,128)} %fusion.1.fluid_ref), custom_call_target="tpu_custom_call" | custom-call | tf_op jit(solution)/shard_map/pallas_call | solution.py:128
  (6 shorter events, 0.1 us)
Async XLA Ops:
  7.2 42.9 %all-gather.2.cloned.1.call-start = ((), (), s32[]{:S(2)}) async-start(), calls=%async_computation.2 | async-start | bytes 4718592 | tf_op jit(solution)/shard_map/all_gather | solution.py:165
  19.2 63.3 %all-to-all-start = ((s32[8,1,320]{2,1,0:T(1,128)}), s32[8,1,320]{2,1,0:T(1,128)S(1)}, u32[]{:S(2)}, u32[]{:S(2)}) async-start(s32[8,1,320]{2,1,0:T(1,128)} %all_to_all.9), calls=%async_computation | async-start | bytes 24576 | tf_op jit(solution)/shard_map/all_to_all | solution.py:200
  26.2 63.2 %collective-permute-start.1 = (bf16[1,64,6,256]{3,1,2,0:T(8,128)(2,1)}, bf16[1,64,6,256]{3,1,2,0:T(8,128)(2,1)S(1)}, u32[]{:S(2)}, u32[]{:S(2)}) collective-permute-start(bf16[1,64,6,256]{3,1,2,0:T(8,128)(2,1)} %get-tuple-element.8), channel_id=1, source_target_pairs={{8,0},{16,8},{24,16},{0,24},{9,1},{17,9},{25,17},{1,25},{10,2},{18... | collective-permute-start | bytes 589832 | tf_op jit(solution)/shard_map/ppermute | solution.py:20
  29.8 59.4 %collective-permute-start = (bf16[1,64,6,256]{3,1,2,0:T(8,128)(2,1)}, bf16[1,64,6,256]{3,1,2,0:T(8,128)(2,1)S(1)}, u32[]{:S(2)}, u32[]{:S(2)}) collective-permute-start(bf16[1,64,6,256]{3,1,2,0:T(8,128)(2,1)} %get-tuple-element.9), channel_id=1, source_target_pairs={{0,8},{8,16},{16,24},{24,0},{1,9},{9,17},{17,25},{25,1},{2,10},{10... | collective-permute-start | bytes 589832 | tf_op jit(solution)/shard_map/ppermute | solution.py:18
  82.5 6.7 %copy-start = (bf16[16,64,6,256]{3,1,2,0:T(8,128)(2,1)S(1)}, bf16[16,64,6,256]{3,1,2,0:T(8,128)(2,1)}, u32[]{:S(2)}) copy-start(bf16[16,64,6,256]{3,1,2,0:T(8,128)(2,1)} %param.9) | copy-start | bytes 9437188
  82.5 37.9 %all-to-all-start.1 = ((bf16[8,320,256]{2,1,0:T(8,128)(2,1)}), bf16[8,320,256]{2,1,0:T(8,128)(2,1)}, u32[]{:S(2)}, u32[]{:S(2)}) async-start(bf16[8,320,256]{2,1,0:T(8,128)(2,1)} %bitcast.40), calls=%async_computation.1 | async-start | bytes 2621440 | tf_op jit(solution)/shard_map/all_to_all | solution.py:199
  89.4 1.8 %copy-start.1 = (bf16[18,64,6,256]{3,1,2,0:T(8,128)(2,1)}, bf16[18,64,6,256]{3,1,2,0:T(8,128)(2,1)S(1)}, u32[]{:S(2)}) copy-start(bf16[18,64,6,256]{3,1,2,0:T(8,128)(2,1)S(1)} %constant_dynamic-update-slice_fusion) | copy-start | bytes 10616836
  91.4 15.6 %collective-permute-start.2 = (bf16[18,1,6,256]{3,1,2,0:T(2,128)(2,1)S(1)}, bf16[18,1,6,256]{3,1,2,0:T(2,128)(2,1)S(1)}, u32[]{:S(2)}, u32[]{:S(2)}) collective-permute-start(bf16[18,1,6,256]{3,1,2,0:T(2,128)(2,1)S(1)} %get-tuple-element.6), channel_id=1, source_target_pairs={{0,1},{1,2},{2,3},{3,4},{4,5},{5,6},{6,7},{7,0},{8,9},{9,10},{10,1... | collective-permute-start | bytes 165896 | tf_op jit(solution)/shard_map/ppermute | solution.py:18
  91.8 15.2 %collective-permute-start.3 = (bf16[18,1,6,256]{3,1,2,0:T(2,128)(2,1)S(1)}, bf16[18,1,6,256]{3,1,2,0:T(2,128)(2,1)S(1)}, u32[]{:S(2)}, u32[]{:S(2)}) collective-permute-start(bf16[18,1,6,256]{3,1,2,0:T(2,128)(2,1)S(1)} %get-tuple-element.7), channel_id=1, source_target_pairs={{1,0},{2,1},{3,2},{4,3},{5,4},{6,5},{7,6},{0,7},{9,8},{10,9},{11,1... | collective-permute-start | bytes 165896 | tf_op jit(solution)/shard_map/ppermute | solution.py:20
Sparse Core Ops, SparseCore 0:
  10.5 39.5 all-gather.1

commit v2 on v1

--- a/solution.py
+++ b/solution.py
@@ -73,7 +73,7 @@
     )(near_cells, kernel, source_cells, areas.reshape(targets, 1))
 
 
-def stiff_kernel(s_ref, rows_ref, fluid_ref, out_ref, sel_ref, band_ref, *, degrees):
+def stiff_kernel(s_ref, rows_ref, out_ref, sel_ref, band_ref, *, degrees):
     a = pl.program_id(0)
     nodes = s_ref.shape[1]
     offsets = band_ref.shape[0]
@@ -115,11 +115,10 @@
     for d in range(offsets):
         part = jnp.dot(band_ref[d], rows_ref[a + d], preferred_element_type=jnp.float32)
         acc = part if acc is None else acc + part
-    out_ref[0, :nodes, :] = acc[:nodes] - fluid_ref[0]
-    out_ref[0, nodes:, :] = acc[nodes:]
-
-
-def banded_force(blocks, rows_in, fluid, degrees):
+    out_ref[0] = acc
+
+
+def banded_force(blocks, rows_in, degrees):
     axial_rows, nodes, width = blocks.shape
     offsets = 3
     band_cols = rows_in.shape[1]
@@ -131,7 +130,6 @@
         in_specs=[
             pl.BlockSpec((1, nodes, width), lambda a: (a, 0, 0)),
             pl.BlockSpec(rows_in.shape, lambda a: (0, 0, 0)),
-            pl.BlockSpec((1, nodes, vectors), lambda a: (a, 0, 0)),
         ],
         out_specs=pl.BlockSpec((1, band_rows, vectors), lambda a: (a, 0, 0)),
         out_shape=jax.ShapeDtypeStruct((axial_rows, band_rows, vectors), jnp.float32),
@@ -139,7 +137,7 @@
             pltpu.VMEM((width, offsets * degrees * 128), jnp.bfloat16),
             pltpu.VMEM((offsets, band_rows, band_cols), jnp.bfloat16),
         ],
-    )(blocks, rows_in, fluid)
+    )(blocks, rows_in)
 
 
 def body(
@@ -163,8 +161,6 @@
 
     radial = displacement[:, :, 0, :].reshape(node_count, vectors)
     table = lax.all_gather(radial, "circ", axis=0, tiled=True)
-    slot_index = source_owner[:, 0] * node_count + source_node
-    velocity = jnp.take(table, slot_index, axis=0, mode="clip")
 
     padded = extended(displacement, (("ax", 0), ("circ", 1)), 1)
     rows_in = padded.reshape(axial_rows + 2, (circum_rows + 2) * degrees, vectors)
@@ -174,6 +170,11 @@
         global_row[:, None] + lane_step[None, :] < axial_total
     )
     blocks = jnp.where(inside[:, None, :], stiffness, jnp.zeros_like(stiffness))
+    force = banded_force(blocks, rows_in, degrees)
+
+    force, table = lax.optimization_barrier((force, table))
+    slot_index = source_owner[:, 0] * node_count + source_node
+    velocity = jnp.take(table, slot_index, axis=0, mode="clip")
 
     panel_size = kernel.shape[3]
     source_cells = velocity.reshape(-1, panel_size, vectors)
@@ -203,7 +204,7 @@
     ).astype(jnp.bfloat16)
     fluid = jnp.dot(selector, arrived.reshape(-1, vectors), preferred_element_type=jnp.float32)
     fluid = fluid.reshape(axial_rows, circum_rows, vectors)
-    force = banded_force(blocks, rows_in, fluid, degrees)
+    force = force.at[:, :circum_rows, :].add(-fluid)
     shell_force = jnp.transpose(
         force.reshape(axial_rows, degrees, circum_rows, vectors), (0, 2, 1, 3)
     )

time: 154 us -> 152 us (0.987)
    all_to_all x1, waiting for transfers between devices: 0.01 us -> 17.3 us  [body(): lax.all_to_all(outgoing, 'circ', split_axis=0, concat_axis=0, tiled=True)]
    all_gather x1, waiting for transfers between devices: 15.8 us -> 0.01 us  [body(): table = lax.all_gather(radial, 'circ', axis=0, tiled=True)]
    ppermute x2, waiting for transfers between devices: 12.6 us -> 11 us  [extended(): lax.ppermute(tail, axis, [(i, (i + 1) % count) for i in range(count)])]
  transfers between devices with their start and end apart: 7 -> 7, of which waited for: 2 -> 3; matrix products, arithmetic and copies ran while one was open for 36% -> 35% of each run, Pallas kernels for 6% -> 21%
where the time goes in v2:
time: 152 us; the launch traced here: 151 us
  local copies, waits for them, and re-layouts  41.1 us (27%)
  Pallas kernels  31.9 us (21%)
  waiting for transfers between devices  28.4 us (19%)
  starting transfers between devices  15.2 us (10%)
  between operations  14.2 us (9%)
  other arithmetic  12.1 us (8%)
  matrix products  7.97 us (5%)
    pallas_call x1, Pallas kernels, banded_force(): pl.pallas_call(functools.partial(stiff_kernel, degrees=degrees), grid=(ax...  22.3 us
    gather x1, local copies, waits for them, and re-layouts, body(): velocity = jnp.take(table, slot_index, axis=0, mode='clip')  18.7 us
    all_to_all x1, waiting for transfers between devices, body(): lax.all_to_all(outgoing, 'circ', split_axis=0, concat_axis=0, tiled=True)  17.3 us
    ppermute x2, waiting for transfers between devices, extended(): lax.ppermute(tail, axis, [(i, (i + 1) % count) for i in range(count)])  11 us
    pallas_call x1, Pallas kernels, near_field(): pl.pallas_call(pressure_kernel, grid_spec=grid_spec, out_shape=[jax.Shape...  9.6 us
    ppermute x2, starting transfers between devices, extended(): lax.ppermute(head, axis, [((i + 1) % count, i) for i in range(count)])  6.38 us
    reshape x1, local copies, waits for them, and re-layouts, body(): padded.reshape(axial_rows + 2, (circum_rows + 2) * degrees, vectors)  6.21 us
    all_to_all x1, starting transfers between devices, body(): lax.all_to_all(node_slot, 'circ', split_axis=0, concat_axis=0, tiled=True)  5.17 us
  transfers between devices with their start and end apart: 7, of which 3 were waited for; matrix products, arithmetic and copies ran while one was open for 35% of the time, Pallas kernels for 21%

profile of v2, /device:TPU:0, one launch (start us, length us, event | category | flops | bytes accessed | tf_op | source)
XLA Modules:
  0.0 150.9 jit_solution(11029269921147394848)
XLA Ops:
  7.2 0.0 copy-start
  7.2 0.0 copy-start.5
  7.2 0.0 all-gather.2.cloned.1.call-start
  7.2 2.1 %slice.49 = bf16[16,64,1,256]{3,1,2,0:T(8,128)(2,1)} slice(bf16[16,64,6,256]{3,1,2,0:T(8,128)(2,1)} %param.11), slice={[0:16], [0:64], [0:1], [0:256]} | slice | bytes 1048576 | tf_op jit(solution)/shard_map/slice | solution.py:162
  9.3 0.0 all-gather.2.cloned.1.call-update
  9.3 0.7 fusion.19
  10.0 2.3 %reduce-window.6 = s32[8,8,128]{2,1,0:T(8,128)S(1)} reduce-window(s32[8,8,128]{2,1,0:T(8,128)S(1)} %fusion.19, s32[]{:T(128)} %constant.58.clone.1), window={size=1x1x128 pad=0_0x0_0x127_0}, to_apply=%region_0.1 | reduce-window | flops 1040384 | bytes 65540 | tf_op jit(solution)/shard_map/reduce-window
  12.3 0.3 slice_reduce_fusion
  12.6 0.2 reduce-window.9
  12.7 0.1 add_bitcast_fusion
  12.8 0.7 fusion.18
  13.5 0.0 copy-start.3
  13.5 0.7 compare_select_fusion
  14.2 0.0 copy-done.3
  14.3 4.5 %scatter_custom_fusion = s32[2560]{0:T(1024)S(1)} fusion(s32[1024]{0:T(1024)S(1)} %bitcast.48, s32[1024]{0:T(1024)} %param.19, s32[]{:T(128)} %constant.59.clone.1), kind=kCustom, calls=%fused_computation.34 | custom fusion | bytes 10752 | tf_op jit(solution)/shard_map/scatter | solution.py:197
  18.7 0.7 all_to_all.9
  19.4 5.2 %all-to-all-start = ((s32[8,1,320]{2,1,0:T(1,128)}), s32[8,1,320]{2,1,0:T(1,128)}, u32[]{:S(2)}, u32[]{:S(2)}) async-start(s32[8,1,320]{2,1,0:T(1,128)} %all_to_all.9), calls=%async_computation | async-start | bytes 24576 | tf_op jit(solution)/shard_map/all_to_all | solution.py:201
  24.6 1.8 %fusion.28 = (bf16[1,64,6,256]{3,1,2,0:T(8,128)(2,1)}, bf16[1,64,6,256]{3,1,2,0:T(8,128)(2,1)}) fusion(bf16[16,64,6,256]{3,1,2,0:T(8,128)(2,1)} %param.11), kind=kLoop, calls=%fused_computation.47 | loop fusion | bytes 786432 | tf_op jit(solution)/shard_map/slice | solution.py:14
  26.4 3.7 %collective-permute-start.1 = (bf16[1,64,6,256]{3,1,2,0:T(8,128)(2,1)}, bf16[1,64,6,256]{3,1,2,0:T(8,128)(2,1)S(1)}, u32[]{:S(2)}, u32[]{:S(2)}) collective-permute-start(bf16[1,64,6,256]{3,1,2,0:T(8,128)(2,1)} %get-tuple-element.24), channel_id=1, source_target_pairs={{8,0},{16,8},{24,16},{0,24},{9,1},{17,9},{25,17},{1,25},{10,2},{18... | collective-permute-start | bytes 589832 | tf_op jit(solution)/shard_map/ppermute | solution.py:20
  30.1 0.0 collective-permute-start
  30.1 0.1 fusion.20
  30.2 2.1 %broadcast_select_fusion.s_ref = bf16[16,64,324]{2,1,0:T(8,128)(2,1)} fusion(bf16[16,64,324]{2,1,0:T(8,128)(2,1)} %param.12, pred[16,324]{1,0:T(8,128)(4,1)S(1)} %fusion.20), kind=kLoop, calls=%fused_computation.14 | loop fusion | flops 331776 | bytes 1332288 | tf_op jit(solution)/shard_map/jit(_where)/select_n | solution.py:172
  32.3 0.0 copy-done.5
  32.4 0.7 add_clamp_fusion
  33.1 7.0 %collective-permute-done = bf16[1,64,6,256]{3,1,2,0:T(8,128)(2,1)S(1)} collective-permute-done((bf16[1,64,6,256]{3,1,2,0:T(8,128)(2,1)}, bf16[1,64,6,256]{3,1,2,0:T(8,128)(2,1)S(1)}, u32[]{:S(2)}, u32[]{:S(2)}) %collective-permute-start) | collective-permute-done | bytes 196640 | tf_op jit(solution)/shard_map/ppermute | solution.py:18
  40.2 0.0 copy-done
  40.2 0.0 copy-start.2
  40.2 0.0 copy-start.4
  40.2 0.0 copy-start.6
  40.2 0.4 constant_dynamic-update-slice_fusion.1
  40.6 0.0 collective-permute-done.1
  40.6 0.0 copy-start.1
  40.7 1.8 %copy-done.1 = bf16[18,64,6,256]{3,1,2,0:T(8,128)(2,1)} copy-done((bf16[18,64,6,256]{3,1,2,0:T(8,128)(2,1)}, bf16[18,64,6,256]{3,1,2,0:T(8,128)(2,1)S(1)}, u32[]{:S(2)}) %copy-start.1) | copy-done | bytes 3538968
  42.4 0.2 fusion.27
  42.6 0.1 collective-permute-start.2
  42.7 2.6 %collective-permute-start.3 = (bf16[18,1,6,256]{3,1,2,0:T(2,128)(2,1)S(1)}, bf16[18,1,6,256]{3,1,2,0:T(2,128)(2,1)S(1)}, u32[]{:S(2)}, u32[]{:S(2)}) collective-permute-start(bf16[18,1,6,256]{3,1,2,0:T(2,128)(2,1)S(1)} %get-tuple-element.23), channel_id=1, source_target_pairs={{1,0},{2,1},{3,2},{4,3},{5,4},{6,5},{7,6},{0,7},{9,8},{10,9},{11,1... | collective-permute-start | bytes 165896 | tf_op jit(solution)/shard_map/ppermute | solution.py:20
  45.3 0.0 copy-done.2
  45.3 0.0 copy-done.4
  45.3 0.0 copy-done.6
  45.3 1.1 copy.13.area_ref
  46.4 4.0 %collective-permute-done.2 = bf16[18,1,6,256]{3,1,2,0:T(2,128)(2,1)S(1)} collective-permute-done((bf16[18,1,6,256]{3,1,2,0:T(2,128)(2,1)S(1)}, bf16[18,1,6,256]{3,1,2,0:T(2,128)(2,1)S(1)}, u32[]{:S(2)}, u32[]{:S(2)}) %collective-permute-start.2) | collective-permute-done | bytes 55328 | tf_op jit(solution)/shard_map/ppermute | solution.py:18
  50.4 0.0 collective-permute-done.3
  50.4 3.8 %pad_maximum_fusion = bf16[18,66,6,256]{3,1,2,0:T(8,128)(2,1)S(1)} fusion(bf16[18,1,6,256]{3,1,2,0:T(2,128)(2,1)S(1)} %collective-permute-done.3, bf16[18,64,6,256]{3,1,2,0:T(8,128)(2,1)} %copy-done.1, bf16[18,1,6,256]{3,1,2,0:T(2,128)(2,1)S(1)} %collective-permute-done.2), kind=kLoop, calls=%fused_computation.9 | loop fusion | flops 10948608 | bytes 7299072 | tf_op jit(solution)/shard_map/concatenate | solution.py:16
  54.2 3.3 %copy.12 = bf16[18,66,6,256]{3,2,1,0:T(8,128)(2,1)} copy(bf16[18,66,6,256]{3,1,2,0:T(8,128)(2,1)S(1)} %pad_maximum_fusion) | data formatting | bytes 7299072 | tf_op jit(solution)/shard_map/concatenate | solution.py:16
  57.5 6.2 %reshape.150.rows_ref = bf16[18,396,256]{2,1,0:T(8,128)(2,1)} reshape(bf16[18,66,6,256]{3,2,1,0:T(8,128)(2,1)} %copy.12) | data formatting | bytes 7299072 | tf_op jit(solution)/shard_map/reshape | solution.py:166
  63.7 22.3 %shard_map.104 = f32[16,384,256]{2,1,0:T(8,128)} custom-call(bf16[16,64,324]{2,1,0:T(8,128)(2,1)} %broadcast_select_fusion.s_ref, bf16[18,396,256]{2,1,0:T(8,128)(2,1)} %reshape.150.rows_ref), custom_call_target="tpu_custom_call" | custom-call | tf_op jit(solution)/shard_map/pallas_call | solution.py:127
  86.1 0.0 all-gather.2.cloned.1.call-done
  86.1 18.7 %gather_fusion = bf16[4096,256]{1,0:T(8,128)(2,1)} fusion(bf16[8192,256]{1,0:T(8,128)(2,1)} %all-gather.2.cloned.1.call-done, s32[4096]{0:T(1024)S(1)} %add_clamp_fusion), kind=kCustom, calls=%fused_computation | custom fusion | bytes 4210688 | tf_op jit(solution)/shard_map/jit(_take)/gather | solution.py:177
  104.7 9.6 %shard_map.105 = (f32[2,1024,256]{2,1,0:T(8,128)}, bf16[1024,256]{1,0:T(8,128)(2,1)}) custom-call(s32[4,12]{1,0:T(4,128)} %near_ref.1, bf16[4,12,2,256,256]{4,3,2,1,0:T(8,128)(2,1)} %kern_ref.1, bf16[16,256,256]{2,1,0:T(8,128)(2,1)} %bitcast.37, f32[1024,1]{1,0:T(8,128)} %copy.13.area_ref), custom_call_target="tpu_custom_call" | custom-call | tf_op jit(solution)/shard_map/pallas_call | solution.py:66
  114.3 4.1 %fusion.6 = bf16[2560,256]{1,0:T(8,128)(2,1)} fusion(bf16[1024,256]{1,0:T(8,128)(2,1)} %get-tuple-element.20, s32[1024]{0:T(1024)S(1)} %multiply_add_fusion.1), kind=kOutput, calls=%fused_computation.10 | convolution fusion | flops 1345454080 | bytes 1839104 | tf_op jit(solution)/shard_map/dot_general | solution.py:190
  118.5 0.0 all-to-all-done
  118.5 3.6 %all-to-all-start.1 = ((bf16[8,320,256]{2,1,0:T(8,128)(2,1)}), bf16[8,320,256]{2,1,0:T(8,128)(2,1)S(1)}, u32[]{:S(2)}, u32[]{:S(2)}) async-start(bf16[8,320,256]{2,1,0:T(8,128)(2,1)} %bitcast.9), calls=%async_computation.1 | async-start | bytes 2621440 | tf_op jit(solution)/shard_map/all_to_all | solution.py:200
  122.1 0.7 reduce.3
  122.8 0.1 eq.72
  122.9 17.3 %all-to-all-done.1 = bf16[8,320,256]{2,1,0:T(8,128)(2,1)S(1)} async-done(((bf16[8,320,256]{2,1,0:T(8,128)(2,1)}), bf16[8,320,256]{2,1,0:T(8,128)(2,1)S(1)}, u32[]{:S(2)}, u32[]{:S(2)}) %all-to-all-start.1) | async-done | bytes 1310752 | tf_op jit(solution)/shard_map/all_to_all | solution.py:200
  140.2 3.8 %fusion.13 = f32[16,384,256]{2,1,0:T(8,128)} fusion(f32[16,384,256]{2,1,0:T(8,128)} %shard_map.104, bf16[2560,256,1]{1,0,2:T(8,128)(2,1)S(1)} %bitcast.40, s32[16,64]{1,0:T(8,128)S(1)} %multiply_add_fusion, s32[2560]{0:T(1024)S(1)} %eq.72), kind=kOutput, calls=%fused_computation.13 | convolution fusion | flops 1345323008 | bytes 3422208 | tf_op jit(solution)/shard_map/dot_general | solution.py:205
  (7 shorter events, 0.1 us)
Async XLA Ops:
  7.2 33.0 %copy-start = (bf16[16,64,6,256]{3,1,2,0:T(8,128)(2,1)S(1)}, bf16[16,64,6,256]{3,1,2,0:T(8,128)(2,1)}, u32[]{:S(2)}) copy-start(bf16[16,64,6,256]{3,1,2,0:T(8,128)(2,1)} %param.11) | copy-start | bytes 9437188
  7.2 25.2 %copy-start.5 = (s32[4096,1]{0,1:T(1,128)S(1)}, s32[4096,1]{0,1:T(1,128)}, u32[]{:S(2)}) copy-start(s32[4096,1]{0,1:T(1,128)} %param.16) | copy-start | bytes 49156
  7.2 78.9 %all-gather.2.cloned.1.call-start = ((), (), s32[]{:S(2)}) async-start(), calls=%async_computation.2 | async-start | bytes 4718592 | tf_op jit(solution)/shard_map/all_gather | solution.py:163
  13.5 0.7 copy-start.3
  19.4 99.1 %all-to-all-start = ((s32[8,1,320]{2,1,0:T(1,128)}), s32[8,1,320]{2,1,0:T(1,128)}, u32[]{:S(2)}, u32[]{:S(2)}) async-start(s32[8,1,320]{2,1,0:T(1,128)} %all_to_all.9), calls=%async_computation | async-start | bytes 24576 | tf_op jit(solution)/shard_map/all_to_all | solution.py:201
  26.4 14.2 %collective-permute-start.1 = (bf16[1,64,6,256]{3,1,2,0:T(8,128)(2,1)}, bf16[1,64,6,256]{3,1,2,0:T(8,128)(2,1)S(1)}, u32[]{:S(2)}, u32[]{:S(2)}) collective-permute-start(bf16[1,64,6,256]{3,1,2,0:T(8,128)(2,1)} %get-tuple-element.24), channel_id=1, source_target_pairs={{8,0},{16,8},{24,16},{0,24},{9,1},{17,9},{25,17},{1,25},{10,2},{18... | collective-permute-start | bytes 589832 | tf_op jit(solution)/shard_map/ppermute | solution.py:20
  30.1 10.0 %collective-permute-start = (bf16[1,64,6,256]{3,1,2,0:T(8,128)(2,1)}, bf16[1,64,6,256]{3,1,2,0:T(8,128)(2,1)S(1)}, u32[]{:S(2)}, u32[]{:S(2)}) collective-permute-start(bf16[1,64,6,256]{3,1,2,0:T(8,128)(2,1)} %get-tuple-element.25), channel_id=1, source_target_pairs={{0,8},{8,16},{16,24},{24,0},{1,9},{9,17},{17,25},{25,1},{2,10},{10... | collective-permute-start | bytes 589832 | tf_op jit(solution)/shard_map/ppermute | solution.py:18
  40.2 5.2 %copy-start.2 = (s32[1024,1]{0,1:T(1,128)S(1)}, s32[1024,1]{0,1:T(1,128)}, u32[]{:S(2)}) copy-start(s32[1024,1]{0,1:T(1,128)} %param.18) | copy-start | bytes 12292
  40.2 5.1 %copy-start.4 = (s32[1024]{0:T(1024)S(1)}, s32[1024]{0:T(1024)}, u32[]{:S(2)}) copy-start(s32[1024]{0:T(1024)} %copy-done.3) | copy-start | bytes 12292
  40.2 5.1 %copy-start.6 = (f32[1024]{0:T(1024)S(1)}, f32[1024]{0:T(1024)}, u32[]{:S(2)}) copy-start(f32[1024]{0:T(1024)} %param.14) | copy-start | bytes 12292
  40.6 1.8 %copy-start.1 = (bf16[18,64,6,256]{3,1,2,0:T(8,128)(2,1)}, bf16[18,64,6,256]{3,1,2,0:T(8,128)(2,1)S(1)}, u32[]{:S(2)}) copy-start(bf16[18,64,6,256]{3,1,2,0:T(8,128)(2,1)S(1)} %constant_dynamic-update-slice_fusion) | copy-start | bytes 10616836
  42.6 7.8 %collective-permute-start.2 = (bf16[18,1,6,256]{3,1,2,0:T(2,128)(2,1)S(1)}, bf16[18,1,6,256]{3,1,2,0:T(2,128)(2,1)S(1)}, u32[]{:S(2)}, u32[]{:S(2)}) collective-permute-start(bf16[18,1,6,256]{3,1,2,0:T(2,128)(2,1)S(1)} %get-tuple-element.22), channel_id=1, source_target_pairs={{0,1},{1,2},{2,3},{3,4},{4,5},{5,6},{6,7},{7,0},{8,9},{9,10},{10,1... | collective-permute-start | bytes 165896 | tf_op jit(solution)/shard_map/ppermute | solution.py:18
  42.7 7.7 %collective-permute-start.3 = (bf16[18,1,6,256]{3,1,2,0:T(2,128)(2,1)S(1)}, bf16[18,1,6,256]{3,1,2,0:T(2,128)(2,1)S(1)}, u32[]{:S(2)}, u32[]{:S(2)}) collective-permute-start(bf16[18,1,6,256]{3,1,2,0:T(2,128)(2,1)S(1)} %get-tuple-element.23), channel_id=1, source_target_pairs={{1,0},{2,1},{3,2},{4,3},{5,4},{6,5},{7,6},{0,7},{9,8},{10,9},{11,1... | collective-permute-start | bytes 165896 | tf_op jit(solution)/shard_map/ppermute | solution.py:20
  118.5 21.7 %all-to-all-start.1 = ((bf16[8,320,256]{2,1,0:T(8,128)(2,1)}), bf16[8,320,256]{2,1,0:T(8,128)(2,1)S(1)}, u32[]{:S(2)}, u32[]{:S(2)}) async-start(bf16[8,320,256]{2,1,0:T(8,128)(2,1)} %bitcast.9), calls=%async_computation.1 | async-start | bytes 2621440 | tf_op jit(solution)/shard_map/all_to_all | solution.py:200
Sparse Core Ops, SparseCore 0:
  9.9 40.4 all-gather.1

commit v3 on v2

--- a/solution.py
+++ b/solution.py
@@ -73,15 +73,17 @@
     )(near_cells, kernel, source_cells, areas.reshape(targets, 1))
 
 
-def stiff_kernel(s_ref, rows_ref, out_ref, sel_ref, band_ref, *, degrees):
-    a = pl.program_id(0)
+def stiff_kernel(s_ref, rows_ref, *rest, degrees, first):
+    out_ref, sel_ref, band_ref = rest[-3:]
+    step = pl.program_id(0)
+    a = step + first
     nodes = s_ref.shape[1]
     offsets = band_ref.shape[0]
     group = 128
     span = offsets * degrees
     wide = ((band_ref.shape[2] + group - 1) // group) * group
 
-    @pl.when(a == 0)
+    @pl.when(step == 0)
     def _():
         k = lax.broadcasted_iota(jnp.int32, sel_ref.shape, 0)
         y = lax.broadcasted_iota(jnp.int32, sel_ref.shape, 1)
@@ -118,26 +120,34 @@
     out_ref[0] = acc
 
 
-def banded_force(blocks, rows_in, degrees):
+def banded_force(blocks, rows_in, degrees, first, count, previous=None):
     axial_rows, nodes, width = blocks.shape
     offsets = 3
     band_cols = rows_in.shape[1]
     vectors = rows_in.shape[-1]
     band_rows = degrees * nodes
+    in_specs = [
+        pl.BlockSpec((1, nodes, width), lambda a: (a + first, 0, 0)),
+        pl.BlockSpec(rows_in.shape, lambda a: (0, 0, 0)),
+    ]
+    operands = [blocks, rows_in]
+    aliases = {}
+    if previous is not None:
+        in_specs.append(pl.BlockSpec(memory_space=pl.ANY))
+        operands.append(previous)
+        aliases = {2: 0}
     return pl.pallas_call(
-        functools.partial(stiff_kernel, degrees=degrees),
-        grid=(axial_rows,),
-        in_specs=[
-            pl.BlockSpec((1, nodes, width), lambda a: (a, 0, 0)),
-            pl.BlockSpec(rows_in.shape, lambda a: (0, 0, 0)),
-        ],
-        out_specs=pl.BlockSpec((1, band_rows, vectors), lambda a: (a, 0, 0)),
+        functools.partial(stiff_kernel, degrees=degrees, first=first),
+        grid=(count,),
+        in_specs=in_specs,
+        out_specs=pl.BlockSpec((1, band_rows, vectors), lambda a: (a + first, 0, 0)),
         out_shape=jax.ShapeDtypeStruct((axial_rows, band_rows, vectors), jnp.float32),
         scratch_shapes=[
             pltpu.VMEM((width, offsets * degrees * 128), jnp.bfloat16),
             pltpu.VMEM((offsets, band_rows, band_cols), jnp.bfloat16),
         ],
-    )(blocks, rows_in)
+        input_output_aliases=aliases,
+    )(*operands)
 
 
 def body(
@@ -170,7 +180,8 @@
         global_row[:, None] + lane_step[None, :] < axial_total
     )
     blocks = jnp.where(inside[:, None, :], stiffness, jnp.zeros_like(stiffness))
-    force = banded_force(blocks, rows_in, degrees)
+    half = axial_rows // 2
+    force = banded_force(blocks, rows_in, degrees, 0, half)
 
     force, table = lax.optimization_barrier((force, table))
     slot_index = source_owner[:, 0] * node_count + source_node
@@ -197,7 +208,9 @@
         .set(target_node)
         .reshape(sectors, load_capacity)
     )
+    outgoing, force = lax.optimization_barrier((outgoing, force))
     arrived = lax.all_to_all(outgoing, "circ", split_axis=0, concat_axis=0, tiled=True)
+    force = banded_force(blocks, rows_in, degrees, half, axial_rows - half, force)
     arrived_node = lax.all_to_all(node_slot, "circ", split_axis=0, concat_axis=0, tiled=True)
     selector = (
         arrived_node.reshape(-1)[None, :] == jnp.arange(node_count, dtype=jnp.int32)[:, None]

time: 152 us -> 137 us (0.901)
  waiting for transfers between devices: 28.4 us -> 9.6 us
  Pallas kernels: 31.9 us -> 35.2 us
    all_to_all x1, waiting for transfers between devices: 17.3 us -> 5.27 us  [body(): lax.all_to_all(outgoing, 'circ', split_axis=0, concat_axis=0, tiled=True)]
    ppermute x2, waiting for transfers between devices: 11 us -> 4.1 us  [extended(): lax.ppermute(tail, axis, [(i, (i + 1) % count) for i in range(count)])]
    ppermute x2, starting transfers between devices: 0.06 us -> 3.58 us  [extended(): lax.ppermute(tail, axis, [(i, (i + 1) % count) for i in range(count)])]
    pallas_call x1 -> x2, Pallas kernels: 22.3 us -> 25.6 us  [banded_force(): pl.pallas_call(functools.partial(stiff_kernel, degrees=degrees, first=fir...]
    ppermute x2, starting transfers between devices: 6.38 us -> 4.26 us  [extended(): lax.ppermute(head, axis, [((i + 1) % count, i) for i in range(count)])]
    unnamed x16 -> x14, local copies, waits for them, and re-layouts: 2.24 us -> 3.25 us
  transfers between devices with their start and end apart: 7 -> 7, of which waited for: 3 -> 3; matrix products, arithmetic and copies ran while one was open for 35% -> 38% of each run, Pallas kernels for 21% -> 26%
where the time goes in v3:
time: 137 us; the launch traced here: 136 us
  local copies, waits for them, and re-layouts  42 us (31%)
  Pallas kernels  35.2 us (26%)
  starting transfers between devices  16.2 us (12%)
  between operations  14.2 us (10%)
  other arithmetic  10.8 us (8%)
  waiting for transfers between devices  9.6 us (7%)
  matrix products  7.95 us (6%)
    pallas_call x2, Pallas kernels, banded_force(): pl.pallas_call(functools.partial(stiff_kernel, degrees=degrees, first=fir...  25.6 us
    gather x1, local copies, waits for them, and re-layouts, body(): velocity = jnp.take(table, slot_index, axis=0, mode='clip')  18.7 us
    pallas_call x1, Pallas kernels, near_field(): pl.pallas_call(pressure_kernel, grid_spec=grid_spec, out_shape=[jax.Shape...  9.61 us
    reshape x1, local copies, waits for them, and re-layouts, body(): padded.reshape(axial_rows + 2, (circum_rows + 2) * degrees, vectors)  6.22 us
    all_to_all x1, waiting for transfers between devices, body(): lax.all_to_all(outgoing, 'circ', split_axis=0, concat_axis=0, tiled=True)  5.27 us
    scatter x1, local copies, waits for them, and re-layouts, body(): node_slot = jnp.full((sectors * load_capacity,), -1, jnp.int32).at[load_s...  4.49 us
    all_to_all x1, starting transfers between devices, body(): lax.all_to_all(outgoing, 'circ', split_axis=0, concat_axis=0, tiled=True)  4.4 us
    ppermute x2, starting transfers between devices, extended(): lax.ppermute(head, axis, [((i + 1) % count, i) for i in range(count)])  4.26 us
  transfers between devices with their start and end apart: 7, of which 3 were waited for; matrix products, arithmetic and copies ran while one was open for 38% of the time, Pallas kernels for 26%

profile of v3, /device:TPU:0, one launch (start us, length us, event | category | flops | bytes accessed | tf_op | source)
XLA Modules:
  0.0 136.0 jit_solution(8761825512494339890)
XLA Ops:
  7.2 0.0 copy-start
  7.2 0.0 copy-start.4
  7.2 0.0 copy-start.3
  7.2 0.0 all-gather.2.cloned.1.call-start
  7.2 2.0 %slice.51 = bf16[16,64,1,256]{3,1,2,0:T(8,128)(2,1)} slice(bf16[16,64,6,256]{3,1,2,0:T(8,128)(2,1)} %param.11), slice={[0:16], [0:64], [0:1], [0:256]} | slice | bytes 1048576 | tf_op jit(solution)/shard_map/slice | solution.py:172
  9.3 0.0 all-gather.2.cloned.1.call-update
  9.3 1.8 %fusion.23 = (bf16[1,64,6,256]{3,1,2,0:T(8,128)(2,1)}, bf16[1,64,6,256]{3,1,2,0:T(8,128)(2,1)}) fusion(bf16[16,64,6,256]{3,1,2,0:T(8,128)(2,1)} %param.11), kind=kLoop, calls=%fused_computation.47 | loop fusion | bytes 786432 | tf_op jit(solution)/shard_map/slice | solution.py:14
  11.1 3.0 %collective-permute-start = (bf16[1,64,6,256]{3,1,2,0:T(8,128)(2,1)}, bf16[1,64,6,256]{3,1,2,0:T(8,128)(2,1)}, u32[]{:S(2)}, u32[]{:S(2)}) collective-permute-start(bf16[1,64,6,256]{3,1,2,0:T(8,128)(2,1)} %get-tuple-element.29), channel_id=1, source_target_pairs={{0,8},{8,16},{16,24},{24,0},{1,9},{9,17},{17,25},{25,1},{2,10},{10... | collective-permute-start | bytes 589832 | tf_op jit(solution)/shard_map/ppermute | solution.py:18
  14.1 2.0 %collective-permute-start.1 = (bf16[1,64,6,256]{3,1,2,0:T(8,128)(2,1)}, bf16[1,64,6,256]{3,1,2,0:T(8,128)(2,1)S(1)}, u32[]{:S(2)}, u32[]{:S(2)}) collective-permute-start(bf16[1,64,6,256]{3,1,2,0:T(8,128)(2,1)} %get-tuple-element.28), channel_id=1, source_target_pairs={{8,0},{16,8},{24,16},{0,24},{9,1},{17,9},{25,17},{1,25},{10,2},{18... | collective-permute-start | bytes 589832 | tf_op jit(solution)/shard_map/ppermute | solution.py:20
  16.1 0.7 fusion.14
  16.8 2.3 %reduce-window.6 = s32[8,8,128]{2,1,0:T(8,128)S(1)} reduce-window(s32[8,8,128]{2,1,0:T(8,128)S(1)} %fusion.14, s32[]{:T(128)} %constant.58.clone.1), window={size=1x1x128 pad=0_0x0_0x127_0}, to_apply=%region_0.1 | reduce-window | flops 1040384 | bytes 65540 | tf_op jit(solution)/shard_map/reduce-window
  19.1 0.3 slice_reduce_fusion
  19.4 0.2 reduce-window.9
  19.5 0.1 add_bitcast_fusion
  19.6 0.7 fusion.13
  20.3 0.7 compare_select_fusion
  21.0 4.5 %scatter_custom_fusion = s32[2560]{0:T(1024)S(1)} fusion(s32[1024]{0:T(1024)S(1)} %bitcast.47, s32[1024]{0:T(1024)} %param.19, s32[]{:T(128)} %constant.59.clone.1), kind=kCustom, calls=%fused_computation.34 | custom fusion | bytes 10752 | tf_op jit(solution)/shard_map/scatter | solution.py:208
  25.5 0.7 all_to_all.9
  26.2 3.9 %all-to-all-start = ((s32[8,1,320]{2,1,0:T(1,128)}), s32[8,1,320]{2,1,0:T(1,128)S(1)}, u32[]{:S(2)}, u32[]{:S(2)}) async-start(s32[8,1,320]{2,1,0:T(1,128)} %all_to_all.9), calls=%async_computation | async-start | bytes 24576 | tf_op jit(solution)/shard_map/all_to_all | solution.py:214
  30.2 0.1 fusion.15
  30.2 2.1 %broadcast_select_fusion.s_ref = bf16[16,64,324]{2,1,0:T(8,128)(2,1)} fusion(bf16[16,64,324]{2,1,0:T(8,128)(2,1)} %param.12, pred[16,324]{1,0:T(8,128)(4,1)S(1)} %fusion.15), kind=kLoop, calls=%fused_computation.14 | loop fusion | flops 331776 | bytes 1332288 | tf_op jit(solution)/shard_map/jit(_where)/select_n | solution.py:182
  32.4 0.0 copy-done.4
  32.4 0.0 copy-done.3
  32.4 0.0 collective-permute-done
  32.4 0.9 constant_dynamic-update-slice_fusion.2
  33.4 0.0 copy-done
  33.4 0.0 copy-start.2
  33.4 0.0 copy-start.5
  33.4 0.4 constant_dynamic-update-slice_fusion.1
  33.8 0.0 collective-permute-done.1
  33.9 0.0 copy-start.1
  33.9 1.9 %copy-done.1 = bf16[18,64,6,256]{3,1,2,0:T(8,128)(2,1)} copy-done((bf16[18,64,6,256]{3,1,2,0:T(8,128)(2,1)}, bf16[18,64,6,256]{3,1,2,0:T(8,128)(2,1)S(1)}, u32[]{:S(2)}) %copy-start.1) | copy-done | bytes 3538968
  35.8 0.2 fusion.22
  35.9 0.6 collective-permute-start.2
  36.5 2.2 %collective-permute-start.3 = (bf16[18,1,6,256]{3,1,2,0:T(2,128)(2,1)S(1)}, bf16[18,1,6,256]{3,1,2,0:T(2,128)(2,1)S(1)}, u32[]{:S(2)}, u32[]{:S(2)}) collective-permute-start(bf16[18,1,6,256]{3,1,2,0:T(2,128)(2,1)S(1)} %get-tuple-element.27), channel_id=1, source_target_pairs={{1,0},{2,1},{3,2},{4,3},{5,4},{6,5},{7,6},{0,7},{9,8},{10,9},{11,1... | collective-permute-start | bytes 165896 | tf_op jit(solution)/shard_map/ppermute | solution.py:20
  38.7 0.0 copy-done.2
  38.7 0.0 copy-done.5
  38.7 1.0 copy.14.area_ref
  39.8 4.1 %collective-permute-done.2 = bf16[18,1,6,256]{3,1,2,0:T(2,128)(2,1)S(1)} collective-permute-done((bf16[18,1,6,256]{3,1,2,0:T(2,128)(2,1)S(1)}, bf16[18,1,6,256]{3,1,2,0:T(2,128)(2,1)S(1)}, u32[]{:S(2)}, u32[]{:S(2)}) %collective-permute-start.2) | collective-permute-done | bytes 55328 | tf_op jit(solution)/shard_map/ppermute | solution.py:18
  43.8 0.2 collective-permute-done.3
  44.1 3.8 %pad_maximum_fusion = bf16[18,66,6,256]{3,1,2,0:T(8,128)(2,1)S(1)} fusion(bf16[18,1,6,256]{3,1,2,0:T(2,128)(2,1)S(1)} %collective-permute-done.3, bf16[18,64,6,256]{3,1,2,0:T(8,128)(2,1)} %copy-done.1, bf16[18,1,6,256]{3,1,2,0:T(2,128)(2,1)S(1)} %collective-permute-done.2), kind=kLoop, calls=%fused_computation.9 | loop fusion | flops 10948608 | bytes 7299072 | tf_op jit(solution)/shard_map/concatenate | solution.py:16
  47.9 3.3 %copy.13 = bf16[18,66,6,256]{3,2,1,0:T(8,128)(2,1)} copy(bf16[18,66,6,256]{3,1,2,0:T(8,128)(2,1)S(1)} %pad_maximum_fusion) | data formatting | bytes 7299072 | tf_op jit(solution)/shard_map/concatenate | solution.py:16
  51.2 6.2 %reshape.150.rows_ref = bf16[18,396,256]{2,1,0:T(8,128)(2,1)} reshape(bf16[18,66,6,256]{3,2,1,0:T(8,128)(2,1)} %copy.13) | data formatting | bytes 7299072 | tf_op jit(solution)/shard_map/reshape | solution.py:176
  57.5 12.8 %shard_map.104.rest_0_ = f32[16,384,256]{2,1,0:T(8,128)} custom-call(bf16[16,64,324]{2,1,0:T(8,128)(2,1)} %broadcast_select_fusion.s_ref, bf16[18,396,256]{2,1,0:T(8,128)(2,1)} %reshape.150.rows_ref), custom_call_target="tpu_custom_call" | custom-call | tf_op jit(solution)/shard_map/pallas_call | solution.py:139
  70.3 0.0 all-gather.2.cloned.1.call-done
  70.3 18.7 %gather_fusion = bf16[4096,256]{1,0:T(8,128)(2,1)} fusion(bf16[8192,256]{1,0:T(8,128)(2,1)} %all-gather.2.cloned.1.call-done, s32[4096]{0:T(1024)S(1)} %add_clamp_fusion), kind=kCustom, calls=%fused_computation | custom fusion | bytes 4210688 | tf_op jit(solution)/shard_map/jit(_take)/gather | solution.py:188
  88.9 9.6 %shard_map.105 = (f32[2,1024,256]{2,1,0:T(8,128)}, bf16[1024,256]{1,0:T(8,128)(2,1)}) custom-call(s32[4,12]{1,0:T(4,128)} %near_ref.1, bf16[4,12,2,256,256]{4,3,2,1,0:T(8,128)(2,1)} %kern_ref.1, bf16[16,256,256]{2,1,0:T(8,128)(2,1)} %bitcast.37, f32[1024,1]{1,0:T(8,128)} %copy.14.area_ref), custom_call_target="tpu_custom_call" | custom-call | tf_op jit(solution)/shard_map/pallas_call | solution.py:66
  98.5 4.1 %fusion.6 = bf16[2560,256]{1,0:T(8,128)(2,1)} fusion(bf16[1024,256]{1,0:T(8,128)(2,1)} %get-tuple-element.21, s32[1024]{0:T(1024)S(1)} %multiply_add_fusion.1), kind=kOutput, calls=%fused_computation.10 | convolution fusion | flops 1345454080 | bytes 1839104 | tf_op jit(solution)/shard_map/dot_general | solution.py:201
  102.7 0.0 all-to-all-done
  102.7 4.4 %all-to-all-start.1 = ((bf16[8,320,256]{2,1,0:T(8,128)(2,1)}), bf16[8,320,256]{2,1,0:T(8,128)(2,1)S(1)}, u32[]{:S(2)}, u32[]{:S(2)}) async-start(bf16[8,320,256]{2,1,0:T(8,128)(2,1)} %bitcast.7), calls=%async_computation.1 | async-start | bytes 2621440 | tf_op jit(solution)/shard_map/all_to_all | solution.py:212
  107.1 0.1 eq.72
  107.2 12.8 %shard_map.106 = f32[16,384,256]{2,1,0:T(8,128)} custom-call(bf16[16,64,324]{2,1,0:T(8,128)(2,1)} %broadcast_select_fusion.s_ref, bf16[18,396,256]{2,1,0:T(8,128)(2,1)} %reshape.150.rows_ref, f32[16,384,256]{2,1,0:T(8,128)} %shard_map.104.rest_0_), custom_call_target="tpu_custom_call", output_to_operand_aliasing={{}: (2, {})} | custom-call | tf_op jit(solution)/shard_map/pallas_call | solution.py:139
  120.0 5.3 %all-to-all-done.1 = bf16[8,320,256]{2,1,0:T(8,128)(2,1)S(1)} async-done(((bf16[8,320,256]{2,1,0:T(8,128)(2,1)}), bf16[8,320,256]{2,1,0:T(8,128)(2,1)S(1)}, u32[]{:S(2)}, u32[]{:S(2)}) %all-to-all-start.1) | async-done | bytes 1310752 | tf_op jit(solution)/shard_map/all_to_all | solution.py:212
  125.3 3.8 %fusion.10 = f32[16,384,256]{2,1,0:T(8,128)} fusion(f32[16,384,256]{2,1,0:T(8,128)} %shard_map.106, bf16[2560,256,1]{1,0,2:T(8,128)(2,1)S(1)} %bitcast.39, s32[16,64]{1,0:T(8,128)S(1)} %multiply_add_fusion, s32[2560]{0:T(1024)S(1)} %eq.72), kind=kOutput, calls=%fused_computation.13 | convolution fusion | flops 1345323008 | bytes 3422208 | tf_op jit(solution)/shard_map/dot_general | solution.py:218
  (8 shorter events, 0.1 us)
Async XLA Ops:
  7.2 26.2 %copy-start = (bf16[16,64,6,256]{3,1,2,0:T(8,128)(2,1)S(1)}, bf16[16,64,6,256]{3,1,2,0:T(8,128)(2,1)}, u32[]{:S(2)}) copy-start(bf16[16,64,6,256]{3,1,2,0:T(8,128)(2,1)} %param.11) | copy-start | bytes 9437188
  7.2 25.2 %copy-start.4 = (s32[4096,1]{0,1:T(1,128)S(1)}, s32[4096,1]{0,1:T(1,128)}, u32[]{:S(2)}) copy-start(s32[4096,1]{0,1:T(1,128)} %param.16) | copy-start | bytes 49156
  7.2 25.2 %copy-start.3 = (s32[4096]{0:T(1024)S(1)}, s32[4096]{0:T(1024)}, u32[]{:S(2)}) copy-start(s32[4096]{0:T(1024)} %param.17) | copy-start | bytes 49156
  7.2 63.1 %all-gather.2.cloned.1.call-start = ((), (), s32[]{:S(2)}) async-start(), calls=%async_computation.2 | async-start | bytes 4718592 | tf_op jit(solution)/shard_map/all_gather | solution.py:173
  11.1 21.4 %collective-permute-start = (bf16[1,64,6,256]{3,1,2,0:T(8,128)(2,1)}, bf16[1,64,6,256]{3,1,2,0:T(8,128)(2,1)}, u32[]{:S(2)}, u32[]{:S(2)}) collective-permute-start(bf16[1,64,6,256]{3,1,2,0:T(8,128)(2,1)} %get-tuple-element.29), channel_id=1, source_target_pairs={{0,8},{8,16},{16,24},{24,0},{1,9},{9,17},{17,25},{25,1},{2,10},{10... | collective-permute-start | bytes 589832 | tf_op jit(solution)/shard_map/ppermute | solution.py:18
  14.1 19.7 %collective-permute-start.1 = (bf16[1,64,6,256]{3,1,2,0:T(8,128)(2,1)}, bf16[1,64,6,256]{3,1,2,0:T(8,128)(2,1)S(1)}, u32[]{:S(2)}, u32[]{:S(2)}) collective-permute-start(bf16[1,64,6,256]{3,1,2,0:T(8,128)(2,1)} %get-tuple-element.28), channel_id=1, source_target_pairs={{8,0},{16,8},{24,16},{0,24},{9,1},{17,9},{25,17},{1,25},{10,2},{18... | collective-permute-start | bytes 589832 | tf_op jit(solution)/shard_map/ppermute | solution.py:20
  26.2 76.5 %all-to-all-start = ((s32[8,1,320]{2,1,0:T(1,128)}), s32[8,1,320]{2,1,0:T(1,128)S(1)}, u32[]{:S(2)}, u32[]{:S(2)}) async-start(s32[8,1,320]{2,1,0:T(1,128)} %all_to_all.9), calls=%async_computation | async-start | bytes 24576 | tf_op jit(solution)/shard_map/all_to_all | solution.py:214
  33.4 5.3 %copy-start.2 = (s32[1024,1]{0,1:T(1,128)S(1)}, s32[1024,1]{0,1:T(1,128)}, u32[]{:S(2)}) copy-start(s32[1024,1]{0,1:T(1,128)} %param.18) | copy-start | bytes 12292
  33.4 5.3 %copy-start.5 = (f32[1024]{0:T(1024)S(1)}, f32[1024]{0:T(1024)}, u32[]{:S(2)}) copy-start(f32[1024]{0:T(1024)} %param.14) | copy-start | bytes 12292
  33.9 1.9 %copy-start.1 = (bf16[18,64,6,256]{3,1,2,0:T(8,128)(2,1)}, bf16[18,64,6,256]{3,1,2,0:T(8,128)(2,1)S(1)}, u32[]{:S(2)}) copy-start(bf16[18,64,6,256]{3,1,2,0:T(8,128)(2,1)S(1)} %constant_dynamic-update-slice_fusion) | copy-start | bytes 10616836
  35.9 7.9 %collective-permute-start.2 = (bf16[18,1,6,256]{3,1,2,0:T(2,128)(2,1)S(1)}, bf16[18,1,6,256]{3,1,2,0:T(2,128)(2,1)S(1)}, u32[]{:S(2)}, u32[]{:S(2)}) collective-permute-start(bf16[18,1,6,256]{3,1,2,0:T(2,128)(2,1)S(1)} %get-tuple-element.26), channel_id=1, source_target_pairs={{0,1},{1,2},{2,3},{3,4},{4,5},{5,6},{6,7},{7,0},{8,9},{9,10},{10,1... | collective-permute-start | bytes 165896 | tf_op jit(solution)/shard_map/ppermute | solution.py:18
  36.5 7.6 %collective-permute-start.3 = (bf16[18,1,6,256]{3,1,2,0:T(2,128)(2,1)S(1)}, bf16[18,1,6,256]{3,1,2,0:T(2,128)(2,1)S(1)}, u32[]{:S(2)}, u32[]{:S(2)}) collective-permute-start(bf16[18,1,6,256]{3,1,2,0:T(2,128)(2,1)S(1)} %get-tuple-element.27), channel_id=1, source_target_pairs={{1,0},{2,1},{3,2},{4,3},{5,4},{6,5},{7,6},{0,7},{9,8},{10,9},{11,1... | collective-permute-start | bytes 165896 | tf_op jit(solution)/shard_map/ppermute | solution.py:20
  102.7 22.6 %all-to-all-start.1 = ((bf16[8,320,256]{2,1,0:T(8,128)(2,1)}), bf16[8,320,256]{2,1,0:T(8,128)(2,1)S(1)}, u32[]{:S(2)}, u32[]{:S(2)}) async-start(bf16[8,320,256]{2,1,0:T(8,128)(2,1)} %bitcast.7), calls=%async_computation.1 | async-start | bytes 2621440 | tf_op jit(solution)/shard_map/all_to_all | solution.py:212
Sparse Core Ops, SparseCore 0:
  10.5 41.6 all-gather.1

commit v4 on v3

--- a/solution.py
+++ b/solution.py
@@ -73,15 +73,17 @@
     )(near_cells, kernel, source_cells, areas.reshape(targets, 1))
 
 
-def stiff_kernel(s_ref, rows_ref, *rest, degrees, first):
+def stiff_kernel(s_ref, rows_ref, top_ref, bottom_ref, halo_ref, *rest, degrees, first):
     out_ref, sel_ref, band_ref = rest[-3:]
     step = pl.program_id(0)
     a = step + first
+    last = rows_ref.shape[0] - 1
     nodes = s_ref.shape[1]
     offsets = band_ref.shape[0]
     group = 128
     span = offsets * degrees
-    wide = ((band_ref.shape[2] + group - 1) // group) * group
+    wide = band_ref.shape[2]
+    inner = nodes * degrees
 
     @pl.when(step == 0)
     def _():
@@ -105,37 +107,39 @@
             piece = jnp.concatenate([spread[:, blk * group : (blk + 1) * group], pad], axis=1)
             parts = []
             for g in range(nodes // 8):
-                rows = piece[g * 8 : (g + 1) * 8]
-                if g:
-                    rows = pltpu.roll(rows, g * 8 * degrees, 1)
+                rows = pltpu.roll(piece[g * 8 : (g + 1) * 8], (g * 8 * degrees - degrees) % wide, 1)
                 parts.append(pltpu.roll(rows, 0, 1, stride=degrees, stride_axis=0))
             skewed = jnp.concatenate(parts, axis=0)
-            band_ref[d, i * nodes : (i + 1) * nodes, :] = skewed[:, : band_ref.shape[2]].astype(
-                band_ref.dtype
-            )
+            band_ref[d, i * nodes : (i + 1) * nodes, :] = skewed.astype(band_ref.dtype)
+    above = jnp.where(a == 0, top_ref[0], rows_ref[jnp.maximum(a - 1, 0)])
+    below = jnp.where(a == last, bottom_ref[0], rows_ref[jnp.minimum(a + 1, last)])
     acc = None
-    for d in range(offsets):
-        part = jnp.dot(band_ref[d], rows_ref[a + d], preferred_element_type=jnp.float32)
+    for d, rows in enumerate((above, rows_ref[a], below)):
+        part = jnp.dot(band_ref[d, :, :inner], rows, preferred_element_type=jnp.float32)
+        part += jnp.dot(band_ref[d, :, inner:], halo_ref[a + d], preferred_element_type=jnp.float32)
         acc = part if acc is None else acc + part
     out_ref[0] = acc
 
 
-def banded_force(blocks, rows_in, degrees, first, count, previous=None):
+def banded_force(blocks, rows, top, bottom, halo, degrees, first, count, previous=None):
     axial_rows, nodes, width = blocks.shape
     offsets = 3
-    band_cols = rows_in.shape[1]
-    vectors = rows_in.shape[-1]
+    vectors = rows.shape[-1]
     band_rows = degrees * nodes
+    band_cols = band_rows + halo.shape[1]
     in_specs = [
         pl.BlockSpec((1, nodes, width), lambda a: (a + first, 0, 0)),
-        pl.BlockSpec(rows_in.shape, lambda a: (0, 0, 0)),
+        pl.BlockSpec(rows.shape, lambda a: (0, 0, 0)),
+        pl.BlockSpec(top.shape, lambda a: (0, 0, 0)),
+        pl.BlockSpec(bottom.shape, lambda a: (0, 0, 0)),
+        pl.BlockSpec(halo.shape, lambda a: (0, 0, 0)),
     ]
-    operands = [blocks, rows_in]
+    operands = [blocks, rows, top, bottom, halo]
     aliases = {}
     if previous is not None:
         in_specs.append(pl.BlockSpec(memory_space=pl.ANY))
         operands.append(previous)
-        aliases = {2: 0}
+        aliases = {len(operands) - 1: 0}
     return pl.pallas_call(
         functools.partial(stiff_kernel, degrees=degrees, first=first),
         grid=(count,),
@@ -172,8 +176,20 @@
     radial = displacement[:, :, 0, :].reshape(node_count, vectors)
     table = lax.all_gather(radial, "circ", axis=0, tiled=True)
 
-    padded = extended(displacement, (("ax", 0), ("circ", 1)), 1)
-    rows_in = padded.reshape(axial_rows + 2, (circum_rows + 2) * degrees, vectors)
+    node_rows = displacement.reshape(axial_rows, circum_rows * degrees, vectors)
+    count_ax = lax.axis_size("ax")
+    top = lax.ppermute(node_rows[-1:], "ax", [(i, (i + 1) % count_ax) for i in range(count_ax)])
+    bottom = lax.ppermute(node_rows[:1], "ax", [((i + 1) % count_ax, i) for i in range(count_ax)])
+    first_nodes = jnp.concatenate(
+        [top[:, :degrees], node_rows[:, :degrees], bottom[:, :degrees]], axis=0
+    )
+    last_nodes = jnp.concatenate(
+        [top[:, -degrees:], node_rows[:, -degrees:], bottom[:, -degrees:]], axis=0
+    )
+    left = lax.ppermute(last_nodes, "circ", [(i, (i + 1) % sectors) for i in range(sectors)])
+    right = lax.ppermute(first_nodes, "circ", [((i + 1) % sectors, i) for i in range(sectors)])
+    gap = jnp.zeros((axial_rows + 2, 128 - 2 * degrees, vectors), displacement.dtype)
+    halo = jnp.concatenate([right, gap, left], axis=1)
     global_row = lax.axis_index("ax") * axial_rows + jnp.arange(axial_rows, dtype=jnp.int32)
     lane_step = jnp.arange(stiffness.shape[2], dtype=jnp.int32) // (3 * degrees * degrees) - 1
     inside = (global_row[:, None] + lane_step[None, :] >= 0) & (
@@ -181,7 +197,7 @@
     )
     blocks = jnp.where(inside[:, None, :], stiffness, jnp.zeros_like(stiffness))
     half = axial_rows // 2
-    force = banded_force(blocks, rows_in, degrees, 0, half)
+    force = banded_force(blocks, node_rows, top, bottom, halo, degrees, 0, half)
 
     force, table = lax.optimization_barrier((force, table))
     slot_index = source_owner[:, 0] * node_count + source_node
@@ -210,7 +226,9 @@
     )
     outgoing, force = lax.optimization_barrier((outgoing, force))
     arrived = lax.all_to_all(outgoing, "circ", split_axis=0, concat_axis=0, tiled=True)
-    force = banded_force(blocks, rows_in, degrees, half, axial_rows - half, force)
+    force = banded_force(
+        blocks, node_rows, top, bottom, halo, degrees, half, axial_rows - half, force
+    )
     arrived_node = lax.all_to_all(node_slot, "circ", split_axis=0, concat_axis=0, tiled=True)
     selector = (
         arrived_node.reshape(-1)[None, :] == jnp.arange(node_count, dtype=jnp.int32)[:, None]

time: 137 us -> 129 us (0.942)
  local copies, waits for them, and re-layouts: 42 us -> 35.3 us
  Pallas kernels: 35.2 us -> 39 us
  other arithmetic: 10.8 us -> 8.03 us
    reshape x1, local copies, waits for them, and re-layouts: 6.22 us -> 1.09 us  [body(): node_rows = displacement.reshape(axial_rows, circum_rows * degrees, vectors)]
    pallas_call x2, Pallas kernels: 25.6 us -> 29.4 us  [banded_force(): pl.pallas_call(functools.partial(stiff_kernel, degrees=degrees, first=fir...]
    concatenate x2 -> x1, local copies, waits for them, and re-layouts: 3.33 us -> 0.08 us  [body(): halo = jnp.concatenate([right, gap, left], axis=1)]
    slice x2 -> x8, local copies, waits for them, and re-layouts: 1.95 us -> 5.09 us  [the longest x3 3.51 us: body(): node_rows[:1]]
    all_to_all x1, waiting for transfers between devices: 5.27 us -> 3.16 us  [body(): lax.all_to_all(outgoing, 'circ', split_axis=0, concat_axis=0, tiled=True)]
    unnamed x14 -> x15, local copies, waits for them, and re-layouts: 3.25 us -> 1.81 us
    concatenate x1 -> x3, other arithmetic: 3.85 us -> 2.56 us  [the longest x1 1.22 us: body(): halo = jnp.concatenate([right, gap, left], axis=1)]
  transfers between devices with their start and end apart: 7 -> 7, of which waited for: 3 -> 3; matrix products, arithmetic and copies ran while one was open for 38% -> 35% of each run, Pallas kernels for 26% -> 30%
where the time goes in v4:
time: 129 us
  Pallas kernels  39 us (30%)
  local copies, waits for them, and re-layouts  35.3 us (27%)
  starting transfers between devices  15.5 us (12%)
  between operations  14.2 us (11%)
  waiting for transfers between devices  8.5 us (7%)
  other arithmetic  8.03 us (6%)
  matrix products  7.97 us (6%)
    pallas_call x2, Pallas kernels, banded_force(): pl.pallas_call(functools.partial(stiff_kernel, degrees=degrees, first=fir...  29.4 us
    gather x1, local copies, waits for them, and re-layouts, body(): velocity = jnp.take(table, slot_index, axis=0, mode='clip')  18.7 us
    pallas_call x1, Pallas kernels, near_field(): pl.pallas_call(pressure_kernel, grid_spec=grid_spec, out_shape=[jax.Shape...  9.59 us
    scatter x1, local copies, waits for them, and re-layouts, body(): node_slot = jnp.full((sectors * load_capacity,), -1, jnp.int32).at[load_s...  4.49 us
    dot_general x1, matrix products, body(): jnp.dot(gather_slot, load_value, preferred_element_type=jnp.float32)  4.14 us
    all_to_all x1, starting transfers between devices, body(): lax.all_to_all(node_slot, 'circ', split_axis=0, concat_axis=0, tiled=True)  3.94 us
    dot_general x1, matrix products, body(): jnp.dot(selector, arrived.reshape(-1, vectors), preferred_element_type=jn...  3.83 us
    all_to_all x1, starting transfers between devices, body(): lax.all_to_all(outgoing, 'circ', split_axis=0, concat_axis=0, tiled=True)  3.75 us
  transfers between devices with their start and end apart: 7, of which 3 were waited for; matrix products, arithmetic and copies ran while one was open for 35% of the time, Pallas kernels for 30%

profile of v4, /device:TPU:0, one launch (start us, length us, event | category | flops | bytes accessed | tf_op | source)
XLA Modules:
  0.0 128.5 jit_solution(16449869189692515309)
XLA Ops:
  7.2 0.0 copy-start.1
  7.2 0.0 copy-start.3
  7.2 0.0 all-gather.2.cloned.1.call-start
  7.2 2.0 %slice.75 = bf16[16,64,1,256]{3,1,2,0:T(8,128)(2,1)} slice(bf16[16,64,6,256]{3,1,2,0:T(8,128)(2,1)} %param.11), slice={[0:16], [0:64], [0:1], [0:256]} | slice | bytes 1048576 | tf_op jit(solution)/shard_map/slice | solution.py:176
  9.3 0.0 all-gather.2.cloned.1.call-update
  9.3 1.7 %fusion.23 = (bf16[1,64,6,256]{3,1,2,0:T(8,128)(2,1)}, bf16[1,64,6,256]{3,1,2,0:T(8,128)(2,1)S(1)}) fusion(bf16[16,64,6,256]{3,1,2,0:T(8,128)(2,1)} %param.11), kind=kLoop, calls=%fused_computation.46 | loop fusion | bytes 786432 | tf_op jit(solution)/shard_map/slice | solution.py:182
  11.0 0.1 copy.16
  11.1 0.7 slice.64
  11.9 3.0 %collective-permute-start = (bf16[1,384,256]{2,1,0:T(8,128)(2,1)}, bf16[1,384,256]{2,1,0:T(8,128)(2,1)}, u32[]{:S(2)}, u32[]{:S(2)}) collective-permute-start(bf16[1,384,256]{2,1,0:T(8,128)(2,1)} %slice.64), channel_id=1, source_target_pairs={{0,8},{8,16},{16,24},{24,0},{1,9},{9,17},{17,25},{25,1},{2,10},{10... | collective-permute-start | bytes 589832 | tf_op jit(solution)/shard_map/ppermute | solution.py:181
  14.9 1.0 copy.17
  15.9 0.7 slice.66
  16.7 2.0 %collective-permute-start.1 = (bf16[1,384,256]{2,1,0:T(8,128)(2,1)}, bf16[1,384,256]{2,1,0:T(8,128)(2,1)S(1)}, u32[]{:S(2)}, u32[]{:S(2)}) collective-permute-start(bf16[1,384,256]{2,1,0:T(8,128)(2,1)} %slice.66), channel_id=1, source_target_pairs={{8,0},{16,8},{24,16},{0,24},{9,1},{17,9},{25,17},{1,25},{10,2},{18... | collective-permute-start | bytes 589832 | tf_op jit(solution)/shard_map/ppermute | solution.py:182
  18.7 0.0 copy-done.3
  18.7 2.3 %reduce-window.6 = s32[8,8,128]{2,1,0:T(8,128)S(1)} reduce-window(s32[8,8,128]{2,1,0:T(8,128)S(1)} %fusion.14, s32[]{:T(128)} %constant.59.clone.1), window={size=1x1x128 pad=0_0x0_0x127_0}, to_apply=%region_0.1 | reduce-window | flops 1040384 | bytes 65540 | tf_op jit(solution)/shard_map/reduce-window
  21.0 0.3 slice_reduce_fusion
  21.3 0.2 reduce-window.9
  21.4 0.1 add_bitcast_fusion
  21.6 4.5 %scatter_custom_fusion = s32[2560]{0:T(1024)S(1)} fusion(s32[1024]{0:T(1024)S(1)} %bitcast.49, s32[1024]{0:T(1024)} %param.19, s32[]{:T(128)} %constant.60.clone.1), kind=kCustom, calls=%fused_computation.33 | custom fusion | bytes 10752 | tf_op jit(solution)/shard_map/scatter | solution.py:224
  26.1 0.7 all_to_all.9
  26.7 3.9 %all-to-all-start = ((s32[8,1,320]{2,1,0:T(1,128)}), s32[8,1,320]{2,1,0:T(1,128)S(1)}, u32[]{:S(2)}, u32[]{:S(2)}) async-start(s32[8,1,320]{2,1,0:T(1,128)} %all_to_all.9), calls=%async_computation | async-start | bytes 24576 | tf_op jit(solution)/shard_map/all_to_all | solution.py:232
  30.7 0.0 copy-done.1
  30.7 1.8 %copy.15 = bf16[16,64,6,256]{3,0,2,1:T(8,128)(2,1)S(1)} copy(bf16[16,64,6,256]{3,1,2,0:T(8,128)(2,1)S(1)} %copy-done.1) | data formatting | bytes 6291456 | tf_op args[0]
  32.5 0.0 copy-start.5
  32.5 0.0 copy-start.4
  32.5 0.0 copy-start.6
  32.5 1.1 copy.22.rows_ref
  33.6 0.0 copy-start
  33.6 0.1 fusion.15
  33.7 2.8 %broadcast_select_fusion.s_ref = bf16[16,64,324]{2,1,0:T(8,128)(2,1)} fusion(bf16[16,64,324]{2,1,0:T(8,128)(2,1)} %param.12, pred[16,324]{1,0:T(8,128)(4,1)S(1)} %fusion.15), kind=kLoop, calls=%fused_computation.14 | loop fusion | flops 331776 | bytes 1332288 | tf_op jit(solution)/shard_map/jit(_where)/select_n | solution.py:198
  36.5 0.0 copy-done.5
  36.5 0.0 copy-done.4
  36.6 0.0 collective-permute-done.top_ref
  36.6 0.7 fusion.24
  37.3 0.0 collective-permute-done.1.bottom_ref
  37.3 0.0 copy-start.2
  37.3 0.7 pad_maximum_fusion.1
  38.0 2.7 %collective-permute-start.2 = (bf16[18,6,256]{2,1,0:T(8,128)(2,1)}, bf16[18,6,256]{2,1,0:T(8,128)(2,1)S(1)}, u32[]{:S(2)}, u32[]{:S(2)}) collective-permute-start(bf16[18,6,256]{2,1,0:T(8,128)(2,1)} %pad_maximum_fusion.1), channel_id=1, source_target_pairs={{1,0},{2,1},{3,2},{4,3},{5,4},{6,5},{7,6},{0,7},{9,8},{10,9},{11,1... | collective-permute-start | bytes 165896 | tf_op jit(solution)/shard_map/ppermute | solution.py:190
  40.6 0.7 pad_maximum_fusion.2
  41.3 0.0 collective-permute-start.3
  41.3 0.0 copy-done.6
  41.3 1.0 copy.21.area_ref
  42.3 0.1 pad.3.clone
  42.4 2.6 %collective-permute-done.2 = bf16[18,6,256]{2,1,0:T(8,128)(2,1)S(1)} collective-permute-done((bf16[18,6,256]{2,1,0:T(8,128)(2,1)}, bf16[18,6,256]{2,1,0:T(8,128)(2,1)S(1)}, u32[]{:S(2)}, u32[]{:S(2)}) %collective-permute-start.2) | collective-permute-done | bytes 55328 | tf_op jit(solution)/shard_map/ppermute | solution.py:190
  45.0 2.7 %collective-permute-done.3 = bf16[18,6,256]{2,1,0:T(8,128)(2,1)S(1)} collective-permute-done((bf16[18,6,256]{2,1,0:T(8,128)(2,1)}, bf16[18,6,256]{2,1,0:T(8,128)(2,1)S(1)}, u32[]{:S(2)}, u32[]{:S(2)}) %collective-permute-start.3) | collective-permute-done | bytes 55328 | tf_op jit(solution)/shard_map/ppermute | solution.py:189
  47.7 1.2 pad_maximum_fusion.halo_ref
  49.0 0.0 copy-done
  49.0 0.0 copy-done.2
  49.0 14.8 %shard_map.104.rest_0_ = f32[16,384,256]{2,1,0:T(8,128)} custom-call(bf16[16,64,324]{2,1,0:T(8,128)(2,1)} %broadcast_select_fusion.s_ref, bf16[16,384,256]{2,1,0:T(8,128)(2,1)} %copy-done, bf16[1,384,256]{2,1,0:T(8,128)(2,1)} %collective-permute-done.top_ref, bf16[1,384,256]{2,1,0:T(8,128)(2,1)} %copy-done.2, bf16[18,128,256]{2,1,0:T(8,128)(2,1)} %pad_maximum_fusion.halo_ref), custom_call_target="tpu_custom_call" | custom-call | tf_op jit(solution)/shard_map/pallas_call | solution.py:143
  63.7 0.0 all-gather.2.cloned.1.call-done
  63.7 18.7 %gather_fusion = bf16[4096,256]{1,0:T(8,128)(2,1)} fusion(bf16[8192,256]{1,0:T(8,128)(2,1)} %all-gather.2.cloned.1.call-done, s32[4096]{0:T(1024)S(1)} %add_clamp_fusion), kind=kCustom, calls=%fused_computation | custom fusion | bytes 4210688 | tf_op jit(solution)/shard_map/jit(_take)/gather | solution.py:204
  82.4 9.6 %shard_map.105 = (f32[2,1024,256]{2,1,0:T(8,128)}, bf16[1024,256]{1,0:T(8,128)(2,1)}) custom-call(s32[4,12]{1,0:T(4,128)} %near_ref.1, bf16[4,12,2,256,256]{4,3,2,1,0:T(8,128)(2,1)} %kern_ref.1, bf16[16,256,256]{2,1,0:T(8,128)(2,1)} %bitcast.39, f32[1024,1]{1,0:T(8,128)} %copy.21.area_ref), custom_call_target="tpu_custom_call" | custom-call | tf_op jit(solution)/shard_map/pallas_call | solution.py:66
  92.0 4.1 %fusion.6 = bf16[2560,256]{1,0:T(8,128)(2,1)} fusion(bf16[1024,256]{1,0:T(8,128)(2,1)} %get-tuple-element.21, s32[1024]{0:T(1024)S(1)} %multiply_add_fusion.1), kind=kOutput, calls=%fused_computation.9 | convolution fusion | flops 1345454080 | bytes 1839104 | tf_op jit(solution)/shard_map/dot_general | solution.py:217
  96.1 0.0 all-to-all-done
  96.1 3.8 %all-to-all-start.1 = ((bf16[8,320,256]{2,1,0:T(8,128)(2,1)}), bf16[8,320,256]{2,1,0:T(8,128)(2,1)S(1)}, u32[]{:S(2)}, u32[]{:S(2)}) async-start(bf16[8,320,256]{2,1,0:T(8,128)(2,1)} %bitcast.8), calls=%async_computation.1 | async-start | bytes 2621440 | tf_op jit(solution)/shard_map/all_to_all | solution.py:228
  99.9 0.1 eq.72
  100.0 14.7 %shard_map.106 = f32[16,384,256]{2,1,0:T(8,128)} custom-call(bf16[16,64,324]{2,1,0:T(8,128)(2,1)} %broadcast_select_fusion.s_ref, bf16[16,384,256]{2,1,0:T(8,128)(2,1)} %copy-done, bf16[1,384,256]{2,1,0:T(8,128)(2,1)} %collective-permute-done.top_ref, bf16[1,384,256]{2,1,0:T(8,128)(2,1)} %copy-done.2, ...), custom_call_target="tpu_custom_call", output_to_operand_aliasing={{}: (5, {})} | custom-call | tf_op jit(solution)/shard_map/pallas_call | solution.py:143
  114.7 3.2 %all-to-all-done.1 = bf16[8,320,256]{2,1,0:T(8,128)(2,1)S(1)} async-done(((bf16[8,320,256]{2,1,0:T(8,128)(2,1)}), bf16[8,320,256]{2,1,0:T(8,128)(2,1)S(1)}, u32[]{:S(2)}, u32[]{:S(2)}) %all-to-all-start.1) | async-done | bytes 1310752 | tf_op jit(solution)/shard_map/all_to_all | solution.py:228
  117.8 3.8 %fusion.10 = f32[16,384,256]{2,1,0:T(8,128)} fusion(f32[16,384,256]{2,1,0:T(8,128)} %shard_map.106, bf16[2560,256,1]{1,0,2:T(8,128)(2,1)S(1)} %bitcast.41, s32[16,64]{1,0:T(8,128)S(1)} %multiply_add_fusion, s32[2560]{0:T(1024)S(1)} %eq.72), kind=kOutput, calls=%fused_computation.13 | convolution fusion | flops 1345323008 | bytes 3422208 | tf_op jit(solution)/shard_map/dot_general | solution.py:236
  (13 shorter events, 0.2 us)
Async XLA Ops:
  7.2 23.5 %copy-start.1 = (bf16[16,64,6,256]{3,1,2,0:T(8,128)(2,1)S(1)}, bf16[16,64,6,256]{3,1,2,0:T(8,128)(2,1)}, u32[]{:S(2)}) copy-start(bf16[16,64,6,256]{3,1,2,0:T(8,128)(2,1)} %param.11) | copy-start | bytes 9437188
  7.2 11.5 %copy-start.3 = (s32[1024,1]{0,1:T(1,128)S(1)}, s32[1024,1]{0,1:T(1,128)}, u32[]{:S(2)}) copy-start(s32[1024,1]{0,1:T(1,128)} %param.18) | copy-start | bytes 12292
  7.2 56.5 %all-gather.2.cloned.1.call-start = ((), (), s32[]{:S(2)}) async-start(), calls=%async_computation.2 | async-start | bytes 4718592 | tf_op jit(solution)/shard_map/all_gather | solution.py:177
  11.9 24.7 %collective-permute-start = (bf16[1,384,256]{2,1,0:T(8,128)(2,1)}, bf16[1,384,256]{2,1,0:T(8,128)(2,1)}, u32[]{:S(2)}, u32[]{:S(2)}) collective-permute-start(bf16[1,384,256]{2,1,0:T(8,128)(2,1)} %slice.64), channel_id=1, source_target_pairs={{0,8},{8,16},{16,24},{24,0},{1,9},{9,17},{17,25},{25,1},{2,10},{10... | collective-permute-start | bytes 589832 | tf_op jit(solution)/shard_map/ppermute | solution.py:181
  16.7 20.6 %collective-permute-start.1 = (bf16[1,384,256]{2,1,0:T(8,128)(2,1)}, bf16[1,384,256]{2,1,0:T(8,128)(2,1)S(1)}, u32[]{:S(2)}, u32[]{:S(2)}) collective-permute-start(bf16[1,384,256]{2,1,0:T(8,128)(2,1)} %slice.66), channel_id=1, source_target_pairs={{8,0},{16,8},{24,16},{0,24},{9,1},{17,9},{25,17},{1,25},{10,2},{18... | collective-permute-start | bytes 589832 | tf_op jit(solution)/shard_map/ppermute | solution.py:182
  26.7 69.4 %all-to-all-start = ((s32[8,1,320]{2,1,0:T(1,128)}), s32[8,1,320]{2,1,0:T(1,128)S(1)}, u32[]{:S(2)}, u32[]{:S(2)}) async-start(s32[8,1,320]{2,1,0:T(1,128)} %all_to_all.9), calls=%async_computation | async-start | bytes 24576 | tf_op jit(solution)/shard_map/all_to_all | solution.py:232
  32.5 4.0 %copy-start.5 = (s32[4096,1]{0,1:T(1,128)S(1)}, s32[4096,1]{0,1:T(1,128)}, u32[]{:S(2)}) copy-start(s32[4096,1]{0,1:T(1,128)} %param.16) | copy-start | bytes 49156
  32.5 4.0 %copy-start.4 = (s32[4096]{0:T(1024)S(1)}, s32[4096]{0:T(1024)}, u32[]{:S(2)}) copy-start(s32[4096]{0:T(1024)} %param.17) | copy-start | bytes 49156
  32.5 8.8 %copy-start.6 = (f32[1024]{0:T(1024)S(1)}, f32[1024]{0:T(1024)}, u32[]{:S(2)}) copy-start(f32[1024]{0:T(1024)} %param.14) | copy-start | bytes 12292
  33.6 15.4 %copy-start = (bf16[16,384,256]{2,1,0:T(8,128)(2,1)}, bf16[16,384,256]{2,1,0:T(8,128)(2,1)S(1)}, u32[]{:S(2)}) copy-start(bf16[16,384,256]{2,1,0:T(8,128)(2,1)S(1)} %copy.22.rows_ref) | copy-start | bytes 9437188
  37.3 11.7 %copy-start.2 = (bf16[1,384,256]{2,1,0:T(8,128)(2,1)}, bf16[1,384,256]{2,1,0:T(8,128)(2,1)S(1)}, u32[]{:S(2)}) copy-start(bf16[1,384,256]{2,1,0:T(8,128)(2,1)S(1)} %collective-permute-done.1.bottom_ref) | copy-start | bytes 589828
  38.0 7.0 %collective-permute-start.2 = (bf16[18,6,256]{2,1,0:T(8,128)(2,1)}, bf16[18,6,256]{2,1,0:T(8,128)(2,1)S(1)}, u32[]{:S(2)}, u32[]{:S(2)}) collective-permute-start(bf16[18,6,256]{2,1,0:T(8,128)(2,1)} %pad_maximum_fusion.1), channel_id=1, source_target_pairs={{1,0},{2,1},{3,2},{4,3},{5,4},{6,5},{7,6},{0,7},{9,8},{10,9},{11,1... | collective-permute-start | bytes 165896 | tf_op jit(solution)/shard_map/ppermute | solution.py:190
  41.3 6.4 %collective-permute-start.3 = (bf16[18,6,256]{2,1,0:T(8,128)(2,1)}, bf16[18,6,256]{2,1,0:T(8,128)(2,1)S(1)}, u32[]{:S(2)}, u32[]{:S(2)}) collective-permute-start(bf16[18,6,256]{2,1,0:T(8,128)(2,1)} %pad_maximum_fusion.2), channel_id=1, source_target_pairs={{0,1},{1,2},{2,3},{3,4},{4,5},{5,6},{6,7},{7,0},{8,9},{9,10},{10,1... | collective-permute-start | bytes 165896 | tf_op jit(solution)/shard_map/ppermute | solution.py:189
  96.1 21.7 %all-to-all-start.1 = ((bf16[8,320,256]{2,1,0:T(8,128)(2,1)}), bf16[8,320,256]{2,1,0:T(8,128)(2,1)S(1)}, u32[]{:S(2)}, u32[]{:S(2)}) async-start(bf16[8,320,256]{2,1,0:T(8,128)(2,1)} %bitcast.8), calls=%async_computation.1 | async-start | bytes 2621440 | tf_op jit(solution)/shard_map/all_to_all | solution.py:228
Sparse Core Ops, SparseCore 0:
  10.5 40.9 all-gather.1

commit v5 on v4

--- a/solution.py
+++ b/solution.py
@@ -170,7 +170,6 @@
     degrees = displacement.shape[2]
     vectors = displacement.shape[3]
     sectors = lax.axis_size("circ")
-    axial_total = axial_rows * lax.axis_size("ax")
     node_count = axial_rows * circum_rows
 
     radial = displacement[:, :, 0, :].reshape(node_count, vectors)
@@ -180,6 +179,9 @@
     count_ax = lax.axis_size("ax")
     top = lax.ppermute(node_rows[-1:], "ax", [(i, (i + 1) % count_ax) for i in range(count_ax)])
     bottom = lax.ppermute(node_rows[:1], "ax", [((i + 1) % count_ax, i) for i in range(count_ax)])
+    ax_index = lax.axis_index("ax")
+    top = jnp.where(ax_index == 0, jnp.zeros_like(top), top)
+    bottom = jnp.where(ax_index == count_ax - 1, jnp.zeros_like(bottom), bottom)
     first_nodes = jnp.concatenate(
         [top[:, :degrees], node_rows[:, :degrees], bottom[:, :degrees]], axis=0
     )
@@ -190,12 +192,7 @@
     right = lax.ppermute(first_nodes, "circ", [((i + 1) % sectors, i) for i in range(sectors)])
     gap = jnp.zeros((axial_rows + 2, 128 - 2 * degrees, vectors), displacement.dtype)
     halo = jnp.concatenate([right, gap, left], axis=1)
-    global_row = lax.axis_index("ax") * axial_rows + jnp.arange(axial_rows, dtype=jnp.int32)
-    lane_step = jnp.arange(stiffness.shape[2], dtype=jnp.int32) // (3 * degrees * degrees) - 1
-    inside = (global_row[:, None] + lane_step[None, :] >= 0) & (
-        global_row[:, None] + lane_step[None, :] < axial_total
-    )
-    blocks = jnp.where(inside[:, None, :], stiffness, jnp.zeros_like(stiffness))
+    blocks = stiffness
     half = axial_rows // 2
     force = banded_force(blocks, node_rows, top, bottom, halo, degrees, 0, half)
 
@@ -218,12 +215,12 @@
         jnp.bfloat16
     )
     outgoing = outgoing.reshape(sectors, load_capacity, vectors)
-    node_slot = (
-        jnp.full((sectors * load_capacity,), -1, jnp.int32)
-        .at[load_slot]
-        .set(target_node)
-        .reshape(sectors, load_capacity)
-    )
+    node_slot = jnp.dot(
+        gather_slot.astype(jnp.float32),
+        target_node.astype(jnp.float32),
+        precision=lax.Precision.HIGHEST,
+    )
+    node_slot = jnp.round(node_slot).astype(jnp.int32).reshape(sectors, load_capacity)
     outgoing, force = lax.optimization_barrier((outgoing, force))
     arrived = lax.all_to_all(outgoing, "circ", split_axis=0, concat_axis=0, tiled=True)
     force = banded_force(

time: 129 us -> 132 us (1.023)
  matrix products: 7.97 us -> 12.6 us
    dot_general x0 -> x1, matrix products: none -> 4.67 us  [body(): jnp.dot(gather_slot.astype(jnp.float32), target_node.astype(jnp.float32),...]
    scatter x1 -> x0, local copies, waits for them, and re-layouts: 4.49 us -> none  [body(): node_slot = jnp.full((sectors * load_capacity,), -1, jnp.int32).at[load_s...]
    unnamed x15 -> x21, local copies, waits for them, and re-layouts: 1.81 us -> 4.06 us
    reshape x1, local copies, waits for them, and re-layouts: 1.09 us -> 3.08 us  [body(): node_rows = displacement.reshape(axial_rows, circum_rows * degrees, vectors)]
    select_n x2, other arithmetic: 2.78 us -> 1.22 us  [the longest x1 1.19 us: body(): bottom = jnp.where(ax_index == count_ax - 1, jnp.zeros_like(bottom), bottom)]
  transfers between devices with their start and end apart: 7 -> 7, of which waited for: 3 -> 3; matrix products, arithmetic and copies ran while one was open for 35% -> 37% of each run, Pallas kernels for 30% -> 30%
where the time goes in v5:
time: 132 us
  Pallas kernels  39.1 us (30%)
  local copies, waits for them, and re-layouts  35 us (27%)
  starting transfers between devices  15.4 us (12%)
  between operations  14.2 us (11%)
  matrix products  12.6 us (10%)
  other arithmetic  8 us (6%)
  waiting for transfers between devices  7.4 us (6%)
    pallas_call x2, Pallas kernels, banded_force(): pl.pallas_call(functools.partial(stiff_kernel, degrees=degrees, first=fir...  29.4 us
    gather x1, local copies, waits for them, and re-layouts, body(): velocity = jnp.take(table, slot_index, axis=0, mode='clip')  18.7 us
    pallas_call x1, Pallas kernels, near_field(): pl.pallas_call(pressure_kernel, grid_spec=grid_spec, out_shape=[jax.Shape...  9.72 us
    dot_general x1, matrix products, body(): jnp.dot(gather_slot.astype(jnp.float32), target_node.astype(jnp.float32),...  4.67 us
    dot_general x1, matrix products, body(): jnp.dot(gather_slot, load_value, preferred_element_type=jnp.float32)  4.12 us
    unnamed x21, local copies, waits for them, and re-layouts  4.06 us
    all_to_all x1, starting transfers between devices, body(): lax.all_to_all(node_slot, 'circ', split_axis=0, concat_axis=0, tiled=True)  3.94 us
    dot_general x1, matrix products, body(): jnp.dot(selector, arrived.reshape(-1, vectors), preferred_element_type=jn...  3.83 us
  transfers between devices with their start and end apart: 7, of which 3 were waited for; matrix products, arithmetic and copies ran while one was open for 37% of the time, Pallas kernels for 30%

profile of v5, /device:TPU:0, one launch (start us, length us, event | category | flops | bytes accessed | tf_op | source)
XLA Modules:
  0.0 131.7 jit_solution(17141028317076601879)
XLA Ops:
  7.2 0.0 copy-start.4
  7.2 0.0 copy-start.9
  7.2 0.0 all-gather.2.cloned.1.call-start
  7.2 1.9 %slice.75 = bf16[16,64,1,256]{3,1,2,0:T(8,128)(2,1)} slice(bf16[16,64,6,256]{3,1,2,0:T(8,128)(2,1)} %param.11), slice={[0:16], [0:64], [0:1], [0:256]} | slice | bytes 1048576 | tf_op jit(solution)/shard_map/slice | solution.py:175
  9.1 0.0 all-gather.2.cloned.1.call-update
  9.1 1.7 %fusion.19 = (bf16[1,64,6,256]{3,1,2,0:T(8,128)(2,1)}, bf16[1,64,6,256]{3,1,2,0:T(8,128)(2,1)S(1)}) fusion(bf16[16,64,6,256]{3,1,2,0:T(8,128)(2,1)} %param.11), kind=kLoop, calls=%fused_computation.35 | loop fusion | bytes 786432 | tf_op jit(solution)/shard_map/slice | solution.py:181
  10.9 0.1 copy.16
  11.0 0.8 slice.64
  11.7 0.0 copy-start.1
  11.7 3.0 %collective-permute-start = (bf16[1,384,256]{2,1,0:T(8,128)(2,1)}, bf16[1,384,256]{2,1,0:T(8,128)(2,1)}, u32[]{:S(2)}, u32[]{:S(2)}) collective-permute-start(bf16[1,384,256]{2,1,0:T(8,128)(2,1)} %slice.64), channel_id=1, source_target_pairs={{0,8},{8,16},{16,24},{24,0},{1,9},{9,17},{17,25},{25,1},{2,10},{10... | collective-permute-start | bytes 589832 | tf_op jit(solution)/shard_map/ppermute | solution.py:180
  14.8 1.0 copy.17
  15.8 0.8 slice.66
  16.6 2.2 %collective-permute-start.1 = (bf16[1,384,256]{2,1,0:T(8,128)(2,1)}, bf16[1,384,256]{2,1,0:T(8,128)(2,1)}, u32[]{:S(2)}, u32[]{:S(2)}) collective-permute-start(bf16[1,384,256]{2,1,0:T(8,128)(2,1)} %slice.66), channel_id=1, source_target_pairs={{8,0},{16,8},{24,16},{0,24},{9,1},{17,9},{25,17},{1,25},{10,2},{18... | collective-permute-start | bytes 589832 | tf_op jit(solution)/shard_map/ppermute | solution.py:181
  18.7 0.0 copy-done.4
  18.8 2.3 %reduce-window.6 = s32[8,8,128]{2,1,0:T(8,128)S(1)} reduce-window(s32[8,8,128]{2,1,0:T(8,128)S(1)} %fusion.17, s32[]{:T(128)} %constant.42.clone.1), window={size=1x1x128 pad=0_0x0_0x127_0}, to_apply=%region_0.1 | reduce-window | flops 1040384 | bytes 65540 | tf_op jit(solution)/shard_map/reduce-window
  21.0 0.3 slice_reduce_fusion
  21.3 0.2 reduce-window.9
  21.5 0.0 copy-done.9
  21.5 0.1 add_bitcast_fusion
  21.6 0.0 copy-start.7
  21.6 0.6 copy-done.7
  22.2 4.7 %fusion.12 = f32[2560]{0:T(1024)S(1)} fusion(f32[1024,1]{0,1:T(1,128)S(1)} %bitcast.48, s32[1024]{0:T(1024)S(1)} %multiply_add_fusion.1), kind=kOutput, calls=%fused_computation.13 | convolution fusion | flops 34078720 | bytes 18432 | tf_op jit(solution)/shard_map/dot_general | solution.py:218
  26.9 0.7 all_to_all.9
  27.5 3.9 %all-to-all-start = ((s32[8,1,320]{2,1,0:T(1,128)}), s32[8,1,320]{2,1,0:T(1,128)}, u32[]{:S(2)}, u32[]{:S(2)}) async-start(s32[8,1,320]{2,1,0:T(1,128)} %all_to_all.9), calls=%async_computation | async-start | bytes 24576 | tf_op jit(solution)/shard_map/all_to_all | solution.py:229
  31.5 0.0 copy-done.1
  31.5 3.4 %copy.15 = bf16[16,64,6,256]{3,0,2,1:T(8,128)(2,1)} copy(bf16[16,64,6,256]{3,1,2,0:T(8,128)(2,1)S(1)} %copy-done.1) | data formatting | bytes 6291456 | tf_op args[0]
  34.9 0.0 copy-start.6
  34.9 0.0 copy-start.5
  34.9 3.1 %copy.22.rows_ref = bf16[16,384,256]{2,1,0:T(8,128)(2,1)S(1)} copy(bf16[16,384,256]{2,0,1:T(8,128)(2,1)} %bitcast.38) | data formatting | bytes 6291456 | tf_op jit(solution)/shard_map/reshape | solution.py:178
  38.0 0.0 copy-done.6
  38.0 0.0 copy-start
  38.1 0.0 collective-permute-done
  38.1 0.0 copy-start.2
  38.2 0.0 collective-permute-done.1
  38.2 1.2 broadcast_select_fusion.bottom_ref
  39.4 0.0 copy-start.3
  39.4 0.7 pad_maximum_fusion.1
  40.1 2.7 %collective-permute-start.2 = (bf16[18,6,256]{2,1,0:T(8,128)(2,1)}, bf16[18,6,256]{2,1,0:T(8,128)(2,1)}, u32[]{:S(2)}, u32[]{:S(2)}) collective-permute-start(bf16[18,6,256]{2,1,0:T(8,128)(2,1)} %pad_maximum_fusion.1), channel_id=1, source_target_pairs={{1,0},{2,1},{3,2},{4,3},{5,4},{6,5},{7,6},{0,7},{9,8},{10,9},{11,1... | collective-permute-start | bytes 165896 | tf_op jit(solution)/shard_map/ppermute | solution.py:192
  42.7 0.7 pad_maximum_fusion.2
  43.4 0.0 collective-permute-start.3
  43.4 0.0 copy-done.5
  43.4 1.7 %copy.21.area_ref = f32[1024,1]{1,0:T(8,128)} copy(f32[1024,1]{0,1:T(1,128)} %bitcast.47) | data formatting | bytes 8192 | tf_op jit(solution)/shard_map/reshape | solution.py:73
  45.1 0.1 pad.3.clone
  45.2 1.9 %collective-permute-done.2 = bf16[18,6,256]{2,1,0:T(8,128)(2,1)} collective-permute-done((bf16[18,6,256]{2,1,0:T(8,128)(2,1)}, bf16[18,6,256]{2,1,0:T(8,128)(2,1)}, u32[]{:S(2)}, u32[]{:S(2)}) %collective-permute-start.2) | collective-permute-done | bytes 55328 | tf_op jit(solution)/shard_map/ppermute | solution.py:192
  47.1 2.8 %collective-permute-done.3 = bf16[18,6,256]{2,1,0:T(8,128)(2,1)} collective-permute-done((bf16[18,6,256]{2,1,0:T(8,128)(2,1)}, bf16[18,6,256]{2,1,0:T(8,128)(2,1)}, u32[]{:S(2)}, u32[]{:S(2)}) %collective-permute-start.3) | collective-permute-done | bytes 55328 | tf_op jit(solution)/shard_map/ppermute | solution.py:191
  49.9 2.1 %pad_maximum_fusion.halo_ref = bf16[18,128,256]{2,1,0:T(8,128)(2,1)} fusion(bf16[18,6,256]{2,1,0:T(8,128)(2,1)} %collective-permute-done.3, bf16[18,6,256]{2,1,0:T(8,128)(2,1)} %collective-permute-done.2, bf16[128]{0:T(256)(128)(2,1)S(1)} %pad.3.clone), kind=kLoop, calls=%fused_computation.12 | loop fusion | flops 3538944 | bytes 1290496 | tf_op jit(solution)/shard_map/concatenate | solution.py:194
  52.1 0.0 copy-done
  52.1 0.0 copy-done.2
  52.1 0.0 copy-done.3
  52.1 14.7 %shard_map.104.rest_0_ = f32[16,384,256]{2,1,0:T(8,128)} custom-call(bf16[16,64,324]{2,1,0:T(8,128)(2,1)} %s_ref.3, bf16[16,384,256]{2,1,0:T(8,128)(2,1)} %copy-done, bf16[1,384,256]{2,1,0:T(8,128)(2,1)} %copy-done.2, bf16[1,384,256]{2,1,0:T(8,128)(2,1)} %copy-done.3, bf16[18,128,256]{2,1,0:T(8,128)(2,1)} %pad_maximum_fusion.halo_ref), custom_call_target="tpu_custom_call" | custom-call | tf_op jit(solution)/shard_map/pallas_call | solution.py:143
  66.8 0.0 all-gather.2.cloned.1.call-done
  66.8 18.7 %gather_fusion = bf16[4096,256]{1,0:T(8,128)(2,1)} fusion(bf16[8192,256]{1,0:T(8,128)(2,1)} %all-gather.2.cloned.1.call-done, s32[4096]{0:T(1024)S(1)} %add_clamp_fusion), kind=kCustom, calls=%fused_computation | custom fusion | bytes 4210688 | tf_op jit(solution)/shard_map/jit(_take)/gather | solution.py:201
  85.5 0.0 copy-start.8
  85.5 9.7 %shard_map.105 = (f32[2,1024,256]{2,1,0:T(8,128)}, bf16[1024,256]{1,0:T(8,128)(2,1)}) custom-call(s32[4,12]{1,0:T(4,128)} %near_ref.1, bf16[4,12,2,256,256]{4,3,2,1,0:T(8,128)(2,1)} %kern_ref.1, bf16[16,256,256]{2,1,0:T(8,128)(2,1)} %bitcast.39, f32[1024,1]{1,0:T(8,128)} %copy.21.area_ref), custom_call_target="tpu_custom_call" | custom-call | tf_op jit(solution)/shard_map/pallas_call | solution.py:66
  95.2 0.0 copy-done.8
  95.2 4.1 %fusion.8 = bf16[2560,256]{1,0:T(8,128)(2,1)} fusion(bf16[1024,256]{1,0:T(8,128)(2,1)} %get-tuple-element.21, s32[1024]{0:T(1024)S(1)} %copy-done.8), kind=kOutput, calls=%fused_computation.10 | convolution fusion | flops 1345454080 | bytes 1839104 | tf_op jit(solution)/shard_map/dot_general | solution.py:214
  99.3 0.0 all-to-all-done
  99.3 3.6 %all-to-all-start.1 = ((bf16[8,320,256]{2,1,0:T(8,128)(2,1)}), bf16[8,320,256]{2,1,0:T(8,128)(2,1)S(1)}, u32[]{:S(2)}, u32[]{:S(2)}) async-start(bf16[8,320,256]{2,1,0:T(8,128)(2,1)} %bitcast.8), calls=%async_computation.1 | async-start | bytes 2621440 | tf_op jit(solution)/shard_map/all_to_all | solution.py:225
  102.9 0.7 reduce.4
  103.7 0.1 eq.80
  103.7 14.7 %shard_map.106 = f32[16,384,256]{2,1,0:T(8,128)} custom-call(bf16[16,64,324]{2,1,0:T(8,128)(2,1)} %s_ref.3, bf16[16,384,256]{2,1,0:T(8,128)(2,1)} %copy-done, bf16[1,384,256]{2,1,0:T(8,128)(2,1)} %copy-done.2, bf16[1,384,256]{2,1,0:T(8,128)(2,1)} %copy-done.3, bf16[18,128,256]{2,1,0:T(8,128)(2,1)} %pad_maximum_fusion.halo_ref, ...), custom_call_target="tpu_custom_call", output_to_operand_aliasing={{}: (5, {})} | custom-call | tf_op jit(solution)/shard_map/pallas_call | solution.py:143
  118.4 2.6 %all-to-all-done.1 = bf16[8,320,256]{2,1,0:T(8,128)(2,1)S(1)} async-done(((bf16[8,320,256]{2,1,0:T(8,128)(2,1)}), bf16[8,320,256]{2,1,0:T(8,128)(2,1)S(1)}, u32[]{:S(2)}, u32[]{:S(2)}) %all-to-all-start.1) | async-done | bytes 1310752 | tf_op jit(solution)/shard_map/all_to_all | solution.py:225
  121.1 3.8 %fusion.13 = f32[16,384,256]{2,1,0:T(8,128)} fusion(f32[16,384,256]{2,1,0:T(8,128)} %shard_map.106, bf16[2560,256,1]{1,0,2:T(8,128)(2,1)S(1)} %bitcast.41, s32[16,64]{1,0:T(8,128)S(1)} %multiply_add_fusion, s32[2560]{0:T(1024)S(1)} %eq.80), kind=kOutput, calls=%fused_computation.15 | convolution fusion | flops 1345323008 | bytes 3422208 | tf_op jit(solution)/shard_map/dot_general | solution.py:233
  (13 shorter events, 0.1 us)
Async XLA Ops:
  7.2 11.6 %copy-start.4 = (s32[1024,1]{0,1:T(1,128)S(1)}, s32[1024,1]{0,1:T(1,128)}, u32[]{:S(2)}) copy-start(s32[1024,1]{0,1:T(1,128)} %param.18) | copy-start | bytes 12292
  7.2 14.3 %copy-start.9 = (s32[1024]{0:T(1024)S(1)}, s32[1024]{0:T(1024)}, u32[]{:S(2)}) copy-start(s32[1024]{0:T(1024)} %param.19) | copy-start | bytes 12292
  7.2 59.6 %all-gather.2.cloned.1.call-start = ((), (), s32[]{:S(2)}) async-start(), calls=%async_computation.2 | async-start | bytes 4718592 | tf_op jit(solution)/shard_map/all_gather | solution.py:176
  11.7 19.8 %copy-start.1 = (bf16[16,64,6,256]{3,1,2,0:T(8,128)(2,1)S(1)}, bf16[16,64,6,256]{3,1,2,0:T(8,128)(2,1)}, u32[]{:S(2)}) copy-start(bf16[16,64,6,256]{3,1,2,0:T(8,128)(2,1)} %param.11) | copy-start | bytes 9437188
  11.7 26.4 %collective-permute-start = (bf16[1,384,256]{2,1,0:T(8,128)(2,1)}, bf16[1,384,256]{2,1,0:T(8,128)(2,1)}, u32[]{:S(2)}, u32[]{:S(2)}) collective-permute-start(bf16[1,384,256]{2,1,0:T(8,128)(2,1)} %slice.64), channel_id=1, source_target_pairs={{0,8},{8,16},{16,24},{24,0},{1,9},{9,17},{17,25},{25,1},{2,10},{10... | collective-permute-start | bytes 589832 | tf_op jit(solution)/shard_map/ppermute | solution.py:180
  16.6 21.6 %collective-permute-start.1 = (bf16[1,384,256]{2,1,0:T(8,128)(2,1)}, bf16[1,384,256]{2,1,0:T(8,128)(2,1)}, u32[]{:S(2)}, u32[]{:S(2)}) collective-permute-start(bf16[1,384,256]{2,1,0:T(8,128)(2,1)} %slice.66), channel_id=1, source_target_pairs={{8,0},{16,8},{24,16},{0,24},{9,1},{17,9},{25,17},{1,25},{10,2},{18... | collective-permute-start | bytes 589832 | tf_op jit(solution)/shard_map/ppermute | solution.py:181
  21.6 0.6 copy-start.7
  27.5 71.8 %all-to-all-start = ((s32[8,1,320]{2,1,0:T(1,128)}), s32[8,1,320]{2,1,0:T(1,128)}, u32[]{:S(2)}, u32[]{:S(2)}) async-start(s32[8,1,320]{2,1,0:T(1,128)} %all_to_all.9), calls=%async_computation | async-start | bytes 24576 | tf_op jit(solution)/shard_map/all_to_all | solution.py:229
  34.9 3.1 %copy-start.6 = (s32[4096,1]{0,1:T(1,128)S(1)}, s32[4096,1]{0,1:T(1,128)}, u32[]{:S(2)}) copy-start(s32[4096,1]{0,1:T(1,128)} %param.16) | copy-start | bytes 49156
  34.9 8.5 %copy-start.5 = (s32[4096]{0:T(1024)S(1)}, s32[4096]{0:T(1024)}, u32[]{:S(2)}) copy-start(s32[4096]{0:T(1024)} %param.17) | copy-start | bytes 49156
  38.0 14.0 %copy-start = (bf16[16,384,256]{2,1,0:T(8,128)(2,1)}, bf16[16,384,256]{2,1,0:T(8,128)(2,1)S(1)}, u32[]{:S(2)}) copy-start(bf16[16,384,256]{2,1,0:T(8,128)(2,1)S(1)} %copy.22.rows_ref) | copy-start | bytes 9437188
  38.1 13.9 %copy-start.2 = (bf16[1,384,256]{2,1,0:T(8,128)(2,1)}, bf16[1,384,256]{2,1,0:T(8,128)(2,1)S(1)}, u32[]{:S(2)}) copy-start(bf16[1,384,256]{2,1,0:T(8,128)(2,1)S(1)} %broadcast_select_fusion.1.top_ref) | copy-start | bytes 589828
  39.4 12.7 %copy-start.3 = (bf16[1,384,256]{2,1,0:T(8,128)(2,1)}, bf16[1,384,256]{2,1,0:T(8,128)(2,1)S(1)}, u32[]{:S(2)}) copy-start(bf16[1,384,256]{2,1,0:T(8,128)(2,1)S(1)} %broadcast_select_fusion.bottom_ref) | copy-start | bytes 589828
  40.1 7.0 %collective-permute-start.2 = (bf16[18,6,256]{2,1,0:T(8,128)(2,1)}, bf16[18,6,256]{2,1,0:T(8,128)(2,1)}, u32[]{:S(2)}, u32[]{:S(2)}) collective-permute-start(bf16[18,6,256]{2,1,0:T(8,128)(2,1)} %pad_maximum_fusion.1), channel_id=1, source_target_pairs={{1,0},{2,1},{3,2},{4,3},{5,4},{6,5},{7,6},{0,7},{9,8},{10,9},{11,1... | collective-permute-start | bytes 165896 | tf_op jit(solution)/shard_map/ppermute | solution.py:192
  43.4 6.5 %collective-permute-start.3 = (bf16[18,6,256]{2,1,0:T(8,128)(2,1)}, bf16[18,6,256]{2,1,0:T(8,128)(2,1)}, u32[]{:S(2)}, u32[]{:S(2)}) collective-permute-start(bf16[18,6,256]{2,1,0:T(8,128)(2,1)} %pad_maximum_fusion.2), channel_id=1, source_target_pairs={{0,1},{1,2},{2,3},{3,4},{4,5},{5,6},{6,7},{7,0},{8,9},{9,10},{10,1... | collective-permute-start | bytes 165896 | tf_op jit(solution)/shard_map/ppermute | solution.py:191
  85.5 9.7 %copy-start.8 = (s32[1024]{0:T(1024)S(1)}, s32[1024]{0:T(1024)}, u32[]{:S(2)}) copy-start(s32[1024]{0:T(1024)} %copy-done.7) | copy-start | bytes 12292
  99.3 21.7 %all-to-all-start.1 = ((bf16[8,320,256]{2,1,0:T(8,128)(2,1)}), bf16[8,320,256]{2,1,0:T(8,128)(2,1)S(1)}, u32[]{:S(2)}, u32[]{:S(2)}) async-start(bf16[8,320,256]{2,1,0:T(8,128)(2,1)} %bitcast.8), calls=%async_computation.1 | async-start | bytes 2621440 | tf_op jit(solution)/shard_map/all_to_all | solution.py:225
Sparse Core Ops, SparseCore 0:
  10.5 40.8 all-gather.1

commit v6 on v4

--- a/solution.py
+++ b/solution.py
@@ -83,7 +83,6 @@
     group = 128
     span = offsets * degrees
     wide = band_ref.shape[2]
-    inner = nodes * degrees
 
     @pl.when(step == 0)
     def _():
@@ -115,8 +114,8 @@
     below = jnp.where(a == last, bottom_ref[0], rows_ref[jnp.minimum(a + 1, last)])
     acc = None
     for d, rows in enumerate((above, rows_ref[a], below)):
-        part = jnp.dot(band_ref[d, :, :inner], rows, preferred_element_type=jnp.float32)
-        part += jnp.dot(band_ref[d, :, inner:], halo_ref[a + d], preferred_element_type=jnp.float32)
+        both = jnp.concatenate([rows, halo_ref[a + d]], axis=0)
+        part = jnp.dot(band_ref[d], both, preferred_element_type=jnp.float32)
         acc = part if acc is None else acc + part
     out_ref[0] = acc
 

time: 129 us -> 127 us (0.984)
  Pallas kernels: 39 us -> 34.6 us
  waiting for transfers between devices: 8.5 us -> 10.7 us
    pallas_call x2, Pallas kernels: 29.4 us -> 25 us  [banded_force(): pl.pallas_call(functools.partial(stiff_kernel, degrees=degrees, first=fir...]
    all_to_all x1, waiting for transfers between devices: 3.16 us -> 5.33 us  [body(): lax.all_to_all(outgoing, 'circ', split_axis=0, concat_axis=0, tiled=True)]
  transfers between devices with their start and end apart: 7 -> 7, of which waited for: 3 -> 3; matrix products, arithmetic and copies ran while one was open for 35% -> 35% of each run, Pallas kernels for 30% -> 27%
where the time goes in v6:
time: 127 us; the launch traced here: 126 us
  local copies, waits for them, and re-layouts  35.3 us (28%)
  Pallas kernels  34.6 us (27%)
  starting transfers between devices  15.5 us (12%)
  between operations  14.2 us (11%)
  waiting for transfers between devices  10.7 us (8%)
  other arithmetic  8.03 us (6%)
  matrix products  7.97 us (6%)
    pallas_call x2, Pallas kernels, banded_force(): pl.pallas_call(functools.partial(stiff_kernel, degrees=degrees, first=fir...  25 us
    gather x1, local copies, waits for them, and re-layouts, body(): velocity = jnp.take(table, slot_index, axis=0, mode='clip')  18.7 us
    pallas_call x1, Pallas kernels, near_field(): pl.pallas_call(pressure_kernel, grid_spec=grid_spec, out_shape=[jax.Shape...  9.59 us
    all_to_all x1, waiting for transfers between devices, body(): lax.all_to_all(outgoing, 'circ', split_axis=0, concat_axis=0, tiled=True)  5.33 us
    scatter x1, local copies, waits for them, and re-layouts, body(): node_slot = jnp.full((sectors * load_capacity,), -1, jnp.int32).at[load_s...  4.49 us
    dot_general x1, matrix products, body(): jnp.dot(gather_slot, load_value, preferred_element_type=jnp.float32)  4.14 us
    all_to_all x1, starting transfers between devices, body(): lax.all_to_all(node_slot, 'circ', split_axis=0, concat_axis=0, tiled=True)  3.94 us
    dot_general x1, matrix products, body(): jnp.dot(selector, arrived.reshape(-1, vectors), preferred_element_type=jn...  3.83 us
  transfers between devices with their start and end apart: 7, of which 3 were waited for; matrix products, arithmetic and copies ran while one was open for 35% of the time, Pallas kernels for 27%

profile of v6, /device:TPU:0, one launch (start us, length us, event | category | flops | bytes accessed | tf_op | source)
XLA Modules:
  0.0 126.3 jit_solution(3163071246186654047)
XLA Ops:
  7.2 0.0 copy-start.1
  7.2 0.0 copy-start.3
  7.2 0.0 all-gather.2.cloned.1.call-start
  7.2 2.0 %slice.75 = bf16[16,64,1,256]{3,1,2,0:T(8,128)(2,1)} slice(bf16[16,64,6,256]{3,1,2,0:T(8,128)(2,1)} %param.11), slice={[0:16], [0:64], [0:1], [0:256]} | slice | bytes 1048576 | tf_op jit(solution)/shard_map/slice | solution.py:175
  9.3 0.0 all-gather.2.cloned.1.call-update
  9.3 1.7 %fusion.23 = (bf16[1,64,6,256]{3,1,2,0:T(8,128)(2,1)}, bf16[1,64,6,256]{3,1,2,0:T(8,128)(2,1)S(1)}) fusion(bf16[16,64,6,256]{3,1,2,0:T(8,128)(2,1)} %param.11), kind=kLoop, calls=%fused_computation.46 | loop fusion | bytes 786432 | tf_op jit(solution)/shard_map/slice | solution.py:181
  11.0 0.1 copy.16
  11.1 0.7 slice.64
  11.9 3.0 %collective-permute-start = (bf16[1,384,256]{2,1,0:T(8,128)(2,1)}, bf16[1,384,256]{2,1,0:T(8,128)(2,1)}, u32[]{:S(2)}, u32[]{:S(2)}) collective-permute-start(bf16[1,384,256]{2,1,0:T(8,128)(2,1)} %slice.64), channel_id=1, source_target_pairs={{0,8},{8,16},{16,24},{24,0},{1,9},{9,17},{17,25},{25,1},{2,10},{10... | collective-permute-start | bytes 589832 | tf_op jit(solution)/shard_map/ppermute | solution.py:180
  14.9 1.0 copy.17
  15.9 0.7 slice.66
  16.7 2.0 %collective-permute-start.1 = (bf16[1,384,256]{2,1,0:T(8,128)(2,1)}, bf16[1,384,256]{2,1,0:T(8,128)(2,1)S(1)}, u32[]{:S(2)}, u32[]{:S(2)}) collective-permute-start(bf16[1,384,256]{2,1,0:T(8,128)(2,1)} %slice.66), channel_id=1, source_target_pairs={{8,0},{16,8},{24,16},{0,24},{9,1},{17,9},{25,17},{1,25},{10,2},{18... | collective-permute-start | bytes 589832 | tf_op jit(solution)/shard_map/ppermute | solution.py:181
  18.7 0.0 copy-done.3
  18.7 2.3 %reduce-window.6 = s32[8,8,128]{2,1,0:T(8,128)S(1)} reduce-window(s32[8,8,128]{2,1,0:T(8,128)S(1)} %fusion.14, s32[]{:T(128)} %constant.59.clone.1), window={size=1x1x128 pad=0_0x0_0x127_0}, to_apply=%region_0.1 | reduce-window | flops 1040384 | bytes 65540 | tf_op jit(solution)/shard_map/reduce-window
  21.0 0.3 slice_reduce_fusion
  21.3 0.2 reduce-window.9
  21.4 0.1 add_bitcast_fusion
  21.6 4.5 %scatter_custom_fusion = s32[2560]{0:T(1024)S(1)} fusion(s32[1024]{0:T(1024)S(1)} %bitcast.49, s32[1024]{0:T(1024)} %param.19, s32[]{:T(128)} %constant.60.clone.1), kind=kCustom, calls=%fused_computation.33 | custom fusion | bytes 10752 | tf_op jit(solution)/shard_map/scatter | solution.py:223
  26.1 0.7 all_to_all.9
  26.7 3.9 %all-to-all-start = ((s32[8,1,320]{2,1,0:T(1,128)}), s32[8,1,320]{2,1,0:T(1,128)S(1)}, u32[]{:S(2)}, u32[]{:S(2)}) async-start(s32[8,1,320]{2,1,0:T(1,128)} %all_to_all.9), calls=%async_computation | async-start | bytes 24576 | tf_op jit(solution)/shard_map/all_to_all | solution.py:231
  30.7 0.0 copy-done.1
  30.7 1.8 %copy.15 = bf16[16,64,6,256]{3,0,2,1:T(8,128)(2,1)S(1)} copy(bf16[16,64,6,256]{3,1,2,0:T(8,128)(2,1)S(1)} %copy-done.1) | data formatting | bytes 6291456 | tf_op args[0]
  32.5 0.0 copy-start.5
  32.5 0.0 copy-start.4
  32.5 0.0 copy-start.6
  32.5 1.1 copy.22.rows_ref
  33.6 0.0 copy-start
  33.6 0.1 fusion.15
  33.7 2.8 %broadcast_select_fusion.s_ref = bf16[16,64,324]{2,1,0:T(8,128)(2,1)} fusion(bf16[16,64,324]{2,1,0:T(8,128)(2,1)} %param.12, pred[16,324]{1,0:T(8,128)(4,1)S(1)} %fusion.15), kind=kLoop, calls=%fused_computation.14 | loop fusion | flops 331776 | bytes 1332288 | tf_op jit(solution)/shard_map/jit(_where)/select_n | solution.py:197
  36.5 0.0 copy-done.5
  36.5 0.0 copy-done.4
  36.6 0.0 collective-permute-done.top_ref
  36.6 0.7 fusion.24
  37.3 0.0 collective-permute-done.1.bottom_ref
  37.3 0.0 copy-start.2
  37.3 0.7 pad_maximum_fusion.1
  38.0 2.7 %collective-permute-start.2 = (bf16[18,6,256]{2,1,0:T(8,128)(2,1)}, bf16[18,6,256]{2,1,0:T(8,128)(2,1)S(1)}, u32[]{:S(2)}, u32[]{:S(2)}) collective-permute-start(bf16[18,6,256]{2,1,0:T(8,128)(2,1)} %pad_maximum_fusion.1), channel_id=1, source_target_pairs={{1,0},{2,1},{3,2},{4,3},{5,4},{6,5},{7,6},{0,7},{9,8},{10,9},{11,1... | collective-permute-start | bytes 165896 | tf_op jit(solution)/shard_map/ppermute | solution.py:189
  40.6 0.7 pad_maximum_fusion.2
  41.3 0.0 collective-permute-start.3
  41.3 0.0 copy-done.6
  41.3 1.0 copy.21.area_ref
  42.3 0.1 pad.3.clone
  42.4 2.6 %collective-permute-done.2 = bf16[18,6,256]{2,1,0:T(8,128)(2,1)S(1)} collective-permute-done((bf16[18,6,256]{2,1,0:T(8,128)(2,1)}, bf16[18,6,256]{2,1,0:T(8,128)(2,1)S(1)}, u32[]{:S(2)}, u32[]{:S(2)}) %collective-permute-start.2) | collective-permute-done | bytes 55328 | tf_op jit(solution)/shard_map/ppermute | solution.py:189
  45.0 2.7 %collective-permute-done.3 = bf16[18,6,256]{2,1,0:T(8,128)(2,1)S(1)} collective-permute-done((bf16[18,6,256]{2,1,0:T(8,128)(2,1)}, bf16[18,6,256]{2,1,0:T(8,128)(2,1)S(1)}, u32[]{:S(2)}, u32[]{:S(2)}) %collective-permute-start.3) | collective-permute-done | bytes 55328 | tf_op jit(solution)/shard_map/ppermute | solution.py:188
  47.7 1.2 pad_maximum_fusion.halo_ref
  49.0 0.0 copy-done
  49.0 0.0 copy-done.2
  49.0 12.5 %shard_map.104.rest_0_ = f32[16,384,256]{2,1,0:T(8,128)} custom-call(bf16[16,64,324]{2,1,0:T(8,128)(2,1)} %broadcast_select_fusion.s_ref, bf16[16,384,256]{2,1,0:T(8,128)(2,1)} %copy-done, bf16[1,384,256]{2,1,0:T(8,128)(2,1)} %collective-permute-done.top_ref, bf16[1,384,256]{2,1,0:T(8,128)(2,1)} %copy-done.2, bf16[18,128,256]{2,1,0:T(8,128)(2,1)} %pad_maximum_fusion.halo_ref), custom_call_target="tpu_custom_call" | custom-call | tf_op jit(solution)/shard_map/pallas_call | solution.py:142
  61.5 0.0 all-gather.2.cloned.1.call-done
  61.5 18.7 %gather_fusion = bf16[4096,256]{1,0:T(8,128)(2,1)} fusion(bf16[8192,256]{1,0:T(8,128)(2,1)} %all-gather.2.cloned.1.call-done, s32[4096]{0:T(1024)S(1)} %add_clamp_fusion), kind=kCustom, calls=%fused_computation | custom fusion | bytes 4210688 | tf_op jit(solution)/shard_map/jit(_take)/gather | solution.py:203
  80.2 9.6 %shard_map.105 = (f32[2,1024,256]{2,1,0:T(8,128)}, bf16[1024,256]{1,0:T(8,128)(2,1)}) custom-call(s32[4,12]{1,0:T(4,128)} %near_ref.1, bf16[4,12,2,256,256]{4,3,2,1,0:T(8,128)(2,1)} %kern_ref.1, bf16[16,256,256]{2,1,0:T(8,128)(2,1)} %bitcast.39, f32[1024,1]{1,0:T(8,128)} %copy.21.area_ref), custom_call_target="tpu_custom_call" | custom-call | tf_op jit(solution)/shard_map/pallas_call | solution.py:66
  89.7 4.1 %fusion.6 = bf16[2560,256]{1,0:T(8,128)(2,1)} fusion(bf16[1024,256]{1,0:T(8,128)(2,1)} %get-tuple-element.21, s32[1024]{0:T(1024)S(1)} %multiply_add_fusion.1), kind=kOutput, calls=%fused_computation.9 | convolution fusion | flops 1345454080 | bytes 1839104 | tf_op jit(solution)/shard_map/dot_general | solution.py:216
  93.9 0.0 all-to-all-done
  93.9 3.8 %all-to-all-start.1 = ((bf16[8,320,256]{2,1,0:T(8,128)(2,1)}), bf16[8,320,256]{2,1,0:T(8,128)(2,1)S(1)}, u32[]{:S(2)}, u32[]{:S(2)}) async-start(bf16[8,320,256]{2,1,0:T(8,128)(2,1)} %bitcast.8), calls=%async_computation.1 | async-start | bytes 2621440 | tf_op jit(solution)/shard_map/all_to_all | solution.py:227
  97.7 0.1 eq.72
  97.8 12.5 %shard_map.106 = f32[16,384,256]{2,1,0:T(8,128)} custom-call(bf16[16,64,324]{2,1,0:T(8,128)(2,1)} %broadcast_select_fusion.s_ref, bf16[16,384,256]{2,1,0:T(8,128)(2,1)} %copy-done, bf16[1,384,256]{2,1,0:T(8,128)(2,1)} %collective-permute-done.top_ref, bf16[1,384,256]{2,1,0:T(8,128)(2,1)} %copy-done.2, ...), custom_call_target="tpu_custom_call", output_to_operand_aliasing={{}: (5, {})} | custom-call | tf_op jit(solution)/shard_map/pallas_call | solution.py:142
  110.3 5.3 %all-to-all-done.1 = bf16[8,320,256]{2,1,0:T(8,128)(2,1)S(1)} async-done(((bf16[8,320,256]{2,1,0:T(8,128)(2,1)}), bf16[8,320,256]{2,1,0:T(8,128)(2,1)S(1)}, u32[]{:S(2)}, u32[]{:S(2)}) %all-to-all-start.1) | async-done | bytes 1310752 | tf_op jit(solution)/shard_map/all_to_all | solution.py:227
  115.6 3.8 %fusion.10 = f32[16,384,256]{2,1,0:T(8,128)} fusion(f32[16,384,256]{2,1,0:T(8,128)} %shard_map.106, bf16[2560,256,1]{1,0,2:T(8,128)(2,1)S(1)} %bitcast.41, s32[16,64]{1,0:T(8,128)S(1)} %multiply_add_fusion, s32[2560]{0:T(1024)S(1)} %eq.72), kind=kOutput, calls=%fused_computation.13 | convolution fusion | flops 1345323008 | bytes 3422208 | tf_op jit(solution)/shard_map/dot_general | solution.py:235
  (13 shorter events, 0.2 us)
Async XLA Ops:
  7.2 23.5 %copy-start.1 = (bf16[16,64,6,256]{3,1,2,0:T(8,128)(2,1)S(1)}, bf16[16,64,6,256]{3,1,2,0:T(8,128)(2,1)}, u32[]{:S(2)}) copy-start(bf16[16,64,6,256]{3,1,2,0:T(8,128)(2,1)} %param.11) | copy-start | bytes 9437188
  7.2 11.5 %copy-start.3 = (s32[1024,1]{0,1:T(1,128)S(1)}, s32[1024,1]{0,1:T(1,128)}, u32[]{:S(2)}) copy-start(s32[1024,1]{0,1:T(1,128)} %param.18) | copy-start | bytes 12292
  7.2 54.3 %all-gather.2.cloned.1.call-start = ((), (), s32[]{:S(2)}) async-start(), calls=%async_computation.2 | async-start | bytes 4718592 | tf_op jit(solution)/shard_map/all_gather | solution.py:176
  11.9 24.7 %collective-permute-start = (bf16[1,384,256]{2,1,0:T(8,128)(2,1)}, bf16[1,384,256]{2,1,0:T(8,128)(2,1)}, u32[]{:S(2)}, u32[]{:S(2)}) collective-permute-start(bf16[1,384,256]{2,1,0:T(8,128)(2,1)} %slice.64), channel_id=1, source_target_pairs={{0,8},{8,16},{16,24},{24,0},{1,9},{9,17},{17,25},{25,1},{2,10},{10... | collective-permute-start | bytes 589832 | tf_op jit(solution)/shard_map/ppermute | solution.py:180
  16.7 20.6 %collective-permute-start.1 = (bf16[1,384,256]{2,1,0:T(8,128)(2,1)}, bf16[1,384,256]{2,1,0:T(8,128)(2,1)S(1)}, u32[]{:S(2)}, u32[]{:S(2)}) collective-permute-start(bf16[1,384,256]{2,1,0:T(8,128)(2,1)} %slice.66), channel_id=1, source_target_pairs={{8,0},{16,8},{24,16},{0,24},{9,1},{17,9},{25,17},{1,25},{10,2},{18... | collective-permute-start | bytes 589832 | tf_op jit(solution)/shard_map/ppermute | solution.py:181
  26.7 67.2 %all-to-all-start = ((s32[8,1,320]{2,1,0:T(1,128)}), s32[8,1,320]{2,1,0:T(1,128)S(1)}, u32[]{:S(2)}, u32[]{:S(2)}) async-start(s32[8,1,320]{2,1,0:T(1,128)} %all_to_all.9), calls=%async_computation | async-start | bytes 24576 | tf_op jit(solution)/shard_map/all_to_all | solution.py:231
  32.5 4.0 %copy-start.5 = (s32[4096,1]{0,1:T(1,128)S(1)}, s32[4096,1]{0,1:T(1,128)}, u32[]{:S(2)}) copy-start(s32[4096,1]{0,1:T(1,128)} %param.16) | copy-start | bytes 49156
  32.5 4.0 %copy-start.4 = (s32[4096]{0:T(1024)S(1)}, s32[4096]{0:T(1024)}, u32[]{:S(2)}) copy-start(s32[4096]{0:T(1024)} %param.17) | copy-start | bytes 49156
  32.5 8.8 %copy-start.6 = (f32[1024]{0:T(1024)S(1)}, f32[1024]{0:T(1024)}, u32[]{:S(2)}) copy-start(f32[1024]{0:T(1024)} %param.14) | copy-start | bytes 12292
  33.6 15.4 %copy-start = (bf16[16,384,256]{2,1,0:T(8,128)(2,1)}, bf16[16,384,256]{2,1,0:T(8,128)(2,1)S(1)}, u32[]{:S(2)}) copy-start(bf16[16,384,256]{2,1,0:T(8,128)(2,1)S(1)} %copy.22.rows_ref) | copy-start | bytes 9437188
  37.3 11.7 %copy-start.2 = (bf16[1,384,256]{2,1,0:T(8,128)(2,1)}, bf16[1,384,256]{2,1,0:T(8,128)(2,1)S(1)}, u32[]{:S(2)}) copy-start(bf16[1,384,256]{2,1,0:T(8,128)(2,1)S(1)} %collective-permute-done.1.bottom_ref) | copy-start | bytes 589828
  38.0 7.0 %collective-permute-start.2 = (bf16[18,6,256]{2,1,0:T(8,128)(2,1)}, bf16[18,6,256]{2,1,0:T(8,128)(2,1)S(1)}, u32[]{:S(2)}, u32[]{:S(2)}) collective-permute-start(bf16[18,6,256]{2,1,0:T(8,128)(2,1)} %pad_maximum_fusion.1), channel_id=1, source_target_pairs={{1,0},{2,1},{3,2},{4,3},{5,4},{6,5},{7,6},{0,7},{9,8},{10,9},{11,1... | collective-permute-start | bytes 165896 | tf_op jit(solution)/shard_map/ppermute | solution.py:189
  41.3 6.4 %collective-permute-start.3 = (bf16[18,6,256]{2,1,0:T(8,128)(2,1)}, bf16[18,6,256]{2,1,0:T(8,128)(2,1)S(1)}, u32[]{:S(2)}, u32[]{:S(2)}) collective-permute-start(bf16[18,6,256]{2,1,0:T(8,128)(2,1)} %pad_maximum_fusion.2), channel_id=1, source_target_pairs={{0,1},{1,2},{2,3},{3,4},{4,5},{5,6},{6,7},{7,0},{8,9},{9,10},{10,1... | collective-permute-start | bytes 165896 | tf_op jit(solution)/shard_map/ppermute | solution.py:188
  93.9 21.7 %all-to-all-start.1 = ((bf16[8,320,256]{2,1,0:T(8,128)(2,1)}), bf16[8,320,256]{2,1,0:T(8,128)(2,1)S(1)}, u32[]{:S(2)}, u32[]{:S(2)}) async-start(bf16[8,320,256]{2,1,0:T(8,128)(2,1)} %bitcast.8), calls=%async_computation.1 | async-start | bytes 2621440 | tf_op jit(solution)/shard_map/all_to_all | solution.py:227
Sparse Core Ops, SparseCore 0:
  10.5 40.9 all-gather.1

commit v7 on v6

--- a/solution.py
+++ b/solution.py
@@ -33,34 +33,46 @@
 
 def pressure_kernel(near_ref, kern_ref, vel_ref, area_ref, p_ref, load_ref):
     g = pl.program_id(0)
-    near_count = kern_ref.shape[1]
+    chunk = pl.program_id(1)
+    per_chunk = kern_ref.shape[1]
     panel = kern_ref.shape[3]
-    for n in range(near_count):
-        m = near_ref[g, n]
+    acc = None
+    for n in range(per_chunk):
+        m = near_ref[g, chunk * per_chunk + n]
         w = kern_ref[0, n].reshape(2 * panel, panel)
         prod = jnp.dot(w, vel_ref[m], preferred_element_type=jnp.float32)
-        if n == 0:
-            p_ref[...] = prod.reshape(p_ref.shape)
-        else:
-            p_ref[...] += prod.reshape(p_ref.shape)
-    load_ref[...] = (area_ref[...] * p_ref[0]).astype(load_ref.dtype)
+        acc = prod if acc is None else acc + prod
+    acc = acc.reshape(p_ref.shape)
+
+    @pl.when(chunk == 0)
+    def _():
+        p_ref[...] = acc
+
+    @pl.when(chunk > 0)
+    def _():
+        p_ref[...] += acc
+
+    @pl.when(chunk == pl.num_programs(1) - 1)
+    def _():
+        load_ref[...] = (area_ref[...] * p_ref[0]).astype(load_ref.dtype)
 
 
 def near_field(kernel, source_cells, areas, near_cells):
     cells_dev, near_count, _, panel, _ = kernel.shape
     src_cells, _, vectors = source_cells.shape
     targets = cells_dev * panel
+    per_chunk = 4 if near_count % 4 == 0 else near_count
     grid_spec = pltpu.PrefetchScalarGridSpec(
         num_scalar_prefetch=1,
-        grid=(cells_dev,),
+        grid=(cells_dev, near_count // per_chunk),
         in_specs=[
-            pl.BlockSpec((1, near_count, 2, panel, panel), lambda g, near: (g, 0, 0, 0, 0)),
-            pl.BlockSpec((src_cells, panel, vectors), lambda g, near: (0, 0, 0)),
-            pl.BlockSpec((panel, 1), lambda g, near: (g, 0)),
+            pl.BlockSpec((1, per_chunk, 2, panel, panel), lambda g, c, near: (g, c, 0, 0, 0)),
+            pl.BlockSpec((src_cells, panel, vectors), lambda g, c, near: (0, 0, 0)),
+            pl.BlockSpec((panel, 1), lambda g, c, near: (g, 0)),
         ],
         out_specs=[
-            pl.BlockSpec((2, panel, vectors), lambda g, near: (0, g, 0)),
-            pl.BlockSpec((panel, vectors), lambda g, near: (g, 0)),
+            pl.BlockSpec((2, panel, vectors), lambda g, c, near: (0, g, 0)),
+            pl.BlockSpec((panel, vectors), lambda g, c, near: (g, 0)),
         ],
     )
     return pl.pallas_call(

time: 127 us -> 132 us (1.039)
  Pallas kernels: 34.6 us -> 39.4 us
    pallas_call x1, Pallas kernels: 9.59 us -> 14.4 us  [near_field(): pl.pallas_call(pressure_kernel, grid_spec=grid_spec, out_shape=[jax.Shape...]
  transfers between devices with their start and end apart: 7 -> 7, of which waited for: 3 -> 3; matrix products, arithmetic and copies ran while one was open for 35% -> 34% of each run, Pallas kernels for 27% -> 30%
where the time goes in v7:
time: 132 us; the launch traced here: 131 us
  Pallas kernels  39.4 us (30%)
  local copies, waits for them, and re-layouts  35.3 us (27%)
  starting transfers between devices  15.5 us (12%)
  between operations  14.2 us (11%)
  waiting for transfers between devices  10.7 us (8%)
  other arithmetic  8.03 us (6%)
  matrix products  7.97 us (6%)
    pallas_call x2, Pallas kernels, banded_force(): pl.pallas_call(functools.partial(stiff_kernel, degrees=degrees, first=fir...  25 us
    gather x1, local copies, waits for them, and re-layouts, body(): velocity = jnp.take(table, slot_index, axis=0, mode='clip')  18.7 us
    pallas_call x1, Pallas kernels, near_field(): pl.pallas_call(pressure_kernel, grid_spec=grid_spec, out_shape=[jax.Shape...  14.4 us
    all_to_all x1, waiting for transfers between devices, body(): lax.all_to_all(outgoing, 'circ', split_axis=0, concat_axis=0, tiled=True)  5.34 us
    scatter x1, local copies, waits for them, and re-layouts, body(): node_slot = jnp.full((sectors * load_capacity,), -1, jnp.int32).at[load_s...  4.49 us
    dot_general x1, matrix products, body(): jnp.dot(gather_slot, load_value, preferred_element_type=jnp.float32)  4.14 us
    all_to_all x1, starting transfers between devices, body(): lax.all_to_all(node_slot, 'circ', split_axis=0, concat_axis=0, tiled=True)  3.94 us
    dot_general x1, matrix products, body(): jnp.dot(selector, arrived.reshape(-1, vectors), preferred_element_type=jn...  3.83 us
  transfers between devices with their start and end apart: 7, of which 3 were waited for; matrix products, arithmetic and copies ran while one was open for 34% of the time, Pallas kernels for 30%

profile of v7, /device:TPU:0, one launch (start us, length us, event | category | flops | bytes accessed | tf_op | source)
XLA Modules:
  0.0 131.1 jit_solution(2376331133272010400)
XLA Ops:
  7.2 0.0 copy-start.1
  7.2 0.0 copy-start.3
  7.2 0.0 all-gather.2.cloned.1.call-start
  7.2 2.0 %slice.75 = bf16[16,64,1,256]{3,1,2,0:T(8,128)(2,1)} slice(bf16[16,64,6,256]{3,1,2,0:T(8,128)(2,1)} %param.11), slice={[0:16], [0:64], [0:1], [0:256]} | slice | bytes 1048576 | tf_op jit(solution)/shard_map/slice | solution.py:187
  9.3 0.0 all-gather.2.cloned.1.call-update
  9.3 1.7 %fusion.23 = (bf16[1,64,6,256]{3,1,2,0:T(8,128)(2,1)}, bf16[1,64,6,256]{3,1,2,0:T(8,128)(2,1)S(1)}) fusion(bf16[16,64,6,256]{3,1,2,0:T(8,128)(2,1)} %param.11), kind=kLoop, calls=%fused_computation.46 | loop fusion | bytes 786432 | tf_op jit(solution)/shard_map/slice | solution.py:193
  11.0 0.1 copy.16
  11.1 0.7 slice.64
  11.9 3.0 %collective-permute-start = (bf16[1,384,256]{2,1,0:T(8,128)(2,1)}, bf16[1,384,256]{2,1,0:T(8,128)(2,1)}, u32[]{:S(2)}, u32[]{:S(2)}) collective-permute-start(bf16[1,384,256]{2,1,0:T(8,128)(2,1)} %slice.64), channel_id=1, source_target_pairs={{0,8},{8,16},{16,24},{24,0},{1,9},{9,17},{17,25},{25,1},{2,10},{10... | collective-permute-start | bytes 589832 | tf_op jit(solution)/shard_map/ppermute | solution.py:192
  14.9 1.0 copy.17
  15.9 0.7 slice.66
  16.7 2.0 %collective-permute-start.1 = (bf16[1,384,256]{2,1,0:T(8,128)(2,1)}, bf16[1,384,256]{2,1,0:T(8,128)(2,1)S(1)}, u32[]{:S(2)}, u32[]{:S(2)}) collective-permute-start(bf16[1,384,256]{2,1,0:T(8,128)(2,1)} %slice.66), channel_id=1, source_target_pairs={{8,0},{16,8},{24,16},{0,24},{9,1},{17,9},{25,17},{1,25},{10,2},{18... | collective-permute-start | bytes 589832 | tf_op jit(solution)/shard_map/ppermute | solution.py:193
  18.7 0.0 copy-done.3
  18.7 2.3 %reduce-window.6 = s32[8,8,128]{2,1,0:T(8,128)S(1)} reduce-window(s32[8,8,128]{2,1,0:T(8,128)S(1)} %fusion.14, s32[]{:T(128)} %constant.59.clone.1), window={size=1x1x128 pad=0_0x0_0x127_0}, to_apply=%region_0.1 | reduce-window | flops 1040384 | bytes 65540 | tf_op jit(solution)/shard_map/reduce-window
  21.0 0.3 slice_reduce_fusion
  21.3 0.2 reduce-window.9
  21.4 0.1 add_bitcast_fusion
  21.6 4.5 %scatter_custom_fusion = s32[2560]{0:T(1024)S(1)} fusion(s32[1024]{0:T(1024)S(1)} %bitcast.49, s32[1024]{0:T(1024)} %param.19, s32[]{:T(128)} %constant.60.clone.1), kind=kCustom, calls=%fused_computation.33 | custom fusion | bytes 10752 | tf_op jit(solution)/shard_map/scatter | solution.py:235
  26.1 0.7 all_to_all.9
  26.7 3.9 %all-to-all-start = ((s32[8,1,320]{2,1,0:T(1,128)}), s32[8,1,320]{2,1,0:T(1,128)S(1)}, u32[]{:S(2)}, u32[]{:S(2)}) async-start(s32[8,1,320]{2,1,0:T(1,128)} %all_to_all.9), calls=%async_computation | async-start | bytes 24576 | tf_op jit(solution)/shard_map/all_to_all | solution.py:243
  30.7 0.0 copy-done.1
  30.7 1.8 %copy.15 = bf16[16,64,6,256]{3,0,2,1:T(8,128)(2,1)S(1)} copy(bf16[16,64,6,256]{3,1,2,0:T(8,128)(2,1)S(1)} %copy-done.1) | data formatting | bytes 6291456 | tf_op args[0]
  32.5 0.0 copy-start.5
  32.5 0.0 copy-start.4
  32.5 0.0 copy-start.6
  32.5 1.1 copy.22.rows_ref
  33.6 0.0 copy-start
  33.6 0.1 fusion.15
  33.7 2.8 %broadcast_select_fusion.s_ref = bf16[16,64,324]{2,1,0:T(8,128)(2,1)} fusion(bf16[16,64,324]{2,1,0:T(8,128)(2,1)} %param.12, pred[16,324]{1,0:T(8,128)(4,1)S(1)} %fusion.15), kind=kLoop, calls=%fused_computation.14 | loop fusion | flops 331776 | bytes 1332288 | tf_op jit(solution)/shard_map/jit(_where)/select_n | solution.py:209
  36.5 0.0 copy-done.5
  36.5 0.0 copy-done.4
  36.6 0.0 collective-permute-done.top_ref
  36.6 0.7 fusion.24
  37.3 0.0 collective-permute-done.1.bottom_ref
  37.3 0.0 copy-start.2
  37.3 0.7 pad_maximum_fusion.1
  38.0 2.7 %collective-permute-start.2 = (bf16[18,6,256]{2,1,0:T(8,128)(2,1)}, bf16[18,6,256]{2,1,0:T(8,128)(2,1)S(1)}, u32[]{:S(2)}, u32[]{:S(2)}) collective-permute-start(bf16[18,6,256]{2,1,0:T(8,128)(2,1)} %pad_maximum_fusion.1), channel_id=1, source_target_pairs={{1,0},{2,1},{3,2},{4,3},{5,4},{6,5},{7,6},{0,7},{9,8},{10,9},{11,1... | collective-permute-start | bytes 165896 | tf_op jit(solution)/shard_map/ppermute | solution.py:201
  40.6 0.7 pad_maximum_fusion.2
  41.3 0.0 collective-permute-start.3
  41.3 0.0 copy-done.6
  41.3 1.0 copy.21.area_ref
  42.3 0.1 pad.3.clone
  42.4 2.6 %collective-permute-done.2 = bf16[18,6,256]{2,1,0:T(8,128)(2,1)S(1)} collective-permute-done((bf16[18,6,256]{2,1,0:T(8,128)(2,1)}, bf16[18,6,256]{2,1,0:T(8,128)(2,1)S(1)}, u32[]{:S(2)}, u32[]{:S(2)}) %collective-permute-start.2) | collective-permute-done | bytes 55328 | tf_op jit(solution)/shard_map/ppermute | solution.py:201
  45.0 2.7 %collective-permute-done.3 = bf16[18,6,256]{2,1,0:T(8,128)(2,1)S(1)} collective-permute-done((bf16[18,6,256]{2,1,0:T(8,128)(2,1)}, bf16[18,6,256]{2,1,0:T(8,128)(2,1)S(1)}, u32[]{:S(2)}, u32[]{:S(2)}) %collective-permute-start.3) | collective-permute-done | bytes 55328 | tf_op jit(solution)/shard_map/ppermute | solution.py:200
  47.7 1.2 pad_maximum_fusion.halo_ref
  49.0 0.0 copy-done
  49.0 0.0 copy-done.2
  49.0 12.5 %shard_map.104.rest_0_ = f32[16,384,256]{2,1,0:T(8,128)} custom-call(bf16[16,64,324]{2,1,0:T(8,128)(2,1)} %broadcast_select_fusion.s_ref, bf16[16,384,256]{2,1,0:T(8,128)(2,1)} %copy-done, bf16[1,384,256]{2,1,0:T(8,128)(2,1)} %collective-permute-done.top_ref, bf16[1,384,256]{2,1,0:T(8,128)(2,1)} %copy-done.2, bf16[18,128,256]{2,1,0:T(8,128)(2,1)} %pad_maximum_fusion.halo_ref), custom_call_target="tpu_custom_call" | custom-call | tf_op jit(solution)/shard_map/pallas_call | solution.py:154
  61.5 0.0 all-gather.2.cloned.1.call-done
  61.5 18.7 %gather_fusion = bf16[4096,256]{1,0:T(8,128)(2,1)} fusion(bf16[8192,256]{1,0:T(8,128)(2,1)} %all-gather.2.cloned.1.call-done, s32[4096]{0:T(1024)S(1)} %add_clamp_fusion), kind=kCustom, calls=%fused_computation | custom fusion | bytes 4210688 | tf_op jit(solution)/shard_map/jit(_take)/gather | solution.py:215
  80.2 14.4 %shard_map.105 = (f32[2,1024,256]{2,1,0:T(8,128)}, bf16[1024,256]{1,0:T(8,128)(2,1)}) custom-call(s32[4,12]{1,0:T(4,128)} %near_ref.1, bf16[4,12,2,256,256]{4,3,2,1,0:T(8,128)(2,1)} %kern_ref.1, bf16[16,256,256]{2,1,0:T(8,128)(2,1)} %bitcast.39, f32[1024,1]{1,0:T(8,128)} %copy.21.area_ref), custom_call_target="tpu_custom_call" | custom-call | tf_op jit(solution)/shard_map/pallas_call | solution.py:78
  94.5 4.1 %fusion.6 = bf16[2560,256]{1,0:T(8,128)(2,1)} fusion(bf16[1024,256]{1,0:T(8,128)(2,1)} %get-tuple-element.21, s32[1024]{0:T(1024)S(1)} %multiply_add_fusion.1), kind=kOutput, calls=%fused_computation.9 | convolution fusion | flops 1345454080 | bytes 1839104 | tf_op jit(solution)/shard_map/dot_general | solution.py:228
  98.7 0.0 all-to-all-done
  98.7 3.8 %all-to-all-start.1 = ((bf16[8,320,256]{2,1,0:T(8,128)(2,1)}), bf16[8,320,256]{2,1,0:T(8,128)(2,1)S(1)}, u32[]{:S(2)}, u32[]{:S(2)}) async-start(bf16[8,320,256]{2,1,0:T(8,128)(2,1)} %bitcast.8), calls=%async_computation.1 | async-start | bytes 2621440 | tf_op jit(solution)/shard_map/all_to_all | solution.py:239
  102.5 0.1 eq.72
  102.5 12.5 %shard_map.106 = f32[16,384,256]{2,1,0:T(8,128)} custom-call(bf16[16,64,324]{2,1,0:T(8,128)(2,1)} %broadcast_select_fusion.s_ref, bf16[16,384,256]{2,1,0:T(8,128)(2,1)} %copy-done, bf16[1,384,256]{2,1,0:T(8,128)(2,1)} %collective-permute-done.top_ref, bf16[1,384,256]{2,1,0:T(8,128)(2,1)} %copy-done.2, ...), custom_call_target="tpu_custom_call", output_to_operand_aliasing={{}: (5, {})} | custom-call | tf_op jit(solution)/shard_map/pallas_call | solution.py:154
  115.0 5.3 %all-to-all-done.1 = bf16[8,320,256]{2,1,0:T(8,128)(2,1)S(1)} async-done(((bf16[8,320,256]{2,1,0:T(8,128)(2,1)}), bf16[8,320,256]{2,1,0:T(8,128)(2,1)S(1)}, u32[]{:S(2)}, u32[]{:S(2)}) %all-to-all-start.1) | async-done | bytes 1310752 | tf_op jit(solution)/shard_map/all_to_all | solution.py:239
  120.4 3.8 %fusion.10 = f32[16,384,256]{2,1,0:T(8,128)} fusion(f32[16,384,256]{2,1,0:T(8,128)} %shard_map.106, bf16[2560,256,1]{1,0,2:T(8,128)(2,1)S(1)} %bitcast.41, s32[16,64]{1,0:T(8,128)S(1)} %multiply_add_fusion, s32[2560]{0:T(1024)S(1)} %eq.72), kind=kOutput, calls=%fused_computation.13 | convolution fusion | flops 1345323008 | bytes 3422208 | tf_op jit(solution)/shard_map/dot_general | solution.py:247
  (13 shorter events, 0.2 us)
Async XLA Ops:
  7.2 23.5 %copy-start.1 = (bf16[16,64,6,256]{3,1,2,0:T(8,128)(2,1)S(1)}, bf16[16,64,6,256]{3,1,2,0:T(8,128)(2,1)}, u32[]{:S(2)}) copy-start(bf16[16,64,6,256]{3,1,2,0:T(8,128)(2,1)} %param.11) | copy-start | bytes 9437188
  7.2 11.5 %copy-start.3 = (s32[1024,1]{0,1:T(1,128)S(1)}, s32[1024,1]{0,1:T(1,128)}, u32[]{:S(2)}) copy-start(s32[1024,1]{0,1:T(1,128)} %param.18) | copy-start | bytes 12292
  7.2 54.3 %all-gather.2.cloned.1.call-start = ((), (), s32[]{:S(2)}) async-start(), calls=%async_computation.2 | async-start | bytes 4718592 | tf_op jit(solution)/shard_map/all_gather | solution.py:188
  11.9 24.7 %collective-permute-start = (bf16[1,384,256]{2,1,0:T(8,128)(2,1)}, bf16[1,384,256]{2,1,0:T(8,128)(2,1)}, u32[]{:S(2)}, u32[]{:S(2)}) collective-permute-start(bf16[1,384,256]{2,1,0:T(8,128)(2,1)} %slice.64), channel_id=1, source_target_pairs={{0,8},{8,16},{16,24},{24,0},{1,9},{9,17},{17,25},{25,1},{2,10},{10... | collective-permute-start | bytes 589832 | tf_op jit(solution)/shard_map/ppermute | solution.py:192
  16.7 20.6 %collective-permute-start.1 = (bf16[1,384,256]{2,1,0:T(8,128)(2,1)}, bf16[1,384,256]{2,1,0:T(8,128)(2,1)S(1)}, u32[]{:S(2)}, u32[]{:S(2)}) collective-permute-start(bf16[1,384,256]{2,1,0:T(8,128)(2,1)} %slice.66), channel_id=1, source_target_pairs={{8,0},{16,8},{24,16},{0,24},{9,1},{17,9},{25,17},{1,25},{10,2},{18... | collective-permute-start | bytes 589832 | tf_op jit(solution)/shard_map/ppermute | solution.py:193
  26.7 71.9 %all-to-all-start = ((s32[8,1,320]{2,1,0:T(1,128)}), s32[8,1,320]{2,1,0:T(1,128)S(1)}, u32[]{:S(2)}, u32[]{:S(2)}) async-start(s32[8,1,320]{2,1,0:T(1,128)} %all_to_all.9), calls=%async_computation | async-start | bytes 24576 | tf_op jit(solution)/shard_map/all_to_all | solution.py:243
  32.5 4.0 %copy-start.5 = (s32[4096,1]{0,1:T(1,128)S(1)}, s32[4096,1]{0,1:T(1,128)}, u32[]{:S(2)}) copy-start(s32[4096,1]{0,1:T(1,128)} %param.16) | copy-start | bytes 49156
  32.5 4.0 %copy-start.4 = (s32[4096]{0:T(1024)S(1)}, s32[4096]{0:T(1024)}, u32[]{:S(2)}) copy-start(s32[4096]{0:T(1024)} %param.17) | copy-start | bytes 49156
  32.5 8.8 %copy-start.6 = (f32[1024]{0:T(1024)S(1)}, f32[1024]{0:T(1024)}, u32[]{:S(2)}) copy-start(f32[1024]{0:T(1024)} %param.14) | copy-start | bytes 12292
  33.6 15.4 %copy-start = (bf16[16,384,256]{2,1,0:T(8,128)(2,1)}, bf16[16,384,256]{2,1,0:T(8,128)(2,1)S(1)}, u32[]{:S(2)}) copy-start(bf16[16,384,256]{2,1,0:T(8,128)(2,1)S(1)} %copy.22.rows_ref) | copy-start | bytes 9437188
  37.3 11.7 %copy-start.2 = (bf16[1,384,256]{2,1,0:T(8,128)(2,1)}, bf16[1,384,256]{2,1,0:T(8,128)(2,1)S(1)}, u32[]{:S(2)}) copy-start(bf16[1,384,256]{2,1,0:T(8,128)(2,1)S(1)} %collective-permute-done.1.bottom_ref) | copy-start | bytes 589828
  38.0 7.0 %collective-permute-start.2 = (bf16[18,6,256]{2,1,0:T(8,128)(2,1)}, bf16[18,6,256]{2,1,0:T(8,128)(2,1)S(1)}, u32[]{:S(2)}, u32[]{:S(2)}) collective-permute-start(bf16[18,6,256]{2,1,0:T(8,128)(2,1)} %pad_maximum_fusion.1), channel_id=1, source_target_pairs={{1,0},{2,1},{3,2},{4,3},{5,4},{6,5},{7,6},{0,7},{9,8},{10,9},{11,1... | collective-permute-start | bytes 165896 | tf_op jit(solution)/shard_map/ppermute | solution.py:201
  41.3 6.4 %collective-permute-start.3 = (bf16[18,6,256]{2,1,0:T(8,128)(2,1)}, bf16[18,6,256]{2,1,0:T(8,128)(2,1)S(1)}, u32[]{:S(2)}, u32[]{:S(2)}) collective-permute-start(bf16[18,6,256]{2,1,0:T(8,128)(2,1)} %pad_maximum_fusion.2), channel_id=1, source_target_pairs={{0,1},{1,2},{2,3},{3,4},{4,5},{5,6},{6,7},{7,0},{8,9},{9,10},{10,1... | collective-permute-start | bytes 165896 | tf_op jit(solution)/shard_map/ppermute | solution.py:200
  98.7 21.7 %all-to-all-start.1 = ((bf16[8,320,256]{2,1,0:T(8,128)(2,1)}), bf16[8,320,256]{2,1,0:T(8,128)(2,1)S(1)}, u32[]{:S(2)}, u32[]{:S(2)}) async-start(bf16[8,320,256]{2,1,0:T(8,128)(2,1)} %bitcast.8), calls=%async_computation.1 | async-start | bytes 2621440 | tf_op jit(solution)/shard_map/all_to_all | solution.py:239
Sparse Core Ops, SparseCore 0:
  10.5 40.9 all-gather.1

commit v8 on v6

--- a/solution.py
+++ b/solution.py
@@ -25,9 +25,12 @@
 
 
 def slot_positions(owners, sectors, capacity):
-    onehot = (owners[:, None] == jnp.arange(sectors, dtype=jnp.int32)[None, :]).astype(jnp.int32)
-    before = jnp.cumsum(onehot, axis=0) - onehot
-    ranking = jnp.sum(before * onehot, axis=1)
+    onehot = owners[:, None] == jnp.arange(sectors, dtype=jnp.int32)[None, :]
+    count = owners.shape[0]
+    order = jnp.arange(count, dtype=jnp.int32)
+    earlier = (order[None, :] < order[:, None]).astype(jnp.bfloat16)
+    before = jnp.dot(earlier, onehot.astype(jnp.bfloat16), preferred_element_type=jnp.float32)
+    ranking = jnp.sum(jnp.where(onehot, before, 0.0), axis=1).astype(jnp.int32)
     return owners * capacity + ranking
 
 
@@ -169,7 +172,6 @@
     degrees = displacement.shape[2]
     vectors = displacement.shape[3]
     sectors = lax.axis_size("circ")
-    axial_total = axial_rows * lax.axis_size("ax")
     node_count = axial_rows * circum_rows
 
     radial = displacement[:, :, 0, :].reshape(node_count, vectors)
@@ -179,6 +181,9 @@
     count_ax = lax.axis_size("ax")
     top = lax.ppermute(node_rows[-1:], "ax", [(i, (i + 1) % count_ax) for i in range(count_ax)])
     bottom = lax.ppermute(node_rows[:1], "ax", [((i + 1) % count_ax, i) for i in range(count_ax)])
+    ax_index = lax.axis_index("ax")
+    top = jnp.where(ax_index == 0, jnp.zeros_like(top), top)
+    bottom = jnp.where(ax_index == count_ax - 1, jnp.zeros_like(bottom), bottom)
     first_nodes = jnp.concatenate(
         [top[:, :degrees], node_rows[:, :degrees], bottom[:, :degrees]], axis=0
     )
@@ -189,12 +194,7 @@
     right = lax.ppermute(first_nodes, "circ", [((i + 1) % sectors, i) for i in range(sectors)])
     gap = jnp.zeros((axial_rows + 2, 128 - 2 * degrees, vectors), displacement.dtype)
     halo = jnp.concatenate([right, gap, left], axis=1)
-    global_row = lax.axis_index("ax") * axial_rows + jnp.arange(axial_rows, dtype=jnp.int32)
-    lane_step = jnp.arange(stiffness.shape[2], dtype=jnp.int32) // (3 * degrees * degrees) - 1
-    inside = (global_row[:, None] + lane_step[None, :] >= 0) & (
-        global_row[:, None] + lane_step[None, :] < axial_total
-    )
-    blocks = jnp.where(inside[:, None, :], stiffness, jnp.zeros_like(stiffness))
+    blocks = stiffness
     half = axial_rows // 2
     force = banded_force(blocks, node_rows, top, bottom, halo, degrees, 0, half)
 

time: 127 us -> 127 us (level)
  local copies, waits for them, and re-layouts: 35.3 us -> 39.1 us
  other arithmetic: 8.03 us -> 6.05 us
  waiting for transfers between devices: 10.7 us -> 8.8 us
    another operation x2 -> x0, other arithmetic: 2.43 us -> none
    unnamed x15 -> x23, local copies, waits for them, and re-layouts: 1.81 us -> 4.03 us
    reshape x1, local copies, waits for them, and re-layouts: 1.09 us -> 3.02 us  [body(): node_rows = displacement.reshape(axial_rows, circum_rows * degrees, vectors)]
    select_n x1 -> x2, other arithmetic: 2.76 us -> 1.2 us  [the longest x1 1.17 us: body(): bottom = jnp.where(ax_index == count_ax - 1, jnp.zeros_like(bottom), bottom)]
    ppermute x1, waiting for transfers between devices: 2.58 us -> 1.29 us  [body(): lax.ppermute(first_nodes, 'circ', [((i + 1) % sectors, i) for i in range(...]
  transfers between devices with their start and end apart: 7 -> 7, of which waited for: 3 -> 3; matrix products, arithmetic and copies ran while one was open for 35% -> 37% of each run, Pallas kernels for 27% -> 27%
where the time goes in v8:
time: 127 us
  local copies, waits for them, and re-layouts  39.1 us (31%)
  Pallas kernels  34.7 us (27%)
  starting transfers between devices  15.5 us (12%)
  between operations  14.2 us (11%)
  waiting for transfers between devices  8.8 us (7%)
  matrix products  8.45 us (7%)
  other arithmetic  6.05 us (5%)
    pallas_call x2, Pallas kernels, banded_force(): pl.pallas_call(functools.partial(stiff_kernel, degrees=degrees, first=fir...  25 us
    gather x1, local copies, waits for them, and re-layouts, body(): velocity = jnp.take(table, slot_index, axis=0, mode='clip')  18.5 us
    pallas_call x1, Pallas kernels, near_field(): pl.pallas_call(pressure_kernel, grid_spec=grid_spec, out_shape=[jax.Shape...  9.73 us
    all_to_all x1, waiting for transfers between devices, body(): lax.all_to_all(outgoing, 'circ', split_axis=0, concat_axis=0, tiled=True)  4.64 us
    scatter x1, local copies, waits for them, and re-layouts, body(): node_slot = jnp.full((sectors * load_capacity,), -1, jnp.int32).at[load_s...  4.48 us
    dot_general x1, matrix products, body(): jnp.dot(gather_slot, load_value, preferred_element_type=jnp.float32)  4.15 us
    unnamed x23, local copies, waits for them, and re-layouts  4.03 us
    all_to_all x1, starting transfers between devices, body(): lax.all_to_all(node_slot, 'circ', split_axis=0, concat_axis=0, tiled=True)  3.94 us
  transfers between devices with their start and end apart: 7, of which 3 were waited for; matrix products, arithmetic and copies ran while one was open for 37% of the time, Pallas kernels for 27%

profile of v8, /device:TPU:0, one launch (start us, length us, event | category | flops | bytes accessed | tf_op | source)
XLA Modules:
  0.0 126.8 jit_solution(15204347603237817489)
XLA Ops:
  7.2 0.0 copy-start.1
  7.2 0.0 copy-start.5
  7.2 0.0 all-gather.2.cloned.1.call-start
  7.2 2.0 %slice.67 = bf16[16,64,1,256]{3,1,2,0:T(8,128)(2,1)} slice(bf16[16,64,6,256]{3,1,2,0:T(8,128)(2,1)} %param.11), slice={[0:16], [0:64], [0:1], [0:256]} | slice | bytes 1048576 | tf_op jit(solution)/shard_map/slice | solution.py:177
  9.3 0.0 all-gather.2.cloned.1.call-update
  9.3 1.7 %fusion.18 = (bf16[1,64,6,256]{3,1,2,0:T(8,128)(2,1)}, bf16[1,64,6,256]{3,1,2,0:T(8,128)(2,1)S(1)}) fusion(bf16[16,64,6,256]{3,1,2,0:T(8,128)(2,1)} %param.11), kind=kLoop, calls=%fused_computation.32 | loop fusion | bytes 786432 | tf_op jit(solution)/shard_map/slice | solution.py:183
  11.0 0.1 copy.16
  11.1 0.7 slice.58
  11.9 3.0 %collective-permute-start = (bf16[1,384,256]{2,1,0:T(8,128)(2,1)}, bf16[1,384,256]{2,1,0:T(8,128)(2,1)}, u32[]{:S(2)}, u32[]{:S(2)}) collective-permute-start(bf16[1,384,256]{2,1,0:T(8,128)(2,1)} %slice.58), channel_id=1, source_target_pairs={{0,8},{8,16},{16,24},{24,0},{1,9},{9,17},{17,25},{25,1},{2,10},{10... | collective-permute-start | bytes 589832 | tf_op jit(solution)/shard_map/ppermute | solution.py:182
  14.9 1.0 copy.17
  15.9 0.7 slice.60
  16.7 2.0 %collective-permute-start.1 = (bf16[1,384,256]{2,1,0:T(8,128)(2,1)}, bf16[1,384,256]{2,1,0:T(8,128)(2,1)}, u32[]{:S(2)}, u32[]{:S(2)}) collective-permute-start(bf16[1,384,256]{2,1,0:T(8,128)(2,1)} %slice.60), channel_id=1, source_target_pairs={{8,0},{16,8},{24,16},{0,24},{9,1},{17,9},{25,17},{1,25},{10,2},{18... | collective-permute-start | bytes 589832 | tf_op jit(solution)/shard_map/ppermute | solution.py:183
  18.7 0.0 copy-done.5
  18.7 0.5 fusion.12
  19.2 0.0 copy-start.7
  19.2 0.5 copy-done.7
  19.8 4.5 %scatter_custom_fusion = s32[2560]{0:T(1024)S(1)} fusion(s32[1024]{0:T(1024)S(1)} %bitcast.27, s32[1024]{0:T(1024)} %param.19, s32[]{:T(128)} %constant.48.clone.1), kind=kCustom, calls=%fused_computation.28 | custom fusion | bytes 10752 | tf_op jit(solution)/shard_map/scatter | solution.py:223
  24.3 0.7 all_to_all.9
  25.0 3.9 %all-to-all-start = ((s32[8,1,320]{2,1,0:T(1,128)}), s32[8,1,320]{2,1,0:T(1,128)}, u32[]{:S(2)}, u32[]{:S(2)}) async-start(s32[8,1,320]{2,1,0:T(1,128)} %all_to_all.9), calls=%async_computation | async-start | bytes 24576 | tf_op jit(solution)/shard_map/all_to_all | solution.py:231
  28.9 0.0 copy-done.1
  28.9 3.4 %copy.15 = bf16[16,64,6,256]{3,0,2,1:T(8,128)(2,1)} copy(bf16[16,64,6,256]{3,1,2,0:T(8,128)(2,1)S(1)} %copy-done.1) | data formatting | bytes 6291456 | tf_op args[0]
  32.3 0.0 copy-start.9
  32.3 0.0 copy-start.4
  32.3 0.0 copy-start.6
  32.3 0.0 copy-start.8
  32.4 3.0 %copy.22.rows_ref = bf16[16,384,256]{2,1,0:T(8,128)(2,1)S(1)} copy(bf16[16,384,256]{2,0,1:T(8,128)(2,1)} %bitcast.18) | data formatting | bytes 6291456 | tf_op jit(solution)/shard_map/reshape | solution.py:180
  35.4 0.0 copy-start
  35.4 0.0 copy-done.9
  35.4 0.0 copy-done.4
  35.5 0.0 collective-permute-done
  35.5 0.0 copy-start.2
  35.5 0.0 collective-permute-done.1
  35.6 1.2 broadcast_select_fusion.bottom_ref
  36.7 0.0 copy-start.3
  36.8 0.7 pad_maximum_fusion.1
  37.4 2.7 %collective-permute-start.2 = (bf16[18,6,256]{2,1,0:T(8,128)(2,1)}, bf16[18,6,256]{2,1,0:T(8,128)(2,1)}, u32[]{:S(2)}, u32[]{:S(2)}) collective-permute-start(bf16[18,6,256]{2,1,0:T(8,128)(2,1)} %pad_maximum_fusion.1), channel_id=1, source_target_pairs={{1,0},{2,1},{3,2},{4,3},{5,4},{6,5},{7,6},{0,7},{9,8},{10,9},{11,1... | collective-permute-start | bytes 165896 | tf_op jit(solution)/shard_map/ppermute | solution.py:194
  40.1 0.7 pad_maximum_fusion.2
  40.7 0.0 collective-permute-start.3
  40.7 0.0 copy-done.6
  40.7 0.0 copy-done.8
  40.8 0.6 multiply_add_fusion.1
  41.4 1.7 %copy.21.area_ref = f32[1024,1]{1,0:T(8,128)} copy(f32[1024,1]{0,1:T(1,128)} %bitcast.26) | data formatting | bytes 8192 | tf_op jit(solution)/shard_map/reshape | solution.py:76
  43.1 0.1 pad.3.clone
  43.2 1.3 %collective-permute-done.2 = bf16[18,6,256]{2,1,0:T(8,128)(2,1)} collective-permute-done((bf16[18,6,256]{2,1,0:T(8,128)(2,1)}, bf16[18,6,256]{2,1,0:T(8,128)(2,1)}, u32[]{:S(2)}, u32[]{:S(2)}) %collective-permute-start.2) | collective-permute-done | bytes 55328 | tf_op jit(solution)/shard_map/ppermute | solution.py:194
  44.5 2.8 %collective-permute-done.3 = bf16[18,6,256]{2,1,0:T(8,128)(2,1)} collective-permute-done((bf16[18,6,256]{2,1,0:T(8,128)(2,1)}, bf16[18,6,256]{2,1,0:T(8,128)(2,1)}, u32[]{:S(2)}, u32[]{:S(2)}) %collective-permute-start.3) | collective-permute-done | bytes 55328 | tf_op jit(solution)/shard_map/ppermute | solution.py:193
  47.3 2.1 %pad_maximum_fusion.halo_ref = bf16[18,128,256]{2,1,0:T(8,128)(2,1)} fusion(bf16[18,6,256]{2,1,0:T(8,128)(2,1)} %collective-permute-done.3, bf16[18,6,256]{2,1,0:T(8,128)(2,1)} %collective-permute-done.2, bf16[128]{0:T(256)(128)(2,1)S(1)} %pad.3.clone), kind=kLoop, calls=%fused_computation.13 | loop fusion | flops 3538944 | bytes 1290496 | tf_op jit(solution)/shard_map/concatenate | solution.py:196
  49.4 0.0 copy-done
  49.4 0.0 copy-done.2
  49.4 0.0 copy-done.3
  49.4 12.5 %shard_map.104.rest_0_ = f32[16,384,256]{2,1,0:T(8,128)} custom-call(bf16[16,64,324]{2,1,0:T(8,128)(2,1)} %s_ref.3, bf16[16,384,256]{2,1,0:T(8,128)(2,1)} %copy-done, bf16[1,384,256]{2,1,0:T(8,128)(2,1)} %copy-done.2, bf16[1,384,256]{2,1,0:T(8,128)(2,1)} %copy-done.3, bf16[18,128,256]{2,1,0:T(8,128)(2,1)} %pad_maximum_fusion.halo_ref), custom_call_target="tpu_custom_call" | custom-call | tf_op jit(solution)/shard_map/pallas_call | solution.py:145
  62.0 0.0 all-gather.2.cloned.1.call-done
  62.0 18.5 %gather_fusion = bf16[4096,256]{1,0:T(8,128)(2,1)} fusion(bf16[8192,256]{1,0:T(8,128)(2,1)} %all-gather.2.cloned.1.call-done, s32[4096]{0:T(1024)S(1)} %add_clamp_fusion), kind=kCustom, calls=%fused_computation | custom fusion | bytes 4210688 | tf_op jit(solution)/shard_map/jit(_take)/gather | solution.py:203
  80.5 0.0 copy-start.10
  80.5 9.7 %shard_map.105 = (f32[2,1024,256]{2,1,0:T(8,128)}, bf16[1024,256]{1,0:T(8,128)(2,1)}) custom-call(s32[4,12]{1,0:T(4,128)} %near_ref.1, bf16[4,12,2,256,256]{4,3,2,1,0:T(8,128)(2,1)} %kern_ref.1, bf16[16,256,256]{2,1,0:T(8,128)(2,1)} %bitcast.19, f32[1024,1]{1,0:T(8,128)} %copy.21.area_ref), custom_call_target="tpu_custom_call" | custom-call | tf_op jit(solution)/shard_map/pallas_call | solution.py:69
  90.2 0.0 copy-done.10
  90.2 4.2 %fusion.7 = bf16[2560,256]{1,0:T(8,128)(2,1)} fusion(bf16[1024,256]{1,0:T(8,128)(2,1)} %get-tuple-element.21, s32[1024]{0:T(1024)S(1)} %copy-done.10), kind=kOutput, calls=%fused_computation.11 | convolution fusion | flops 1345454080 | bytes 1839104 | tf_op jit(solution)/shard_map/dot_general | solution.py:216
  94.4 0.0 all-to-all-done
  94.4 3.8 %all-to-all-start.1 = ((bf16[8,320,256]{2,1,0:T(8,128)(2,1)}), bf16[8,320,256]{2,1,0:T(8,128)(2,1)S(1)}, u32[]{:S(2)}, u32[]{:S(2)}) async-start(bf16[8,320,256]{2,1,0:T(8,128)(2,1)} %bitcast.6), calls=%async_computation.1 | async-start | bytes 2621440 | tf_op jit(solution)/shard_map/all_to_all | solution.py:227
  98.2 0.7 reduce.2
  98.9 0.1 eq.66
  99.0 12.5 %shard_map.106 = f32[16,384,256]{2,1,0:T(8,128)} custom-call(bf16[16,64,324]{2,1,0:T(8,128)(2,1)} %s_ref.3, bf16[16,384,256]{2,1,0:T(8,128)(2,1)} %copy-done, bf16[1,384,256]{2,1,0:T(8,128)(2,1)} %copy-done.2, bf16[1,384,256]{2,1,0:T(8,128)(2,1)} %copy-done.3, bf16[18,128,256]{2,1,0:T(8,128)(2,1)} %pad_maximum_fusion.halo_ref, ...), custom_call_target="tpu_custom_call", output_to_operand_aliasing={{}: (5, {})} | custom-call | tf_op jit(solution)/shard_map/pallas_call | solution.py:145
  111.5 4.6 %all-to-all-done.1 = bf16[8,320,256]{2,1,0:T(8,128)(2,1)S(1)} async-done(((bf16[8,320,256]{2,1,0:T(8,128)(2,1)}), bf16[8,320,256]{2,1,0:T(8,128)(2,1)S(1)}, u32[]{:S(2)}, u32[]{:S(2)}) %all-to-all-start.1) | async-done | bytes 1310752 | tf_op jit(solution)/shard_map/all_to_all | solution.py:227
  116.1 3.8 %fusion.13 = f32[16,384,256]{2,1,0:T(8,128)} fusion(f32[16,384,256]{2,1,0:T(8,128)} %shard_map.106, bf16[2560,256,1]{1,0,2:T(8,128)(2,1)S(1)} %bitcast.21, s32[16,64]{1,0:T(8,128)S(1)} %multiply_add_fusion, s32[2560]{0:T(1024)S(1)} %eq.66), kind=kOutput, calls=%fused_computation.17 | convolution fusion | flops 1345323008 | bytes 3422208 | tf_op jit(solution)/shard_map/dot_general | solution.py:235
  (10 shorter events, 0.1 us)
Async XLA Ops:
  7.2 21.7 %copy-start.1 = (bf16[16,64,6,256]{3,1,2,0:T(8,128)(2,1)S(1)}, bf16[16,64,6,256]{3,1,2,0:T(8,128)(2,1)}, u32[]{:S(2)}) copy-start(bf16[16,64,6,256]{3,1,2,0:T(8,128)(2,1)} %param.11) | copy-start | bytes 9437188
  7.2 11.5 %copy-start.5 = (s32[1024,1]{0,1:T(1,128)S(1)}, s32[1024,1]{0,1:T(1,128)}, u32[]{:S(2)}) copy-start(s32[1024,1]{0,1:T(1,128)} %param.18) | copy-start | bytes 12292
  7.2 54.8 %all-gather.2.cloned.1.call-start = ((), (), s32[]{:S(2)}) async-start(), calls=%async_computation.2 | async-start | bytes 4718592 | tf_op jit(solution)/shard_map/all_gather | solution.py:178
  11.9 23.6 %collective-permute-start = (bf16[1,384,256]{2,1,0:T(8,128)(2,1)}, bf16[1,384,256]{2,1,0:T(8,128)(2,1)}, u32[]{:S(2)}, u32[]{:S(2)}) collective-permute-start(bf16[1,384,256]{2,1,0:T(8,128)(2,1)} %slice.58), channel_id=1, source_target_pairs={{0,8},{8,16},{16,24},{24,0},{1,9},{9,17},{17,25},{25,1},{2,10},{10... | collective-permute-start | bytes 589832 | tf_op jit(solution)/shard_map/ppermute | solution.py:182
  16.7 18.9 %collective-permute-start.1 = (bf16[1,384,256]{2,1,0:T(8,128)(2,1)}, bf16[1,384,256]{2,1,0:T(8,128)(2,1)}, u32[]{:S(2)}, u32[]{:S(2)}) collective-permute-start(bf16[1,384,256]{2,1,0:T(8,128)(2,1)} %slice.60), channel_id=1, source_target_pairs={{8,0},{16,8},{24,16},{0,24},{9,1},{17,9},{25,17},{1,25},{10,2},{18... | collective-permute-start | bytes 589832 | tf_op jit(solution)/shard_map/ppermute | solution.py:183
  19.2 0.6 copy-start.7
  25.0 69.5 %all-to-all-start = ((s32[8,1,320]{2,1,0:T(1,128)}), s32[8,1,320]{2,1,0:T(1,128)}, u32[]{:S(2)}, u32[]{:S(2)}) async-start(s32[8,1,320]{2,1,0:T(1,128)} %all_to_all.9), calls=%async_computation | async-start | bytes 24576 | tf_op jit(solution)/shard_map/all_to_all | solution.py:231
  32.3 3.1 %copy-start.9 = (s32[4096,1]{0,1:T(1,128)S(1)}, s32[4096,1]{0,1:T(1,128)}, u32[]{:S(2)}) copy-start(s32[4096,1]{0,1:T(1,128)} %param.16) | copy-start | bytes 49156
  32.3 3.1 %copy-start.4 = (s32[4096]{0:T(1024)S(1)}, s32[4096]{0:T(1024)}, u32[]{:S(2)}) copy-start(s32[4096]{0:T(1024)} %param.17) | copy-start | bytes 49156
  32.3 8.4 %copy-start.6 = (s32[1024,1]{0,1:T(1,128)S(1)}, s32[1024,1]{0,1:T(1,128)}, u32[]{:S(2)}) copy-start(s32[1024,1]{0,1:T(1,128)} %param.18) | copy-start | bytes 12292
  32.3 8.4 %copy-start.8 = (f32[1024]{0:T(1024)S(1)}, f32[1024]{0:T(1024)}, u32[]{:S(2)}) copy-start(f32[1024]{0:T(1024)} %copy-done.7) | copy-start | bytes 12292
  35.4 14.1 %copy-start = (bf16[16,384,256]{2,1,0:T(8,128)(2,1)}, bf16[16,384,256]{2,1,0:T(8,128)(2,1)S(1)}, u32[]{:S(2)}) copy-start(bf16[16,384,256]{2,1,0:T(8,128)(2,1)S(1)} %copy.22.rows_ref) | copy-start | bytes 9437188
  35.5 13.9 %copy-start.2 = (bf16[1,384,256]{2,1,0:T(8,128)(2,1)}, bf16[1,384,256]{2,1,0:T(8,128)(2,1)S(1)}, u32[]{:S(2)}) copy-start(bf16[1,384,256]{2,1,0:T(8,128)(2,1)S(1)} %broadcast_select_fusion.1.top_ref) | copy-start | bytes 589828
  36.7 12.7 %copy-start.3 = (bf16[1,384,256]{2,1,0:T(8,128)(2,1)}, bf16[1,384,256]{2,1,0:T(8,128)(2,1)S(1)}, u32[]{:S(2)}) copy-start(bf16[1,384,256]{2,1,0:T(8,128)(2,1)S(1)} %broadcast_select_fusion.bottom_ref) | copy-start | bytes 589828
  37.4 7.0 %collective-permute-start.2 = (bf16[18,6,256]{2,1,0:T(8,128)(2,1)}, bf16[18,6,256]{2,1,0:T(8,128)(2,1)}, u32[]{:S(2)}, u32[]{:S(2)}) collective-permute-start(bf16[18,6,256]{2,1,0:T(8,128)(2,1)} %pad_maximum_fusion.1), channel_id=1, source_target_pairs={{1,0},{2,1},{3,2},{4,3},{5,4},{6,5},{7,6},{0,7},{9,8},{10,9},{11,1... | collective-permute-start | bytes 165896 | tf_op jit(solution)/shard_map/ppermute | solution.py:194
  40.7 6.5 %collective-permute-start.3 = (bf16[18,6,256]{2,1,0:T(8,128)(2,1)}, bf16[18,6,256]{2,1,0:T(8,128)(2,1)}, u32[]{:S(2)}, u32[]{:S(2)}) collective-permute-start(bf16[18,6,256]{2,1,0:T(8,128)(2,1)} %pad_maximum_fusion.2), channel_id=1, source_target_pairs={{0,1},{1,2},{2,3},{3,4},{4,5},{5,6},{6,7},{7,0},{8,9},{9,10},{10,1... | collective-permute-start | bytes 165896 | tf_op jit(solution)/shard_map/ppermute | solution.py:193
  80.5 9.7 %copy-start.10 = (s32[1024]{0:T(1024)S(1)}, s32[1024]{0:T(1024)}, u32[]{:S(2)}) copy-start(s32[1024]{0:T(1024)} %multiply_add_fusion.1) | copy-start | bytes 12292
  94.4 21.7 %all-to-all-start.1 = ((bf16[8,320,256]{2,1,0:T(8,128)(2,1)}), bf16[8,320,256]{2,1,0:T(8,128)(2,1)S(1)}, u32[]{:S(2)}, u32[]{:S(2)}) async-start(bf16[8,320,256]{2,1,0:T(8,128)(2,1)} %bitcast.6), calls=%async_computation.1 | async-start | bytes 2621440 | tf_op jit(solution)/shard_map/all_to_all | solution.py:227
Sparse Core Ops, SparseCore 0:
  10.5 40.8 all-gather.1

commit v9 on v6

--- a/solution.py
+++ b/solution.py
@@ -217,22 +217,35 @@
         jnp.bfloat16
     )
     outgoing = outgoing.reshape(sectors, load_capacity, vectors)
-    node_slot = (
-        jnp.full((sectors * load_capacity,), -1, jnp.int32)
-        .at[load_slot]
-        .set(target_node)
-        .reshape(sectors, load_capacity)
-    )
-    outgoing, force = lax.optimization_barrier((outgoing, force))
-    arrived = lax.all_to_all(outgoing, "circ", split_axis=0, concat_axis=0, tiled=True)
+    radix = 32
+    digits = jnp.stack([target_node // radix, target_node % radix], axis=0).astype(jnp.bfloat16)
+    slot_digits = lax.dot_general(
+        digits, gather_slot, (((1,), (1,)), ((), ())), preferred_element_type=jnp.float32
+    ).astype(jnp.bfloat16)
+    slot_digits = jnp.transpose(slot_digits.reshape(2, sectors, load_capacity), (1, 0, 2))
+    digit_rows = -(-2 * load_capacity // vectors)
+    slot_digits = jnp.pad(
+        slot_digits.reshape(sectors, 2 * load_capacity),
+        ((0, 0), (0, digit_rows * vectors - 2 * load_capacity)),
+    ).reshape(sectors, digit_rows, vectors)
+    packet = jnp.concatenate([outgoing, slot_digits], axis=1)
+    packet, force = lax.optimization_barrier((packet, force))
+    arrived = lax.all_to_all(packet, "circ", split_axis=0, concat_axis=0, tiled=True)
     force = banded_force(
         blocks, node_rows, top, bottom, halo, degrees, half, axial_rows - half, force
     )
-    arrived_node = lax.all_to_all(node_slot, "circ", split_axis=0, concat_axis=0, tiled=True)
+    arrived_load = arrived[:, :load_capacity].reshape(-1, vectors)
+    arrived_digits = (
+        arrived[:, load_capacity:]
+        .reshape(sectors, digit_rows * vectors)[:, : 2 * load_capacity]
+        .reshape(sectors, 2, load_capacity)
+        .astype(jnp.float32)
+    )
+    arrived_node = (arrived_digits[:, 0] * radix + arrived_digits[:, 1]).astype(jnp.int32)
     selector = (
         arrived_node.reshape(-1)[None, :] == jnp.arange(node_count, dtype=jnp.int32)[:, None]
     ).astype(jnp.bfloat16)
-    fluid = jnp.dot(selector, arrived.reshape(-1, vectors), preferred_element_type=jnp.float32)
+    fluid = jnp.dot(selector, arrived_load, preferred_element_type=jnp.float32)
     fluid = fluid.reshape(axial_rows, circum_rows, vectors)
     force = force.at[:, :circum_rows, :].add(-fluid)
     shell_force = jnp.transpose(

time: 127 us -> 116 us (0.913)
  starting transfers between devices: 15.5 us -> 10.3 us
  local copies, waits for them, and re-layouts: 35.3 us -> 30.6 us
  waiting for transfers between devices: 10.7 us -> 8.6 us
    scatter x1 -> x0, local copies, waits for them, and re-layouts: 4.49 us -> none  [body(): node_slot = jnp.full((sectors * load_capacity,), -1, jnp.int32).at[load_s...]
    all_to_all x2 -> x1, starting transfers between devices: 7.69 us -> 3.57 us  [body(): lax.all_to_all(packet, 'circ', split_axis=0, concat_axis=0, tiled=True)]
    ppermute x1, waiting for transfers between devices: 2.58 us -> 0.01 us  [body(): lax.ppermute(first_nodes, 'circ', [((i + 1) % sectors, i) for i in range(...]
    dot_general x1 -> x2, matrix products: 3.83 us -> 5.65 us  [the longest x1 3.84 us: body(): fluid = jnp.dot(selector, arrived_load, preferred_element_type=jnp.float32)]
    all_to_all x2 -> x1, waiting for transfers between devices: 5.33 us -> 5.95 us  [body(): lax.all_to_all(packet, 'circ', split_axis=0, concat_axis=0, tiled=True)]
  transfers between devices with their start and end apart: 7 -> 6, of which waited for: 3 -> 3; matrix products, arithmetic and copies ran while one was open for 35% -> 16% of each run, Pallas kernels for 27% -> 22%
where the time goes in v9:
time: 116 us
  Pallas kernels  34.6 us (30%)
  local copies, waits for them, and re-layouts  30.6 us (26%)
  between operations  14.3 us (12%)
  starting transfers between devices  10.3 us (9%)
  matrix products  8.72 us (8%)
  waiting for transfers between devices  8.6 us (7%)
  other arithmetic  8.6 us (7%)
    pallas_call x2, Pallas kernels, banded_force(): pl.pallas_call(functools.partial(stiff_kernel, degrees=degrees, first=fir...  25 us
    gather x1, local copies, waits for them, and re-layouts, body(): velocity = jnp.take(table, slot_index, axis=0, mode='clip')  18.7 us
    pallas_call x1, Pallas kernels, near_field(): pl.pallas_call(pressure_kernel, grid_spec=grid_spec, out_shape=[jax.Shape...  9.6 us
    all_to_all x1, waiting for transfers between devices, body(): lax.all_to_all(packet, 'circ', split_axis=0, concat_axis=0, tiled=True)  5.95 us
    dot_general x1, matrix products, body(): fluid = jnp.dot(selector, arrived_load, preferred_element_type=jnp.float32)  3.84 us
    all_to_all x1, starting transfers between devices, body(): lax.all_to_all(packet, 'circ', split_axis=0, concat_axis=0, tiled=True)  3.57 us
    slice x3, local copies, waits for them, and re-layouts, body(): node_rows[:1]  3.51 us
    dot_general x1, matrix products, body(): jnp.dot(gather_slot, load_value, preferred_element_type=jnp.float32)  3.07 us
  transfers between devices with their start and end apart: 6, of which 3 were waited for; matrix products, arithmetic and copies ran while one was open for 16% of the time, Pallas kernels for 22%

profile of v9, /device:TPU:0, one launch (start us, length us, event | category | flops | bytes accessed | tf_op | source)
XLA Modules:
  0.0 115.7 jit_solution(2034778333941234296)
XLA Ops:
  7.2 0.0 copy-start.1
  7.2 0.0 all-gather.2.cloned.1.call-start
  7.2 2.0 %slice.90 = bf16[16,64,1,256]{3,1,2,0:T(8,128)(2,1)} slice(bf16[16,64,6,256]{3,1,2,0:T(8,128)(2,1)} %param.11), slice={[0:16], [0:64], [0:1], [0:256]} | slice | bytes 1048576 | tf_op jit(solution)/shard_map/slice | solution.py:175
  9.3 0.0 all-gather.2.cloned.1.call-update
  9.3 1.7 %fusion.34 = (bf16[1,64,6,256]{3,1,2,0:T(8,128)(2,1)}, bf16[1,64,6,256]{3,1,2,0:T(8,128)(2,1)S(1)}) fusion(bf16[16,64,6,256]{3,1,2,0:T(8,128)(2,1)} %param.11), kind=kLoop, calls=%fused_computation.67 | loop fusion | bytes 786432 | tf_op jit(solution)/shard_map/slice | solution.py:181
  11.0 0.1 copy.16
  11.1 0.8 slice.79
  11.9 3.0 %collective-permute-start = (bf16[1,384,256]{2,1,0:T(8,128)(2,1)}, bf16[1,384,256]{2,1,0:T(8,128)(2,1)}, u32[]{:S(2)}, u32[]{:S(2)}) collective-permute-start(bf16[1,384,256]{2,1,0:T(8,128)(2,1)} %slice.79), channel_id=1, source_target_pairs={{0,8},{8,16},{16,24},{24,0},{1,9},{9,17},{17,25},{25,1},{2,10},{10... | collective-permute-start | bytes 589832 | tf_op jit(solution)/shard_map/ppermute | solution.py:180
  14.9 1.0 copy.17
  15.9 0.7 slice.81
  16.7 2.0 %collective-permute-start.1 = (bf16[1,384,256]{2,1,0:T(8,128)(2,1)}, bf16[1,384,256]{2,1,0:T(8,128)(2,1)S(1)}, u32[]{:S(2)}, u32[]{:S(2)}) collective-permute-start(bf16[1,384,256]{2,1,0:T(8,128)(2,1)} %slice.81), channel_id=1, source_target_pairs={{8,0},{16,8},{24,16},{0,24},{9,1},{17,9},{25,17},{1,25},{10,2},{18... | collective-permute-start | bytes 589832 | tf_op jit(solution)/shard_map/ppermute | solution.py:181
  18.7 0.0 copy-done.1
  18.7 1.8 %copy.15 = bf16[16,64,6,256]{3,0,2,1:T(8,128)(2,1)S(1)} copy(bf16[16,64,6,256]{3,1,2,0:T(8,128)(2,1)S(1)} %copy-done.1) | data formatting | bytes 6291456 | tf_op args[0]
  20.5 0.0 copy-start.3
  20.5 0.0 copy-start.7
  20.5 0.0 copy-start.5
  20.5 0.0 copy-start.4
  20.5 1.1 copy.23.rows_ref
  21.6 0.0 copy-start
  21.7 0.0 copy-start.6
  21.7 0.0 copy-done.3
  21.7 2.3 %reduce-window.6 = s32[8,8,128]{2,1,0:T(8,128)S(1)} reduce-window(s32[8,8,128]{2,1,0:T(8,128)S(1)} %fusion.17, s32[]{:T(128)} %constant.80.clone.1), window={size=1x1x128 pad=0_0x0_0x127_0}, to_apply=%region_0.1 | reduce-window | flops 1040384 | bytes 65540 | tf_op jit(solution)/shard_map/reduce-window
  24.0 0.3 slice_reduce_fusion
  24.2 0.2 reduce-window.9
  24.4 0.0 copy-done.7
  24.5 0.1 add_bitcast_fusion
  24.6 0.1 fusion.18
  24.7 0.0 copy-done.5
  24.7 0.0 copy-done.4
  24.8 2.1 %broadcast_select_fusion.s_ref = bf16[16,64,324]{2,1,0:T(8,128)(2,1)} fusion(bf16[16,64,324]{2,1,0:T(8,128)(2,1)} %param.12, pred[16,324]{1,0:T(8,128)(4,1)S(1)} %fusion.18), kind=kLoop, calls=%fused_computation.17 | loop fusion | flops 331776 | bytes 1332288 | tf_op jit(solution)/shard_map/jit(_where)/select_n | solution.py:197
  26.9 0.0 collective-permute-done.top_ref
  26.9 0.7 fusion.35
  27.6 0.0 collective-permute-done.1.bottom_ref
  27.6 0.0 copy-start.2
  27.6 0.7 pad_maximum_fusion.2
  28.3 1.6 %collective-permute-start.2 = (bf16[18,6,256]{2,1,0:T(8,128)(2,1)}, bf16[18,6,256]{2,1,0:T(8,128)(2,1)S(1)}, u32[]{:S(2)}, u32[]{:S(2)}) collective-permute-start(bf16[18,6,256]{2,1,0:T(8,128)(2,1)} %pad_maximum_fusion.2), channel_id=1, source_target_pairs={{1,0},{2,1},{3,2},{4,3},{5,4},{6,5},{7,6},{0,7},{9,8},{10,9},{11,1... | collective-permute-start | bytes 165896 | tf_op jit(solution)/shard_map/ppermute | solution.py:189
  29.9 0.7 pad_maximum_fusion.3
  30.5 0.0 collective-permute-start.3
  30.5 1.8 %fusion.9 = bf16[2,2560]{1,0:T(2,128)(2,1)S(1)} fusion(s32[1024]{0:T(1024)S(1)} %multiply_add_fusion.1, bf16[1,1024]{1,0:T(2,128)(2,1)S(1)} %stack.13, bf16[1,1024]{1,0:T(2,128)(2,1)S(1)} %stack.12), kind=kOutput, calls=%fused_computation.11 | convolution fusion | flops 13120512 | bytes 18432 | tf_op jit(solution)/shard_map/dot_general | solution.py:222
  32.4 0.0 copy-done.6
  32.4 1.0 copy.21.area_ref
  33.4 0.0 copy-done
  33.4 0.1 reshape.180
  33.5 0.1 reshape.181
  33.6 0.1 pad.12.clone
  33.7 0.0 collective-permute-done.2
  33.7 1.7 %collective-permute-done.3 = bf16[18,6,256]{2,1,0:T(8,128)(2,1)S(1)} collective-permute-done((bf16[18,6,256]{2,1,0:T(8,128)(2,1)}, bf16[18,6,256]{2,1,0:T(8,128)(2,1)S(1)}, u32[]{:S(2)}, u32[]{:S(2)}) %collective-permute-start.3) | collective-permute-done | bytes 55328 | tf_op jit(solution)/shard_map/ppermute | solution.py:188
  35.4 1.2 %pad_maximum_fusion.1.halo_ref = bf16[18,128,256]{2,1,0:T(8,128)(2,1)} fusion(bf16[18,6,256]{2,1,0:T(8,128)(2,1)S(1)} %collective-permute-done.3, bf16[18,6,256]{2,1,0:T(8,128)(2,1)S(1)} %collective-permute-done.2, bf16[128]{0:T(256)(128)(2,1)S(1)} %pad.12.clone), kind=kLoop, calls=%fused_computation.14 | loop fusion | flops 3538944 | bytes 1290496 | tf_op jit(solution)/shard_map/concatenate | solution.py:191
  36.6 0.0 copy-done.2
  36.6 12.5 %shard_map.104.rest_0_ = f32[16,384,256]{2,1,0:T(8,128)} custom-call(bf16[16,64,324]{2,1,0:T(8,128)(2,1)} %broadcast_select_fusion.s_ref, bf16[16,384,256]{2,1,0:T(8,128)(2,1)} %copy-done, bf16[1,384,256]{2,1,0:T(8,128)(2,1)} %collective-permute-done.top_ref, bf16[1,384,256]{2,1,0:T(8,128)(2,1)} %copy-done.2, bf16[18,128,256]{2,1,0:T(8,128)(2,1)} %pad_maximum_fusion.1.halo_ref), custom_call_target="tpu_custom_call" | custom-call | tf_op jit(solution)/shard_map/pallas_call | solution.py:142
  49.1 0.9 all-gather.2.cloned.1.call-done
  50.0 18.7 %gather_fusion = bf16[4096,256]{1,0:T(8,128)(2,1)} fusion(bf16[8192,256]{1,0:T(8,128)(2,1)} %all-gather.2.cloned.1.call-done, s32[4096]{0:T(1024)S(1)} %add_clamp_fusion), kind=kCustom, calls=%fused_computation | custom fusion | bytes 4210688 | tf_op jit(solution)/shard_map/jit(_take)/gather | solution.py:203
  68.7 9.6 %shard_map.105 = (f32[2,1024,256]{2,1,0:T(8,128)}, bf16[1024,256]{1,0:T(8,128)(2,1)}) custom-call(s32[4,12]{1,0:T(4,128)} %near_ref.1, bf16[4,12,2,256,256]{4,3,2,1,0:T(8,128)(2,1)} %kern_ref.1, bf16[16,256,256]{2,1,0:T(8,128)(2,1)} %bitcast.43, f32[1024,1]{1,0:T(8,128)} %copy.21.area_ref), custom_call_target="tpu_custom_call" | custom-call | tf_op jit(solution)/shard_map/pallas_call | solution.py:66
  78.3 3.1 %fusion.8 = bf16[2560,256]{1,0:T(8,128)(2,1)S(1)} fusion(bf16[1024,256]{1,0:T(8,128)(2,1)} %get-tuple-element.21, s32[1024]{0:T(1024)S(1)} %multiply_add_fusion.1), kind=kOutput, calls=%fused_computation.10 | convolution fusion | flops 1345454080 | bytes 1839104 | tf_op jit(solution)/shard_map/dot_general | solution.py:216
  81.4 1.2 %pad_maximum_fusion = bf16[8,323,256]{2,1,0:T(8,128)(2,1)} fusion(bf16[8,3,256]{2,1,0:T(4,128)(2,1)S(1)} %reshape.182, bf16[8,320,256]{2,1,0:T(8,128)(2,1)S(1)} %bitcast.46), kind=kLoop, calls=%fused_computation.13 | loop fusion | flops 2646016 | bytes 2646016 | tf_op jit(solution)/shard_map/concatenate | solution.py:231
  82.6 3.6 %all-to-all-start = ((bf16[8,323,256]{2,1,0:T(8,128)(2,1)}), bf16[8,323,256]{2,1,0:T(8,128)(2,1)S(1)}, u32[]{:S(2)}, u32[]{:S(2)}) async-start(bf16[8,323,256]{2,1,0:T(8,128)(2,1)} %pad_maximum_fusion), calls=%async_computation | async-start | bytes 2686976 | tf_op jit(solution)/shard_map/all_to_all | solution.py:233
  86.1 12.5 %shard_map.106 = f32[16,384,256]{2,1,0:T(8,128)} custom-call(bf16[16,64,324]{2,1,0:T(8,128)(2,1)} %broadcast_select_fusion.s_ref, bf16[16,384,256]{2,1,0:T(8,128)(2,1)} %copy-done, bf16[1,384,256]{2,1,0:T(8,128)(2,1)} %collective-permute-done.top_ref, bf16[1,384,256]{2,1,0:T(8,128)(2,1)} %copy-done.2, ...), custom_call_target="tpu_custom_call", output_to_operand_aliasing={{}: (5, {})} | custom-call | tf_op jit(solution)/shard_map/pallas_call | solution.py:142
  98.7 6.0 %all-to-all-done = bf16[8,323,256]{2,1,0:T(8,128)(2,1)S(1)} async-done(((bf16[8,323,256]{2,1,0:T(8,128)(2,1)}), bf16[8,323,256]{2,1,0:T(8,128)(2,1)S(1)}, u32[]{:S(2)}, u32[]{:S(2)}) %all-to-all-start) | async-done | bytes 1323040 | tf_op jit(solution)/shard_map/all_to_all | solution.py:233
  104.7 0.1 reshape.186
  104.8 0.1 fusion.20
  104.8 0.1 convert_element_type.41
  104.9 0.1 slice.111
  105.0 3.8 %fusion.13 = f32[16,384,256]{2,1,0:T(8,128)} fusion(f32[16,384,256]{2,1,0:T(8,128)} %shard_map.106, bf16[2560,256,1]{1,0,2:T(8,128)(2,1)S(1)} %bitcast.45, s32[16,64]{1,0:T(8,128)S(1)} %multiply_add_fusion, s32[2560]{0:T(1024)S(1)} %convert_element_type.41), kind=kOutput, calls=%fused_computation.16 | convolution fusion | flops 1345323008 | bytes 3422208 | tf_op jit(solution)/shard_map/dot_general | solution.py:248
  (20 shorter events, 0.2 us)
Async XLA Ops:
  7.2 11.6 %copy-start.1 = (bf16[16,64,6,256]{3,1,2,0:T(8,128)(2,1)S(1)}, bf16[16,64,6,256]{3,1,2,0:T(8,128)(2,1)}, u32[]{:S(2)}) copy-start(bf16[16,64,6,256]{3,1,2,0:T(8,128)(2,1)} %param.11) | copy-start | bytes 9437188
  7.2 42.8 %all-gather.2.cloned.1.call-start = ((), (), s32[]{:S(2)}) async-start(), calls=%async_computation.1 | async-start | bytes 4718592 | tf_op jit(solution)/shard_map/all_gather | solution.py:176
  11.9 15.0 %collective-permute-start = (bf16[1,384,256]{2,1,0:T(8,128)(2,1)}, bf16[1,384,256]{2,1,0:T(8,128)(2,1)}, u32[]{:S(2)}, u32[]{:S(2)}) collective-permute-start(bf16[1,384,256]{2,1,0:T(8,128)(2,1)} %slice.79), channel_id=1, source_target_pairs={{0,8},{8,16},{16,24},{24,0},{1,9},{9,17},{17,25},{25,1},{2,10},{10... | collective-permute-start | bytes 589832 | tf_op jit(solution)/shard_map/ppermute | solution.py:180
  16.7 10.9 %collective-permute-start.1 = (bf16[1,384,256]{2,1,0:T(8,128)(2,1)}, bf16[1,384,256]{2,1,0:T(8,128)(2,1)S(1)}, u32[]{:S(2)}, u32[]{:S(2)}) collective-permute-start(bf16[1,384,256]{2,1,0:T(8,128)(2,1)} %slice.81), channel_id=1, source_target_pairs={{8,0},{16,8},{24,16},{0,24},{9,1},{17,9},{25,17},{1,25},{10,2},{18... | collective-permute-start | bytes 589832 | tf_op jit(solution)/shard_map/ppermute | solution.py:181
  20.5 1.2 %copy-start.3 = (s32[1024,1]{0,1:T(1,128)S(1)}, s32[1024,1]{0,1:T(1,128)}, u32[]{:S(2)}) copy-start(s32[1024,1]{0,1:T(1,128)} %param.18) | copy-start | bytes 12292
  20.5 3.9 %copy-start.7 = (s32[1024]{0:T(1024)S(1)}, s32[1024]{0:T(1024)}, u32[]{:S(2)}) copy-start(s32[1024]{0:T(1024)} %param.19) | copy-start | bytes 12292
  20.5 4.1 %copy-start.5 = (s32[4096,1]{0,1:T(1,128)S(1)}, s32[4096,1]{0,1:T(1,128)}, u32[]{:S(2)}) copy-start(s32[4096,1]{0,1:T(1,128)} %param.16) | copy-start | bytes 49156
  20.5 4.2 %copy-start.4 = (s32[4096]{0:T(1024)S(1)}, s32[4096]{0:T(1024)}, u32[]{:S(2)}) copy-start(s32[4096]{0:T(1024)} %param.17) | copy-start | bytes 49156
  21.6 11.7 %copy-start = (bf16[16,384,256]{2,1,0:T(8,128)(2,1)}, bf16[16,384,256]{2,1,0:T(8,128)(2,1)S(1)}, u32[]{:S(2)}) copy-start(bf16[16,384,256]{2,1,0:T(8,128)(2,1)S(1)} %copy.23.rows_ref) | copy-start | bytes 9437188
  21.7 10.7 %copy-start.6 = (f32[1024]{0:T(1024)S(1)}, f32[1024]{0:T(1024)}, u32[]{:S(2)}) copy-start(f32[1024]{0:T(1024)} %param.14) | copy-start | bytes 12292
  27.6 9.1 %copy-start.2 = (bf16[1,384,256]{2,1,0:T(8,128)(2,1)}, bf16[1,384,256]{2,1,0:T(8,128)(2,1)S(1)}, u32[]{:S(2)}) copy-start(bf16[1,384,256]{2,1,0:T(8,128)(2,1)S(1)} %collective-permute-done.1.bottom_ref) | copy-start | bytes 589828
  28.3 5.4 %collective-permute-start.2 = (bf16[18,6,256]{2,1,0:T(8,128)(2,1)}, bf16[18,6,256]{2,1,0:T(8,128)(2,1)S(1)}, u32[]{:S(2)}, u32[]{:S(2)}) collective-permute-start(bf16[18,6,256]{2,1,0:T(8,128)(2,1)} %pad_maximum_fusion.2), channel_id=1, source_target_pairs={{1,0},{2,1},{3,2},{4,3},{5,4},{6,5},{7,6},{0,7},{9,8},{10,9},{11,1... | collective-permute-start | bytes 165896 | tf_op jit(solution)/shard_map/ppermute | solution.py:189
  30.5 4.9 %collective-permute-start.3 = (bf16[18,6,256]{2,1,0:T(8,128)(2,1)}, bf16[18,6,256]{2,1,0:T(8,128)(2,1)S(1)}, u32[]{:S(2)}, u32[]{:S(2)}) collective-permute-start(bf16[18,6,256]{2,1,0:T(8,128)(2,1)} %pad_maximum_fusion.3), channel_id=1, source_target_pairs={{0,1},{1,2},{2,3},{3,4},{4,5},{5,6},{6,7},{7,0},{8,9},{9,10},{10,1... | collective-permute-start | bytes 165896 | tf_op jit(solution)/shard_map/ppermute | solution.py:188
  82.6 22.1 %all-to-all-start = ((bf16[8,323,256]{2,1,0:T(8,128)(2,1)}), bf16[8,323,256]{2,1,0:T(8,128)(2,1)S(1)}, u32[]{:S(2)}, u32[]{:S(2)}) async-start(bf16[8,323,256]{2,1,0:T(8,128)(2,1)} %pad_maximum_fusion), calls=%async_computation | async-start | bytes 2686976 | tf_op jit(solution)/shard_map/all_to_all | solution.py:233
Sparse Core Ops, SparseCore 0:
  10.5 39.4 all-gather.1

commit v10 on v9

--- a/solution.py
+++ b/solution.py
@@ -25,9 +25,12 @@
 
 
 def slot_positions(owners, sectors, capacity):
-    onehot = (owners[:, None] == jnp.arange(sectors, dtype=jnp.int32)[None, :]).astype(jnp.int32)
-    before = jnp.cumsum(onehot, axis=0) - onehot
-    ranking = jnp.sum(before * onehot, axis=1)
+    onehot = owners[:, None] == jnp.arange(sectors, dtype=jnp.int32)[None, :]
+    count = owners.shape[0]
+    order = jnp.arange(count, dtype=jnp.int32)
+    earlier = (order[None, :] < order[:, None]).astype(jnp.bfloat16)
+    before = jnp.dot(earlier, onehot.astype(jnp.bfloat16), preferred_element_type=jnp.float32)
+    ranking = jnp.sum(jnp.where(onehot, before, 0.0), axis=1).astype(jnp.int32)
     return owners * capacity + ranking
 
 
@@ -195,7 +198,7 @@
         global_row[:, None] + lane_step[None, :] < axial_total
     )
     blocks = jnp.where(inside[:, None, :], stiffness, jnp.zeros_like(stiffness))
-    half = axial_rows // 2
+    half = (axial_rows * 7) // 16
     force = banded_force(blocks, node_rows, top, bottom, halo, degrees, 0, half)
 
     force, table = lax.optimization_barrier((force, table))

time: 116 us -> 116 us (level)
  other arithmetic: 8.6 us -> 6.44 us
  waiting for transfers between devices: 8.6 us -> 9.97 us
    another operation x3 -> x1, other arithmetic: 2.44 us -> 0.01 us
    all_gather x1, waiting for transfers between devices: 0.89 us -> 2.7 us  [body(): table = lax.all_gather(radial, 'circ', axis=0, tiled=True)]
  transfers between devices with their start and end apart: 6 -> 6, of which waited for: 3 -> 4; matrix products, arithmetic and copies ran while one was open for 16% -> 15% of each run, Pallas kernels for 22% -> 22%
where the time goes in v10:
time: 116 us; the launch traced here: 115 us
  Pallas kernels  34.6 us (30%)
  local copies, waits for them, and re-layouts  30.2 us (26%)
  between operations  14.3 us (12%)
  starting transfers between devices  10.8 us (9%)
  waiting for transfers between devices  9.97 us (9%)
  matrix products  9.18 us (8%)
  other arithmetic  6.44 us (6%)
    pallas_call x2, Pallas kernels, banded_force(): pl.pallas_call(functools.partial(stiff_kernel, degrees=degrees, first=fir...  25 us
    gather x1, local copies, waits for them, and re-layouts, body(): velocity = jnp.take(table, slot_index, axis=0, mode='clip')  18.6 us
    pallas_call x1, Pallas kernels, near_field(): pl.pallas_call(pressure_kernel, grid_spec=grid_spec, out_shape=[jax.Shape...  9.59 us
    all_to_all x1, waiting for transfers between devices, body(): lax.all_to_all(packet, 'circ', split_axis=0, concat_axis=0, tiled=True)  4.85 us
    dot_general x1, matrix products, body(): fluid = jnp.dot(selector, arrived_load, preferred_element_type=jnp.float32)  3.84 us
    all_to_all x1, starting transfers between devices, body(): lax.all_to_all(packet, 'circ', split_axis=0, concat_axis=0, tiled=True)  3.57 us
    slice x3, local copies, waits for them, and re-layouts, body(): node_rows[:1]  3.51 us
    dot_general x1, matrix products, body(): jnp.dot(gather_slot, load_value, preferred_element_type=jnp.float32)  3.06 us
  transfers between devices with their start and end apart: 6, of which 4 were waited for; matrix products, arithmetic and copies ran while one was open for 15% of the time, Pallas kernels for 22%

profile of v10, /device:TPU:0, one launch (start us, length us, event | category | flops | bytes accessed | tf_op | source)
XLA Modules:
  0.0 115.4 jit_solution(3165681248073955773)
XLA Ops:
  7.2 0.0 copy-start.1
  7.2 0.0 all-gather.2.cloned.1.call-start
  7.2 2.0 %slice.82 = bf16[16,64,1,256]{3,1,2,0:T(8,128)(2,1)} slice(bf16[16,64,6,256]{3,1,2,0:T(8,128)(2,1)} %param.11), slice={[0:16], [0:64], [0:1], [0:256]} | slice | bytes 1048576 | tf_op jit(solution)/shard_map/slice | solution.py:178
  9.3 0.0 all-gather.2.cloned.1.call-update
  9.3 1.7 %fusion.34 = (bf16[1,64,6,256]{3,1,2,0:T(8,128)(2,1)}, bf16[1,64,6,256]{3,1,2,0:T(8,128)(2,1)S(1)}) fusion(bf16[16,64,6,256]{3,1,2,0:T(8,128)(2,1)} %param.11), kind=kLoop, calls=%fused_computation.64 | loop fusion | bytes 786432 | tf_op jit(solution)/shard_map/slice | solution.py:184
  11.0 0.1 copy.16
  11.1 0.7 slice.73
  11.9 3.0 %collective-permute-start = (bf16[1,384,256]{2,1,0:T(8,128)(2,1)}, bf16[1,384,256]{2,1,0:T(8,128)(2,1)}, u32[]{:S(2)}, u32[]{:S(2)}) collective-permute-start(bf16[1,384,256]{2,1,0:T(8,128)(2,1)} %slice.73), channel_id=1, source_target_pairs={{0,8},{8,16},{16,24},{24,0},{1,9},{9,17},{17,25},{25,1},{2,10},{10... | collective-permute-start | bytes 589832 | tf_op jit(solution)/shard_map/ppermute | solution.py:183
  14.9 1.0 copy.17
  15.9 0.7 slice.75
  16.7 2.0 %collective-permute-start.1 = (bf16[1,384,256]{2,1,0:T(8,128)(2,1)}, bf16[1,384,256]{2,1,0:T(8,128)(2,1)S(1)}, u32[]{:S(2)}, u32[]{:S(2)}) collective-permute-start(bf16[1,384,256]{2,1,0:T(8,128)(2,1)} %slice.75), channel_id=1, source_target_pairs={{8,0},{16,8},{24,16},{0,24},{9,1},{17,9},{25,17},{1,25},{10,2},{18... | collective-permute-start | bytes 589832 | tf_op jit(solution)/shard_map/ppermute | solution.py:184
  18.7 0.0 copy-done.1
  18.7 1.8 %copy.15 = bf16[16,64,6,256]{3,0,2,1:T(8,128)(2,1)S(1)} copy(bf16[16,64,6,256]{3,1,2,0:T(8,128)(2,1)S(1)} %copy-done.1) | data formatting | bytes 6291456 | tf_op args[0]
  20.5 0.0 copy-start.7
  20.5 0.0 copy-start.6
  20.5 0.0 copy-start.4
  20.5 0.0 copy-start.3
  20.5 1.1 copy.23.rows_ref
  21.6 0.0 copy-start
  21.6 0.0 copy-done.7
  21.7 0.0 copy-done.6
  21.7 0.5 fusion.15
  22.2 0.0 copy-start.5
  22.2 0.1 fusion.17
  22.3 0.0 copy-done.4
  22.3 0.0 copy-done.3
  22.4 2.5 %broadcast_select_fusion.s_ref = bf16[16,64,324]{2,1,0:T(8,128)(2,1)} fusion(bf16[16,64,324]{2,1,0:T(8,128)(2,1)} %param.12, pred[16,324]{1,0:T(8,128)(4,1)S(1)} %fusion.17), kind=kLoop, calls=%fused_computation.21 | loop fusion | flops 331776 | bytes 1332288 | tf_op jit(solution)/shard_map/jit(_where)/select_n | solution.py:200
  24.9 0.0 collective-permute-done.top_ref
  24.9 0.7 fusion.35
  25.6 0.7 collective-permute-done.1.bottom_ref
  26.2 0.0 copy-start.2
  26.2 0.7 pad_maximum_fusion.2
  27.0 2.2 %collective-permute-start.2 = (bf16[18,6,256]{2,1,0:T(8,128)(2,1)}, bf16[18,6,256]{2,1,0:T(8,128)(2,1)S(1)}, u32[]{:S(2)}, u32[]{:S(2)}) collective-permute-start(bf16[18,6,256]{2,1,0:T(8,128)(2,1)} %pad_maximum_fusion.2), channel_id=1, source_target_pairs={{1,0},{2,1},{3,2},{4,3},{5,4},{6,5},{7,6},{0,7},{9,8},{10,9},{11,1... | collective-permute-start | bytes 165896 | tf_op jit(solution)/shard_map/ppermute | solution.py:192
  29.1 0.7 pad_maximum_fusion.3
  29.8 0.0 collective-permute-start.3
  29.8 1.8 %fusion.10 = bf16[2,2560]{1,0:T(2,128)(2,1)S(1)} fusion(s32[1024]{0:T(1024)S(1)} %convert_add_fusion, bf16[1,1024]{1,0:T(2,128)(2,1)S(1)} %stack.13, bf16[1,1024]{1,0:T(2,128)(2,1)S(1)} %stack.12), kind=kOutput, calls=%fused_computation.13 | convolution fusion | flops 13120512 | bytes 18432 | tf_op jit(solution)/shard_map/dot_general | solution.py:225
  31.6 0.0 copy-done
  31.6 0.0 copy-done.5
  31.6 1.0 copy.21.area_ref
  32.6 0.1 reshape.164
  32.7 0.1 reshape.165
  32.9 0.1 pad.12.clone
  32.9 0.0 collective-permute-done.2
  32.9 1.7 %collective-permute-done.3 = bf16[18,6,256]{2,1,0:T(8,128)(2,1)S(1)} collective-permute-done((bf16[18,6,256]{2,1,0:T(8,128)(2,1)}, bf16[18,6,256]{2,1,0:T(8,128)(2,1)S(1)}, u32[]{:S(2)}, u32[]{:S(2)}) %collective-permute-start.3) | collective-permute-done | bytes 55328 | tf_op jit(solution)/shard_map/ppermute | solution.py:191
  34.7 1.2 %pad_maximum_fusion.1.halo_ref = bf16[18,128,256]{2,1,0:T(8,128)(2,1)} fusion(bf16[18,6,256]{2,1,0:T(8,128)(2,1)S(1)} %collective-permute-done.3, bf16[18,6,256]{2,1,0:T(8,128)(2,1)S(1)} %collective-permute-done.2, bf16[128]{0:T(256)(128)(2,1)S(1)} %pad.12.clone), kind=kLoop, calls=%fused_computation.16 | loop fusion | flops 3538944 | bytes 1290496 | tf_op jit(solution)/shard_map/concatenate | solution.py:194
  35.9 0.0 copy-done.2
  35.9 11.3 %shard_map.104.rest_0_ = f32[16,384,256]{2,1,0:T(8,128)} custom-call(bf16[16,64,324]{2,1,0:T(8,128)(2,1)} %broadcast_select_fusion.s_ref, bf16[16,384,256]{2,1,0:T(8,128)(2,1)} %copy-done, bf16[1,384,256]{2,1,0:T(8,128)(2,1)} %collective-permute-done.top_ref, bf16[1,384,256]{2,1,0:T(8,128)(2,1)} %copy-done.2, bf16[18,128,256]{2,1,0:T(8,128)(2,1)} %pad_maximum_fusion.1.halo_ref), custom_call_target="tpu_custom_call" | custom-call | tf_op jit(solution)/shard_map/pallas_call | solution.py:145
  47.2 2.7 %all-gather.2.cloned.1.call-done = bf16[8192,256]{1,0:T(8,128)(2,1)} async-done(((bf16[1024,256]{1,0:T(8,128)(2,1)}), bf16[8192,256]{1,0:T(8,128)(2,1)}) %all-gather.2.cloned.1.call-update) | async-done | bytes 4194320 | tf_op jit(solution)/shard_map/all_gather | solution.py:179
  49.9 18.6 %gather_fusion = bf16[4096,256]{1,0:T(8,128)(2,1)} fusion(bf16[8192,256]{1,0:T(8,128)(2,1)} %all-gather.2.cloned.1.call-done, s32[4096]{0:T(1024)S(1)} %add_clamp_fusion), kind=kCustom, calls=%fused_computation | custom fusion | bytes 4210688 | tf_op jit(solution)/shard_map/jit(_take)/gather | solution.py:206
  68.5 9.6 %shard_map.105 = (f32[2,1024,256]{2,1,0:T(8,128)}, bf16[1024,256]{1,0:T(8,128)(2,1)}) custom-call(s32[4,12]{1,0:T(4,128)} %near_ref.1, bf16[4,12,2,256,256]{4,3,2,1,0:T(8,128)(2,1)} %kern_ref.1, bf16[16,256,256]{2,1,0:T(8,128)(2,1)} %bitcast.23, f32[1024,1]{1,0:T(8,128)} %copy.21.area_ref), custom_call_target="tpu_custom_call" | custom-call | tf_op jit(solution)/shard_map/pallas_call | solution.py:69
  78.1 3.1 %fusion.9 = bf16[2560,256]{1,0:T(8,128)(2,1)S(1)} fusion(bf16[1024,256]{1,0:T(8,128)(2,1)} %get-tuple-element.21, s32[1024]{0:T(1024)S(1)} %convert_add_fusion), kind=kOutput, calls=%fused_computation.12 | convolution fusion | flops 1345454080 | bytes 1839104 | tf_op jit(solution)/shard_map/dot_general | solution.py:219
  81.1 1.2 %pad_maximum_fusion = bf16[8,323,256]{2,1,0:T(8,128)(2,1)} fusion(bf16[8,3,256]{2,1,0:T(4,128)(2,1)S(1)} %reshape.166, bf16[8,320,256]{2,1,0:T(8,128)(2,1)S(1)} %bitcast.26), kind=kLoop, calls=%fused_computation.15 | loop fusion | flops 2646016 | bytes 2646016 | tf_op jit(solution)/shard_map/concatenate | solution.py:234
  82.3 3.6 %all-to-all-start = ((bf16[8,323,256]{2,1,0:T(8,128)(2,1)}), bf16[8,323,256]{2,1,0:T(8,128)(2,1)S(1)}, u32[]{:S(2)}, u32[]{:S(2)}) async-start(bf16[8,323,256]{2,1,0:T(8,128)(2,1)} %pad_maximum_fusion), calls=%async_computation | async-start | bytes 2686976 | tf_op jit(solution)/shard_map/all_to_all | solution.py:236
  85.9 13.6 %shard_map.106 = f32[16,384,256]{2,1,0:T(8,128)} custom-call(bf16[16,64,324]{2,1,0:T(8,128)(2,1)} %broadcast_select_fusion.s_ref, bf16[16,384,256]{2,1,0:T(8,128)(2,1)} %copy-done, bf16[1,384,256]{2,1,0:T(8,128)(2,1)} %collective-permute-done.top_ref, bf16[1,384,256]{2,1,0:T(8,128)(2,1)} %copy-done.2, ...), custom_call_target="tpu_custom_call", output_to_operand_aliasing={{}: (5, {})} | custom-call | tf_op jit(solution)/shard_map/pallas_call | solution.py:145
  99.6 4.8 %all-to-all-done = bf16[8,323,256]{2,1,0:T(8,128)(2,1)S(1)} async-done(((bf16[8,323,256]{2,1,0:T(8,128)(2,1)}), bf16[8,323,256]{2,1,0:T(8,128)(2,1)S(1)}, u32[]{:S(2)}, u32[]{:S(2)}) %all-to-all-start) | async-done | bytes 1323040 | tf_op jit(solution)/shard_map/all_to_all | solution.py:236
  104.5 0.1 reshape.170
  104.5 0.1 fusion.20
  104.6 0.1 convert_element_type.42
  104.7 0.1 slice.102
  104.8 3.8 %fusion.16 = f32[16,384,256]{2,1,0:T(8,128)} fusion(f32[16,384,256]{2,1,0:T(8,128)} %shard_map.106, bf16[2560,256,1]{1,0,2:T(8,128)(2,1)S(1)} %bitcast.25, s32[16,64]{1,0:T(8,128)S(1)} %multiply_add_fusion, s32[2560]{0:T(1024)S(1)} %convert_element_type.42), kind=kOutput, calls=%fused_computation.20 | convolution fusion | flops 1345323008 | bytes 3422208 | tf_op jit(solution)/shard_map/dot_general | solution.py:251
  (18 shorter events, 0.2 us)
Async XLA Ops:
  7.2 11.6 %copy-start.1 = (bf16[16,64,6,256]{3,1,2,0:T(8,128)(2,1)S(1)}, bf16[16,64,6,256]{3,1,2,0:T(8,128)(2,1)}, u32[]{:S(2)}) copy-start(bf16[16,64,6,256]{3,1,2,0:T(8,128)(2,1)} %param.11) | copy-start | bytes 9437188
  7.2 42.8 %all-gather.2.cloned.1.call-start = ((), (), s32[]{:S(2)}) async-start(), calls=%async_computation.1 | async-start | bytes 4718592 | tf_op jit(solution)/shard_map/all_gather | solution.py:179
  11.9 13.0 %collective-permute-start = (bf16[1,384,256]{2,1,0:T(8,128)(2,1)}, bf16[1,384,256]{2,1,0:T(8,128)(2,1)}, u32[]{:S(2)}, u32[]{:S(2)}) collective-permute-start(bf16[1,384,256]{2,1,0:T(8,128)(2,1)} %slice.73), channel_id=1, source_target_pairs={{0,8},{8,16},{16,24},{24,0},{1,9},{9,17},{17,25},{25,1},{2,10},{10... | collective-permute-start | bytes 589832 | tf_op jit(solution)/shard_map/ppermute | solution.py:183
  16.7 9.6 %collective-permute-start.1 = (bf16[1,384,256]{2,1,0:T(8,128)(2,1)}, bf16[1,384,256]{2,1,0:T(8,128)(2,1)S(1)}, u32[]{:S(2)}, u32[]{:S(2)}) collective-permute-start(bf16[1,384,256]{2,1,0:T(8,128)(2,1)} %slice.75), channel_id=1, source_target_pairs={{8,0},{16,8},{24,16},{0,24},{9,1},{17,9},{25,17},{1,25},{10,2},{18... | collective-permute-start | bytes 589832 | tf_op jit(solution)/shard_map/ppermute | solution.py:184
  20.5 1.2 %copy-start.7 = (s32[1024]{0:T(1024)S(1)}, s32[1024]{0:T(1024)}, u32[]{:S(2)}) copy-start(s32[1024]{0:T(1024)} %param.19) | copy-start | bytes 12292
  20.5 1.2 %copy-start.6 = (s32[1024,1]{0,1:T(1,128)S(1)}, s32[1024,1]{0,1:T(1,128)}, u32[]{:S(2)}) copy-start(s32[1024,1]{0,1:T(1,128)} %param.18) | copy-start | bytes 12292
  20.5 1.8 %copy-start.4 = (s32[4096,1]{0,1:T(1,128)S(1)}, s32[4096,1]{0,1:T(1,128)}, u32[]{:S(2)}) copy-start(s32[4096,1]{0,1:T(1,128)} %param.16) | copy-start | bytes 49156
  20.5 1.8 %copy-start.3 = (s32[4096]{0:T(1024)S(1)}, s32[4096]{0:T(1024)}, u32[]{:S(2)}) copy-start(s32[4096]{0:T(1024)} %param.17) | copy-start | bytes 49156
  21.6 10.0 %copy-start = (bf16[16,384,256]{2,1,0:T(8,128)(2,1)}, bf16[16,384,256]{2,1,0:T(8,128)(2,1)S(1)}, u32[]{:S(2)}) copy-start(bf16[16,384,256]{2,1,0:T(8,128)(2,1)S(1)} %copy.23.rows_ref) | copy-start | bytes 9437188
  22.2 9.4 %copy-start.5 = (f32[1024]{0:T(1024)S(1)}, f32[1024]{0:T(1024)}, u32[]{:S(2)}) copy-start(f32[1024]{0:T(1024)} %param.14) | copy-start | bytes 12292
  26.2 9.7 %copy-start.2 = (bf16[1,384,256]{2,1,0:T(8,128)(2,1)}, bf16[1,384,256]{2,1,0:T(8,128)(2,1)S(1)}, u32[]{:S(2)}) copy-start(bf16[1,384,256]{2,1,0:T(8,128)(2,1)S(1)} %collective-permute-done.1.bottom_ref) | copy-start | bytes 589828
  27.0 6.0 %collective-permute-start.2 = (bf16[18,6,256]{2,1,0:T(8,128)(2,1)}, bf16[18,6,256]{2,1,0:T(8,128)(2,1)S(1)}, u32[]{:S(2)}, u32[]{:S(2)}) collective-permute-start(bf16[18,6,256]{2,1,0:T(8,128)(2,1)} %pad_maximum_fusion.2), channel_id=1, source_target_pairs={{1,0},{2,1},{3,2},{4,3},{5,4},{6,5},{7,6},{0,7},{9,8},{10,9},{11,1... | collective-permute-start | bytes 165896 | tf_op jit(solution)/shard_map/ppermute | solution.py:192
  29.8 4.9 %collective-permute-start.3 = (bf16[18,6,256]{2,1,0:T(8,128)(2,1)}, bf16[18,6,256]{2,1,0:T(8,128)(2,1)S(1)}, u32[]{:S(2)}, u32[]{:S(2)}) collective-permute-start(bf16[18,6,256]{2,1,0:T(8,128)(2,1)} %pad_maximum_fusion.3), channel_id=1, source_target_pairs={{0,1},{1,2},{2,3},{3,4},{4,5},{5,6},{6,7},{7,0},{8,9},{9,10},{10,1... | collective-permute-start | bytes 165896 | tf_op jit(solution)/shard_map/ppermute | solution.py:191
  82.3 22.1 %all-to-all-start = ((bf16[8,323,256]{2,1,0:T(8,128)(2,1)}), bf16[8,323,256]{2,1,0:T(8,128)(2,1)S(1)}, u32[]{:S(2)}, u32[]{:S(2)}) async-start(bf16[8,323,256]{2,1,0:T(8,128)(2,1)} %pad_maximum_fusion), calls=%async_computation | async-start | bytes 2686976 | tf_op jit(solution)/shard_map/all_to_all | solution.py:236
Sparse Core Ops, SparseCore 0:
  10.5 39.4 all-gather.1

commit v11 on v10

--- a/solution.py
+++ b/solution.py
@@ -101,18 +101,31 @@
         )
         sel_ref[...] = jnp.where((lane < span) & (k == target), 1.0, 0.0).astype(sel_ref.dtype)
 
+        band_ref[...] = jnp.zeros(band_ref.shape, band_ref.dtype)
+
     spread = jnp.dot(s_ref[0], sel_ref[...], preferred_element_type=jnp.float32)
-    pad = jnp.zeros((nodes, wide - group), jnp.float32)
+    pad = jnp.zeros((8, group), jnp.float32)
+    tiles = wide // group
     for d in range(offsets):
         for i in range(degrees):
             blk = d * degrees + i
-            piece = jnp.concatenate([spread[:, blk * group : (blk + 1) * group], pad], axis=1)
-            parts = []
-            for g in range(nodes // 8):
-                rows = pltpu.roll(piece[g * 8 : (g + 1) * 8], (g * 8 * degrees - degrees) % wide, 1)
-                parts.append(pltpu.roll(rows, 0, 1, stride=degrees, stride_axis=0))
-            skewed = jnp.concatenate(parts, axis=0)
-            band_ref[d, i * nodes : (i + 1) * nodes, :] = skewed.astype(band_ref.dtype)
+            piece = spread[:, blk * group : (blk + 1) * group]
+            for h in range(nodes // 16):
+                base = 16 * h * degrees - degrees
+                tile = base // group
+                parts = []
+                for g in (2 * h, 2 * h + 1):
+                    rows = jnp.concatenate([piece[g * 8 : (g + 1) * 8], pad], axis=1)
+                    shift = 8 * g * degrees - degrees - tile * group
+                    rows = pltpu.roll(rows, shift, 1)
+                    parts.append(pltpu.roll(rows, 0, 1, stride=degrees, stride_axis=0))
+                window = jnp.concatenate(parts, axis=0).astype(band_ref.dtype)
+                top_row = i * nodes + 16 * h
+                for t in range(2):
+                    lane = ((tile + t) % tiles) * group
+                    band_ref[d, top_row : top_row + 16, lane : lane + group] = window[
+                        :, t * group : (t + 1) * group
+                    ]
     above = jnp.where(a == 0, top_ref[0], rows_ref[jnp.maximum(a - 1, 0)])
     below = jnp.where(a == last, bottom_ref[0], rows_ref[jnp.minimum(a + 1, last)])
     acc = None

time: 116 us -> 116 us (level)
  no operation moved by 1% of the time
where the time goes in v11:
time: 116 us; the launch traced here: 115 us
  Pallas kernels  35.2 us (30%)
  local copies, waits for them, and re-layouts  30.2 us (26%)
  between operations  14.3 us (12%)
  starting transfers between devices  10.8 us (9%)
  waiting for transfers between devices  9.3 us (8%)
  matrix products  9.18 us (8%)
  other arithmetic  6.44 us (6%)
    pallas_call x2, Pallas kernels, banded_force(): pl.pallas_call(functools.partial(stiff_kernel, degrees=degrees, first=fir...  25.7 us
    gather x1, local copies, waits for them, and re-layouts, body(): velocity = jnp.take(table, slot_index, axis=0, mode='clip')  18.6 us
    pallas_call x1, Pallas kernels, near_field(): pl.pallas_call(pressure_kernel, grid_spec=grid_spec, out_shape=[jax.Shape...  9.59 us
    all_to_all x1, waiting for transfers between devices, body(): lax.all_to_all(packet, 'circ', split_axis=0, concat_axis=0, tiled=True)  4.52 us
    dot_general x1, matrix products, body(): fluid = jnp.dot(selector, arrived_load, preferred_element_type=jnp.float32)  3.84 us
    all_to_all x1, starting transfers between devices, body(): lax.all_to_all(packet, 'circ', split_axis=0, concat_axis=0, tiled=True)  3.57 us
    slice x3, local copies, waits for them, and re-layouts, body(): node_rows[:1]  3.51 us
    dot_general x1, matrix products, body(): jnp.dot(gather_slot, load_value, preferred_element_type=jnp.float32)  3.06 us
  transfers between devices with their start and end apart: 6, of which 4 were waited for; matrix products, arithmetic and copies ran while one was open for 15% of the time, Pallas kernels for 22%

profile of v11, /device:TPU:0, one launch (start us, length us, event | category | flops | bytes accessed | tf_op | source)
XLA Modules:
  0.0 115.4 jit_solution(1929090828140839652)
XLA Ops:
  7.2 0.0 copy-start.1
  7.2 0.0 all-gather.2.cloned.1.call-start
  7.2 2.0 %slice.82 = bf16[16,64,1,256]{3,1,2,0:T(8,128)(2,1)} slice(bf16[16,64,6,256]{3,1,2,0:T(8,128)(2,1)} %param.11), slice={[0:16], [0:64], [0:1], [0:256]} | slice | bytes 1048576 | tf_op jit(solution)/shard_map/slice | solution.py:191
  9.3 0.0 all-gather.2.cloned.1.call-update
  9.3 1.7 %fusion.34 = (bf16[1,64,6,256]{3,1,2,0:T(8,128)(2,1)}, bf16[1,64,6,256]{3,1,2,0:T(8,128)(2,1)S(1)}) fusion(bf16[16,64,6,256]{3,1,2,0:T(8,128)(2,1)} %param.11), kind=kLoop, calls=%fused_computation.64 | loop fusion | bytes 786432 | tf_op jit(solution)/shard_map/slice | solution.py:197
  11.0 0.1 copy.16
  11.1 0.7 slice.73
  11.9 3.0 %collective-permute-start = (bf16[1,384,256]{2,1,0:T(8,128)(2,1)}, bf16[1,384,256]{2,1,0:T(8,128)(2,1)}, u32[]{:S(2)}, u32[]{:S(2)}) collective-permute-start(bf16[1,384,256]{2,1,0:T(8,128)(2,1)} %slice.73), channel_id=1, source_target_pairs={{0,8},{8,16},{16,24},{24,0},{1,9},{9,17},{17,25},{25,1},{2,10},{10... | collective-permute-start | bytes 589832 | tf_op jit(solution)/shard_map/ppermute | solution.py:196
  14.9 1.0 copy.17
  15.9 0.7 slice.75
  16.7 2.0 %collective-permute-start.1 = (bf16[1,384,256]{2,1,0:T(8,128)(2,1)}, bf16[1,384,256]{2,1,0:T(8,128)(2,1)S(1)}, u32[]{:S(2)}, u32[]{:S(2)}) collective-permute-start(bf16[1,384,256]{2,1,0:T(8,128)(2,1)} %slice.75), channel_id=1, source_target_pairs={{8,0},{16,8},{24,16},{0,24},{9,1},{17,9},{25,17},{1,25},{10,2},{18... | collective-permute-start | bytes 589832 | tf_op jit(solution)/shard_map/ppermute | solution.py:197
  18.7 0.0 copy-done.1
  18.7 1.8 %copy.15 = bf16[16,64,6,256]{3,0,2,1:T(8,128)(2,1)S(1)} copy(bf16[16,64,6,256]{3,1,2,0:T(8,128)(2,1)S(1)} %copy-done.1) | data formatting | bytes 6291456 | tf_op args[0]
  20.5 0.0 copy-start.7
  20.5 0.0 copy-start.6
  20.5 0.0 copy-start.4
  20.5 0.0 copy-start.3
  20.5 1.1 copy.23.rows_ref
  21.6 0.0 copy-start
  21.6 0.0 copy-done.7
  21.7 0.0 copy-done.6
  21.7 0.5 fusion.15
  22.2 0.0 copy-start.5
  22.2 0.1 fusion.17
  22.3 0.0 copy-done.4
  22.3 0.0 copy-done.3
  22.4 2.5 %broadcast_select_fusion.s_ref = bf16[16,64,324]{2,1,0:T(8,128)(2,1)} fusion(bf16[16,64,324]{2,1,0:T(8,128)(2,1)} %param.12, pred[16,324]{1,0:T(8,128)(4,1)S(1)} %fusion.17), kind=kLoop, calls=%fused_computation.21 | loop fusion | flops 331776 | bytes 1332288 | tf_op jit(solution)/shard_map/jit(_where)/select_n | solution.py:213
  24.9 0.0 collective-permute-done.top_ref
  24.9 0.7 fusion.35
  25.6 0.7 collective-permute-done.1.bottom_ref
  26.2 0.0 copy-start.2
  26.2 0.7 pad_maximum_fusion.2
  27.0 2.2 %collective-permute-start.2 = (bf16[18,6,256]{2,1,0:T(8,128)(2,1)}, bf16[18,6,256]{2,1,0:T(8,128)(2,1)S(1)}, u32[]{:S(2)}, u32[]{:S(2)}) collective-permute-start(bf16[18,6,256]{2,1,0:T(8,128)(2,1)} %pad_maximum_fusion.2), channel_id=1, source_target_pairs={{1,0},{2,1},{3,2},{4,3},{5,4},{6,5},{7,6},{0,7},{9,8},{10,9},{11,1... | collective-permute-start | bytes 165896 | tf_op jit(solution)/shard_map/ppermute | solution.py:205
  29.1 0.7 pad_maximum_fusion.3
  29.8 0.0 collective-permute-start.3
  29.8 1.8 %fusion.10 = bf16[2,2560]{1,0:T(2,128)(2,1)S(1)} fusion(s32[1024]{0:T(1024)S(1)} %convert_add_fusion, bf16[1,1024]{1,0:T(2,128)(2,1)S(1)} %stack.13, bf16[1,1024]{1,0:T(2,128)(2,1)S(1)} %stack.12), kind=kOutput, calls=%fused_computation.13 | convolution fusion | flops 13120512 | bytes 18432 | tf_op jit(solution)/shard_map/dot_general | solution.py:238
  31.6 0.0 copy-done
  31.6 0.0 copy-done.5
  31.6 1.0 copy.21.area_ref
  32.6 0.1 reshape.164
  32.7 0.1 reshape.165
  32.9 0.1 pad.12.clone
  32.9 0.0 collective-permute-done.2
  32.9 1.7 %collective-permute-done.3 = bf16[18,6,256]{2,1,0:T(8,128)(2,1)S(1)} collective-permute-done((bf16[18,6,256]{2,1,0:T(8,128)(2,1)}, bf16[18,6,256]{2,1,0:T(8,128)(2,1)S(1)}, u32[]{:S(2)}, u32[]{:S(2)}) %collective-permute-start.3) | collective-permute-done | bytes 55328 | tf_op jit(solution)/shard_map/ppermute | solution.py:204
  34.7 1.2 %pad_maximum_fusion.1.halo_ref = bf16[18,128,256]{2,1,0:T(8,128)(2,1)} fusion(bf16[18,6,256]{2,1,0:T(8,128)(2,1)S(1)} %collective-permute-done.3, bf16[18,6,256]{2,1,0:T(8,128)(2,1)S(1)} %collective-permute-done.2, bf16[128]{0:T(256)(128)(2,1)S(1)} %pad.12.clone), kind=kLoop, calls=%fused_computation.16 | loop fusion | flops 3538944 | bytes 1290496 | tf_op jit(solution)/shard_map/concatenate | solution.py:207
  35.9 0.0 copy-done.2
  35.9 11.7 %shard_map.104.rest_0_ = f32[16,384,256]{2,1,0:T(8,128)} custom-call(bf16[16,64,324]{2,1,0:T(8,128)(2,1)} %broadcast_select_fusion.s_ref, bf16[16,384,256]{2,1,0:T(8,128)(2,1)} %copy-done, bf16[1,384,256]{2,1,0:T(8,128)(2,1)} %collective-permute-done.top_ref, bf16[1,384,256]{2,1,0:T(8,128)(2,1)} %copy-done.2, bf16[18,128,256]{2,1,0:T(8,128)(2,1)} %pad_maximum_fusion.1.halo_ref), custom_call_target="tpu_custom_call" | custom-call | tf_op jit(solution)/shard_map/pallas_call | solution.py:158
  47.6 2.4 %all-gather.2.cloned.1.call-done = bf16[8192,256]{1,0:T(8,128)(2,1)} async-done(((bf16[1024,256]{1,0:T(8,128)(2,1)}), bf16[8192,256]{1,0:T(8,128)(2,1)}) %all-gather.2.cloned.1.call-update) | async-done | bytes 4194320 | tf_op jit(solution)/shard_map/all_gather | solution.py:192
  49.9 18.6 %gather_fusion = bf16[4096,256]{1,0:T(8,128)(2,1)} fusion(bf16[8192,256]{1,0:T(8,128)(2,1)} %all-gather.2.cloned.1.call-done, s32[4096]{0:T(1024)S(1)} %add_clamp_fusion), kind=kCustom, calls=%fused_computation | custom fusion | bytes 4210688 | tf_op jit(solution)/shard_map/jit(_take)/gather | solution.py:219
  68.5 9.6 %shard_map.105 = (f32[2,1024,256]{2,1,0:T(8,128)}, bf16[1024,256]{1,0:T(8,128)(2,1)}) custom-call(s32[4,12]{1,0:T(4,128)} %near_ref.1, bf16[4,12,2,256,256]{4,3,2,1,0:T(8,128)(2,1)} %kern_ref.1, bf16[16,256,256]{2,1,0:T(8,128)(2,1)} %bitcast.23, f32[1024,1]{1,0:T(8,128)} %copy.21.area_ref), custom_call_target="tpu_custom_call" | custom-call | tf_op jit(solution)/shard_map/pallas_call | solution.py:69
  78.1 3.1 %fusion.9 = bf16[2560,256]{1,0:T(8,128)(2,1)S(1)} fusion(bf16[1024,256]{1,0:T(8,128)(2,1)} %get-tuple-element.21, s32[1024]{0:T(1024)S(1)} %convert_add_fusion), kind=kOutput, calls=%fused_computation.12 | convolution fusion | flops 1345454080 | bytes 1839104 | tf_op jit(solution)/shard_map/dot_general | solution.py:232
  81.1 1.2 %pad_maximum_fusion = bf16[8,323,256]{2,1,0:T(8,128)(2,1)} fusion(bf16[8,3,256]{2,1,0:T(4,128)(2,1)S(1)} %reshape.166, bf16[8,320,256]{2,1,0:T(8,128)(2,1)S(1)} %bitcast.26), kind=kLoop, calls=%fused_computation.15 | loop fusion | flops 2646016 | bytes 2646016 | tf_op jit(solution)/shard_map/concatenate | solution.py:247
  82.3 3.6 %all-to-all-start = ((bf16[8,323,256]{2,1,0:T(8,128)(2,1)}), bf16[8,323,256]{2,1,0:T(8,128)(2,1)S(1)}, u32[]{:S(2)}, u32[]{:S(2)}) async-start(bf16[8,323,256]{2,1,0:T(8,128)(2,1)} %pad_maximum_fusion), calls=%async_computation | async-start | bytes 2686976 | tf_op jit(solution)/shard_map/all_to_all | solution.py:249
  85.9 14.0 %shard_map.106 = f32[16,384,256]{2,1,0:T(8,128)} custom-call(bf16[16,64,324]{2,1,0:T(8,128)(2,1)} %broadcast_select_fusion.s_ref, bf16[16,384,256]{2,1,0:T(8,128)(2,1)} %copy-done, bf16[1,384,256]{2,1,0:T(8,128)(2,1)} %collective-permute-done.top_ref, bf16[1,384,256]{2,1,0:T(8,128)(2,1)} %copy-done.2, ...), custom_call_target="tpu_custom_call", output_to_operand_aliasing={{}: (5, {})} | custom-call | tf_op jit(solution)/shard_map/pallas_call | solution.py:158
  99.9 4.5 %all-to-all-done = bf16[8,323,256]{2,1,0:T(8,128)(2,1)S(1)} async-done(((bf16[8,323,256]{2,1,0:T(8,128)(2,1)}), bf16[8,323,256]{2,1,0:T(8,128)(2,1)S(1)}, u32[]{:S(2)}, u32[]{:S(2)}) %all-to-all-start) | async-done | bytes 1323040 | tf_op jit(solution)/shard_map/all_to_all | solution.py:249
  104.5 0.1 reshape.170
  104.5 0.1 fusion.20
  104.6 0.1 convert_element_type.42
  104.7 0.1 slice.102
  104.8 3.8 %fusion.16 = f32[16,384,256]{2,1,0:T(8,128)} fusion(f32[16,384,256]{2,1,0:T(8,128)} %shard_map.106, bf16[2560,256,1]{1,0,2:T(8,128)(2,1)S(1)} %bitcast.25, s32[16,64]{1,0:T(8,128)S(1)} %multiply_add_fusion, s32[2560]{0:T(1024)S(1)} %convert_element_type.42), kind=kOutput, calls=%fused_computation.20 | convolution fusion | flops 1345323008 | bytes 3422208 | tf_op jit(solution)/shard_map/dot_general | solution.py:264
  (18 shorter events, 0.2 us)
Async XLA Ops:
  7.2 11.6 %copy-start.1 = (bf16[16,64,6,256]{3,1,2,0:T(8,128)(2,1)S(1)}, bf16[16,64,6,256]{3,1,2,0:T(8,128)(2,1)}, u32[]{:S(2)}) copy-start(bf16[16,64,6,256]{3,1,2,0:T(8,128)(2,1)} %param.11) | copy-start | bytes 9437188
  7.2 42.8 %all-gather.2.cloned.1.call-start = ((), (), s32[]{:S(2)}) async-start(), calls=%async_computation.1 | async-start | bytes 4718592 | tf_op jit(solution)/shard_map/all_gather | solution.py:192
  11.9 13.0 %collective-permute-start = (bf16[1,384,256]{2,1,0:T(8,128)(2,1)}, bf16[1,384,256]{2,1,0:T(8,128)(2,1)}, u32[]{:S(2)}, u32[]{:S(2)}) collective-permute-start(bf16[1,384,256]{2,1,0:T(8,128)(2,1)} %slice.73), channel_id=1, source_target_pairs={{0,8},{8,16},{16,24},{24,0},{1,9},{9,17},{17,25},{25,1},{2,10},{10... | collective-permute-start | bytes 589832 | tf_op jit(solution)/shard_map/ppermute | solution.py:196
  16.7 9.6 %collective-permute-start.1 = (bf16[1,384,256]{2,1,0:T(8,128)(2,1)}, bf16[1,384,256]{2,1,0:T(8,128)(2,1)S(1)}, u32[]{:S(2)}, u32[]{:S(2)}) collective-permute-start(bf16[1,384,256]{2,1,0:T(8,128)(2,1)} %slice.75), channel_id=1, source_target_pairs={{8,0},{16,8},{24,16},{0,24},{9,1},{17,9},{25,17},{1,25},{10,2},{18... | collective-permute-start | bytes 589832 | tf_op jit(solution)/shard_map/ppermute | solution.py:197
  20.5 1.2 %copy-start.7 = (s32[1024]{0:T(1024)S(1)}, s32[1024]{0:T(1024)}, u32[]{:S(2)}) copy-start(s32[1024]{0:T(1024)} %param.19) | copy-start | bytes 12292
  20.5 1.2 %copy-start.6 = (s32[1024,1]{0,1:T(1,128)S(1)}, s32[1024,1]{0,1:T(1,128)}, u32[]{:S(2)}) copy-start(s32[1024,1]{0,1:T(1,128)} %param.18) | copy-start | bytes 12292
  20.5 1.8 %copy-start.4 = (s32[4096,1]{0,1:T(1,128)S(1)}, s32[4096,1]{0,1:T(1,128)}, u32[]{:S(2)}) copy-start(s32[4096,1]{0,1:T(1,128)} %param.16) | copy-start | bytes 49156
  20.5 1.8 %copy-start.3 = (s32[4096]{0:T(1024)S(1)}, s32[4096]{0:T(1024)}, u32[]{:S(2)}) copy-start(s32[4096]{0:T(1024)} %param.17) | copy-start | bytes 49156
  21.6 10.0 %copy-start = (bf16[16,384,256]{2,1,0:T(8,128)(2,1)}, bf16[16,384,256]{2,1,0:T(8,128)(2,1)S(1)}, u32[]{:S(2)}) copy-start(bf16[16,384,256]{2,1,0:T(8,128)(2,1)S(1)} %copy.23.rows_ref) | copy-start | bytes 9437188
  22.2 9.4 %copy-start.5 = (f32[1024]{0:T(1024)S(1)}, f32[1024]{0:T(1024)}, u32[]{:S(2)}) copy-start(f32[1024]{0:T(1024)} %param.14) | copy-start | bytes 12292
  26.2 9.7 %copy-start.2 = (bf16[1,384,256]{2,1,0:T(8,128)(2,1)}, bf16[1,384,256]{2,1,0:T(8,128)(2,1)S(1)}, u32[]{:S(2)}) copy-start(bf16[1,384,256]{2,1,0:T(8,128)(2,1)S(1)} %collective-permute-done.1.bottom_ref) | copy-start | bytes 589828
  27.0 6.0 %collective-permute-start.2 = (bf16[18,6,256]{2,1,0:T(8,128)(2,1)}, bf16[18,6,256]{2,1,0:T(8,128)(2,1)S(1)}, u32[]{:S(2)}, u32[]{:S(2)}) collective-permute-start(bf16[18,6,256]{2,1,0:T(8,128)(2,1)} %pad_maximum_fusion.2), channel_id=1, source_target_pairs={{1,0},{2,1},{3,2},{4,3},{5,4},{6,5},{7,6},{0,7},{9,8},{10,9},{11,1... | collective-permute-start | bytes 165896 | tf_op jit(solution)/shard_map/ppermute | solution.py:205
  29.8 4.9 %collective-permute-start.3 = (bf16[18,6,256]{2,1,0:T(8,128)(2,1)}, bf16[18,6,256]{2,1,0:T(8,128)(2,1)S(1)}, u32[]{:S(2)}, u32[]{:S(2)}) collective-permute-start(bf16[18,6,256]{2,1,0:T(8,128)(2,1)} %pad_maximum_fusion.3), channel_id=1, source_target_pairs={{0,1},{1,2},{2,3},{3,4},{4,5},{5,6},{6,7},{7,0},{8,9},{9,10},{10,1... | collective-permute-start | bytes 165896 | tf_op jit(solution)/shard_map/ppermute | solution.py:204
  82.3 22.1 %all-to-all-start = ((bf16[8,323,256]{2,1,0:T(8,128)(2,1)}), bf16[8,323,256]{2,1,0:T(8,128)(2,1)S(1)}, u32[]{:S(2)}, u32[]{:S(2)}) async-start(bf16[8,323,256]{2,1,0:T(8,128)(2,1)} %pad_maximum_fusion), calls=%async_computation | async-start | bytes 2686976 | tf_op jit(solution)/shard_map/all_to_all | solution.py:249
Sparse Core Ops, SparseCore 0:
  10.5 39.4 all-gather.1

commit v12 on v11

--- a/solution.py
+++ b/solution.py
@@ -87,36 +87,44 @@
     span = offsets * degrees
     wide = band_ref.shape[2]
 
+    per_tile = group // span
+
     @pl.when(step == 0)
     def _():
         k = lax.broadcasted_iota(jnp.int32, sel_ref.shape, 0)
         y = lax.broadcasted_iota(jnp.int32, sel_ref.shape, 1)
-        blk = y // group
         lane = y % group
+        blk = (y // group) * per_tile + lane // span
+        inner = lane % span
         target = (
             (blk // degrees) * (offsets * degrees * degrees)
-            + (lane // degrees) * (degrees * degrees)
+            + (inner // degrees) * (degrees * degrees)
             + (blk % degrees) * degrees
-            + lane % degrees
+            + inner % degrees
         )
-        sel_ref[...] = jnp.where((lane < span) & (k == target), 1.0, 0.0).astype(sel_ref.dtype)
-
+        valid = (lane < per_tile * span) & (blk < offsets * degrees)
+        sel_ref[...] = jnp.where(valid & (k == target), 1.0, 0.0).astype(sel_ref.dtype)
         band_ref[...] = jnp.zeros(band_ref.shape, band_ref.dtype)
 
     spread = jnp.dot(s_ref[0], sel_ref[...], preferred_element_type=jnp.float32)
     pad = jnp.zeros((8, group), jnp.float32)
     tiles = wide // group
+    lane_id = lax.broadcasted_iota(jnp.int32, (nodes, group), 1)
     for d in range(offsets):
         for i in range(degrees):
             blk = d * degrees + i
-            piece = spread[:, blk * group : (blk + 1) * group]
+            b, q = blk // per_tile, blk % per_tile
+            piece = spread[:, b * group : (b + 1) * group]
+            piece = jnp.where(
+                (lane_id >= q * span) & (lane_id < (q + 1) * span), piece, jnp.zeros_like(piece)
+            )
             for h in range(nodes // 16):
                 base = 16 * h * degrees - degrees
                 tile = base // group
                 parts = []
                 for g in (2 * h, 2 * h + 1):
                     rows = jnp.concatenate([piece[g * 8 : (g + 1) * 8], pad], axis=1)
-                    shift = 8 * g * degrees - degrees - tile * group
+                    shift = (8 * g * degrees - degrees - tile * group - q * span) % (2 * group)
                     rows = pltpu.roll(rows, shift, 1)
                     parts.append(pltpu.roll(rows, 0, 1, stride=degrees, stride_axis=0))
                 window = jnp.concatenate(parts, axis=0).astype(band_ref.dtype)
@@ -142,6 +150,7 @@
     vectors = rows.shape[-1]
     band_rows = degrees * nodes
     band_cols = band_rows + halo.shape[1]
+    sel_cols = -(-offsets * degrees // (128 // (offsets * degrees))) * 128
     in_specs = [
         pl.BlockSpec((1, nodes, width), lambda a: (a + first, 0, 0)),
         pl.BlockSpec(rows.shape, lambda a: (0, 0, 0)),
@@ -162,7 +171,7 @@
         out_specs=pl.BlockSpec((1, band_rows, vectors), lambda a: (a + first, 0, 0)),
         out_shape=jax.ShapeDtypeStruct((axial_rows, band_rows, vectors), jnp.float32),
         scratch_shapes=[
-            pltpu.VMEM((width, offsets * degrees * 128), jnp.bfloat16),
+            pltpu.VMEM((width, sel_cols), jnp.bfloat16),
             pltpu.VMEM((offsets, band_rows, band_cols), jnp.bfloat16),
         ],
         input_output_aliases=aliases,

time: 116 us -> 116 us (level)
  Pallas kernels: 35.2 us -> 33.7 us
  waiting for transfers between devices: 9.3 us -> 10.6 us
    pallas_call x2, Pallas kernels: 25.7 us -> 24.2 us  [banded_force(): pl.pallas_call(functools.partial(stiff_kernel, degrees=degrees, first=fir...]
  transfers between devices with their start and end apart: 6 -> 6, of which waited for: 4 -> 4; matrix products, arithmetic and copies ran while one was open for 15% -> 15% of each run, Pallas kernels for 22% -> 21%
where the time goes in v12:
time: 116 us; the launch traced here: 115 us
  Pallas kernels  33.7 us (29%)
  local copies, waits for them, and re-layouts  30.2 us (26%)
  between operations  14.3 us (12%)
  starting transfers between devices  11 us (9%)
  waiting for transfers between devices  10.6 us (9%)
  matrix products  9.18 us (8%)
  other arithmetic  6.44 us (6%)
    pallas_call x2, Pallas kernels, banded_force(): pl.pallas_call(functools.partial(stiff_kernel, degrees=degrees, first=fir...  24.2 us
    gather x1, local copies, waits for them, and re-layouts, body(): velocity = jnp.take(table, slot_index, axis=0, mode='clip')  18.6 us
    pallas_call x1, Pallas kernels, near_field(): pl.pallas_call(pressure_kernel, grid_spec=grid_spec, out_shape=[jax.Shape...  9.59 us
    all_to_all x1, waiting for transfers between devices, body(): lax.all_to_all(packet, 'circ', split_axis=0, concat_axis=0, tiled=True)  5.12 us
    dot_general x1, matrix products, body(): fluid = jnp.dot(selector, arrived_load, preferred_element_type=jnp.float32)  3.84 us
    all_to_all x1, starting transfers between devices, body(): lax.all_to_all(packet, 'circ', split_axis=0, concat_axis=0, tiled=True)  3.75 us
    slice x3, local copies, waits for them, and re-layouts, body(): node_rows[:1]  3.51 us
    all_gather x1, waiting for transfers between devices, body(): table = lax.all_gather(radial, 'circ', axis=0, tiled=True)  3.07 us
  transfers between devices with their start and end apart: 6, of which 4 were waited for; matrix products, arithmetic and copies ran while one was open for 15% of the time, Pallas kernels for 21%

profile of v12, /device:TPU:0, one launch (start us, length us, event | category | flops | bytes accessed | tf_op | source)
XLA Modules:
  0.0 115.4 jit_solution(5467578722681568190)
XLA Ops:
  7.2 0.0 copy-start.1
  7.2 0.0 all-gather.2.cloned.1.call-start
  7.2 2.0 %slice.82 = bf16[16,64,1,256]{3,1,2,0:T(8,128)(2,1)} slice(bf16[16,64,6,256]{3,1,2,0:T(8,128)(2,1)} %param.11), slice={[0:16], [0:64], [0:1], [0:256]} | slice | bytes 1048576 | tf_op jit(solution)/shard_map/slice | solution.py:200
  9.3 0.0 all-gather.2.cloned.1.call-update
  9.3 1.7 %fusion.34 = (bf16[1,64,6,256]{3,1,2,0:T(8,128)(2,1)}, bf16[1,64,6,256]{3,1,2,0:T(8,128)(2,1)S(1)}) fusion(bf16[16,64,6,256]{3,1,2,0:T(8,128)(2,1)} %param.11), kind=kLoop, calls=%fused_computation.64 | loop fusion | bytes 786432 | tf_op jit(solution)/shard_map/slice | solution.py:206
  11.0 0.1 copy.16
  11.1 0.7 slice.73
  11.9 3.0 %collective-permute-start = (bf16[1,384,256]{2,1,0:T(8,128)(2,1)}, bf16[1,384,256]{2,1,0:T(8,128)(2,1)}, u32[]{:S(2)}, u32[]{:S(2)}) collective-permute-start(bf16[1,384,256]{2,1,0:T(8,128)(2,1)} %slice.73), channel_id=1, source_target_pairs={{0,8},{8,16},{16,24},{24,0},{1,9},{9,17},{17,25},{25,1},{2,10},{10... | collective-permute-start | bytes 589832 | tf_op jit(solution)/shard_map/ppermute | solution.py:205
  14.9 1.0 copy.17
  15.9 0.7 slice.75
  16.7 2.0 %collective-permute-start.1 = (bf16[1,384,256]{2,1,0:T(8,128)(2,1)}, bf16[1,384,256]{2,1,0:T(8,128)(2,1)S(1)}, u32[]{:S(2)}, u32[]{:S(2)}) collective-permute-start(bf16[1,384,256]{2,1,0:T(8,128)(2,1)} %slice.75), channel_id=1, source_target_pairs={{8,0},{16,8},{24,16},{0,24},{9,1},{17,9},{25,17},{1,25},{10,2},{18... | collective-permute-start | bytes 589832 | tf_op jit(solution)/shard_map/ppermute | solution.py:206
  18.7 0.0 copy-done.1
  18.7 1.8 %copy.15 = bf16[16,64,6,256]{3,0,2,1:T(8,128)(2,1)S(1)} copy(bf16[16,64,6,256]{3,1,2,0:T(8,128)(2,1)S(1)} %copy-done.1) | data formatting | bytes 6291456 | tf_op args[0]
  20.5 0.0 copy-start.7
  20.5 0.0 copy-start.6
  20.5 0.0 copy-start.4
  20.5 0.0 copy-start.3
  20.5 1.1 copy.23.rows_ref
  21.6 0.0 copy-start
  21.6 0.0 copy-done.7
  21.7 0.0 copy-done.6
  21.7 0.5 fusion.15
  22.2 0.0 copy-start.5
  22.2 0.1 fusion.17
  22.3 0.0 copy-done.4
  22.3 0.0 copy-done.3
  22.4 2.5 %broadcast_select_fusion.s_ref = bf16[16,64,324]{2,1,0:T(8,128)(2,1)} fusion(bf16[16,64,324]{2,1,0:T(8,128)(2,1)} %param.12, pred[16,324]{1,0:T(8,128)(4,1)S(1)} %fusion.17), kind=kLoop, calls=%fused_computation.21 | loop fusion | flops 331776 | bytes 1332288 | tf_op jit(solution)/shard_map/jit(_where)/select_n | solution.py:222
  24.9 0.0 collective-permute-done.top_ref
  24.9 0.7 fusion.35
  25.6 0.7 collective-permute-done.1.bottom_ref
  26.2 0.0 copy-start.2
  26.2 0.7 pad_maximum_fusion.2
  27.0 2.2 %collective-permute-start.2 = (bf16[18,6,256]{2,1,0:T(8,128)(2,1)}, bf16[18,6,256]{2,1,0:T(8,128)(2,1)S(1)}, u32[]{:S(2)}, u32[]{:S(2)}) collective-permute-start(bf16[18,6,256]{2,1,0:T(8,128)(2,1)} %pad_maximum_fusion.2), channel_id=1, source_target_pairs={{1,0},{2,1},{3,2},{4,3},{5,4},{6,5},{7,6},{0,7},{9,8},{10,9},{11,1... | collective-permute-start | bytes 165896 | tf_op jit(solution)/shard_map/ppermute | solution.py:214
  29.1 0.7 pad_maximum_fusion.3
  29.8 0.0 collective-permute-start.3
  29.8 1.8 %fusion.10 = bf16[2,2560]{1,0:T(2,128)(2,1)S(1)} fusion(s32[1024]{0:T(1024)S(1)} %convert_add_fusion, bf16[1,1024]{1,0:T(2,128)(2,1)S(1)} %stack.13, bf16[1,1024]{1,0:T(2,128)(2,1)S(1)} %stack.12), kind=kOutput, calls=%fused_computation.13 | convolution fusion | flops 13120512 | bytes 18432 | tf_op jit(solution)/shard_map/dot_general | solution.py:247
  31.6 0.0 copy-done
  31.6 0.0 copy-done.5
  31.6 1.0 copy.21.area_ref
  32.6 0.1 reshape.164
  32.7 0.1 reshape.165
  32.9 0.1 pad.12.clone
  32.9 0.0 collective-permute-done.2
  32.9 1.7 %collective-permute-done.3 = bf16[18,6,256]{2,1,0:T(8,128)(2,1)S(1)} collective-permute-done((bf16[18,6,256]{2,1,0:T(8,128)(2,1)}, bf16[18,6,256]{2,1,0:T(8,128)(2,1)S(1)}, u32[]{:S(2)}, u32[]{:S(2)}) %collective-permute-start.3) | collective-permute-done | bytes 55328 | tf_op jit(solution)/shard_map/ppermute | solution.py:213
  34.7 1.2 %pad_maximum_fusion.1.halo_ref = bf16[18,128,256]{2,1,0:T(8,128)(2,1)} fusion(bf16[18,6,256]{2,1,0:T(8,128)(2,1)S(1)} %collective-permute-done.3, bf16[18,6,256]{2,1,0:T(8,128)(2,1)S(1)} %collective-permute-done.2, bf16[128]{0:T(256)(128)(2,1)S(1)} %pad.12.clone), kind=kLoop, calls=%fused_computation.16 | loop fusion | flops 3538944 | bytes 1290496 | tf_op jit(solution)/shard_map/concatenate | solution.py:216
  35.9 0.0 copy-done.2
  35.9 11.0 %shard_map.104.rest_0_ = f32[16,384,256]{2,1,0:T(8,128)} custom-call(bf16[16,64,324]{2,1,0:T(8,128)(2,1)} %broadcast_select_fusion.s_ref, bf16[16,384,256]{2,1,0:T(8,128)(2,1)} %copy-done, bf16[1,384,256]{2,1,0:T(8,128)(2,1)} %collective-permute-done.top_ref, bf16[1,384,256]{2,1,0:T(8,128)(2,1)} %copy-done.2, bf16[18,128,256]{2,1,0:T(8,128)(2,1)} %pad_maximum_fusion.1.halo_ref), custom_call_target="tpu_custom_call" | custom-call | tf_op jit(solution)/shard_map/pallas_call | solution.py:167
  46.9 3.1 %all-gather.2.cloned.1.call-done = bf16[8192,256]{1,0:T(8,128)(2,1)} async-done(((bf16[1024,256]{1,0:T(8,128)(2,1)}), bf16[8192,256]{1,0:T(8,128)(2,1)}) %all-gather.2.cloned.1.call-update) | async-done | bytes 4194320 | tf_op jit(solution)/shard_map/all_gather | solution.py:201
  49.9 18.6 %gather_fusion = bf16[4096,256]{1,0:T(8,128)(2,1)} fusion(bf16[8192,256]{1,0:T(8,128)(2,1)} %all-gather.2.cloned.1.call-done, s32[4096]{0:T(1024)S(1)} %add_clamp_fusion), kind=kCustom, calls=%fused_computation | custom fusion | bytes 4210688 | tf_op jit(solution)/shard_map/jit(_take)/gather | solution.py:228
  68.5 9.6 %shard_map.105 = (f32[2,1024,256]{2,1,0:T(8,128)}, bf16[1024,256]{1,0:T(8,128)(2,1)}) custom-call(s32[4,12]{1,0:T(4,128)} %near_ref.1, bf16[4,12,2,256,256]{4,3,2,1,0:T(8,128)(2,1)} %kern_ref.1, bf16[16,256,256]{2,1,0:T(8,128)(2,1)} %bitcast.23, f32[1024,1]{1,0:T(8,128)} %copy.21.area_ref), custom_call_target="tpu_custom_call" | custom-call | tf_op jit(solution)/shard_map/pallas_call | solution.py:69
  78.1 3.1 %fusion.9 = bf16[2560,256]{1,0:T(8,128)(2,1)S(1)} fusion(bf16[1024,256]{1,0:T(8,128)(2,1)} %get-tuple-element.21, s32[1024]{0:T(1024)S(1)} %convert_add_fusion), kind=kOutput, calls=%fused_computation.12 | convolution fusion | flops 1345454080 | bytes 1839104 | tf_op jit(solution)/shard_map/dot_general | solution.py:241
  81.1 1.2 %pad_maximum_fusion = bf16[8,323,256]{2,1,0:T(8,128)(2,1)} fusion(bf16[8,3,256]{2,1,0:T(4,128)(2,1)S(1)} %reshape.166, bf16[8,320,256]{2,1,0:T(8,128)(2,1)S(1)} %bitcast.26), kind=kLoop, calls=%fused_computation.15 | loop fusion | flops 2646016 | bytes 2646016 | tf_op jit(solution)/shard_map/concatenate | solution.py:256
  82.3 3.8 %all-to-all-start = ((bf16[8,323,256]{2,1,0:T(8,128)(2,1)}), bf16[8,323,256]{2,1,0:T(8,128)(2,1)S(1)}, u32[]{:S(2)}, u32[]{:S(2)}) async-start(bf16[8,323,256]{2,1,0:T(8,128)(2,1)} %pad_maximum_fusion), calls=%async_computation | async-start | bytes 2686976 | tf_op jit(solution)/shard_map/all_to_all | solution.py:258
  86.1 13.2 %shard_map.106 = f32[16,384,256]{2,1,0:T(8,128)} custom-call(bf16[16,64,324]{2,1,0:T(8,128)(2,1)} %broadcast_select_fusion.s_ref, bf16[16,384,256]{2,1,0:T(8,128)(2,1)} %copy-done, bf16[1,384,256]{2,1,0:T(8,128)(2,1)} %collective-permute-done.top_ref, bf16[1,384,256]{2,1,0:T(8,128)(2,1)} %copy-done.2, ...), custom_call_target="tpu_custom_call", output_to_operand_aliasing={{}: (5, {})} | custom-call | tf_op jit(solution)/shard_map/pallas_call | solution.py:167
  99.3 5.1 %all-to-all-done = bf16[8,323,256]{2,1,0:T(8,128)(2,1)S(1)} async-done(((bf16[8,323,256]{2,1,0:T(8,128)(2,1)}), bf16[8,323,256]{2,1,0:T(8,128)(2,1)S(1)}, u32[]{:S(2)}, u32[]{:S(2)}) %all-to-all-start) | async-done | bytes 1323040 | tf_op jit(solution)/shard_map/all_to_all | solution.py:258
  104.5 0.1 reshape.170
  104.5 0.1 fusion.20
  104.6 0.1 convert_element_type.42
  104.7 0.1 slice.102
  104.8 3.8 %fusion.16 = f32[16,384,256]{2,1,0:T(8,128)} fusion(f32[16,384,256]{2,1,0:T(8,128)} %shard_map.106, bf16[2560,256,1]{1,0,2:T(8,128)(2,1)S(1)} %bitcast.25, s32[16,64]{1,0:T(8,128)S(1)} %multiply_add_fusion, s32[2560]{0:T(1024)S(1)} %convert_element_type.42), kind=kOutput, calls=%fused_computation.20 | convolution fusion | flops 1345323008 | bytes 3422208 | tf_op jit(solution)/shard_map/dot_general | solution.py:273
  (18 shorter events, 0.2 us)
Async XLA Ops:
  7.2 11.6 %copy-start.1 = (bf16[16,64,6,256]{3,1,2,0:T(8,128)(2,1)S(1)}, bf16[16,64,6,256]{3,1,2,0:T(8,128)(2,1)}, u32[]{:S(2)}) copy-start(bf16[16,64,6,256]{3,1,2,0:T(8,128)(2,1)} %param.11) | copy-start | bytes 9437188
  7.2 42.8 %all-gather.2.cloned.1.call-start = ((), (), s32[]{:S(2)}) async-start(), calls=%async_computation.1 | async-start | bytes 4718592 | tf_op jit(solution)/shard_map/all_gather | solution.py:201
  11.9 13.0 %collective-permute-start = (bf16[1,384,256]{2,1,0:T(8,128)(2,1)}, bf16[1,384,256]{2,1,0:T(8,128)(2,1)}, u32[]{:S(2)}, u32[]{:S(2)}) collective-permute-start(bf16[1,384,256]{2,1,0:T(8,128)(2,1)} %slice.73), channel_id=1, source_target_pairs={{0,8},{8,16},{16,24},{24,0},{1,9},{9,17},{17,25},{25,1},{2,10},{10... | collective-permute-start | bytes 589832 | tf_op jit(solution)/shard_map/ppermute | solution.py:205
  16.7 9.6 %collective-permute-start.1 = (bf16[1,384,256]{2,1,0:T(8,128)(2,1)}, bf16[1,384,256]{2,1,0:T(8,128)(2,1)S(1)}, u32[]{:S(2)}, u32[]{:S(2)}) collective-permute-start(bf16[1,384,256]{2,1,0:T(8,128)(2,1)} %slice.75), channel_id=1, source_target_pairs={{8,0},{16,8},{24,16},{0,24},{9,1},{17,9},{25,17},{1,25},{10,2},{18... | collective-permute-start | bytes 589832 | tf_op jit(solution)/shard_map/ppermute | solution.py:206
  20.5 1.2 %copy-start.7 = (s32[1024]{0:T(1024)S(1)}, s32[1024]{0:T(1024)}, u32[]{:S(2)}) copy-start(s32[1024]{0:T(1024)} %param.19) | copy-start | bytes 12292
  20.5 1.2 %copy-start.6 = (s32[1024,1]{0,1:T(1,128)S(1)}, s32[1024,1]{0,1:T(1,128)}, u32[]{:S(2)}) copy-start(s32[1024,1]{0,1:T(1,128)} %param.18) | copy-start | bytes 12292
  20.5 1.8 %copy-start.4 = (s32[4096,1]{0,1:T(1,128)S(1)}, s32[4096,1]{0,1:T(1,128)}, u32[]{:S(2)}) copy-start(s32[4096,1]{0,1:T(1,128)} %param.16) | copy-start | bytes 49156
  20.5 1.8 %copy-start.3 = (s32[4096]{0:T(1024)S(1)}, s32[4096]{0:T(1024)}, u32[]{:S(2)}) copy-start(s32[4096]{0:T(1024)} %param.17) | copy-start | bytes 49156
  21.6 10.0 %copy-start = (bf16[16,384,256]{2,1,0:T(8,128)(2,1)}, bf16[16,384,256]{2,1,0:T(8,128)(2,1)S(1)}, u32[]{:S(2)}) copy-start(bf16[16,384,256]{2,1,0:T(8,128)(2,1)S(1)} %copy.23.rows_ref) | copy-start | bytes 9437188
  22.2 9.4 %copy-start.5 = (f32[1024]{0:T(1024)S(1)}, f32[1024]{0:T(1024)}, u32[]{:S(2)}) copy-start(f32[1024]{0:T(1024)} %param.14) | copy-start | bytes 12292
  26.2 9.7 %copy-start.2 = (bf16[1,384,256]{2,1,0:T(8,128)(2,1)}, bf16[1,384,256]{2,1,0:T(8,128)(2,1)S(1)}, u32[]{:S(2)}) copy-start(bf16[1,384,256]{2,1,0:T(8,128)(2,1)S(1)} %collective-permute-done.1.bottom_ref) | copy-start | bytes 589828
  27.0 6.0 %collective-permute-start.2 = (bf16[18,6,256]{2,1,0:T(8,128)(2,1)}, bf16[18,6,256]{2,1,0:T(8,128)(2,1)S(1)}, u32[]{:S(2)}, u32[]{:S(2)}) collective-permute-start(bf16[18,6,256]{2,1,0:T(8,128)(2,1)} %pad_maximum_fusion.2), channel_id=1, source_target_pairs={{1,0},{2,1},{3,2},{4,3},{5,4},{6,5},{7,6},{0,7},{9,8},{10,9},{11,1... | collective-permute-start | bytes 165896 | tf_op jit(solution)/shard_map/ppermute | solution.py:214
  29.8 4.9 %collective-permute-start.3 = (bf16[18,6,256]{2,1,0:T(8,128)(2,1)}, bf16[18,6,256]{2,1,0:T(8,128)(2,1)S(1)}, u32[]{:S(2)}, u32[]{:S(2)}) collective-permute-start(bf16[18,6,256]{2,1,0:T(8,128)(2,1)} %pad_maximum_fusion.3), channel_id=1, source_target_pairs={{0,1},{1,2},{2,3},{3,4},{4,5},{5,6},{6,7},{7,0},{8,9},{9,10},{10,1... | collective-permute-start | bytes 165896 | tf_op jit(solution)/shard_map/ppermute | solution.py:213
  82.3 22.1 %all-to-all-start = ((bf16[8,323,256]{2,1,0:T(8,128)(2,1)}), bf16[8,323,256]{2,1,0:T(8,128)(2,1)S(1)}, u32[]{:S(2)}, u32[]{:S(2)}) async-start(bf16[8,323,256]{2,1,0:T(8,128)(2,1)} %pad_maximum_fusion), calls=%async_computation | async-start | bytes 2686976 | tf_op jit(solution)/shard_map/all_to_all | solution.py:258
Sparse Core Ops, SparseCore 0:
  10.5 39.4 all-gather.1

commit v13 on v12

--- a/solution.py
+++ b/solution.py
@@ -34,46 +34,52 @@
     return owners * capacity + ranking
 
 
-def pressure_kernel(near_ref, kern_ref, vel_ref, area_ref, p_ref, load_ref):
+def pressure_kernel(near_ref, kern_ref, vel_ref, area_ref, *rest, with_load):
+    p_ref = rest[-2] if with_load else rest[-1]
     g = pl.program_id(0)
     near_count = kern_ref.shape[1]
-    panel = kern_ref.shape[3]
     for n in range(near_count):
         m = near_ref[g, n]
-        w = kern_ref[0, n].reshape(2 * panel, panel)
-        prod = jnp.dot(w, vel_ref[m], preferred_element_type=jnp.float32)
+        prod = jnp.dot(kern_ref[0, n, 0], vel_ref[m], preferred_element_type=jnp.float32)
         if n == 0:
-            p_ref[...] = prod.reshape(p_ref.shape)
+            p_ref[0] = prod
         else:
-            p_ref[...] += prod.reshape(p_ref.shape)
-    load_ref[...] = (area_ref[...] * p_ref[0]).astype(load_ref.dtype)
-
-
-def near_field(kernel, source_cells, areas, near_cells):
+            p_ref[0] += prod
+    if with_load:
+        load_ref = rest[-1]
+        load_ref[...] = (area_ref[...] * p_ref[0]).astype(load_ref.dtype)
+
+
+def near_field(kernel, source_cells, areas, near_cells, part, previous=None):
     cells_dev, near_count, _, panel, _ = kernel.shape
     src_cells, _, vectors = source_cells.shape
     targets = cells_dev * panel
+    with_load = previous is None
+    in_specs = [
+        pl.BlockSpec((1, near_count, 1, panel, panel), lambda g, near: (g, 0, part, 0, 0)),
+        pl.BlockSpec((src_cells, panel, vectors), lambda g, near: (0, 0, 0)),
+        pl.BlockSpec((panel, 1), lambda g, near: (g, 0)),
+    ]
+    operands = [near_cells, kernel, source_cells, areas.reshape(targets, 1)]
+    out_specs = [pl.BlockSpec((1, panel, vectors), lambda g, near: (part, g, 0))]
+    out_shape = [jax.ShapeDtypeStruct((2, targets, vectors), jnp.float32)]
+    aliases = {}
+    if with_load:
+        out_specs.append(pl.BlockSpec((panel, vectors), lambda g, near: (g, 0)))
+        out_shape.append(jax.ShapeDtypeStruct((targets, vectors), jnp.bfloat16))
+    else:
+        in_specs.append(pl.BlockSpec(memory_space=pl.ANY))
+        operands.append(previous)
+        aliases = {len(operands) - 1: 0}
     grid_spec = pltpu.PrefetchScalarGridSpec(
-        num_scalar_prefetch=1,
-        grid=(cells_dev,),
-        in_specs=[
-            pl.BlockSpec((1, near_count, 2, panel, panel), lambda g, near: (g, 0, 0, 0, 0)),
-            pl.BlockSpec((src_cells, panel, vectors), lambda g, near: (0, 0, 0)),
-            pl.BlockSpec((panel, 1), lambda g, near: (g, 0)),
-        ],
-        out_specs=[
-            pl.BlockSpec((2, panel, vectors), lambda g, near: (0, g, 0)),
-            pl.BlockSpec((panel, vectors), lambda g, near: (g, 0)),
-        ],
+        num_scalar_prefetch=1, grid=(cells_dev,), in_specs=in_specs, out_specs=out_specs
     )
     return pl.pallas_call(
-        pressure_kernel,
+        functools.partial(pressure_kernel, with_load=with_load),
         grid_spec=grid_spec,
-        out_shape=[
-            jax.ShapeDtypeStruct((2, targets, vectors), jnp.float32),
-            jax.ShapeDtypeStruct((targets, vectors), jnp.bfloat16),
-        ],
-    )(near_cells, kernel, source_cells, areas.reshape(targets, 1))
+        out_shape=out_shape,
+        input_output_aliases=aliases,
+    )(*operands)
 
 
 def stiff_kernel(s_ref, rows_ref, top_ref, bottom_ref, halo_ref, *rest, degrees, first):
@@ -229,7 +235,7 @@
 
     panel_size = kernel.shape[3]
     source_cells = velocity.reshape(-1, panel_size, vectors)
-    pressure, load_value = near_field(kernel, source_cells, areas, near_cells)
+    pressure, load_value = near_field(kernel, source_cells, areas, near_cells, 0)
 
     load_owner = target_owner[:, 0]
     target_count = load_owner.shape[0]
@@ -254,11 +260,12 @@
         ((0, 0), (0, digit_rows * vectors - 2 * load_capacity)),
     ).reshape(sectors, digit_rows, vectors)
     packet = jnp.concatenate([outgoing, slot_digits], axis=1)
-    packet, force = lax.optimization_barrier((packet, force))
+    packet, force, pressure = lax.optimization_barrier((packet, force, pressure))
     arrived = lax.all_to_all(packet, "circ", split_axis=0, concat_axis=0, tiled=True)
     force = banded_force(
         blocks, node_rows, top, bottom, halo, degrees, half, axial_rows - half, force
     )
+    pressure = near_field(kernel, source_cells, areas, near_cells, 1, pressure)[0]
     arrived_load = arrived[:, :load_capacity].reshape(-1, vectors)
     arrived_digits = (
         arrived[:, load_capacity:]

time: 116 us -> 115 us (level)
  waiting for transfers between devices: 10.6 us -> 5.5 us
  Pallas kernels: 33.7 us -> 38.1 us
    all_to_all x1, waiting for transfers between devices: 5.12 us -> 0.01 us  [body(): lax.all_to_all(packet, 'circ', split_axis=0, concat_axis=0, tiled=True)]
    pallas_call x1 -> x2, Pallas kernels: 9.59 us -> 14 us  [near_field(): pl.pallas_call(functools.partial(pressure_kernel, with_load=with_load), g...]
  transfers between devices with their start and end apart: 6 -> 6, of which waited for: 4 -> 3; matrix products, arithmetic and copies ran while one was open for 15% -> 15% of each run, Pallas kernels for 21% -> 27%
where the time goes in v13:
time: 115 us
  Pallas kernels  38.1 us (33%)
  local copies, waits for them, and re-layouts  30.2 us (26%)
  between operations  14.3 us (12%)
  starting transfers between devices  11 us (10%)
  matrix products  9.18 us (8%)
  other arithmetic  6.44 us (6%)
  waiting for transfers between devices  5.5 us (5%)
    pallas_call x2, Pallas kernels, banded_force(): pl.pallas_call(functools.partial(stiff_kernel, degrees=degrees, first=fir...  24.1 us
    gather x1, local copies, waits for them, and re-layouts, body(): velocity = jnp.take(table, slot_index, axis=0, mode='clip')  18.6 us
    pallas_call x2, Pallas kernels, near_field(): pl.pallas_call(functools.partial(pressure_kernel, with_load=with_load), g...  14 us
    dot_general x1, matrix products, body(): fluid = jnp.dot(selector, arrived_load, preferred_element_type=jnp.float32)  3.84 us
    all_to_all x1, starting transfers between devices, body(): lax.all_to_all(packet, 'circ', split_axis=0, concat_axis=0, tiled=True)  3.75 us
    slice x3, local copies, waits for them, and re-layouts, body(): node_rows[:1]  3.51 us
    all_gather x1, waiting for transfers between devices, body(): table = lax.all_gather(radial, 'circ', axis=0, tiled=True)  3.07 us
    dot_general x1, matrix products, body(): jnp.dot(gather_slot, load_value, preferred_element_type=jnp.float32)  3.06 us
  transfers between devices with their start and end apart: 6, of which 3 were waited for; matrix products, arithmetic and copies ran while one was open for 15% of the time, Pallas kernels for 27%

profile of v13, /device:TPU:0, one launch (start us, length us, event | category | flops | bytes accessed | tf_op | source)
XLA Modules:
  0.0 114.7 jit_solution(2063212162940735511)
XLA Ops:
  7.2 0.0 copy-start.1
  7.2 0.0 all-gather.2.cloned.1.call-start
  7.2 2.0 %slice.82 = bf16[16,64,1,256]{3,1,2,0:T(8,128)(2,1)} slice(bf16[16,64,6,256]{3,1,2,0:T(8,128)(2,1)} %param.11), slice={[0:16], [0:64], [0:1], [0:256]} | slice | bytes 1048576 | tf_op jit(solution)/shard_map/slice | solution.py:206
  9.3 0.0 all-gather.2.cloned.1.call-update
  9.3 1.7 %fusion.34 = (bf16[1,64,6,256]{3,1,2,0:T(8,128)(2,1)}, bf16[1,64,6,256]{3,1,2,0:T(8,128)(2,1)S(1)}) fusion(bf16[16,64,6,256]{3,1,2,0:T(8,128)(2,1)} %param.11), kind=kLoop, calls=%fused_computation.64 | loop fusion | bytes 786432 | tf_op jit(solution)/shard_map/slice | solution.py:212
  11.0 0.1 copy.17
  11.1 0.7 slice.73
  11.9 3.0 %collective-permute-start = (bf16[1,384,256]{2,1,0:T(8,128)(2,1)}, bf16[1,384,256]{2,1,0:T(8,128)(2,1)}, u32[]{:S(2)}, u32[]{:S(2)}) collective-permute-start(bf16[1,384,256]{2,1,0:T(8,128)(2,1)} %slice.73), channel_id=1, source_target_pairs={{0,8},{8,16},{16,24},{24,0},{1,9},{9,17},{17,25},{25,1},{2,10},{10... | collective-permute-start | bytes 589832 | tf_op jit(solution)/shard_map/ppermute | solution.py:211
  14.9 1.0 copy.18
  15.9 0.7 slice.75
  16.7 2.0 %collective-permute-start.1 = (bf16[1,384,256]{2,1,0:T(8,128)(2,1)}, bf16[1,384,256]{2,1,0:T(8,128)(2,1)S(1)}, u32[]{:S(2)}, u32[]{:S(2)}) collective-permute-start(bf16[1,384,256]{2,1,0:T(8,128)(2,1)} %slice.75), channel_id=1, source_target_pairs={{8,0},{16,8},{24,16},{0,24},{9,1},{17,9},{25,17},{1,25},{10,2},{18... | collective-permute-start | bytes 589832 | tf_op jit(solution)/shard_map/ppermute | solution.py:212
  18.7 0.0 copy-done.1
  18.7 1.8 %copy.16 = bf16[16,64,6,256]{3,0,2,1:T(8,128)(2,1)S(1)} copy(bf16[16,64,6,256]{3,1,2,0:T(8,128)(2,1)S(1)} %copy-done.1) | data formatting | bytes 6291456 | tf_op args[0]
  20.5 0.0 copy-start.7
  20.5 0.0 copy-start.6
  20.5 0.0 copy-start.4
  20.5 0.0 copy-start.3
  20.5 1.1 copy.24.rows_ref
  21.6 0.0 copy-start
  21.6 0.0 copy-done.7
  21.7 0.0 copy-done.6
  21.7 0.5 fusion.15
  22.2 0.0 copy-start.5
  22.2 0.1 fusion.17
  22.3 0.0 copy-done.4
  22.3 0.0 copy-done.3
  22.4 2.5 %broadcast_select_fusion.s_ref = bf16[16,64,324]{2,1,0:T(8,128)(2,1)} fusion(bf16[16,64,324]{2,1,0:T(8,128)(2,1)} %param.12, pred[16,324]{1,0:T(8,128)(4,1)S(1)} %fusion.17), kind=kLoop, calls=%fused_computation.21 | loop fusion | flops 331776 | bytes 1332288 | tf_op jit(solution)/shard_map/jit(_where)/select_n | solution.py:228
  24.9 0.0 collective-permute-done.top_ref
  24.9 0.7 fusion.35
  25.6 0.7 collective-permute-done.1.bottom_ref
  26.2 0.0 copy-start.2
  26.2 0.7 pad_maximum_fusion.2
  27.0 2.2 %collective-permute-start.2 = (bf16[18,6,256]{2,1,0:T(8,128)(2,1)}, bf16[18,6,256]{2,1,0:T(8,128)(2,1)S(1)}, u32[]{:S(2)}, u32[]{:S(2)}) collective-permute-start(bf16[18,6,256]{2,1,0:T(8,128)(2,1)} %pad_maximum_fusion.2), channel_id=1, source_target_pairs={{1,0},{2,1},{3,2},{4,3},{5,4},{6,5},{7,6},{0,7},{9,8},{10,9},{11,1... | collective-permute-start | bytes 165896 | tf_op jit(solution)/shard_map/ppermute | solution.py:220
  29.1 0.7 pad_maximum_fusion.3
  29.8 0.0 collective-permute-start.3
  29.8 1.8 %fusion.10 = bf16[2,2560]{1,0:T(2,128)(2,1)S(1)} fusion(s32[1024]{0:T(1024)S(1)} %convert_add_fusion, bf16[1,1024]{1,0:T(2,128)(2,1)S(1)} %stack.13, bf16[1,1024]{1,0:T(2,128)(2,1)S(1)} %stack.12), kind=kOutput, calls=%fused_computation.13 | convolution fusion | flops 13120512 | bytes 18432 | tf_op jit(solution)/shard_map/dot_general | solution.py:253
  31.6 0.0 copy-done
  31.6 0.0 copy-done.5
  31.6 1.0 copy.22.area_ref
  32.6 0.1 reshape.165
  32.7 0.1 reshape.166
  32.9 0.1 pad.12.clone
  32.9 0.0 collective-permute-done.2
  32.9 1.7 %collective-permute-done.3 = bf16[18,6,256]{2,1,0:T(8,128)(2,1)S(1)} collective-permute-done((bf16[18,6,256]{2,1,0:T(8,128)(2,1)}, bf16[18,6,256]{2,1,0:T(8,128)(2,1)S(1)}, u32[]{:S(2)}, u32[]{:S(2)}) %collective-permute-start.3) | collective-permute-done | bytes 55328 | tf_op jit(solution)/shard_map/ppermute | solution.py:219
  34.7 1.2 %pad_maximum_fusion.1.halo_ref = bf16[18,128,256]{2,1,0:T(8,128)(2,1)} fusion(bf16[18,6,256]{2,1,0:T(8,128)(2,1)S(1)} %collective-permute-done.3, bf16[18,6,256]{2,1,0:T(8,128)(2,1)S(1)} %collective-permute-done.2, bf16[128]{0:T(256)(128)(2,1)S(1)} %pad.12.clone), kind=kLoop, calls=%fused_computation.16 | loop fusion | flops 3538944 | bytes 1290496 | tf_op jit(solution)/shard_map/concatenate | solution.py:222
  35.9 0.0 copy-done.2
  35.9 11.0 %shard_map.104.rest_0_ = f32[16,384,256]{2,1,0:T(8,128)} custom-call(bf16[16,64,324]{2,1,0:T(8,128)(2,1)} %broadcast_select_fusion.s_ref, bf16[16,384,256]{2,1,0:T(8,128)(2,1)} %copy-done, bf16[1,384,256]{2,1,0:T(8,128)(2,1)} %collective-permute-done.top_ref, bf16[1,384,256]{2,1,0:T(8,128)(2,1)} %copy-done.2, bf16[18,128,256]{2,1,0:T(8,128)(2,1)} %pad_maximum_fusion.1.halo_ref), custom_call_target="tpu_custom_call" | custom-call | tf_op jit(solution)/shard_map/pallas_call | solution.py:173
  46.9 3.1 %all-gather.2.cloned.1.call-done = bf16[8192,256]{1,0:T(8,128)(2,1)} async-done(((bf16[1024,256]{1,0:T(8,128)(2,1)}), bf16[8192,256]{1,0:T(8,128)(2,1)}) %all-gather.2.cloned.1.call-update) | async-done | bytes 4194320 | tf_op jit(solution)/shard_map/all_gather | solution.py:207
  49.9 18.6 %gather_fusion = bf16[4096,256]{1,0:T(8,128)(2,1)} fusion(bf16[8192,256]{1,0:T(8,128)(2,1)} %all-gather.2.cloned.1.call-done, s32[4096]{0:T(1024)S(1)} %add_clamp_fusion), kind=kCustom, calls=%fused_computation | custom fusion | bytes 4210688 | tf_op jit(solution)/shard_map/jit(_take)/gather | solution.py:234
  68.5 7.1 %shard_map.105 = (f32[2,1024,256]{2,1,0:T(8,128)}, bf16[1024,256]{1,0:T(8,128)(2,1)}) custom-call(s32[4,12]{1,0:T(4,128)} %near_ref.3, bf16[4,12,2,256,256]{4,3,2,1,0:T(8,128)(2,1)} %kern_ref.3, bf16[16,256,256]{2,1,0:T(8,128)(2,1)} %bitcast.22, f32[1024,1]{1,0:T(8,128)} %copy.22.area_ref), custom_call_target="tpu_custom_call" | custom-call | tf_op jit(solution)/shard_map/pallas_call | solution.py:77
  75.6 3.1 %fusion.9 = bf16[2560,256]{1,0:T(8,128)(2,1)S(1)} fusion(bf16[1024,256]{1,0:T(8,128)(2,1)} %get-tuple-element.22, s32[1024]{0:T(1024)S(1)} %convert_add_fusion), kind=kOutput, calls=%fused_computation.12 | convolution fusion | flops 1345454080 | bytes 1839104 | tf_op jit(solution)/shard_map/dot_general | solution.py:247
  78.6 1.2 %pad_maximum_fusion = bf16[8,323,256]{2,1,0:T(8,128)(2,1)} fusion(bf16[8,3,256]{2,1,0:T(4,128)(2,1)S(1)} %reshape.167, bf16[8,320,256]{2,1,0:T(8,128)(2,1)S(1)} %bitcast.27), kind=kLoop, calls=%fused_computation.15 | loop fusion | flops 2646016 | bytes 2646016 | tf_op jit(solution)/shard_map/concatenate | solution.py:262
  79.8 3.8 %all-to-all-start = ((bf16[8,323,256]{2,1,0:T(8,128)(2,1)}), bf16[8,323,256]{2,1,0:T(8,128)(2,1)S(1)}, u32[]{:S(2)}, u32[]{:S(2)}) async-start(bf16[8,323,256]{2,1,0:T(8,128)(2,1)} %pad_maximum_fusion), calls=%async_computation | async-start | bytes 2686976 | tf_op jit(solution)/shard_map/all_to_all | solution.py:264
  83.6 6.9 %shard_map.107 = f32[2,1024,256]{2,1,0:T(8,128)} custom-call(s32[4,12]{1,0:T(4,128)} %near_ref.3, bf16[4,12,2,256,256]{4,3,2,1,0:T(8,128)(2,1)} %kern_ref.3, bf16[16,256,256]{2,1,0:T(8,128)(2,1)} %bitcast.23, f32[1024,1]{1,0:T(8,128)} %copy.22.area_ref, f32[2,1024,256]{2,1,0:T(8,128)} %get-tuple-element.27.rest_0_), custom_call_target="tpu_custom_call", output_to_operand_aliasing={{}: (4, {})} | custom-call | tf_op jit(solution)/shard_map/pallas_call | solution.py:77
  90.5 13.2 %shard_map.106 = f32[16,384,256]{2,1,0:T(8,128)} custom-call(bf16[16,64,324]{2,1,0:T(8,128)(2,1)} %broadcast_select_fusion.s_ref, bf16[16,384,256]{2,1,0:T(8,128)(2,1)} %copy-done, bf16[1,384,256]{2,1,0:T(8,128)(2,1)} %collective-permute-done.top_ref, bf16[1,384,256]{2,1,0:T(8,128)(2,1)} %copy-done.2, ...), custom_call_target="tpu_custom_call", output_to_operand_aliasing={{}: (5, {})} | custom-call | tf_op jit(solution)/shard_map/pallas_call | solution.py:173
  103.7 0.0 all-to-all-done
  103.7 0.1 reshape.171
  103.8 0.1 fusion.20
  103.9 0.1 convert_element_type.42
  103.9 0.1 slice.102
  104.0 3.8 %fusion.16 = f32[16,384,256]{2,1,0:T(8,128)} fusion(f32[16,384,256]{2,1,0:T(8,128)} %shard_map.106, bf16[2560,256,1]{1,0,2:T(8,128)(2,1)S(1)} %bitcast.26, s32[16,64]{1,0:T(8,128)S(1)} %multiply_add_fusion, s32[2560]{0:T(1024)S(1)} %convert_element_type.42), kind=kOutput, calls=%fused_computation.20 | convolution fusion | flops 1345323008 | bytes 3422208 | tf_op jit(solution)/shard_map/dot_general | solution.py:280
  (18 shorter events, 0.2 us)
Async XLA Ops:
  7.2 11.6 %copy-start.1 = (bf16[16,64,6,256]{3,1,2,0:T(8,128)(2,1)S(1)}, bf16[16,64,6,256]{3,1,2,0:T(8,128)(2,1)}, u32[]{:S(2)}) copy-start(bf16[16,64,6,256]{3,1,2,0:T(8,128)(2,1)} %param.11) | copy-start | bytes 9437188
  7.2 42.8 %all-gather.2.cloned.1.call-start = ((), (), s32[]{:S(2)}) async-start(), calls=%async_computation.1 | async-start | bytes 4718592 | tf_op jit(solution)/shard_map/all_gather | solution.py:207
  11.9 13.0 %collective-permute-start = (bf16[1,384,256]{2,1,0:T(8,128)(2,1)}, bf16[1,384,256]{2,1,0:T(8,128)(2,1)}, u32[]{:S(2)}, u32[]{:S(2)}) collective-permute-start(bf16[1,384,256]{2,1,0:T(8,128)(2,1)} %slice.73), channel_id=1, source_target_pairs={{0,8},{8,16},{16,24},{24,0},{1,9},{9,17},{17,25},{25,1},{2,10},{10... | collective-permute-start | bytes 589832 | tf_op jit(solution)/shard_map/ppermute | solution.py:211
  16.7 9.6 %collective-permute-start.1 = (bf16[1,384,256]{2,1,0:T(8,128)(2,1)}, bf16[1,384,256]{2,1,0:T(8,128)(2,1)S(1)}, u32[]{:S(2)}, u32[]{:S(2)}) collective-permute-start(bf16[1,384,256]{2,1,0:T(8,128)(2,1)} %slice.75), channel_id=1, source_target_pairs={{8,0},{16,8},{24,16},{0,24},{9,1},{17,9},{25,17},{1,25},{10,2},{18... | collective-permute-start | bytes 589832 | tf_op jit(solution)/shard_map/ppermute | solution.py:212
  20.5 1.2 %copy-start.7 = (s32[1024]{0:T(1024)S(1)}, s32[1024]{0:T(1024)}, u32[]{:S(2)}) copy-start(s32[1024]{0:T(1024)} %param.19) | copy-start | bytes 12292
  20.5 1.2 %copy-start.6 = (s32[1024,1]{0,1:T(1,128)S(1)}, s32[1024,1]{0,1:T(1,128)}, u32[]{:S(2)}) copy-start(s32[1024,1]{0,1:T(1,128)} %param.18) | copy-start | bytes 12292
  20.5 1.8 %copy-start.4 = (s32[4096,1]{0,1:T(1,128)S(1)}, s32[4096,1]{0,1:T(1,128)}, u32[]{:S(2)}) copy-start(s32[4096,1]{0,1:T(1,128)} %param.16) | copy-start | bytes 49156
  20.5 1.8 %copy-start.3 = (s32[4096]{0:T(1024)S(1)}, s32[4096]{0:T(1024)}, u32[]{:S(2)}) copy-start(s32[4096]{0:T(1024)} %param.17) | copy-start | bytes 49156
  21.6 10.0 %copy-start = (bf16[16,384,256]{2,1,0:T(8,128)(2,1)}, bf16[16,384,256]{2,1,0:T(8,128)(2,1)S(1)}, u32[]{:S(2)}) copy-start(bf16[16,384,256]{2,1,0:T(8,128)(2,1)S(1)} %copy.24.rows_ref) | copy-start | bytes 9437188
  22.2 9.4 %copy-start.5 = (f32[1024]{0:T(1024)S(1)}, f32[1024]{0:T(1024)}, u32[]{:S(2)}) copy-start(f32[1024]{0:T(1024)} %param.14) | copy-start | bytes 12292
  26.2 9.7 %copy-start.2 = (bf16[1,384,256]{2,1,0:T(8,128)(2,1)}, bf16[1,384,256]{2,1,0:T(8,128)(2,1)S(1)}, u32[]{:S(2)}) copy-start(bf16[1,384,256]{2,1,0:T(8,128)(2,1)S(1)} %collective-permute-done.1.bottom_ref) | copy-start | bytes 589828
  27.0 6.0 %collective-permute-start.2 = (bf16[18,6,256]{2,1,0:T(8,128)(2,1)}, bf16[18,6,256]{2,1,0:T(8,128)(2,1)S(1)}, u32[]{:S(2)}, u32[]{:S(2)}) collective-permute-start(bf16[18,6,256]{2,1,0:T(8,128)(2,1)} %pad_maximum_fusion.2), channel_id=1, source_target_pairs={{1,0},{2,1},{3,2},{4,3},{5,4},{6,5},{7,6},{0,7},{9,8},{10,9},{11,1... | collective-permute-start | bytes 165896 | tf_op jit(solution)/shard_map/ppermute | solution.py:220
  29.8 4.9 %collective-permute-start.3 = (bf16[18,6,256]{2,1,0:T(8,128)(2,1)}, bf16[18,6,256]{2,1,0:T(8,128)(2,1)S(1)}, u32[]{:S(2)}, u32[]{:S(2)}) collective-permute-start(bf16[18,6,256]{2,1,0:T(8,128)(2,1)} %pad_maximum_fusion.3), channel_id=1, source_target_pairs={{0,1},{1,2},{2,3},{3,4},{4,5},{5,6},{6,7},{7,0},{8,9},{9,10},{10,1... | collective-permute-start | bytes 165896 | tf_op jit(solution)/shard_map/ppermute | solution.py:219
  79.8 23.9 %all-to-all-start = ((bf16[8,323,256]{2,1,0:T(8,128)(2,1)}), bf16[8,323,256]{2,1,0:T(8,128)(2,1)S(1)}, u32[]{:S(2)}, u32[]{:S(2)}) async-start(bf16[8,323,256]{2,1,0:T(8,128)(2,1)} %pad_maximum_fusion), calls=%async_computation | async-start | bytes 2686976 | tf_op jit(solution)/shard_map/all_to_all | solution.py:264
Sparse Core Ops, SparseCore 0:
  10.5 39.4 all-gather.1

commit v14 on v13

--- a/solution.py
+++ b/solution.py
@@ -226,7 +226,7 @@
         global_row[:, None] + lane_step[None, :] < axial_total
     )
     blocks = jnp.where(inside[:, None, :], stiffness, jnp.zeros_like(stiffness))
-    half = (axial_rows * 7) // 16
+    half = axial_rows // 2
     force = banded_force(blocks, node_rows, top, bottom, halo, degrees, 0, half)
 
     force, table = lax.optimization_barrier((force, table))

time: 115 us -> 114 us (level)
  no operation moved by 1% of the time
where the time goes in v14:
time: 114 us
  Pallas kernels  38.1 us (33%)
  local copies, waits for them, and re-layouts  30.2 us (26%)
  between operations  14.3 us (13%)
  starting transfers between devices  11 us (10%)
  matrix products  9.18 us (8%)
  other arithmetic  6.44 us (6%)
  waiting for transfers between devices  4.4 us (4%)
    pallas_call x2, Pallas kernels, banded_force(): pl.pallas_call(functools.partial(stiff_kernel, degrees=degrees, first=fir...  24.1 us
    gather x1, local copies, waits for them, and re-layouts, body(): velocity = jnp.take(table, slot_index, axis=0, mode='clip')  18.6 us
    pallas_call x2, Pallas kernels, near_field(): pl.pallas_call(functools.partial(pressure_kernel, with_load=with_load), g...  14 us
    dot_general x1, matrix products, body(): fluid = jnp.dot(selector, arrived_load, preferred_element_type=jnp.float32)  3.84 us
    all_to_all x1, starting transfers between devices, body(): lax.all_to_all(packet, 'circ', split_axis=0, concat_axis=0, tiled=True)  3.75 us
    slice x3, local copies, waits for them, and re-layouts, body(): node_rows[:1]  3.51 us
    dot_general x1, matrix products, body(): jnp.dot(gather_slot, load_value, preferred_element_type=jnp.float32)  3.06 us
    ppermute x1, starting transfers between devices, body(): lax.ppermute(node_rows[-1:], 'ax', [(i, (i + 1) % count_ax) for i in rang...  3.02 us
  transfers between devices with their start and end apart: 6, of which 3 were waited for; matrix products, arithmetic and copies ran while one was open for 15% of the time, Pallas kernels for 27%

profile of v14, /device:TPU:0, one launch (start us, length us, event | category | flops | bytes accessed | tf_op | source)
XLA Modules:
  0.0 113.6 jit_solution(13783892498806135571)
XLA Ops:
  7.2 0.0 copy-start.1
  7.2 0.0 all-gather.2.cloned.1.call-start
  7.2 2.0 %slice.82 = bf16[16,64,1,256]{3,1,2,0:T(8,128)(2,1)} slice(bf16[16,64,6,256]{3,1,2,0:T(8,128)(2,1)} %param.11), slice={[0:16], [0:64], [0:1], [0:256]} | slice | bytes 1048576 | tf_op jit(solution)/shard_map/slice | solution.py:206
  9.3 0.0 all-gather.2.cloned.1.call-update
  9.3 1.7 %fusion.34 = (bf16[1,64,6,256]{3,1,2,0:T(8,128)(2,1)}, bf16[1,64,6,256]{3,1,2,0:T(8,128)(2,1)S(1)}) fusion(bf16[16,64,6,256]{3,1,2,0:T(8,128)(2,1)} %param.11), kind=kLoop, calls=%fused_computation.64 | loop fusion | bytes 786432 | tf_op jit(solution)/shard_map/slice | solution.py:212
  11.0 0.1 copy.17
  11.1 0.7 slice.73
  11.9 3.0 %collective-permute-start = (bf16[1,384,256]{2,1,0:T(8,128)(2,1)}, bf16[1,384,256]{2,1,0:T(8,128)(2,1)}, u32[]{:S(2)}, u32[]{:S(2)}) collective-permute-start(bf16[1,384,256]{2,1,0:T(8,128)(2,1)} %slice.73), channel_id=1, source_target_pairs={{0,8},{8,16},{16,24},{24,0},{1,9},{9,17},{17,25},{25,1},{2,10},{10... | collective-permute-start | bytes 589832 | tf_op jit(solution)/shard_map/ppermute | solution.py:211
  14.9 1.0 copy.18
  15.9 0.7 slice.75
  16.7 2.0 %collective-permute-start.1 = (bf16[1,384,256]{2,1,0:T(8,128)(2,1)}, bf16[1,384,256]{2,1,0:T(8,128)(2,1)S(1)}, u32[]{:S(2)}, u32[]{:S(2)}) collective-permute-start(bf16[1,384,256]{2,1,0:T(8,128)(2,1)} %slice.75), channel_id=1, source_target_pairs={{8,0},{16,8},{24,16},{0,24},{9,1},{17,9},{25,17},{1,25},{10,2},{18... | collective-permute-start | bytes 589832 | tf_op jit(solution)/shard_map/ppermute | solution.py:212
  18.7 0.0 copy-done.1
  18.7 1.8 %copy.16 = bf16[16,64,6,256]{3,0,2,1:T(8,128)(2,1)S(1)} copy(bf16[16,64,6,256]{3,1,2,0:T(8,128)(2,1)S(1)} %copy-done.1) | data formatting | bytes 6291456 | tf_op args[0]
  20.5 0.0 copy-start.7
  20.5 0.0 copy-start.6
  20.5 0.0 copy-start.4
  20.5 0.0 copy-start.3
  20.5 1.1 copy.24.rows_ref
  21.6 0.0 copy-start
  21.6 0.0 copy-done.7
  21.7 0.0 copy-done.6
  21.7 0.5 fusion.15
  22.2 0.0 copy-start.5
  22.2 0.1 fusion.17
  22.3 0.0 copy-done.4
  22.3 0.0 copy-done.3
  22.4 2.5 %broadcast_select_fusion.s_ref = bf16[16,64,324]{2,1,0:T(8,128)(2,1)} fusion(bf16[16,64,324]{2,1,0:T(8,128)(2,1)} %param.12, pred[16,324]{1,0:T(8,128)(4,1)S(1)} %fusion.17), kind=kLoop, calls=%fused_computation.21 | loop fusion | flops 331776 | bytes 1332288 | tf_op jit(solution)/shard_map/jit(_where)/select_n | solution.py:228
  24.9 0.0 collective-permute-done.top_ref
  24.9 0.7 fusion.35
  25.6 0.7 collective-permute-done.1.bottom_ref
  26.2 0.0 copy-start.2
  26.2 0.7 pad_maximum_fusion.2
  27.0 2.2 %collective-permute-start.2 = (bf16[18,6,256]{2,1,0:T(8,128)(2,1)}, bf16[18,6,256]{2,1,0:T(8,128)(2,1)S(1)}, u32[]{:S(2)}, u32[]{:S(2)}) collective-permute-start(bf16[18,6,256]{2,1,0:T(8,128)(2,1)} %pad_maximum_fusion.2), channel_id=1, source_target_pairs={{1,0},{2,1},{3,2},{4,3},{5,4},{6,5},{7,6},{0,7},{9,8},{10,9},{11,1... | collective-permute-start | bytes 165896 | tf_op jit(solution)/shard_map/ppermute | solution.py:220
  29.1 0.7 pad_maximum_fusion.3
  29.8 0.0 collective-permute-start.3
  29.8 1.8 %fusion.10 = bf16[2,2560]{1,0:T(2,128)(2,1)S(1)} fusion(s32[1024]{0:T(1024)S(1)} %convert_add_fusion, bf16[1,1024]{1,0:T(2,128)(2,1)S(1)} %stack.13, bf16[1,1024]{1,0:T(2,128)(2,1)S(1)} %stack.12), kind=kOutput, calls=%fused_computation.13 | convolution fusion | flops 13120512 | bytes 18432 | tf_op jit(solution)/shard_map/dot_general | solution.py:253
  31.6 0.0 copy-done
  31.6 0.0 copy-done.5
  31.6 1.0 copy.22.area_ref
  32.6 0.1 reshape.165
  32.7 0.1 reshape.166
  32.9 0.1 pad.12.clone
  32.9 0.0 collective-permute-done.2
  32.9 1.7 %collective-permute-done.3 = bf16[18,6,256]{2,1,0:T(8,128)(2,1)S(1)} collective-permute-done((bf16[18,6,256]{2,1,0:T(8,128)(2,1)}, bf16[18,6,256]{2,1,0:T(8,128)(2,1)S(1)}, u32[]{:S(2)}, u32[]{:S(2)}) %collective-permute-start.3) | collective-permute-done | bytes 55328 | tf_op jit(solution)/shard_map/ppermute | solution.py:219
  34.7 1.2 %pad_maximum_fusion.1.halo_ref = bf16[18,128,256]{2,1,0:T(8,128)(2,1)} fusion(bf16[18,6,256]{2,1,0:T(8,128)(2,1)S(1)} %collective-permute-done.3, bf16[18,6,256]{2,1,0:T(8,128)(2,1)S(1)} %collective-permute-done.2, bf16[128]{0:T(256)(128)(2,1)S(1)} %pad.12.clone), kind=kLoop, calls=%fused_computation.16 | loop fusion | flops 3538944 | bytes 1290496 | tf_op jit(solution)/shard_map/concatenate | solution.py:222
  35.9 0.0 copy-done.2
  35.9 12.1 %shard_map.104.rest_0_ = f32[16,384,256]{2,1,0:T(8,128)} custom-call(bf16[16,64,324]{2,1,0:T(8,128)(2,1)} %broadcast_select_fusion.s_ref, bf16[16,384,256]{2,1,0:T(8,128)(2,1)} %copy-done, bf16[1,384,256]{2,1,0:T(8,128)(2,1)} %collective-permute-done.top_ref, bf16[1,384,256]{2,1,0:T(8,128)(2,1)} %copy-done.2, bf16[18,128,256]{2,1,0:T(8,128)(2,1)} %pad_maximum_fusion.1.halo_ref), custom_call_target="tpu_custom_call" | custom-call | tf_op jit(solution)/shard_map/pallas_call | solution.py:173
  48.0 2.0 %all-gather.2.cloned.1.call-done = bf16[8192,256]{1,0:T(8,128)(2,1)} async-done(((bf16[1024,256]{1,0:T(8,128)(2,1)}), bf16[8192,256]{1,0:T(8,128)(2,1)}) %all-gather.2.cloned.1.call-update) | async-done | bytes 4194320 | tf_op jit(solution)/shard_map/all_gather | solution.py:207
  49.9 18.6 %gather_fusion = bf16[4096,256]{1,0:T(8,128)(2,1)} fusion(bf16[8192,256]{1,0:T(8,128)(2,1)} %all-gather.2.cloned.1.call-done, s32[4096]{0:T(1024)S(1)} %add_clamp_fusion), kind=kCustom, calls=%fused_computation | custom fusion | bytes 4210688 | tf_op jit(solution)/shard_map/jit(_take)/gather | solution.py:234
  68.5 7.1 %shard_map.105 = (f32[2,1024,256]{2,1,0:T(8,128)}, bf16[1024,256]{1,0:T(8,128)(2,1)}) custom-call(s32[4,12]{1,0:T(4,128)} %near_ref.3, bf16[4,12,2,256,256]{4,3,2,1,0:T(8,128)(2,1)} %kern_ref.3, bf16[16,256,256]{2,1,0:T(8,128)(2,1)} %bitcast.22, f32[1024,1]{1,0:T(8,128)} %copy.22.area_ref), custom_call_target="tpu_custom_call" | custom-call | tf_op jit(solution)/shard_map/pallas_call | solution.py:77
  75.6 3.1 %fusion.9 = bf16[2560,256]{1,0:T(8,128)(2,1)S(1)} fusion(bf16[1024,256]{1,0:T(8,128)(2,1)} %get-tuple-element.22, s32[1024]{0:T(1024)S(1)} %convert_add_fusion), kind=kOutput, calls=%fused_computation.12 | convolution fusion | flops 1345454080 | bytes 1839104 | tf_op jit(solution)/shard_map/dot_general | solution.py:247
  78.6 1.2 %pad_maximum_fusion = bf16[8,323,256]{2,1,0:T(8,128)(2,1)} fusion(bf16[8,3,256]{2,1,0:T(4,128)(2,1)S(1)} %reshape.167, bf16[8,320,256]{2,1,0:T(8,128)(2,1)S(1)} %bitcast.27), kind=kLoop, calls=%fused_computation.15 | loop fusion | flops 2646016 | bytes 2646016 | tf_op jit(solution)/shard_map/concatenate | solution.py:262
  79.8 3.8 %all-to-all-start = ((bf16[8,323,256]{2,1,0:T(8,128)(2,1)}), bf16[8,323,256]{2,1,0:T(8,128)(2,1)S(1)}, u32[]{:S(2)}, u32[]{:S(2)}) async-start(bf16[8,323,256]{2,1,0:T(8,128)(2,1)} %pad_maximum_fusion), calls=%async_computation | async-start | bytes 2686976 | tf_op jit(solution)/shard_map/all_to_all | solution.py:264
  83.6 6.9 %shard_map.107 = f32[2,1024,256]{2,1,0:T(8,128)} custom-call(s32[4,12]{1,0:T(4,128)} %near_ref.3, bf16[4,12,2,256,256]{4,3,2,1,0:T(8,128)(2,1)} %kern_ref.3, bf16[16,256,256]{2,1,0:T(8,128)(2,1)} %bitcast.23, f32[1024,1]{1,0:T(8,128)} %copy.22.area_ref, f32[2,1024,256]{2,1,0:T(8,128)} %get-tuple-element.27.rest_0_), custom_call_target="tpu_custom_call", output_to_operand_aliasing={{}: (4, {})} | custom-call | tf_op jit(solution)/shard_map/pallas_call | solution.py:77
  90.5 12.1 %shard_map.106 = f32[16,384,256]{2,1,0:T(8,128)} custom-call(bf16[16,64,324]{2,1,0:T(8,128)(2,1)} %broadcast_select_fusion.s_ref, bf16[16,384,256]{2,1,0:T(8,128)(2,1)} %copy-done, bf16[1,384,256]{2,1,0:T(8,128)(2,1)} %collective-permute-done.top_ref, bf16[1,384,256]{2,1,0:T(8,128)(2,1)} %copy-done.2, ...), custom_call_target="tpu_custom_call", output_to_operand_aliasing={{}: (5, {})} | custom-call | tf_op jit(solution)/shard_map/pallas_call | solution.py:173
  102.6 0.0 all-to-all-done
  102.6 0.1 reshape.171
  102.7 0.1 fusion.20
  102.8 0.1 convert_element_type.42
  102.8 0.1 slice.102
  102.9 3.8 %fusion.16 = f32[16,384,256]{2,1,0:T(8,128)} fusion(f32[16,384,256]{2,1,0:T(8,128)} %shard_map.106, bf16[2560,256,1]{1,0,2:T(8,128)(2,1)S(1)} %bitcast.26, s32[16,64]{1,0:T(8,128)S(1)} %multiply_add_fusion, s32[2560]{0:T(1024)S(1)} %convert_element_type.42), kind=kOutput, calls=%fused_computation.20 | convolution fusion | flops 1345323008 | bytes 3422208 | tf_op jit(solution)/shard_map/dot_general | solution.py:280
  (18 shorter events, 0.2 us)
Async XLA Ops:
  7.2 11.6 %copy-start.1 = (bf16[16,64,6,256]{3,1,2,0:T(8,128)(2,1)S(1)}, bf16[16,64,6,256]{3,1,2,0:T(8,128)(2,1)}, u32[]{:S(2)}) copy-start(bf16[16,64,6,256]{3,1,2,0:T(8,128)(2,1)} %param.11) | copy-start | bytes 9437188
  7.2 42.8 %all-gather.2.cloned.1.call-start = ((), (), s32[]{:S(2)}) async-start(), calls=%async_computation.1 | async-start | bytes 4718592 | tf_op jit(solution)/shard_map/all_gather | solution.py:207
  11.9 13.0 %collective-permute-start = (bf16[1,384,256]{2,1,0:T(8,128)(2,1)}, bf16[1,384,256]{2,1,0:T(8,128)(2,1)}, u32[]{:S(2)}, u32[]{:S(2)}) collective-permute-start(bf16[1,384,256]{2,1,0:T(8,128)(2,1)} %slice.73), channel_id=1, source_target_pairs={{0,8},{8,16},{16,24},{24,0},{1,9},{9,17},{17,25},{25,1},{2,10},{10... | collective-permute-start | bytes 589832 | tf_op jit(solution)/shard_map/ppermute | solution.py:211
  16.7 9.6 %collective-permute-start.1 = (bf16[1,384,256]{2,1,0:T(8,128)(2,1)}, bf16[1,384,256]{2,1,0:T(8,128)(2,1)S(1)}, u32[]{:S(2)}, u32[]{:S(2)}) collective-permute-start(bf16[1,384,256]{2,1,0:T(8,128)(2,1)} %slice.75), channel_id=1, source_target_pairs={{8,0},{16,8},{24,16},{0,24},{9,1},{17,9},{25,17},{1,25},{10,2},{18... | collective-permute-start | bytes 589832 | tf_op jit(solution)/shard_map/ppermute | solution.py:212
  20.5 1.2 %copy-start.7 = (s32[1024]{0:T(1024)S(1)}, s32[1024]{0:T(1024)}, u32[]{:S(2)}) copy-start(s32[1024]{0:T(1024)} %param.19) | copy-start | bytes 12292
  20.5 1.2 %copy-start.6 = (s32[1024,1]{0,1:T(1,128)S(1)}, s32[1024,1]{0,1:T(1,128)}, u32[]{:S(2)}) copy-start(s32[1024,1]{0,1:T(1,128)} %param.18) | copy-start | bytes 12292
  20.5 1.8 %copy-start.4 = (s32[4096,1]{0,1:T(1,128)S(1)}, s32[4096,1]{0,1:T(1,128)}, u32[]{:S(2)}) copy-start(s32[4096,1]{0,1:T(1,128)} %param.16) | copy-start | bytes 49156
  20.5 1.8 %copy-start.3 = (s32[4096]{0:T(1024)S(1)}, s32[4096]{0:T(1024)}, u32[]{:S(2)}) copy-start(s32[4096]{0:T(1024)} %param.17) | copy-start | bytes 49156
  21.6 10.0 %copy-start = (bf16[16,384,256]{2,1,0:T(8,128)(2,1)}, bf16[16,384,256]{2,1,0:T(8,128)(2,1)S(1)}, u32[]{:S(2)}) copy-start(bf16[16,384,256]{2,1,0:T(8,128)(2,1)S(1)} %copy.24.rows_ref) | copy-start | bytes 9437188
  22.2 9.4 %copy-start.5 = (f32[1024]{0:T(1024)S(1)}, f32[1024]{0:T(1024)}, u32[]{:S(2)}) copy-start(f32[1024]{0:T(1024)} %param.14) | copy-start | bytes 12292
  26.2 9.7 %copy-start.2 = (bf16[1,384,256]{2,1,0:T(8,128)(2,1)}, bf16[1,384,256]{2,1,0:T(8,128)(2,1)S(1)}, u32[]{:S(2)}) copy-start(bf16[1,384,256]{2,1,0:T(8,128)(2,1)S(1)} %collective-permute-done.1.bottom_ref) | copy-start | bytes 589828
  27.0 6.0 %collective-permute-start.2 = (bf16[18,6,256]{2,1,0:T(8,128)(2,1)}, bf16[18,6,256]{2,1,0:T(8,128)(2,1)S(1)}, u32[]{:S(2)}, u32[]{:S(2)}) collective-permute-start(bf16[18,6,256]{2,1,0:T(8,128)(2,1)} %pad_maximum_fusion.2), channel_id=1, source_target_pairs={{1,0},{2,1},{3,2},{4,3},{5,4},{6,5},{7,6},{0,7},{9,8},{10,9},{11,1... | collective-permute-start | bytes 165896 | tf_op jit(solution)/shard_map/ppermute | solution.py:220
  29.8 4.9 %collective-permute-start.3 = (bf16[18,6,256]{2,1,0:T(8,128)(2,1)}, bf16[18,6,256]{2,1,0:T(8,128)(2,1)S(1)}, u32[]{:S(2)}, u32[]{:S(2)}) collective-permute-start(bf16[18,6,256]{2,1,0:T(8,128)(2,1)} %pad_maximum_fusion.3), channel_id=1, source_target_pairs={{0,1},{1,2},{2,3},{3,4},{4,5},{5,6},{6,7},{7,0},{8,9},{9,10},{10,1... | collective-permute-start | bytes 165896 | tf_op jit(solution)/shard_map/ppermute | solution.py:219
  79.8 22.8 %all-to-all-start = ((bf16[8,323,256]{2,1,0:T(8,128)(2,1)}), bf16[8,323,256]{2,1,0:T(8,128)(2,1)S(1)}, u32[]{:S(2)}, u32[]{:S(2)}) async-start(bf16[8,323,256]{2,1,0:T(8,128)(2,1)} %pad_maximum_fusion), calls=%async_computation | async-start | bytes 2686976 | tf_op jit(solution)/shard_map/all_to_all | solution.py:264
Sparse Core Ops, SparseCore 0:
  10.5 39.4 all-gather.1

commit v15 on v14

--- a/solution.py
+++ b/solution.py
@@ -226,7 +226,7 @@
         global_row[:, None] + lane_step[None, :] < axial_total
     )
     blocks = jnp.where(inside[:, None, :], stiffness, jnp.zeros_like(stiffness))
-    half = axial_rows // 2
+    half = (axial_rows * 9) // 16
     force = banded_force(blocks, node_rows, top, bottom, halo, degrees, 0, half)
 
     force, table = lax.optimization_barrier((force, table))

time: 114 us -> 113 us (level)
  transfers between devices with their start and end apart: 6 -> 6, of which waited for: 3 -> 4; matrix products, arithmetic and copies ran while one was open for 15% -> 15% of each run, Pallas kernels for 27% -> 28%
where the time goes in v15:
time: 113 us
  Pallas kernels  38.1 us (34%)
  local copies, waits for them, and re-layouts  30.2 us (27%)
  between operations  14.3 us (13%)
  starting transfers between devices  11 us (10%)
  matrix products  9.18 us (8%)
  other arithmetic  6.44 us (6%)
  waiting for transfers between devices  3.71 us (3%)
    pallas_call x2, Pallas kernels, banded_force(): pl.pallas_call(functools.partial(stiff_kernel, degrees=degrees, first=fir...  24.1 us
    gather x1, local copies, waits for them, and re-layouts, body(): velocity = jnp.take(table, slot_index, axis=0, mode='clip')  18.6 us
    pallas_call x2, Pallas kernels, near_field(): pl.pallas_call(functools.partial(pressure_kernel, with_load=with_load), g...  14 us
    dot_general x1, matrix products, body(): fluid = jnp.dot(selector, arrived_load, preferred_element_type=jnp.float32)  3.84 us
    all_to_all x1, starting transfers between devices, body(): lax.all_to_all(packet, 'circ', split_axis=0, concat_axis=0, tiled=True)  3.75 us
    slice x3, local copies, waits for them, and re-layouts, body(): node_rows[:1]  3.51 us
    dot_general x1, matrix products, body(): jnp.dot(gather_slot, load_value, preferred_element_type=jnp.float32)  3.06 us
    ppermute x1, starting transfers between devices, body(): lax.ppermute(node_rows[-1:], 'ax', [(i, (i + 1) % count_ax) for i in rang...  3.02 us
  transfers between devices with their start and end apart: 6, of which 4 were waited for; matrix products, arithmetic and copies ran while one was open for 15% of the time, Pallas kernels for 28%

profile of v15, /device:TPU:0, one launch (start us, length us, event | category | flops | bytes accessed | tf_op | source)
XLA Modules:
  0.0 112.9 jit_solution(18241579023981481640)
XLA Ops:
  7.2 0.0 copy-start.1
  7.2 0.0 all-gather.2.cloned.1.call-start
  7.2 2.0 %slice.82 = bf16[16,64,1,256]{3,1,2,0:T(8,128)(2,1)} slice(bf16[16,64,6,256]{3,1,2,0:T(8,128)(2,1)} %param.11), slice={[0:16], [0:64], [0:1], [0:256]} | slice | bytes 1048576 | tf_op jit(solution)/shard_map/slice | solution.py:206
  9.3 0.0 all-gather.2.cloned.1.call-update
  9.3 1.7 %fusion.34 = (bf16[1,64,6,256]{3,1,2,0:T(8,128)(2,1)}, bf16[1,64,6,256]{3,1,2,0:T(8,128)(2,1)S(1)}) fusion(bf16[16,64,6,256]{3,1,2,0:T(8,128)(2,1)} %param.11), kind=kLoop, calls=%fused_computation.64 | loop fusion | bytes 786432 | tf_op jit(solution)/shard_map/slice | solution.py:212
  11.0 0.1 copy.17
  11.1 0.7 slice.73
  11.9 3.0 %collective-permute-start = (bf16[1,384,256]{2,1,0:T(8,128)(2,1)}, bf16[1,384,256]{2,1,0:T(8,128)(2,1)}, u32[]{:S(2)}, u32[]{:S(2)}) collective-permute-start(bf16[1,384,256]{2,1,0:T(8,128)(2,1)} %slice.73), channel_id=1, source_target_pairs={{0,8},{8,16},{16,24},{24,0},{1,9},{9,17},{17,25},{25,1},{2,10},{10... | collective-permute-start | bytes 589832 | tf_op jit(solution)/shard_map/ppermute | solution.py:211
  14.9 1.0 copy.18
  15.9 0.7 slice.75
  16.7 2.0 %collective-permute-start.1 = (bf16[1,384,256]{2,1,0:T(8,128)(2,1)}, bf16[1,384,256]{2,1,0:T(8,128)(2,1)S(1)}, u32[]{:S(2)}, u32[]{:S(2)}) collective-permute-start(bf16[1,384,256]{2,1,0:T(8,128)(2,1)} %slice.75), channel_id=1, source_target_pairs={{8,0},{16,8},{24,16},{0,24},{9,1},{17,9},{25,17},{1,25},{10,2},{18... | collective-permute-start | bytes 589832 | tf_op jit(solution)/shard_map/ppermute | solution.py:212
  18.7 0.0 copy-done.1
  18.7 1.8 %copy.16 = bf16[16,64,6,256]{3,0,2,1:T(8,128)(2,1)S(1)} copy(bf16[16,64,6,256]{3,1,2,0:T(8,128)(2,1)S(1)} %copy-done.1) | data formatting | bytes 6291456 | tf_op args[0]
  20.5 0.0 copy-start.7
  20.5 0.0 copy-start.6
  20.5 0.0 copy-start.4
  20.5 0.0 copy-start.3
  20.5 1.1 copy.24.rows_ref
  21.6 0.0 copy-start
  21.6 0.0 copy-done.7
  21.7 0.0 copy-done.6
  21.7 0.5 fusion.15
  22.2 0.0 copy-start.5
  22.2 0.1 fusion.17
  22.3 0.0 copy-done.4
  22.3 0.0 copy-done.3
  22.4 2.5 %broadcast_select_fusion.s_ref = bf16[16,64,324]{2,1,0:T(8,128)(2,1)} fusion(bf16[16,64,324]{2,1,0:T(8,128)(2,1)} %param.12, pred[16,324]{1,0:T(8,128)(4,1)S(1)} %fusion.17), kind=kLoop, calls=%fused_computation.21 | loop fusion | flops 331776 | bytes 1332288 | tf_op jit(solution)/shard_map/jit(_where)/select_n | solution.py:228
  24.9 0.0 collective-permute-done.top_ref
  24.9 0.7 fusion.35
  25.6 0.7 collective-permute-done.1.bottom_ref
  26.2 0.0 copy-start.2
  26.2 0.7 pad_maximum_fusion.2
  27.0 2.2 %collective-permute-start.2 = (bf16[18,6,256]{2,1,0:T(8,128)(2,1)}, bf16[18,6,256]{2,1,0:T(8,128)(2,1)S(1)}, u32[]{:S(2)}, u32[]{:S(2)}) collective-permute-start(bf16[18,6,256]{2,1,0:T(8,128)(2,1)} %pad_maximum_fusion.2), channel_id=1, source_target_pairs={{1,0},{2,1},{3,2},{4,3},{5,4},{6,5},{7,6},{0,7},{9,8},{10,9},{11,1... | collective-permute-start | bytes 165896 | tf_op jit(solution)/shard_map/ppermute | solution.py:220
  29.1 0.7 pad_maximum_fusion.3
  29.8 0.0 collective-permute-start.3
  29.8 1.8 %fusion.10 = bf16[2,2560]{1,0:T(2,128)(2,1)S(1)} fusion(s32[1024]{0:T(1024)S(1)} %convert_add_fusion, bf16[1,1024]{1,0:T(2,128)(2,1)S(1)} %stack.13, bf16[1,1024]{1,0:T(2,128)(2,1)S(1)} %stack.12), kind=kOutput, calls=%fused_computation.13 | convolution fusion | flops 13120512 | bytes 18432 | tf_op jit(solution)/shard_map/dot_general | solution.py:253
  31.6 0.0 copy-done
  31.6 0.0 copy-done.5
  31.6 1.0 copy.22.area_ref
  32.6 0.1 reshape.165
  32.7 0.1 reshape.166
  32.9 0.1 pad.12.clone
  32.9 0.0 collective-permute-done.2
  32.9 1.7 %collective-permute-done.3 = bf16[18,6,256]{2,1,0:T(8,128)(2,1)S(1)} collective-permute-done((bf16[18,6,256]{2,1,0:T(8,128)(2,1)}, bf16[18,6,256]{2,1,0:T(8,128)(2,1)S(1)}, u32[]{:S(2)}, u32[]{:S(2)}) %collective-permute-start.3) | collective-permute-done | bytes 55328 | tf_op jit(solution)/shard_map/ppermute | solution.py:219
  34.7 1.2 %pad_maximum_fusion.1.halo_ref = bf16[18,128,256]{2,1,0:T(8,128)(2,1)} fusion(bf16[18,6,256]{2,1,0:T(8,128)(2,1)S(1)} %collective-permute-done.3, bf16[18,6,256]{2,1,0:T(8,128)(2,1)S(1)} %collective-permute-done.2, bf16[128]{0:T(256)(128)(2,1)S(1)} %pad.12.clone), kind=kLoop, calls=%fused_computation.16 | loop fusion | flops 3538944 | bytes 1290496 | tf_op jit(solution)/shard_map/concatenate | solution.py:222
  35.9 0.0 copy-done.2
  35.9 13.2 %shard_map.104.rest_0_ = f32[16,384,256]{2,1,0:T(8,128)} custom-call(bf16[16,64,324]{2,1,0:T(8,128)(2,1)} %broadcast_select_fusion.s_ref, bf16[16,384,256]{2,1,0:T(8,128)(2,1)} %copy-done, bf16[1,384,256]{2,1,0:T(8,128)(2,1)} %collective-permute-done.top_ref, bf16[1,384,256]{2,1,0:T(8,128)(2,1)} %copy-done.2, bf16[18,128,256]{2,1,0:T(8,128)(2,1)} %pad_maximum_fusion.1.halo_ref), custom_call_target="tpu_custom_call" | custom-call | tf_op jit(solution)/shard_map/pallas_call | solution.py:173
  49.1 0.9 all-gather.2.cloned.1.call-done
  49.9 18.6 %gather_fusion = bf16[4096,256]{1,0:T(8,128)(2,1)} fusion(bf16[8192,256]{1,0:T(8,128)(2,1)} %all-gather.2.cloned.1.call-done, s32[4096]{0:T(1024)S(1)} %add_clamp_fusion), kind=kCustom, calls=%fused_computation | custom fusion | bytes 4210688 | tf_op jit(solution)/shard_map/jit(_take)/gather | solution.py:234
  68.5 7.1 %shard_map.105 = (f32[2,1024,256]{2,1,0:T(8,128)}, bf16[1024,256]{1,0:T(8,128)(2,1)}) custom-call(s32[4,12]{1,0:T(4,128)} %near_ref.3, bf16[4,12,2,256,256]{4,3,2,1,0:T(8,128)(2,1)} %kern_ref.3, bf16[16,256,256]{2,1,0:T(8,128)(2,1)} %bitcast.22, f32[1024,1]{1,0:T(8,128)} %copy.22.area_ref), custom_call_target="tpu_custom_call" | custom-call | tf_op jit(solution)/shard_map/pallas_call | solution.py:77
  75.6 3.1 %fusion.9 = bf16[2560,256]{1,0:T(8,128)(2,1)S(1)} fusion(bf16[1024,256]{1,0:T(8,128)(2,1)} %get-tuple-element.22, s32[1024]{0:T(1024)S(1)} %convert_add_fusion), kind=kOutput, calls=%fused_computation.12 | convolution fusion | flops 1345454080 | bytes 1839104 | tf_op jit(solution)/shard_map/dot_general | solution.py:247
  78.6 1.2 %pad_maximum_fusion = bf16[8,323,256]{2,1,0:T(8,128)(2,1)} fusion(bf16[8,3,256]{2,1,0:T(4,128)(2,1)S(1)} %reshape.167, bf16[8,320,256]{2,1,0:T(8,128)(2,1)S(1)} %bitcast.27), kind=kLoop, calls=%fused_computation.15 | loop fusion | flops 2646016 | bytes 2646016 | tf_op jit(solution)/shard_map/concatenate | solution.py:262
  79.8 3.8 %all-to-all-start = ((bf16[8,323,256]{2,1,0:T(8,128)(2,1)}), bf16[8,323,256]{2,1,0:T(8,128)(2,1)S(1)}, u32[]{:S(2)}, u32[]{:S(2)}) async-start(bf16[8,323,256]{2,1,0:T(8,128)(2,1)} %pad_maximum_fusion), calls=%async_computation | async-start | bytes 2686976 | tf_op jit(solution)/shard_map/all_to_all | solution.py:264
  83.6 6.9 %shard_map.107 = f32[2,1024,256]{2,1,0:T(8,128)} custom-call(s32[4,12]{1,0:T(4,128)} %near_ref.3, bf16[4,12,2,256,256]{4,3,2,1,0:T(8,128)(2,1)} %kern_ref.3, bf16[16,256,256]{2,1,0:T(8,128)(2,1)} %bitcast.23, f32[1024,1]{1,0:T(8,128)} %copy.22.area_ref, f32[2,1024,256]{2,1,0:T(8,128)} %get-tuple-element.27.rest_0_), custom_call_target="tpu_custom_call", output_to_operand_aliasing={{}: (4, {})} | custom-call | tf_op jit(solution)/shard_map/pallas_call | solution.py:77
  90.5 11.0 %shard_map.106 = f32[16,384,256]{2,1,0:T(8,128)} custom-call(bf16[16,64,324]{2,1,0:T(8,128)(2,1)} %broadcast_select_fusion.s_ref, bf16[16,384,256]{2,1,0:T(8,128)(2,1)} %copy-done, bf16[1,384,256]{2,1,0:T(8,128)(2,1)} %collective-permute-done.top_ref, bf16[1,384,256]{2,1,0:T(8,128)(2,1)} %copy-done.2, ...), custom_call_target="tpu_custom_call", output_to_operand_aliasing={{}: (5, {})} | custom-call | tf_op jit(solution)/shard_map/pallas_call | solution.py:173
  101.5 0.4 all-to-all-done
  101.9 0.1 reshape.171
  102.0 0.1 fusion.20
  102.1 0.1 convert_element_type.42
  102.1 0.1 slice.102
  102.2 3.8 %fusion.16 = f32[16,384,256]{2,1,0:T(8,128)} fusion(f32[16,384,256]{2,1,0:T(8,128)} %shard_map.106, bf16[2560,256,1]{1,0,2:T(8,128)(2,1)S(1)} %bitcast.26, s32[16,64]{1,0:T(8,128)S(1)} %multiply_add_fusion, s32[2560]{0:T(1024)S(1)} %convert_element_type.42), kind=kOutput, calls=%fused_computation.20 | convolution fusion | flops 1345323008 | bytes 3422208 | tf_op jit(solution)/shard_map/dot_general | solution.py:280
  (18 shorter events, 0.2 us)
Async XLA Ops:
  7.2 11.6 %copy-start.1 = (bf16[16,64,6,256]{3,1,2,0:T(8,128)(2,1)S(1)}, bf16[16,64,6,256]{3,1,2,0:T(8,128)(2,1)}, u32[]{:S(2)}) copy-start(bf16[16,64,6,256]{3,1,2,0:T(8,128)(2,1)} %param.11) | copy-start | bytes 9437188
  7.2 42.8 %all-gather.2.cloned.1.call-start = ((), (), s32[]{:S(2)}) async-start(), calls=%async_computation.1 | async-start | bytes 4718592 | tf_op jit(solution)/shard_map/all_gather | solution.py:207
  11.9 13.0 %collective-permute-start = (bf16[1,384,256]{2,1,0:T(8,128)(2,1)}, bf16[1,384,256]{2,1,0:T(8,128)(2,1)}, u32[]{:S(2)}, u32[]{:S(2)}) collective-permute-start(bf16[1,384,256]{2,1,0:T(8,128)(2,1)} %slice.73), channel_id=1, source_target_pairs={{0,8},{8,16},{16,24},{24,0},{1,9},{9,17},{17,25},{25,1},{2,10},{10... | collective-permute-start | bytes 589832 | tf_op jit(solution)/shard_map/ppermute | solution.py:211
  16.7 9.6 %collective-permute-start.1 = (bf16[1,384,256]{2,1,0:T(8,128)(2,1)}, bf16[1,384,256]{2,1,0:T(8,128)(2,1)S(1)}, u32[]{:S(2)}, u32[]{:S(2)}) collective-permute-start(bf16[1,384,256]{2,1,0:T(8,128)(2,1)} %slice.75), channel_id=1, source_target_pairs={{8,0},{16,8},{24,16},{0,24},{9,1},{17,9},{25,17},{1,25},{10,2},{18... | collective-permute-start | bytes 589832 | tf_op jit(solution)/shard_map/ppermute | solution.py:212
  20.5 1.2 %copy-start.7 = (s32[1024]{0:T(1024)S(1)}, s32[1024]{0:T(1024)}, u32[]{:S(2)}) copy-start(s32[1024]{0:T(1024)} %param.19) | copy-start | bytes 12292
  20.5 1.2 %copy-start.6 = (s32[1024,1]{0,1:T(1,128)S(1)}, s32[1024,1]{0,1:T(1,128)}, u32[]{:S(2)}) copy-start(s32[1024,1]{0,1:T(1,128)} %param.18) | copy-start | bytes 12292
  20.5 1.8 %copy-start.4 = (s32[4096,1]{0,1:T(1,128)S(1)}, s32[4096,1]{0,1:T(1,128)}, u32[]{:S(2)}) copy-start(s32[4096,1]{0,1:T(1,128)} %param.16) | copy-start | bytes 49156
  20.5 1.8 %copy-start.3 = (s32[4096]{0:T(1024)S(1)}, s32[4096]{0:T(1024)}, u32[]{:S(2)}) copy-start(s32[4096]{0:T(1024)} %param.17) | copy-start | bytes 49156
  21.6 10.0 %copy-start = (bf16[16,384,256]{2,1,0:T(8,128)(2,1)}, bf16[16,384,256]{2,1,0:T(8,128)(2,1)S(1)}, u32[]{:S(2)}) copy-start(bf16[16,384,256]{2,1,0:T(8,128)(2,1)S(1)} %copy.24.rows_ref) | copy-start | bytes 9437188
  22.2 9.4 %copy-start.5 = (f32[1024]{0:T(1024)S(1)}, f32[1024]{0:T(1024)}, u32[]{:S(2)}) copy-start(f32[1024]{0:T(1024)} %param.14) | copy-start | bytes 12292
  26.2 9.7 %copy-start.2 = (bf16[1,384,256]{2,1,0:T(8,128)(2,1)}, bf16[1,384,256]{2,1,0:T(8,128)(2,1)S(1)}, u32[]{:S(2)}) copy-start(bf16[1,384,256]{2,1,0:T(8,128)(2,1)S(1)} %collective-permute-done.1.bottom_ref) | copy-start | bytes 589828
  27.0 6.0 %collective-permute-start.2 = (bf16[18,6,256]{2,1,0:T(8,128)(2,1)}, bf16[18,6,256]{2,1,0:T(8,128)(2,1)S(1)}, u32[]{:S(2)}, u32[]{:S(2)}) collective-permute-start(bf16[18,6,256]{2,1,0:T(8,128)(2,1)} %pad_maximum_fusion.2), channel_id=1, source_target_pairs={{1,0},{2,1},{3,2},{4,3},{5,4},{6,5},{7,6},{0,7},{9,8},{10,9},{11,1... | collective-permute-start | bytes 165896 | tf_op jit(solution)/shard_map/ppermute | solution.py:220
  29.8 4.9 %collective-permute-start.3 = (bf16[18,6,256]{2,1,0:T(8,128)(2,1)}, bf16[18,6,256]{2,1,0:T(8,128)(2,1)S(1)}, u32[]{:S(2)}, u32[]{:S(2)}) collective-permute-start(bf16[18,6,256]{2,1,0:T(8,128)(2,1)} %pad_maximum_fusion.3), channel_id=1, source_target_pairs={{0,1},{1,2},{2,3},{3,4},{4,5},{5,6},{6,7},{7,0},{8,9},{9,10},{10,1... | collective-permute-start | bytes 165896 | tf_op jit(solution)/shard_map/ppermute | solution.py:219
  79.8 22.1 %all-to-all-start = ((bf16[8,323,256]{2,1,0:T(8,128)(2,1)}), bf16[8,323,256]{2,1,0:T(8,128)(2,1)S(1)}, u32[]{:S(2)}, u32[]{:S(2)}) async-start(bf16[8,323,256]{2,1,0:T(8,128)(2,1)} %pad_maximum_fusion), calls=%async_computation | async-start | bytes 2686976 | tf_op jit(solution)/shard_map/all_to_all | solution.py:264
Sparse Core Ops, SparseCore 0:
  10.5 39.4 all-gather.1

commit v16 on v14

--- a/solution.py
+++ b/solution.py
@@ -231,7 +231,7 @@
 
     force, table = lax.optimization_barrier((force, table))
     slot_index = source_owner[:, 0] * node_count + source_node
-    velocity = jnp.take(table, slot_index, axis=0, mode="clip")
+    velocity = table.at[slot_index].get(mode="promise_in_bounds")
 
     panel_size = kernel.shape[3]
     source_cells = velocity.reshape(-1, panel_size, vectors)

time: 114 us -> 114 us (level)
  no operation moved by 1% of the time
where the time goes in v16:
time: 114 us
  Pallas kernels  38.1 us (33%)
  local copies, waits for them, and re-layouts  30.2 us (26%)
  between operations  14.3 us (13%)
  starting transfers between devices  11 us (10%)
  matrix products  9.18 us (8%)
  other arithmetic  6.44 us (6%)
  waiting for transfers between devices  4.4 us (4%)
    pallas_call x2, Pallas kernels, banded_force(): pl.pallas_call(functools.partial(stiff_kernel, degrees=degrees, first=fir...  24.1 us
    gather x1, local copies, waits for them, and re-layouts, body(): velocity = table.at[slot_index].get(mode='promise_in_bounds')  18.6 us
    pallas_call x2, Pallas kernels, near_field(): pl.pallas_call(functools.partial(pressure_kernel, with_load=with_load), g...  14 us
    dot_general x1, matrix products, body(): fluid = jnp.dot(selector, arrived_load, preferred_element_type=jnp.float32)  3.84 us
    all_to_all x1, starting transfers between devices, body(): lax.all_to_all(packet, 'circ', split_axis=0, concat_axis=0, tiled=True)  3.75 us
    slice x3, local copies, waits for them, and re-layouts, body(): node_rows[:1]  3.51 us
    dot_general x1, matrix products, body(): jnp.dot(gather_slot, load_value, preferred_element_type=jnp.float32)  3.06 us
    ppermute x1, starting transfers between devices, body(): lax.ppermute(node_rows[-1:], 'ax', [(i, (i + 1) % count_ax) for i in rang...  3.02 us
  transfers between devices with their start and end apart: 6, of which 3 were waited for; matrix products, arithmetic and copies ran while one was open for 15% of the time, Pallas kernels for 27%

profile of v16, /device:TPU:0, one launch (start us, length us, event | category | flops | bytes accessed | tf_op | source)
XLA Modules:
  0.0 113.6 jit_solution(4358799246862640832)
XLA Ops:
  7.2 0.0 copy-start.1
  7.2 0.0 all-gather.2.cloned.1.call-start
  7.2 2.0 %slice.82 = bf16[16,64,1,256]{3,1,2,0:T(8,128)(2,1)} slice(bf16[16,64,6,256]{3,1,2,0:T(8,128)(2,1)} %param.11), slice={[0:16], [0:64], [0:1], [0:256]} | slice | bytes 1048576 | tf_op jit(solution)/shard_map/slice | solution.py:206
  9.3 0.0 all-gather.2.cloned.1.call-update
  9.3 1.7 %fusion.35 = (bf16[1,64,6,256]{3,1,2,0:T(8,128)(2,1)}, bf16[1,64,6,256]{3,1,2,0:T(8,128)(2,1)S(1)}) fusion(bf16[16,64,6,256]{3,1,2,0:T(8,128)(2,1)} %param.11), kind=kLoop, calls=%fused_computation.65 | loop fusion | bytes 786432 | tf_op jit(solution)/shard_map/slice | solution.py:212
  11.0 0.1 copy.17
  11.1 0.7 slice.73
  11.9 3.0 %collective-permute-start = (bf16[1,384,256]{2,1,0:T(8,128)(2,1)}, bf16[1,384,256]{2,1,0:T(8,128)(2,1)}, u32[]{:S(2)}, u32[]{:S(2)}) collective-permute-start(bf16[1,384,256]{2,1,0:T(8,128)(2,1)} %slice.73), channel_id=1, source_target_pairs={{0,8},{8,16},{16,24},{24,0},{1,9},{9,17},{17,25},{25,1},{2,10},{10... | collective-permute-start | bytes 589832 | tf_op jit(solution)/shard_map/ppermute | solution.py:211
  14.9 1.0 copy.18
  15.9 0.7 slice.75
  16.7 2.0 %collective-permute-start.1 = (bf16[1,384,256]{2,1,0:T(8,128)(2,1)}, bf16[1,384,256]{2,1,0:T(8,128)(2,1)S(1)}, u32[]{:S(2)}, u32[]{:S(2)}) collective-permute-start(bf16[1,384,256]{2,1,0:T(8,128)(2,1)} %slice.75), channel_id=1, source_target_pairs={{8,0},{16,8},{24,16},{0,24},{9,1},{17,9},{25,17},{1,25},{10,2},{18... | collective-permute-start | bytes 589832 | tf_op jit(solution)/shard_map/ppermute | solution.py:212
  18.7 0.0 copy-done.1
  18.7 1.8 %copy.16 = bf16[16,64,6,256]{3,0,2,1:T(8,128)(2,1)S(1)} copy(bf16[16,64,6,256]{3,1,2,0:T(8,128)(2,1)S(1)} %copy-done.1) | data formatting | bytes 6291456 | tf_op args[0]
  20.5 0.0 copy-start.7
  20.5 0.0 copy-start.6
  20.5 0.0 copy-start.4
  20.5 0.0 copy-start.3
  20.5 1.1 copy.24.rows_ref
  21.6 0.0 copy-start
  21.6 0.0 copy-done.7
  21.7 0.0 copy-done.6
  21.7 0.5 fusion.15
  22.2 0.0 copy-start.5
  22.2 0.1 fusion.17
  22.3 0.0 copy-done.4
  22.3 0.0 copy-done.3
  22.4 2.5 %broadcast_select_fusion.s_ref = bf16[16,64,324]{2,1,0:T(8,128)(2,1)} fusion(bf16[16,64,324]{2,1,0:T(8,128)(2,1)} %param.12, pred[16,324]{1,0:T(8,128)(4,1)S(1)} %fusion.17), kind=kLoop, calls=%fused_computation.21 | loop fusion | flops 331776 | bytes 1332288 | tf_op jit(solution)/shard_map/jit(_where)/select_n | solution.py:228
  24.9 0.0 collective-permute-done.top_ref
  24.9 0.7 fusion.36
  25.6 0.7 collective-permute-done.1.bottom_ref
  26.2 0.0 copy-start.2
  26.2 0.7 pad_maximum_fusion.2
  27.0 2.2 %collective-permute-start.2 = (bf16[18,6,256]{2,1,0:T(8,128)(2,1)}, bf16[18,6,256]{2,1,0:T(8,128)(2,1)S(1)}, u32[]{:S(2)}, u32[]{:S(2)}) collective-permute-start(bf16[18,6,256]{2,1,0:T(8,128)(2,1)} %pad_maximum_fusion.2), channel_id=1, source_target_pairs={{1,0},{2,1},{3,2},{4,3},{5,4},{6,5},{7,6},{0,7},{9,8},{10,9},{11,1... | collective-permute-start | bytes 165896 | tf_op jit(solution)/shard_map/ppermute | solution.py:220
  29.1 0.7 pad_maximum_fusion.3
  29.8 0.0 collective-permute-start.3
  29.8 1.8 %fusion.10 = bf16[2,2560]{1,0:T(2,128)(2,1)S(1)} fusion(s32[1024]{0:T(1024)S(1)} %convert_add_fusion, bf16[1,1024]{1,0:T(2,128)(2,1)S(1)} %stack.13, bf16[1,1024]{1,0:T(2,128)(2,1)S(1)} %stack.12), kind=kOutput, calls=%fused_computation.13 | convolution fusion | flops 13120512 | bytes 18432 | tf_op jit(solution)/shard_map/dot_general | solution.py:253
  31.6 0.0 copy-done
  31.6 0.0 copy-done.5
  31.6 1.0 copy.22.area_ref
  32.6 0.1 reshape.165
  32.7 0.1 reshape.166
  32.9 0.1 pad.12.clone
  32.9 0.0 collective-permute-done.2
  32.9 1.7 %collective-permute-done.3 = bf16[18,6,256]{2,1,0:T(8,128)(2,1)S(1)} collective-permute-done((bf16[18,6,256]{2,1,0:T(8,128)(2,1)}, bf16[18,6,256]{2,1,0:T(8,128)(2,1)S(1)}, u32[]{:S(2)}, u32[]{:S(2)}) %collective-permute-start.3) | collective-permute-done | bytes 55328 | tf_op jit(solution)/shard_map/ppermute | solution.py:219
  34.7 1.2 %pad_maximum_fusion.1.halo_ref = bf16[18,128,256]{2,1,0:T(8,128)(2,1)} fusion(bf16[18,6,256]{2,1,0:T(8,128)(2,1)S(1)} %collective-permute-done.3, bf16[18,6,256]{2,1,0:T(8,128)(2,1)S(1)} %collective-permute-done.2, bf16[128]{0:T(256)(128)(2,1)S(1)} %pad.12.clone), kind=kLoop, calls=%fused_computation.16 | loop fusion | flops 3538944 | bytes 1290496 | tf_op jit(solution)/shard_map/concatenate | solution.py:222
  35.9 0.0 copy-done.2
  35.9 12.1 %shard_map.104.rest_0_ = f32[16,384,256]{2,1,0:T(8,128)} custom-call(bf16[16,64,324]{2,1,0:T(8,128)(2,1)} %broadcast_select_fusion.s_ref, bf16[16,384,256]{2,1,0:T(8,128)(2,1)} %copy-done, bf16[1,384,256]{2,1,0:T(8,128)(2,1)} %collective-permute-done.top_ref, bf16[1,384,256]{2,1,0:T(8,128)(2,1)} %copy-done.2, bf16[18,128,256]{2,1,0:T(8,128)(2,1)} %pad_maximum_fusion.1.halo_ref), custom_call_target="tpu_custom_call" | custom-call | tf_op jit(solution)/shard_map/pallas_call | solution.py:173
  48.0 2.0 %all-gather.2.cloned.1.call-done = bf16[8192,256]{1,0:T(8,128)(2,1)} async-done(((bf16[1024,256]{1,0:T(8,128)(2,1)}), bf16[8192,256]{1,0:T(8,128)(2,1)}) %all-gather.2.cloned.1.call-update) | async-done | bytes 4194320 | tf_op jit(solution)/shard_map/all_gather | solution.py:207
  49.9 18.6 %gather_fusion = bf16[4096,256]{1,0:T(8,128)(2,1)} fusion(bf16[8192,256]{1,0:T(8,128)(2,1)} %all-gather.2.cloned.1.call-done, s32[4096]{0:T(1024)S(1)} %fusion.18), kind=kCustom, calls=%fused_computation | custom fusion | bytes 4210688 | tf_op jit(solution)/shard_map/gather | solution.py:234
  68.5 7.1 %shard_map.105 = (f32[2,1024,256]{2,1,0:T(8,128)}, bf16[1024,256]{1,0:T(8,128)(2,1)}) custom-call(s32[4,12]{1,0:T(4,128)} %near_ref.3, bf16[4,12,2,256,256]{4,3,2,1,0:T(8,128)(2,1)} %kern_ref.3, bf16[16,256,256]{2,1,0:T(8,128)(2,1)} %bitcast.22, f32[1024,1]{1,0:T(8,128)} %copy.22.area_ref), custom_call_target="tpu_custom_call" | custom-call | tf_op jit(solution)/shard_map/pallas_call | solution.py:77
  75.6 3.1 %fusion.9 = bf16[2560,256]{1,0:T(8,128)(2,1)S(1)} fusion(bf16[1024,256]{1,0:T(8,128)(2,1)} %get-tuple-element.22, s32[1024]{0:T(1024)S(1)} %convert_add_fusion), kind=kOutput, calls=%fused_computation.12 | convolution fusion | flops 1345454080 | bytes 1839104 | tf_op jit(solution)/shard_map/dot_general | solution.py:247
  78.6 1.2 %pad_maximum_fusion = bf16[8,323,256]{2,1,0:T(8,128)(2,1)} fusion(bf16[8,3,256]{2,1,0:T(4,128)(2,1)S(1)} %reshape.167, bf16[8,320,256]{2,1,0:T(8,128)(2,1)S(1)} %bitcast.27), kind=kLoop, calls=%fused_computation.15 | loop fusion | flops 2646016 | bytes 2646016 | tf_op jit(solution)/shard_map/concatenate | solution.py:262
  79.8 3.8 %all-to-all-start = ((bf16[8,323,256]{2,1,0:T(8,128)(2,1)}), bf16[8,323,256]{2,1,0:T(8,128)(2,1)S(1)}, u32[]{:S(2)}, u32[]{:S(2)}) async-start(bf16[8,323,256]{2,1,0:T(8,128)(2,1)} %pad_maximum_fusion), calls=%async_computation | async-start | bytes 2686976 | tf_op jit(solution)/shard_map/all_to_all | solution.py:264
  83.6 6.9 %shard_map.107 = f32[2,1024,256]{2,1,0:T(8,128)} custom-call(s32[4,12]{1,0:T(4,128)} %near_ref.3, bf16[4,12,2,256,256]{4,3,2,1,0:T(8,128)(2,1)} %kern_ref.3, bf16[16,256,256]{2,1,0:T(8,128)(2,1)} %bitcast.23, f32[1024,1]{1,0:T(8,128)} %copy.22.area_ref, f32[2,1024,256]{2,1,0:T(8,128)} %get-tuple-element.27.rest_0_), custom_call_target="tpu_custom_call", output_to_operand_aliasing={{}: (4, {})} | custom-call | tf_op jit(solution)/shard_map/pallas_call | solution.py:77
  90.5 12.1 %shard_map.106 = f32[16,384,256]{2,1,0:T(8,128)} custom-call(bf16[16,64,324]{2,1,0:T(8,128)(2,1)} %broadcast_select_fusion.s_ref, bf16[16,384,256]{2,1,0:T(8,128)(2,1)} %copy-done, bf16[1,384,256]{2,1,0:T(8,128)(2,1)} %collective-permute-done.top_ref, bf16[1,384,256]{2,1,0:T(8,128)(2,1)} %copy-done.2, ...), custom_call_target="tpu_custom_call", output_to_operand_aliasing={{}: (5, {})} | custom-call | tf_op jit(solution)/shard_map/pallas_call | solution.py:173
  102.6 0.0 all-to-all-done
  102.6 0.1 reshape.171
  102.7 0.1 fusion.21
  102.8 0.1 convert_element_type.42
  102.8 0.1 slice.102
  102.9 3.8 %fusion.16 = f32[16,384,256]{2,1,0:T(8,128)} fusion(f32[16,384,256]{2,1,0:T(8,128)} %shard_map.106, bf16[2560,256,1]{1,0,2:T(8,128)(2,1)S(1)} %bitcast.26, s32[16,64]{1,0:T(8,128)S(1)} %multiply_add_fusion, s32[2560]{0:T(1024)S(1)} %convert_element_type.42), kind=kOutput, calls=%fused_computation.20 | convolution fusion | flops 1345323008 | bytes 3422208 | tf_op jit(solution)/shard_map/dot_general | solution.py:280
  (18 shorter events, 0.2 us)
Async XLA Ops:
  7.2 11.6 %copy-start.1 = (bf16[16,64,6,256]{3,1,2,0:T(8,128)(2,1)S(1)}, bf16[16,64,6,256]{3,1,2,0:T(8,128)(2,1)}, u32[]{:S(2)}) copy-start(bf16[16,64,6,256]{3,1,2,0:T(8,128)(2,1)} %param.11) | copy-start | bytes 9437188
  7.2 42.8 %all-gather.2.cloned.1.call-start = ((), (), s32[]{:S(2)}) async-start(), calls=%async_computation.1 | async-start | bytes 4718592 | tf_op jit(solution)/shard_map/all_gather | solution.py:207
  11.9 13.0 %collective-permute-start = (bf16[1,384,256]{2,1,0:T(8,128)(2,1)}, bf16[1,384,256]{2,1,0:T(8,128)(2,1)}, u32[]{:S(2)}, u32[]{:S(2)}) collective-permute-start(bf16[1,384,256]{2,1,0:T(8,128)(2,1)} %slice.73), channel_id=1, source_target_pairs={{0,8},{8,16},{16,24},{24,0},{1,9},{9,17},{17,25},{25,1},{2,10},{10... | collective-permute-start | bytes 589832 | tf_op jit(solution)/shard_map/ppermute | solution.py:211
  16.7 9.6 %collective-permute-start.1 = (bf16[1,384,256]{2,1,0:T(8,128)(2,1)}, bf16[1,384,256]{2,1,0:T(8,128)(2,1)S(1)}, u32[]{:S(2)}, u32[]{:S(2)}) collective-permute-start(bf16[1,384,256]{2,1,0:T(8,128)(2,1)} %slice.75), channel_id=1, source_target_pairs={{8,0},{16,8},{24,16},{0,24},{9,1},{17,9},{25,17},{1,25},{10,2},{18... | collective-permute-start | bytes 589832 | tf_op jit(solution)/shard_map/ppermute | solution.py:212
  20.5 1.2 %copy-start.7 = (s32[1024]{0:T(1024)S(1)}, s32[1024]{0:T(1024)}, u32[]{:S(2)}) copy-start(s32[1024]{0:T(1024)} %param.19) | copy-start | bytes 12292
  20.5 1.2 %copy-start.6 = (s32[1024,1]{0,1:T(1,128)S(1)}, s32[1024,1]{0,1:T(1,128)}, u32[]{:S(2)}) copy-start(s32[1024,1]{0,1:T(1,128)} %param.18) | copy-start | bytes 12292
  20.5 1.8 %copy-start.4 = (s32[4096,1]{0,1:T(1,128)S(1)}, s32[4096,1]{0,1:T(1,128)}, u32[]{:S(2)}) copy-start(s32[4096,1]{0,1:T(1,128)} %param.16) | copy-start | bytes 49156
  20.5 1.8 %copy-start.3 = (s32[4096]{0:T(1024)S(1)}, s32[4096]{0:T(1024)}, u32[]{:S(2)}) copy-start(s32[4096]{0:T(1024)} %param.17) | copy-start | bytes 49156
  21.6 10.0 %copy-start = (bf16[16,384,256]{2,1,0:T(8,128)(2,1)}, bf16[16,384,256]{2,1,0:T(8,128)(2,1)S(1)}, u32[]{:S(2)}) copy-start(bf16[16,384,256]{2,1,0:T(8,128)(2,1)S(1)} %copy.24.rows_ref) | copy-start | bytes 9437188
  22.2 9.4 %copy-start.5 = (f32[1024]{0:T(1024)S(1)}, f32[1024]{0:T(1024)}, u32[]{:S(2)}) copy-start(f32[1024]{0:T(1024)} %param.14) | copy-start | bytes 12292
  26.2 9.7 %copy-start.2 = (bf16[1,384,256]{2,1,0:T(8,128)(2,1)}, bf16[1,384,256]{2,1,0:T(8,128)(2,1)S(1)}, u32[]{:S(2)}) copy-start(bf16[1,384,256]{2,1,0:T(8,128)(2,1)S(1)} %collective-permute-done.1.bottom_ref) | copy-start | bytes 589828
  27.0 6.0 %collective-permute-start.2 = (bf16[18,6,256]{2,1,0:T(8,128)(2,1)}, bf16[18,6,256]{2,1,0:T(8,128)(2,1)S(1)}, u32[]{:S(2)}, u32[]{:S(2)}) collective-permute-start(bf16[18,6,256]{2,1,0:T(8,128)(2,1)} %pad_maximum_fusion.2), channel_id=1, source_target_pairs={{1,0},{2,1},{3,2},{4,3},{5,4},{6,5},{7,6},{0,7},{9,8},{10,9},{11,1... | collective-permute-start | bytes 165896 | tf_op jit(solution)/shard_map/ppermute | solution.py:220
  29.8 4.9 %collective-permute-start.3 = (bf16[18,6,256]{2,1,0:T(8,128)(2,1)}, bf16[18,6,256]{2,1,0:T(8,128)(2,1)S(1)}, u32[]{:S(2)}, u32[]{:S(2)}) collective-permute-start(bf16[18,6,256]{2,1,0:T(8,128)(2,1)} %pad_maximum_fusion.3), channel_id=1, source_target_pairs={{0,1},{1,2},{2,3},{3,4},{4,5},{5,6},{6,7},{7,0},{8,9},{9,10},{10,1... | collective-permute-start | bytes 165896 | tf_op jit(solution)/shard_map/ppermute | solution.py:219
  79.8 22.8 %all-to-all-start = ((bf16[8,323,256]{2,1,0:T(8,128)(2,1)}), bf16[8,323,256]{2,1,0:T(8,128)(2,1)S(1)}, u32[]{:S(2)}, u32[]{:S(2)}) async-start(bf16[8,323,256]{2,1,0:T(8,128)(2,1)} %pad_maximum_fusion), calls=%async_computation | async-start | bytes 2686976 | tf_op jit(solution)/shard_map/all_to_all | solution.py:264
Sparse Core Ops, SparseCore 0:
  10.5 39.4 all-gather.1
